TPU v7x, 32 devices: a whole 2x2x4 slice. The times are simulated.
32 devices in a mesh: grp: 2 (over y), seq: 8 (over z, x), outer: 2 (over core).
Axes of the slice: x: 2, y: 2, z: 4, core: 2. Of those that a mesh axis runs over, the one named last changes fastest.
Arguments:
- keys: bfloat16 [4096, 512], P(('grp', 'seq', 'outer')), parts along dimension 0, may hold values from -6 to 6
- values: bfloat16 [4096, 512], P(('grp', 'seq', 'outer')), parts along dimension 0, may hold values from -6 to 6
- queries: bfloat16 [4096, 512], P(('grp', 'seq', 'outer')), parts along dimension 0, may hold values from -6 to 6
- learn_rate: float32 [4096], P(('grp', 'seq', 'outer')), parts along dimension 0, may hold values from 0.0006629126 to 0.006629126
- w_gate: bfloat16 [1024, 512], P('grp'), parts along dimension 0, may hold values from -0.25 to 0.25
- w_up: bfloat16 [1024, 512], P('grp'), parts along dimension 0, may hold values from -0.25 to 0.25
- w_out: bfloat16 [1024, 512], P('grp'), parts along dimension 0, may hold values from -0.25 to 0.25
Outputs:
- output: bfloat16 [4096, 512], P(('grp', 'seq', 'outer')), parts along dimension 0
There are 2 independent parts, one for each index of `grp`. A program takes and returns all parts, laid end to end along the dimension named above; each array names one. Nothing has to cross between parts.
All inputs are finite; a program needn't handle non-finite values.
Results may differ from a plain program's by a relative error of at most 0.0098.
Values may be sent and summed in bfloat16 or wider, within the bound.
No kernel may reach another device: no remote copies, remote signals or barrier semaphores. Data moves between devices by JAX's collectives and lax.ppermute only.
A program may use at most 64 MiB of HBM per device.

v0:
```python
import jax
import jax.numpy as jnp
from jax import lax
from jax.sharding import PartitionSpec as P

epsilon = 1e-06


def silu_grad(inputs):
    sigma = jax.nn.sigmoid(inputs)
    return sigma * (1.0 + inputs * (1.0 - sigma))


def renorm(weight, grads):
    old = weight.astype(jnp.float32)
    update = old + grads
    factor = jnp.sqrt(jnp.mean(old * old, axis=1, keepdims=True) + epsilon) / jnp.sqrt(
        jnp.mean(update * update, axis=1, keepdims=True) + epsilon
    )
    return (update * factor).astype(jnp.bfloat16)


def local(keys, values, queries, learn_rate, w_gate, w_up, w_out):
    hidden = w_gate.shape[1]
    shards = lax.axis_size(("seq", "outer"))
    rows_gate = w_gate.shape[0] // shards
    rows_out = w_out.shape[0] // shards
    position = lax.axis_index(("seq", "outer"))
    contract_last = (((1,), (1,)), ((), ()))
    contract_first = (((0,), (0,)), ((), ()))
    scaled = (learn_rate[:, None] * values.astype(jnp.float32)).astype(jnp.bfloat16)
    gate_pre = jnp.dot(keys, w_gate, preferred_element_type=jnp.float32)
    up_pre = jnp.dot(keys, w_up, preferred_element_type=jnp.float32)
    back_grad = lax.dot_general(scaled, w_out, contract_last, preferred_element_type=jnp.float32)
    activation = (jax.nn.silu(gate_pre) * up_pre).astype(jnp.bfloat16)
    d_gate = (back_grad * up_pre * silu_grad(gate_pre)).astype(jnp.bfloat16)
    d_up = (back_grad * jax.nn.silu(gate_pre)).astype(jnp.bfloat16)
    both_grads = jnp.concatenate([d_gate, d_up], axis=1)
    full_in = lax.dot_general(keys, both_grads, contract_first, preferred_element_type=jnp.float32)
    full_out = lax.dot_general(
        activation, scaled, contract_first, preferred_element_type=jnp.float32
    )
    grad_in = lax.psum_scatter(full_in, ("seq", "outer"), scatter_dimension=0, tiled=True)
    grad_out = lax.psum_scatter(full_out, ("seq", "outer"), scatter_dimension=0, tiled=True)
    own_gate = lax.dynamic_slice_in_dim(w_gate, position * rows_gate, rows_gate, 0)
    own_up = lax.dynamic_slice_in_dim(w_up, position * rows_gate, rows_gate, 0)
    own_out = lax.dynamic_slice_in_dim(w_out, position * rows_out, rows_out, 0)
    new_gate = renorm(own_gate, grad_in[:, :hidden])
    new_up = renorm(own_up, grad_in[:, hidden:])
    new_out = renorm(own_out, grad_out)
    full_gate, full_up, full_out_w = (
        lax.all_gather(new_gate, ("seq", "outer"), axis=0, tiled=True),
        lax.all_gather(new_up, ("seq", "outer"), axis=0, tiled=True),
        lax.all_gather(new_out, ("seq", "outer"), axis=0, tiled=True),
    )
    q_gate = jnp.dot(queries, full_gate, preferred_element_type=jnp.float32)
    q_up = jnp.dot(queries, full_up, preferred_element_type=jnp.float32)
    q_act = (jax.nn.silu(q_gate) * q_up).astype(jnp.bfloat16)
    return jnp.dot(q_act, full_out_w, preferred_element_type=jnp.float32).astype(jnp.bfloat16)


def solution(mesh):
    placed = (
        P(("grp", "seq", "outer"), None),
        P(("grp", "seq", "outer"), None),
        P(("grp", "seq", "outer"), None),
        P(("grp", "seq", "outer")),
        P("grp", None),
        P("grp", None),
        P("grp", None),
    )
    return jax.shard_map(
        local,
        mesh=mesh,
        in_specs=placed,
        out_specs=P(("grp", "seq", "outer"), None),
        check_vma=False,
    )
```

profile of v0, /device:TPU:0, one launch (start us, length us, event | category | flops | bytes accessed | tf_op | source)
XLA Modules:
  0.0 187.8 jit_solution(12545988453108368266)
XLA Ops:
  6.5 0.0 copy-start
  6.5 0.0 copy-start.3
  6.5 0.0 copy-start.1
  6.5 0.0 reduce-scatter.5.cloned.1.call-start
  6.5 0.9 copy-done
  7.4 1.3 fusion.21
  8.7 1.4 fusion.16
  10.2 1.4 multiply_convert_fusion.2
  11.5 0.0 copy-done.3
  11.5 0.0 copy-done.1
  11.6 1.3 fusion.11
  12.9 0.0 reduce-scatter.5.cloned.1.call-update
  12.9 0.0 reduce-scatter.7.cloned.1.call-start
  13.0 0.5 convolution_bitcast_fusion
  13.4 1.9 %copy.22 = f32[512,1024]{1,0:T(8,128)} copy(f32[512,1024]{0,1:T(8,128)S(1)} %convolution_bitcast_fusion) | data formatting | bytes 4194304
  15.3 0.0 copy-start.2
  15.3 0.0 reduce-scatter.7.cloned.1.call-update
  15.3 57.8 %reduce-scatter.5.cloned.1.call-done = f32[32,512]{1,0:T(8,128)} async-done(((f32[512,512]{1,0:T(8,128)}), f32[32,512]{1,0:T(8,128)}) %reduce-scatter.5.cloned.1.call-update) | async-done | bytes 65552 | tf_op jit(solution)/shard_map/reduce_scatter | solution.py:44
  73.1 1.0 fusion.15
  74.1 0.9 multiply_convert_fusion.5
  75.0 20.9 %all_gather.11 = bf16[512,512]{1,0:T(8,128)(2,1)S(1)} all-gather(bf16[32,512]{1,0:T(8,128)(2,1)S(1)} %multiply_convert_fusion.5), channel_id=1, replica_groups=mesh['grp'=2,'seq'=8,'outer'=2] {'seq','outer'}, dimensions={0}, use_global_device_ids=true | all-gather | bytes 557056 | tf_op jit(solution)/shard_map/all_gather | solution.py:54
  95.9 42.1 %reduce-scatter.7.cloned.1.call-done = f32[32,1024]{1,0:T(8,128)} async-done(((f32[512,1024]{1,0:T(8,128)}), f32[32,1024]{1,0:T(8,128)}) %reduce-scatter.7.cloned.1.call-update) | async-done | bytes 131088 | tf_op jit(solution)/shard_map/reduce_scatter | solution.py:43
  138.0 1.1 fusion.13
  139.1 1.0 multiply_convert_fusion.7
  140.0 20.8 %all_gather.9 = bf16[512,512]{1,0:T(8,128)(2,1)S(1)} all-gather(bf16[32,512]{1,0:T(8,128)(2,1)S(1)} %get-tuple-element.13), channel_id=1, replica_groups=mesh['grp'=2,'seq'=8,'outer'=2] {'seq','outer'}, dimensions={0}, use_global_device_ids=true | all-gather | bytes 557056 | tf_op jit(solution)/shard_map/all_gather | solution.py:52
  160.8 18.9 %all_gather.10 = bf16[512,512]{1,0:T(8,128)(2,1)S(1)} all-gather(bf16[32,512]{1,0:T(8,128)(2,1)S(1)} %get-tuple-element.14), channel_id=1, replica_groups=mesh['grp'=2,'seq'=8,'outer'=2] {'seq','outer'}, dimensions={0}, use_global_device_ids=true | all-gather | bytes 557056 | tf_op jit(solution)/shard_map/all_gather | solution.py:53
  179.7 0.0 copy-done.2
  179.7 0.2 convolution_bitcast_fusion.2
  179.9 1.1 convolution_convert_fusion
  (2 shorter events, 0.0 us)
Async XLA Ops:
  6.5 0.9 copy-start
  6.5 5.0 %copy-start.3 = (f32[128]{0:T(128)S(1)}, f32[128]{0:T(128)}, u32[]{:S(2)}) copy-start(f32[128]{0:T(128)} %param.10) | copy-start | bytes 1540
  6.5 5.0 %copy-start.1 = (bf16[128,512]{1,0:T(8,128)(2,1)S(1)}, bf16[128,512]{1,0:T(8,128)(2,1)}, u32[]{:S(2)}) copy-start(bf16[128,512]{1,0:T(8,128)(2,1)} %param.8) | copy-start | bytes 393220
  6.5 66.6 %reduce-scatter.5.cloned.1.call-start = ((), (), s32[]{:S(2)}) async-start(), calls=%async_computation.2 | async-start | bytes 1114112 | tf_op jit(solution)/shard_map/reduce_scatter | solution.py:44
  12.9 125.0 %reduce-scatter.7.cloned.1.call-start = ((), (), s32[]{:S(2)}) async-start(), calls=%async_computation.3 | async-start | bytes 2228224 | tf_op jit(solution)/shard_map/reduce_scatter | solution.py:43
  15.3 164.4 %copy-start.2 = (bf16[128,512]{1,0:T(8,128)(2,1)S(1)}, bf16[128,512]{1,0:T(8,128)(2,1)}, u32[]{:S(2)}) copy-start(bf16[128,512]{1,0:T(8,128)(2,1)} %param.9) | copy-start | bytes 393220
Sparse Core Ops, SparseCore 0:
  13.1 60.0 reduce-scatter.4
  77.3 60.6 reduce-scatter.6
where the time goes:
time: 188 us
  waiting for transfers between devices  99.9 us (53%)
  blocking collectives  60.6 us (32%)
  between operations  13.5 us (7%)
  matrix products  7.17 us (4%)
  other arithmetic  3.95 us (2%)
  local copies, waits for them, and re-layouts  2.78 us (1%)
    reduce_scatter x1, waiting for transfers between devices, local(): lax.psum_scatter(full_out, ('seq', 'outer'), scatter_dimension=0, tiled=T...  57.8 us
    reduce_scatter x1, waiting for transfers between devices, local(): lax.psum_scatter(full_in, ('seq', 'outer'), scatter_dimension=0, tiled=True)  42.1 us
    all_gather x1, blocking collectives, local(): lax.all_gather(new_out, ('seq', 'outer'), axis=0, tiled=True)  20.9 us
    all_gather x1, blocking collectives, local(): lax.all_gather(new_gate, ('seq', 'outer'), axis=0, tiled=True)  20.8 us
    all_gather x1, blocking collectives, local(): lax.all_gather(new_up, ('seq', 'outer'), axis=0, tiled=True)  18.9 us
  transfers between devices with their start and end apart: 2, of which 2 were waited for; matrix products, arithmetic and copies ran while one was open for 2% of the time, Pallas kernels for 0%

commit v1 on v0

v1 whole, which is shorter than its diff:
```python
import jax
import jax.numpy as jnp
from jax import lax
from jax.sharding import PartitionSpec as P

epsilon = 1e-06
GATHER_LIMIT_BYTES = 16 * 1024 * 1024


def silu_grad(inputs):
    sigma = jax.nn.sigmoid(inputs)
    return sigma * (1.0 + inputs * (1.0 - sigma))


def renorm(weight, grads):
    old = weight.astype(jnp.float32)
    update = old + grads
    factor = jnp.sqrt(jnp.mean(old * old, axis=1, keepdims=True) + epsilon) / jnp.sqrt(
        jnp.mean(update * update, axis=1, keepdims=True) + epsilon
    )
    return (update * factor).astype(jnp.bfloat16)


contract_last = (((1,), (1,)), ((), ()))
contract_first = (((0,), (0,)), ((), ()))


def gradients(keys, scaled, w_gate, w_up, w_out):
    gate_pre = jnp.dot(keys, w_gate, preferred_element_type=jnp.float32)
    up_pre = jnp.dot(keys, w_up, preferred_element_type=jnp.float32)
    back_grad = lax.dot_general(scaled, w_out, contract_last, preferred_element_type=jnp.float32)
    activation = (jax.nn.silu(gate_pre) * up_pre).astype(jnp.bfloat16)
    d_gate = (back_grad * up_pre * silu_grad(gate_pre)).astype(jnp.bfloat16)
    d_up = (back_grad * jax.nn.silu(gate_pre)).astype(jnp.bfloat16)
    both_grads = jnp.concatenate([d_gate, d_up], axis=1)
    full_in = lax.dot_general(keys, both_grads, contract_first, preferred_element_type=jnp.float32)
    full_out = lax.dot_general(activation, scaled, contract_first, preferred_element_type=jnp.float32)
    return full_in, full_out


def apply(queries, full_gate, full_up, full_out_w):
    q_gate = jnp.dot(queries, full_gate, preferred_element_type=jnp.float32)
    q_up = jnp.dot(queries, full_up, preferred_element_type=jnp.float32)
    q_act = (jax.nn.silu(q_gate) * q_up).astype(jnp.bfloat16)
    return jnp.dot(q_act, full_out_w, preferred_element_type=jnp.float32).astype(jnp.bfloat16)


def local_gather(keys, values, queries, learn_rate, w_gate, w_up, w_out):
    hidden = w_gate.shape[1]
    shards = lax.axis_size(("seq", "outer"))
    rows = keys.shape[0]
    width = keys.shape[1]
    scaled = (learn_rate[:, None] * values.astype(jnp.float32)).astype(jnp.bfloat16)
    both = jnp.concatenate([keys, scaled], axis=0)
    full = lax.all_gather(both, ("seq", "outer"), axis=0, tiled=True)
    full = full.reshape(shards, 2, rows, width)
    all_keys = full[:, 0].reshape(shards * rows, width)
    all_scaled = full[:, 1].reshape(shards * rows, width)
    full_in, full_out = gradients(all_keys, all_scaled, w_gate, w_up, w_out)
    new_gate = renorm(w_gate, full_in[:, :hidden])
    new_up = renorm(w_up, full_in[:, hidden:])
    new_out = renorm(w_out, full_out)
    return apply(queries, new_gate, new_up, new_out)


def local_scatter(keys, values, queries, learn_rate, w_gate, w_up, w_out):
    hidden = w_gate.shape[1]
    shards = lax.axis_size(("seq", "outer"))
    rows_gate = w_gate.shape[0] // shards
    rows_out = w_out.shape[0] // shards
    position = lax.axis_index(("seq", "outer"))
    scaled = (learn_rate[:, None] * values.astype(jnp.float32)).astype(jnp.bfloat16)
    full_in, full_out = gradients(keys, scaled, w_gate, w_up, w_out)
    grad_in = lax.psum_scatter(full_in, ("seq", "outer"), scatter_dimension=0, tiled=True)
    grad_out = lax.psum_scatter(full_out, ("seq", "outer"), scatter_dimension=0, tiled=True)
    own_gate = lax.dynamic_slice_in_dim(w_gate, position * rows_gate, rows_gate, 0)
    own_up = lax.dynamic_slice_in_dim(w_up, position * rows_gate, rows_gate, 0)
    own_out = lax.dynamic_slice_in_dim(w_out, position * rows_out, rows_out, 0)
    new_gate = renorm(own_gate, grad_in[:, :hidden])
    new_up = renorm(own_up, grad_in[:, hidden:])
    new_out = renorm(own_out, grad_out)
    full_gate, full_up, full_out_w = (
        lax.all_gather(new_gate, ("seq", "outer"), axis=0, tiled=True),
        lax.all_gather(new_up, ("seq", "outer"), axis=0, tiled=True),
        lax.all_gather(new_out, ("seq", "outer"), axis=0, tiled=True),
    )
    return apply(queries, full_gate, full_up, full_out_w)


def solution(mesh):
    placed = (
        P(("grp", "seq", "outer"), None),
        P(("grp", "seq", "outer"), None),
        P(("grp", "seq", "outer"), None),
        P(("grp", "seq", "outer")),
        P("grp", None),
        P("grp", None),
        P("grp", None),
    )
    shards = mesh.shape["seq"] * mesh.shape["outer"]

    def run(keys, values, queries, learn_rate, w_gate, w_up, w_out):
        per_part = keys.shape[0] // mesh.shape["grp"]
        gathered_bytes = 2 * per_part * keys.shape[1] * keys.dtype.itemsize
        body = local_gather if gathered_bytes <= GATHER_LIMIT_BYTES else local_scatter
        return jax.shard_map(
            body,
            mesh=mesh,
            in_specs=placed,
            out_specs=P(("grp", "seq", "outer"), None),
            check_vma=False,
        )(keys, values, queries, learn_rate, w_gate, w_up, w_out)

    del shards
    return run
```

time: 188 us -> 87.7 us (0.47)
  blocking collectives: 60.6 us -> 0 us
  waiting for transfers between devices: 99.9 us -> 52.2 us
  matrix products: 7.17 us -> 14.5 us
    reduce_scatter x2 -> x0, waiting for transfers between devices: 99.8 us -> none  [the longest x1 57.8 us: local(): lax.psum_scatter(full_out, ('seq', 'outer'), scatter_dimension=0, tiled=T...]
    all_gather x3 -> x0, blocking collectives: 60.6 us -> none  [the longest x1 20.9 us: local(): lax.all_gather(new_out, ('seq', 'outer'), axis=0, tiled=True)]
    all_gather x0 -> x1, waiting for transfers between devices: none -> 52.2 us  [local_gather(): full = lax.all_gather(both, ('seq', 'outer'), axis=0, tiled=True)]
    dot_general x7, matrix products: 7.17 us -> 14.5 us  [the longest x1 3.54 us: gradients(): gate_pre = jnp.dot(keys, w_gate, preferred_element_type=jnp.float32)]
    slice x0 -> x1, local copies, waits for them, and re-layouts: none -> 2.73 us  [local_gather(): all_scaled = full[:, 1].reshape(shards * rows, width)]
    reduce_sum x2 -> x1, other arithmetic: 2.04 us -> 0.15 us  [renorm(): jnp.mean(old * old, axis=1, keepdims=True) + epsilon]
  transfers between devices with their start and end apart: 2 -> 1, of which waited for: 2 -> 1; matrix products, arithmetic and copies ran while one was open for 2% -> 2% of each run, Pallas kernels for 0% -> 0%
where the time goes in v1:
time: 87.7 us; the launch traced here: 87.5 us
  waiting for transfers between devices  52.2 us (60%)
  matrix products  14.5 us (17%)
  between operations  13.5 us (15%)
  local copies, waits for them, and re-layouts  4.01 us (5%)
  other arithmetic  3.33 us (4%)
    all_gather x1, waiting for transfers between devices, local_gather(): full = lax.all_gather(both, ('seq', 'outer'), axis=0, tiled=True)  52.2 us
    dot_general x1, matrix products, gradients(): gate_pre = jnp.dot(keys, w_gate, preferred_element_type=jnp.float32)  3.54 us
    dot_general x1, matrix products, apply(): jnp.dot(q_act, full_out_w, preferred_element_type=jnp.float32)  2.75 us
    slice x1, local copies, waits for them, and re-layouts, local_gather(): all_scaled = full[:, 1].reshape(shards * rows, width)  2.73 us
    dot_general x1, matrix products, gradients(): lax.dot_general(activation, scaled, contract_first, preferred_element_typ...  2.7 us
    dot_general x1, matrix products, gradients(): lax.dot_general(keys, both_grads, contract_first, preferred_element_type=...  2.38 us
  transfers between devices with their start and end apart: 1, of which 1 were waited for; matrix products, arithmetic and copies ran while one was open for 2% of the time, Pallas kernels for 0%

profile of v1, /device:TPU:0, one launch (start us, length us, event | category | flops | bytes accessed | tf_op | source)
XLA Modules:
  0.0 87.5 jit_solution(6934133537905628567)
XLA Ops:
  6.5 0.0 copy-start
  6.5 0.0 all-gather.2.cloned.1.call-start
  6.5 1.0 %multiply_convert_fusion.13 = bf16[128,512]{1,0:T(8,128)(2,1)S(1)} fusion(bf16[128,512]{1,0:T(8,128)(2,1)} %param.8, f32[128]{0:T(128)} %param.10), kind=kLoop, calls=%fused_computation.39 | loop fusion | flops 196608 | bytes 262656 | tf_op jit(solution)/shard_map/convert_element_type | solution.py:53
  7.6 1.6 %pad_maximum_fusion = bf16[256,512]{1,0:T(8,128)(2,1)} fusion(bf16[128,512]{1,0:T(8,128)(2,1)S(1)} %multiply_convert_fusion.13, bf16[128,512]{1,0:T(8,128)(2,1)} %param.7), kind=kLoop, calls=%fused_computation.33 | loop fusion | flops 524288 | bytes 524288 | tf_op jit(solution)/shard_map/concatenate | solution.py:54
  9.2 0.0 all-gather.2.cloned.1.call-update
  9.2 1.3 %copy.8 = bf16[512,512]{0,1:T(8,128)(2,1)S(1)} copy(bf16[512,512]{1,0:T(8,128)(2,1)} %param.13) | data formatting | bytes 1048576 | tf_op args[6]
  10.5 0.2 fusion.10
  10.6 52.2 %all-gather.2.cloned.1.call-done = bf16[4096,512]{1,0:T(8,128)(2,1)} async-done(((bf16[256,512]{1,0:T(8,128)(2,1)}), bf16[4096,512]{1,0:T(8,128)(2,1)}) %all-gather.2.cloned.1.call-update) | async-done | bytes 4194320 | tf_op jit(solution)/shard_map/all_gather | solution.py:55
  62.8 0.0 copy-start.2
  62.8 2.7 %fusion.25 = (bf16[16,1,128,512]{3,2,1,0:T(8,128)(2,1)S(1)}, bf16[16,1,128,512]{3,2,1,0:T(8,128)(2,1)S(1)}) fusion(bf16[16,2,128,512]{3,2,1,0:T(8,128)(2,1)} %bitcast.28), kind=kLoop, calls=%fused_computation.47 | loop fusion | bytes 8388608 | tf_op jit(solution)/shard_map/slice | solution.py:58
  65.6 0.0 copy-done.2
  65.6 0.0 copy-start.1
  65.6 1.3 %fusion.26 = f32[2048,512]{0,1:T(8,128)S(1)} fusion(bf16[2048,512]{1,0:T(8,128)(2,1)S(1)} %bitcast.26, bf16[512,512]{1,0:T(8,128)(2,1)S(1)} %copy-done.2), kind=kOutput, calls=%fused_computation.48 | convolution fusion | flops 1073741824 | bytes 6815744 | tf_op jit(solution)/shard_map/dot_general | solution.py:31
  66.9 0.0 copy-done.1
  66.9 0.0 copy-start.3
  66.9 1.3 %fusion.27 = f32[2048,512]{0,1:T(8,128)S(1)} fusion(bf16[2048,512]{1,0:T(8,128)(2,1)S(1)} %bitcast.23, bf16[512,512]{1,0:T(8,128)(2,1)S(1)} %copy-done.1), kind=kOutput, calls=%fused_computation.49 | convolution fusion | flops 1073741824 | bytes 6815744 | tf_op jit(solution)/shard_map/dot_general | solution.py:30
  68.2 0.0 copy-done.3
  68.2 3.5 %multiply_convert_fusion.2 = (bf16[2048,512]{0,1:T(8,128)(2,1)S(1)}, bf16[2048,512]{0,1:T(8,128)(2,1)S(1)}, f32[2048,512]{0,1:T(8,128)S(1)}) fusion(f32[2048,512]{0,1:T(8,128)S(1)} %fusion.26, f32[2048,512]{0,1:T(8,128)S(1)} %fusion.27, bf16[2048,512]{1,0:T(8,128)(2,1)S(1)} %bitcast.24, bf16[512,512]{1,0:T(8,128)(2,1)S(1)} %copy-done.3), kind=kOutput, calls=%fused_computation.6 | convolution fusion | flops 1087373312 | bytes 19398656 | tf_op jit(solution)/shard_map/dot_general | solution.py:29
  71.8 2.7 %multiply_reduce_fusion = (f32[512]{0:T(512)S(1)}, f32[512,512]{0,1:T(8,128)}) fusion(bf16[2048,512]{1,0:T(8,128)(2,1)S(1)} %bitcast.27, f32[2048,512]{0,1:T(8,128)S(1)} %fusion.27, f32[2048,512]{0,1:T(8,128)S(1)} %get-tuple-element.13, bf16[512,512]{0,1:T(8,128)(2,1)S(1)} %copy.8), kind=kOutput, calls=%fused_computation.25 | convolution fusion | flops 1081081344 | bytes 12060672 | tf_op jit(solution)/shard_map/dot_general | solution.py:37
  74.5 2.4 %fusion = f32[512,1024]{1,0:T(8,128)S(1)} fusion(bf16[2048,512]{1,0:T(8,128)(2,1)S(1)} %bitcast.25, bf16[2048,512]{0,1:T(8,128)(2,1)S(1)} %get-tuple-element.10, bf16[2048,512]{0,1:T(8,128)(2,1)S(1)} %get-tuple-element.9), kind=kOutput, calls=%fused_computation | convolution fusion | flops 2155872256 | bytes 8388608 | tf_op jit(solution)/shard_map/dot_general | solution.py:36
  76.9 0.5 multiply_reduce_fusion.2
  77.4 0.0 copy-done
  77.4 0.5 convolution_bitcast_fusion.1
  77.9 2.7 %convolution_convert_fusion = bf16[128,512]{1,0:T(8,128)(2,1)} fusion(bf16[128,512]{1,0:T(8,128)(2,1)S(1)} %copy-done, f32[512,1024]{1,0:T(8,128)S(1)} %fusion, bf16[512,512]{1,0:T(8,128)(2,1)S(1)} %copy-done.1, f32[512,512]{0,1:T(8,128)} %get-tuple-element.15, f32[512]{0:T(512)S(1)} %rsqrt_multiply_fusion, f32[512]{0:T(512)S(1)} %get-tuple-element.16, ...), kind=kOutput, calls=%fused_computation.20 | convolution fusion | flops 136249344 | bytes 3149824 | tf_op jit(solution)/shard_map/dot_general | solution.py:45
  (2 shorter events, 0.0 us)
Async XLA Ops:
  6.5 70.9 %copy-start = (bf16[128,512]{1,0:T(8,128)(2,1)S(1)}, bf16[128,512]{1,0:T(8,128)(2,1)}, u32[]{:S(2)}) copy-start(bf16[128,512]{1,0:T(8,128)(2,1)} %param.9) | copy-start | bytes 393220
  6.5 56.3 %all-gather.2.cloned.1.call-start = ((), (), s32[]{:S(2)}) async-start(), calls=%async_computation | async-start | bytes 4456448 | tf_op jit(solution)/shard_map/all_gather | solution.py:55
  62.8 2.7 %copy-start.2 = (bf16[512,512]{1,0:T(8,128)(2,1)S(1)}, bf16[512,512]{1,0:T(8,128)(2,1)}, u32[]{:S(2)}) copy-start(bf16[512,512]{1,0:T(8,128)(2,1)} %param.13) | copy-start | bytes 1572868
  65.6 1.3 %copy-start.1 = (bf16[512,512]{1,0:T(8,128)(2,1)S(1)}, bf16[512,512]{1,0:T(8,128)(2,1)}, u32[]{:S(2)}) copy-start(bf16[512,512]{1,0:T(8,128)(2,1)} %param.12) | copy-start | bytes 1572868
  66.9 1.3 %copy-start.3 = (bf16[512,512]{1,0:T(8,128)(2,1)S(1)}, bf16[512,512]{1,0:T(8,128)(2,1)}, u32[]{:S(2)}) copy-start(bf16[512,512]{1,0:T(8,128)(2,1)} %param.11) | copy-start | bytes 1572868
Sparse Core Ops, SparseCore 0:
  9.5 53.2 all-gather.1

commit v2 on v1

--- a/solution.py
+++ b/solution.py
@@ -87,6 +87,75 @@
     return apply(queries, full_gate, full_up, full_out_w)
 
 
+def chip_ring(mesh):
+    seq = mesh.shape["seq"]
+    try:
+        places = [tuple(mesh.devices[0, s, 0].coords) for s in range(seq)]
+    except (AttributeError, TypeError):
+        return None
+    columns = sorted({p[0] for p in places})
+    if len(columns) != 2 or len({p[1] for p in places}) != 1:
+        return None
+    first = sorted((p[2], s) for s, p in enumerate(places) if p[0] == columns[0])
+    second = sorted((p[2], s) for s, p in enumerate(places) if p[0] == columns[1])
+    return [s for _, s in first] + [s for _, s in reversed(second)]
+
+
+def add_grads(total, keys_part, scaled_part, w_gate, w_up, w_out):
+    full_in, full_out = gradients(keys_part, scaled_part, w_gate, w_up, w_out)
+    if total is None:
+        return full_in, full_out
+    return total[0] + full_in, total[1] + full_out
+
+
+def make_local_ring(ring):
+    chips = len(ring)
+    cw_perm = []
+    ccw_perm = []
+    for p in range(chips):
+        for c in range(2):
+            cw_perm.append((ring[p] * 2 + c, ring[(p + 1) % chips] * 2 + c))
+            ccw_perm.append((ring[p] * 2 + c, ring[(p - 1) % chips] * 2 + c))
+    swap = [(i, i ^ 1) for i in range(chips * 2)]
+    cw_steps = chips // 2
+    ccw_steps = (chips - 1) // 2
+    axes = ("seq", "outer")
+
+    def split(chunks):
+        rows = chunks[0].shape[0] // 2
+        keys_part = jnp.concatenate([ch[:rows] for ch in chunks], axis=0)
+        scaled_part = jnp.concatenate([ch[rows:] for ch in chunks], axis=0)
+        return keys_part, scaled_part
+
+    def local_ring(keys, values, queries, learn_rate, w_gate, w_up, w_out):
+        hidden = w_gate.shape[1]
+        scaled = (learn_rate[:, None] * values.astype(jnp.float32)).astype(jnp.bfloat16)
+        own = jnp.concatenate([keys, scaled], axis=0)
+        sib = lax.ppermute(own, axes, swap)
+        total = add_grads(None, *split([own, sib]), w_gate, w_up, w_out)
+        cw = own
+        ccw = own
+        for step in range(1, cw_steps + 1):
+            cw = lax.ppermute(cw, axes, cw_perm)
+            arrived = [cw]
+            if step <= ccw_steps:
+                ccw = lax.ppermute(ccw, axes, ccw_perm)
+                arrived.append(ccw)
+            both = jnp.concatenate(arrived, axis=0)
+            sib_both = lax.ppermute(both, axes, swap)
+            rows = own.shape[0]
+            chunks = [both[j * rows:(j + 1) * rows] for j in range(len(arrived))]
+            chunks += [sib_both[j * rows:(j + 1) * rows] for j in range(len(arrived))]
+            total = add_grads(total, *split(chunks), w_gate, w_up, w_out)
+        full_in, full_out = total
+        new_gate = renorm(w_gate, full_in[:, :hidden])
+        new_up = renorm(w_up, full_in[:, hidden:])
+        new_out = renorm(w_out, full_out)
+        return apply(queries, new_gate, new_up, new_out)
+
+    return local_ring
+
+
 def solution(mesh):
     placed = (
         P(("grp", "seq", "outer"), None),
@@ -97,12 +166,18 @@
         P("grp", None),
         P("grp", None),
     )
-    shards = mesh.shape["seq"] * mesh.shape["outer"]
+    ring = chip_ring(mesh) if mesh.shape["outer"] == 2 else None
+    local_ring = make_local_ring(ring) if ring else None
 
     def run(keys, values, queries, learn_rate, w_gate, w_up, w_out):
         per_part = keys.shape[0] // mesh.shape["grp"]
         gathered_bytes = 2 * per_part * keys.shape[1] * keys.dtype.itemsize
-        body = local_gather if gathered_bytes <= GATHER_LIMIT_BYTES else local_scatter
+        if gathered_bytes > GATHER_LIMIT_BYTES:
+            body = local_scatter
+        elif local_ring is not None:
+            body = local_ring
+        else:
+            body = local_gather
         return jax.shard_map(
             body,
             mesh=mesh,
@@ -111,5 +186,4 @@
             check_vma=False,
         )(keys, values, queries, learn_rate, w_gate, w_up, w_out)
 
-    del shards
     return run

time: 87.7 us -> 58.7 us (0.67)
  waiting for transfers between devices: 52.2 us -> 25.3 us
  between operations: 13.5 us -> 0.39 us
  starting transfers between devices: 0.01 us -> 8.09 us
  matrix products: 14.5 us -> 17.7 us
  local copies, waits for them, and re-layouts: 4.01 us -> 2.52 us
  other arithmetic: 3.33 us -> 4.44 us
    all_gather x1 -> x0, waiting for transfers between devices: 52.2 us -> none  [local_gather(): full = lax.all_gather(both, ('seq', 'outer'), axis=0, tiled=True)]
    ppermute x0 -> x12, waiting for transfers between devices: none -> 25.3 us  [the longest x3 15.9 us: local_ring(): ccw = lax.ppermute(ccw, axes, ccw_perm)]
    ppermute x0 -> x12, starting transfers between devices: none -> 8.09 us  [the longest x3 5.75 us: local_ring(): ccw = lax.ppermute(ccw, axes, ccw_perm)]
    dot_general x1 -> x5, matrix products: 1.31 us -> 3.36 us  [gradients(): lax.dot_general(scaled, w_out, contract_last, preferred_element_type=jnp....]
    dot_general x1 -> x5, matrix products: 3.54 us -> 2.04 us  [gradients(): gate_pre = jnp.dot(keys, w_gate, preferred_element_type=jnp.float32)]
    slice x1 -> x12, local copies, waits for them, and re-layouts: 2.73 us -> 1.25 us  [split(): keys_part = jnp.concatenate([ch[:rows] for ch in chunks], axis=0)]
    dot_general x1 -> x5, matrix products: 2.7 us -> 3.79 us  [gradients(): lax.dot_general(activation, scaled, contract_first, preferred_element_typ...]
    concatenate x1 -> x4, other arithmetic: 1.61 us -> 2.67 us  [the longest x1 1.61 us: local_ring(): own = jnp.concatenate([keys, scaled], axis=0)]
  transfers between devices with their start and end apart: 1 -> 12, of which waited for: 1 -> 8; matrix products, arithmetic and copies ran while one was open for 2% -> 19% of each run, Pallas kernels for 0% -> 0%
where the time goes in v2:
time: 58.7 us; the launch traced here: 58.4 us
  waiting for transfers between devices  25.3 us (43%)
  matrix products  17.7 us (30%)
  starting transfers between devices  8.09 us (14%)
  other arithmetic  4.44 us (8%)
  local copies, waits for them, and re-layouts  2.52 us (4%)
    ppermute x3, waiting for transfers between devices, local_ring(): ccw = lax.ppermute(ccw, axes, ccw_perm)  15.9 us
    ppermute x4, waiting for transfers between devices, local_ring(): cw = lax.ppermute(cw, axes, cw_perm)  8.65 us
    ppermute x3, starting transfers between devices, local_ring(): ccw = lax.ppermute(ccw, axes, ccw_perm)  5.75 us
    dot_general x5, matrix products, gradients(): lax.dot_general(activation, scaled, contract_first, preferred_element_typ...  3.79 us
    dot_general x5, matrix products, gradients(): lax.dot_general(scaled, w_out, contract_last, preferred_element_type=jnp....  3.36 us
    dot_general x5, matrix products, gradients(): lax.dot_general(keys, both_grads, contract_first, preferred_element_type=...  3.28 us
    dot_general x1, matrix products, apply(): jnp.dot(q_act, full_out_w, preferred_element_type=jnp.float32)  2.75 us
    dot_general x5, matrix products, gradients(): gate_pre = jnp.dot(keys, w_gate, preferred_element_type=jnp.float32)  2.04 us
  transfers between devices with their start and end apart: 12, of which 8 were waited for; matrix products, arithmetic and copies ran while one was open for 19% of the time, Pallas kernels for 0%

profile of v2, /device:TPU:0, one launch (start us, length us, event | category | flops | bytes accessed | tf_op | source)
XLA Modules:
  0.0 58.4 jit_solution(3947404104329898814)
XLA Ops:
  0.0 1.1 %multiply_convert_fusion.27 = bf16[128,512]{1,0:T(8,128)(2,1)S(1)} fusion(bf16[128,512]{1,0:T(8,128)(2,1)} %param.8, f32[128]{0:T(128)} %param.10), kind=kLoop, calls=%fused_computation.94 | loop fusion | flops 196608 | bytes 262656 | tf_op jit(solution)/shard_map/convert_element_type | solution.py:132
  1.1 1.6 %pad_maximum_fusion.9 = bf16[256,512]{1,0:T(8,128)(2,1)} fusion(bf16[128,512]{1,0:T(8,128)(2,1)} %param.7, bf16[128,512]{1,0:T(8,128)(2,1)S(1)} %multiply_convert_fusion.27), kind=kLoop, calls=%fused_computation.84 | loop fusion | flops 524288 | bytes 524288 | tf_op jit(solution)/shard_map/concatenate | solution.py:133
  3.2 2.5 %collective-permute-start.2 = (bf16[256,512]{1,0:T(8,128)(2,1)}, bf16[256,512]{1,0:T(8,128)(2,1)S(1)}, u32[]{:S(2)}, u32[]{:S(2)}) collective-permute-start(bf16[256,512]{1,0:T(8,128)(2,1)} %pad_maximum_fusion.9), channel_id=1, source_target_pairs={{0,2},{1,3},{4,0},{5,1},{8,4},{9,5},{12,8},{13,9},{14,12},{15,13},... | collective-permute-start | bytes 786440 | tf_op jit(solution)/shard_map/ppermute | solution.py:142
  5.8 1.3 %copy.8 = bf16[512,512]{0,1:T(8,128)(2,1)S(1)} copy(bf16[512,512]{1,0:T(8,128)(2,1)} %param.13) | data formatting | bytes 1048576 | tf_op args[6]
  7.8 5.1 %collective-permute-done.2 = bf16[256,512]{1,0:T(8,128)(2,1)S(1)} collective-permute-done((bf16[256,512]{1,0:T(8,128)(2,1)}, bf16[256,512]{1,0:T(8,128)(2,1)S(1)}, u32[]{:S(2)}, u32[]{:S(2)}) %collective-permute-start.2) | collective-permute-done | bytes 262176 | tf_op jit(solution)/shard_map/ppermute | solution.py:142
  12.9 1.5 %collective-permute-done.1 = bf16[256,512]{1,0:T(8,128)(2,1)} collective-permute-done((bf16[256,512]{1,0:T(8,128)(2,1)}, bf16[256,512]{1,0:T(8,128)(2,1)}, u32[]{:S(2)}, u32[]{:S(2)}) %collective-permute-start.1) | collective-permute-done | bytes 262176 | tf_op jit(solution)/shard_map/ppermute | solution.py:139
  14.4 1.0 %pad_maximum_fusion = bf16[512,512]{1,0:T(8,128)(2,1)S(1)} fusion(bf16[256,512]{1,0:T(8,128)(2,1)S(1)} %collective-permute-done.2, bf16[256,512]{1,0:T(8,128)(2,1)} %collective-permute-done.1), kind=kLoop, calls=%fused_computation.59 | loop fusion | flops 1048576 | bytes 1048576 | tf_op jit(solution)/shard_map/concatenate | solution.py:144
  16.0 1.6 %collective-permute-start.5 = (bf16[256,512]{1,0:T(8,128)(2,1)S(1)}, bf16[256,512]{1,0:T(8,128)(2,1)S(1)}, u32[]{:S(2)}, u32[]{:S(2)}) collective-permute-start(bf16[256,512]{1,0:T(8,128)(2,1)S(1)} %collective-permute-done.2), channel_id=1, source_target_pairs={{0,2},{1,3},{4,0},{5,1},{8,4},{9,5},{12,8},{13,9},{14,12},{15,13},... | collective-permute-start | bytes 786440 | tf_op jit(solution)/shard_map/ppermute | solution.py:142
  18.5 1.0 %fusion.95 = (bf16[128,512]{1,0:T(8,128)(2,1)S(1)}, bf16[128,512]{1,0:T(8,128)(2,1)S(1)}) fusion(bf16[256,512]{1,0:T(8,128)(2,1)} %collective-permute-done.1), kind=kLoop, calls=%fused_computation.144 | loop fusion | bytes 524288 | tf_op jit(solution)/shard_map/slice | solution.py:126
  19.5 5.2 %collective-permute-done.5 = bf16[256,512]{1,0:T(8,128)(2,1)S(1)} collective-permute-done((bf16[256,512]{1,0:T(8,128)(2,1)S(1)}, bf16[256,512]{1,0:T(8,128)(2,1)S(1)}, u32[]{:S(2)}, u32[]{:S(2)}) %collective-permute-start.5) | collective-permute-done | bytes 262176 | tf_op jit(solution)/shard_map/ppermute | solution.py:142
  24.7 1.5 %collective-permute-done.4 = bf16[256,512]{1,0:T(8,128)(2,1)S(1)} collective-permute-done((bf16[256,512]{1,0:T(8,128)(2,1)}, bf16[256,512]{1,0:T(8,128)(2,1)S(1)}, u32[]{:S(2)}, u32[]{:S(2)}) %collective-permute-start.4) | collective-permute-done | bytes 262176 | tf_op jit(solution)/shard_map/ppermute | solution.py:139
  26.4 1.6 %collective-permute-start.8 = (bf16[256,512]{1,0:T(8,128)(2,1)S(1)}, bf16[256,512]{1,0:T(8,128)(2,1)S(1)}, u32[]{:S(2)}, u32[]{:S(2)}) collective-permute-start(bf16[256,512]{1,0:T(8,128)(2,1)S(1)} %collective-permute-done.5), channel_id=1, source_target_pairs={{0,2},{1,3},{4,0},{5,1},{8,4},{9,5},{12,8},{13,9},{14,12},{15,13},... | collective-permute-start | bytes 786440 | tf_op jit(solution)/shard_map/ppermute | solution.py:142
  28.6 0.5 fusion.88
  29.5 5.5 %collective-permute-done.8 = bf16[256,512]{1,0:T(8,128)(2,1)S(1)} collective-permute-done((bf16[256,512]{1,0:T(8,128)(2,1)S(1)}, bf16[256,512]{1,0:T(8,128)(2,1)S(1)}, u32[]{:S(2)}, u32[]{:S(2)}) %collective-permute-start.8) | collective-permute-done | bytes 262176 | tf_op jit(solution)/shard_map/ppermute | solution.py:142
  35.1 1.3 %collective-permute-done.7 = bf16[256,512]{1,0:T(8,128)(2,1)S(1)} collective-permute-done((bf16[256,512]{1,0:T(8,128)(2,1)S(1)}, bf16[256,512]{1,0:T(8,128)(2,1)S(1)}, u32[]{:S(2)}, u32[]{:S(2)}) %collective-permute-start.7) | collective-permute-done | bytes 262176 | tf_op jit(solution)/shard_map/ppermute | solution.py:139
  36.5 0.8 %multiply_convert_fusion.11 = (bf16[512,512]{0,1:T(8,128)(2,1)S(1)}, bf16[512,512]{0,1:T(8,128)(2,1)S(1)}) fusion(f32[512,512]{0,1:T(8,128)S(1)} %fusion.88, f32[512,512]{0,1:T(8,128)S(1)} %fusion.89, bf16[512,512]{1,0:T(8,128)(2,1)S(1)} %copy-done.4, bf16[128,512]{1,0:T(8,128)(2,1)S(1)} %get-tuple-element.20, bf16[128,512]{1,0:T(8,128)(2,1)S(1)} %get-tuple-element.21, ...), kind=kOutput, calls=%fused_computation.49 | convolution fusion | flops 273940480 | bytes 4194304 | tf_op jit(solution)/shard_map/dot_general | solution.py:31
  37.4 0.7 %collective-permute-start.10 = (bf16[256,512]{1,0:T(8,128)(2,1)S(1)}, bf16[256,512]{1,0:T(8,128)(2,1)S(1)}, u32[]{:S(2)}, u32[]{:S(2)}) collective-permute-start(bf16[256,512]{1,0:T(8,128)(2,1)S(1)} %collective-permute-done.7), channel_id=1, source_target_pairs={{0,4},{1,5},{4,8},{5,9},{8,12},{9,13},{12,14},{13,15},{14,10},{15,... | collective-permute-start | bytes 786440 | tf_op jit(solution)/shard_map/ppermute | solution.py:139
  38.0 0.8 %fusion.8 = f32[512,1024]{1,0:T(8,128)S(1)} fusion(bf16[512,512]{0,1:T(8,128)(2,1)S(1)} %get-tuple-element.10, bf16[512,512]{0,1:T(8,128)(2,1)S(1)} %get-tuple-element.9, bf16[128,512]{1,0:T(8,128)(2,1)S(1)} %get-tuple-element.22, bf16[128,512]{1,0:T(8,128)(2,1)S(1)} %get-tuple-element.19, bf16[128,512]{1,0:T(8,128)(2,1)S(1)} %get-tuple-element.37, ...), kind=kOutput, calls=%fused_computation.19 | convolution fusion | flops 541065216 | bytes 3670016 | tf_op jit(solution)/shard_map/dot_general | solution.py:36
  38.8 0.6 %fusion.23 = f32[512,512]{0,1:T(8,128)S(1)} fusion(f32[512,512]{0,1:T(8,128)S(1)} %fusion.89, f32[512,512]{0,1:T(8,128)S(1)} %fusion.88, bf16[128,512]{1,0:T(8,128)(2,1)S(1)} %get-tuple-element.20, bf16[128,512]{1,0:T(8,128)(2,1)S(1)} %get-tuple-element.21, bf16[128,512]{1,0:T(8,128)(2,1)S(1)} %get-tuple-element.38, bf16[128,512]{1,0:T(8,128)(2,1)S(1)} %get-tuple-element.36), kind=kOutput, calls=%fused_computation.52 | convolution fusion | flops 272105472 | bytes 3670016 | tf_op jit(solution)/shard_map/dot_general | solution.py:37
  39.5 0.5 fusion.86
  40.5 0.8 %multiply_convert_fusion.9 = (bf16[512,512]{0,1:T(8,128)(2,1)S(1)}, bf16[512,512]{0,1:T(8,128)(2,1)S(1)}) fusion(f32[512,512]{0,1:T(8,128)S(1)} %fusion.86, f32[512,512]{0,1:T(8,128)S(1)} %fusion.87, bf16[512,512]{1,0:T(8,128)(2,1)S(1)} %copy-done.4, bf16[128,512]{1,0:T(8,128)(2,1)S(1)} %get-tuple-element.24, bf16[128,512]{1,0:T(8,128)(2,1)S(1)} %get-tuple-element.25, ...), kind=kOutput, calls=%fused_computation.45 | convolution fusion | flops 273940480 | bytes 4194304 | tf_op jit(solution)/shard_map/dot_general | solution.py:31
  41.3 0.6 %fusion.24 = f32[512,512]{0,1:T(8,128)S(1)} fusion(f32[512,512]{0,1:T(8,128)S(1)} %fusion.87, f32[512,512]{0,1:T(8,128)S(1)} %fusion.86, bf16[128,512]{1,0:T(8,128)(2,1)S(1)} %get-tuple-element.24, bf16[128,512]{1,0:T(8,128)(2,1)S(1)} %get-tuple-element.25, bf16[128,512]{1,0:T(8,128)(2,1)S(1)} %get-tuple-element.44, bf16[128,512]{1,0:T(8,128)(2,1)S(1)} %get-tuple-element.42), kind=kOutput, calls=%fused_computation.53 | convolution fusion | flops 272105472 | bytes 3670016 | tf_op jit(solution)/shard_map/dot_general | solution.py:37
  41.9 4.4 %collective-permute-done.10 = bf16[256,512]{1,0:T(8,128)(2,1)S(1)} collective-permute-done((bf16[256,512]{1,0:T(8,128)(2,1)S(1)}, bf16[256,512]{1,0:T(8,128)(2,1)S(1)}, u32[]{:S(2)}, u32[]{:S(2)}) %collective-permute-start.10) | collective-permute-done | bytes 262176 | tf_op jit(solution)/shard_map/ppermute | solution.py:139
  46.3 0.8 %fusion.12 = f32[512,1024]{1,0:T(8,128)S(1)} fusion(bf16[512,512]{0,1:T(8,128)(2,1)S(1)} %get-tuple-element.12, bf16[512,512]{0,1:T(8,128)(2,1)S(1)} %get-tuple-element.11, bf16[128,512]{1,0:T(8,128)(2,1)S(1)} %get-tuple-element.26, bf16[128,512]{1,0:T(8,128)(2,1)S(1)} %get-tuple-element.23, bf16[128,512]{1,0:T(8,128)(2,1)S(1)} %get-tuple-element.43, ...), kind=kOutput, calls=%fused_computation.23 | convolution fusion | flops 541065216 | bytes 3670016 | tf_op jit(solution)/shard_map/dot_general | solution.py:36
  47.1 0.7 %collective-permute-done.11 = bf16[256,512]{1,0:T(8,128)(2,1)S(1)} collective-permute-done((bf16[256,512]{1,0:T(8,128)(2,1)S(1)}, bf16[256,512]{1,0:T(8,128)(2,1)S(1)}, u32[]{:S(2)}, u32[]{:S(2)}) %collective-permute-start.11) | collective-permute-done | bytes 262176 | tf_op jit(solution)/shard_map/ppermute | solution.py:145
  49.5 0.6 %fusion.25 = f32[512,512]{0,1:T(8,128)S(1)} fusion(f32[512,512]{0,1:T(8,128)S(1)} %fusion.85, f32[512,512]{0,1:T(8,128)S(1)} %fusion.84, bf16[128,512]{1,0:T(8,128)(2,1)S(1)} %get-tuple-element.28, bf16[128,512]{1,0:T(8,128)(2,1)S(1)} %get-tuple-element.29, bf16[128,512]{1,0:T(8,128)(2,1)S(1)} %get-tuple-element.48, bf16[128,512]{1,0:T(8,128)(2,1)S(1)} %get-tuple-element.46), kind=kOutput, calls=%fused_computation.54 | convolution fusion | flops 272105472 | bytes 3670016 | tf_op jit(solution)/shard_map/dot_general | solution.py:37
  50.1 0.8 %multiply_convert_fusion.7 = (bf16[512,512]{0,1:T(8,128)(2,1)S(1)}, bf16[512,512]{0,1:T(8,128)(2,1)S(1)}) fusion(f32[512,512]{0,1:T(8,128)S(1)} %fusion.84, f32[512,512]{0,1:T(8,128)S(1)} %fusion.85, bf16[512,512]{1,0:T(8,128)(2,1)S(1)} %copy-done.4, bf16[128,512]{1,0:T(8,128)(2,1)S(1)} %get-tuple-element.28, bf16[128,512]{1,0:T(8,128)(2,1)S(1)} %get-tuple-element.29, ...), kind=kOutput, calls=%fused_computation.41 | convolution fusion | flops 273940480 | bytes 4194304 | tf_op jit(solution)/shard_map/dot_general | solution.py:31
  51.9 1.5 %multiply_reduce_fusion = (f32[512]{0:T(512)S(1)}, f32[512,512]{0,1:T(8,128)}) fusion(f32[512,512]{0,1:T(8,128)S(1)} %fusion.2, bf16[128,512]{1,0:T(8,128)(2,1)S(1)} %get-tuple-element.34, bf16[128,512]{1,0:T(8,128)(2,1)S(1)} %get-tuple-element.32, f32[256,512]{1,0:T(8,128)S(1)} %fusion.56, f32[256,512]{1,0:T(8,128)S(1)} %fusion.55, ...), kind=kOutput, calls=%fused_computation.32 | convolution fusion | flops 136838656 | bytes 3934208 | tf_op jit(solution)/shard_map/dot_general | solution.py:37
  53.3 0.8 %fusion.16 = f32[512,1024]{1,0:T(8,128)S(1)} fusion(bf16[512,512]{0,1:T(8,128)(2,1)S(1)} %get-tuple-element.14, bf16[512,512]{0,1:T(8,128)(2,1)S(1)} %get-tuple-element.13, bf16[128,512]{1,0:T(8,128)(2,1)S(1)} %get-tuple-element.30, bf16[128,512]{1,0:T(8,128)(2,1)S(1)} %get-tuple-element.27, bf16[128,512]{1,0:T(8,128)(2,1)S(1)} %get-tuple-element.47, ...), kind=kOutput, calls=%fused_computation.27 | convolution fusion | flops 541065216 | bytes 3670016 | tf_op jit(solution)/shard_map/dot_general | solution.py:36
  54.1 0.6 add_add_fusion
  54.7 0.5 multiply_reduce_fusion.2
  55.6 2.7 %convolution_convert_fusion = bf16[128,512]{1,0:T(8,128)(2,1)} fusion(bf16[128,512]{1,0:T(8,128)(2,1)S(1)} %copy-done, f32[512,1024]{1,0:T(8,128)S(1)} %add_add_fusion, bf16[512,512]{1,0:T(8,128)(2,1)S(1)} %copy-done.2, f32[512,512]{0,1:T(8,128)} %get-tuple-element.50, f32[512]{0:T(512)S(1)} %rsqrt_multiply_fusion, f32[512]{0:T(512)S(1)} %get-tuple-element.51, ...), kind=kOutput, calls=%fused_computation.15 | convolution fusion | flops 136249344 | bytes 3149824 | tf_op jit(solution)/shard_map/dot_general | solution.py:45
  (51 shorter events, 7.5 us)
Async XLA Ops:
  0.0 55.2 %copy-start = (bf16[128,512]{1,0:T(8,128)(2,1)S(1)}, bf16[128,512]{1,0:T(8,128)(2,1)}, u32[]{:S(2)}) copy-start(bf16[128,512]{1,0:T(8,128)(2,1)} %param.9) | copy-start | bytes 393220
  0.0 7.2 %copy-start.3 = (bf16[128,512]{1,0:T(8,128)(2,1)S(1)}, bf16[128,512]{1,0:T(8,128)(2,1)}, u32[]{:S(2)}) copy-start(bf16[128,512]{1,0:T(8,128)(2,1)} %param.7) | copy-start | bytes 393220
  0.0 7.2 %copy-start.1 = (bf16[512,512]{1,0:T(8,128)(2,1)S(1)}, bf16[512,512]{1,0:T(8,128)(2,1)}, u32[]{:S(2)}) copy-start(bf16[512,512]{1,0:T(8,128)(2,1)} %param.11) | copy-start | bytes 1572868
  0.0 7.5 %copy-start.2 = (bf16[512,512]{1,0:T(8,128)(2,1)S(1)}, bf16[512,512]{1,0:T(8,128)(2,1)}, u32[]{:S(2)}) copy-start(bf16[512,512]{1,0:T(8,128)(2,1)} %param.12) | copy-start | bytes 1572868
  2.7 4.5 %collective-permute-start = (bf16[256,512]{1,0:T(8,128)(2,1)}, bf16[256,512]{1,0:T(8,128)(2,1)S(1)}, u32[]{:S(2)}, u32[]{:S(2)}) collective-permute-start(bf16[256,512]{1,0:T(8,128)(2,1)} %pad_maximum_fusion.9), channel_id=1, source_target_pairs={{0,1},{1,0},{2,3},{3,2},{4,5},{5,4},{6,7},{7,6},{8,9},{9,8},{10,11... | collective-permute-start | bytes 786440 | tf_op jit(solution)/shard_map/ppermute | solution.py:134
  3.2 9.8 %collective-permute-start.2 = (bf16[256,512]{1,0:T(8,128)(2,1)}, bf16[256,512]{1,0:T(8,128)(2,1)S(1)}, u32[]{:S(2)}, u32[]{:S(2)}) collective-permute-start(bf16[256,512]{1,0:T(8,128)(2,1)} %pad_maximum_fusion.9), channel_id=1, source_target_pairs={{0,2},{1,3},{4,0},{5,1},{8,4},{9,5},{12,8},{13,9},{14,12},{15,13},... | collective-permute-start | bytes 786440 | tf_op jit(solution)/shard_map/ppermute | solution.py:142
  5.7 8.8 %collective-permute-start.1 = (bf16[256,512]{1,0:T(8,128)(2,1)}, bf16[256,512]{1,0:T(8,128)(2,1)}, u32[]{:S(2)}, u32[]{:S(2)}) collective-permute-start(bf16[256,512]{1,0:T(8,128)(2,1)} %pad_maximum_fusion.9), channel_id=1, source_target_pairs={{0,4},{1,5},{4,8},{5,9},{8,12},{9,13},{12,14},{13,15},{14,10},{15,... | collective-permute-start | bytes 786440 | tf_op jit(solution)/shard_map/ppermute | solution.py:139
  7.2 8.3 %copy-start.4 = (bf16[512,512]{1,0:T(8,128)(2,1)S(1)}, bf16[512,512]{1,0:T(8,128)(2,1)}, u32[]{:S(2)}) copy-start(bf16[512,512]{1,0:T(8,128)(2,1)} %param.13) | copy-start | bytes 1572868
  15.4 13.1 %collective-permute-start.3 = (bf16[512,512]{1,0:T(8,128)(2,1)S(1)}, bf16[512,512]{1,0:T(8,128)(2,1)S(1)}, u32[]{:S(2)}, u32[]{:S(2)}) collective-permute-start(bf16[512,512]{1,0:T(8,128)(2,1)S(1)} %pad_maximum_fusion), channel_id=1, source_target_pairs={{0,1},{1,0},{2,3},{3,2},{4,5},{5,4},{6,7},{7,6},{8,9},{9,8},{10,11... | collective-permute-start | bytes 1572872 | tf_op jit(solution)/shard_map/ppermute | solution.py:145
  16.0 8.8 %collective-permute-start.5 = (bf16[256,512]{1,0:T(8,128)(2,1)S(1)}, bf16[256,512]{1,0:T(8,128)(2,1)S(1)}, u32[]{:S(2)}, u32[]{:S(2)}) collective-permute-start(bf16[256,512]{1,0:T(8,128)(2,1)S(1)} %collective-permute-done.2), channel_id=1, source_target_pairs={{0,2},{1,3},{4,0},{5,1},{8,4},{9,5},{12,8},{13,9},{14,12},{15,13},... | collective-permute-start | bytes 786440 | tf_op jit(solution)/shard_map/ppermute | solution.py:142
  17.6 8.6 %collective-permute-start.4 = (bf16[256,512]{1,0:T(8,128)(2,1)}, bf16[256,512]{1,0:T(8,128)(2,1)S(1)}, u32[]{:S(2)}, u32[]{:S(2)}) collective-permute-start(bf16[256,512]{1,0:T(8,128)(2,1)} %collective-permute-done.1), channel_id=1, source_target_pairs={{0,4},{1,5},{4,8},{5,9},{8,12},{9,13},{12,14},{13,15},{14,10},{15,... | collective-permute-start | bytes 786440 | tf_op jit(solution)/shard_map/ppermute | solution.py:139
  26.3 13.1 %collective-permute-start.6 = (bf16[512,512]{1,0:T(8,128)(2,1)S(1)}, bf16[512,512]{1,0:T(8,128)(2,1)S(1)}, u32[]{:S(2)}, u32[]{:S(2)}) collective-permute-start(bf16[512,512]{1,0:T(8,128)(2,1)S(1)} %pad_maximum_fusion.3), channel_id=1, source_target_pairs={{0,1},{1,0},{2,3},{3,2},{4,5},{5,4},{6,7},{7,6},{8,9},{9,8},{10,11... | collective-permute-start | bytes 1572872 | tf_op jit(solution)/shard_map/ppermute | solution.py:145
  26.4 8.7 %collective-permute-start.8 = (bf16[256,512]{1,0:T(8,128)(2,1)S(1)}, bf16[256,512]{1,0:T(8,128)(2,1)S(1)}, u32[]{:S(2)}, u32[]{:S(2)}) collective-permute-start(bf16[256,512]{1,0:T(8,128)(2,1)S(1)} %collective-permute-done.5), channel_id=1, source_target_pairs={{0,2},{1,3},{4,0},{5,1},{8,4},{9,5},{12,8},{13,9},{14,12},{15,13},... | collective-permute-start | bytes 786440 | tf_op jit(solution)/shard_map/ppermute | solution.py:142
  28.0 8.4 %collective-permute-start.7 = (bf16[256,512]{1,0:T(8,128)(2,1)S(1)}, bf16[256,512]{1,0:T(8,128)(2,1)S(1)}, u32[]{:S(2)}, u32[]{:S(2)}) collective-permute-start(bf16[256,512]{1,0:T(8,128)(2,1)S(1)} %collective-permute-done.4), channel_id=1, source_target_pairs={{0,4},{1,5},{4,8},{5,9},{8,12},{9,13},{12,14},{13,15},{14,10},{15,... | collective-permute-start | bytes 786440 | tf_op jit(solution)/shard_map/ppermute | solution.py:139
  36.4 12.1 %collective-permute-start.9 = (bf16[512,512]{1,0:T(8,128)(2,1)S(1)}, bf16[512,512]{1,0:T(8,128)(2,1)S(1)}, u32[]{:S(2)}, u32[]{:S(2)}) collective-permute-start(bf16[512,512]{1,0:T(8,128)(2,1)S(1)} %pad_maximum_fusion.6), channel_id=1, source_target_pairs={{0,1},{1,0},{2,3},{3,2},{4,5},{5,4},{6,7},{7,6},{8,9},{9,8},{10,11... | collective-permute-start | bytes 1572872 | tf_op jit(solution)/shard_map/ppermute | solution.py:145
  37.4 8.9 %collective-permute-start.10 = (bf16[256,512]{1,0:T(8,128)(2,1)S(1)}, bf16[256,512]{1,0:T(8,128)(2,1)S(1)}, u32[]{:S(2)}, u32[]{:S(2)}) collective-permute-start(bf16[256,512]{1,0:T(8,128)(2,1)S(1)} %collective-permute-done.7), channel_id=1, source_target_pairs={{0,4},{1,5},{4,8},{5,9},{8,12},{9,13},{12,14},{13,15},{14,10},{15,... | collective-permute-start | bytes 786440 | tf_op jit(solution)/shard_map/ppermute | solution.py:139
  46.3 1.5 %collective-permute-start.11 = (bf16[256,512]{1,0:T(8,128)(2,1)S(1)}, bf16[256,512]{1,0:T(8,128)(2,1)S(1)}, u32[]{:S(2)}, u32[]{:S(2)}) collective-permute-start(bf16[256,512]{1,0:T(8,128)(2,1)S(1)} %collective-permute-done.10), channel_id=1, source_target_pairs={{0,1},{1,0},{2,3},{3,2},{4,5},{5,4},{6,7},{7,6},{8,9},{9,8},{10,11... | collective-permute-start | bytes 786440 | tf_op jit(solution)/shard_map/ppermute | solution.py:145

commit v3 on v2

--- a/solution.py
+++ b/solution.py
@@ -133,20 +133,14 @@
         own = jnp.concatenate([keys, scaled], axis=0)
         sib = lax.ppermute(own, axes, swap)
         total = add_grads(None, *split([own, sib]), w_gate, w_up, w_out)
-        cw = own
-        ccw = own
+        arrived = [own, own]
         for step in range(1, cw_steps + 1):
-            cw = lax.ppermute(cw, axes, cw_perm)
-            arrived = [cw]
+            sent = [lax.ppermute(arrived[0], axes, cw_perm)]
             if step <= ccw_steps:
-                ccw = lax.ppermute(ccw, axes, ccw_perm)
-                arrived.append(ccw)
-            both = jnp.concatenate(arrived, axis=0)
-            sib_both = lax.ppermute(both, axes, swap)
-            rows = own.shape[0]
-            chunks = [both[j * rows:(j + 1) * rows] for j in range(len(arrived))]
-            chunks += [sib_both[j * rows:(j + 1) * rows] for j in range(len(arrived))]
-            total = add_grads(total, *split(chunks), w_gate, w_up, w_out)
+                sent.append(lax.ppermute(arrived[1], axes, ccw_perm))
+            arrived = sent
+            from_sib = [lax.ppermute(chunk, axes, swap) for chunk in arrived]
+            total = add_grads(total, *split(arrived + from_sib), w_gate, w_up, w_out)
         full_in, full_out = total
         new_gate = renorm(w_gate, full_in[:, :hidden])
         new_up = renorm(w_up, full_in[:, hidden:])

time: 58.7 us -> 53.4 us (0.910)
  waiting for transfers between devices: 25.3 us -> 20.1 us
  other arithmetic: 4.44 us -> 3.4 us
  starting transfers between devices: 8.09 us -> 8.86 us
    ppermute x11 -> x14, waiting for transfers between devices: 25.3 us -> 20.1 us  [the longest x3 10.4 us: local_ring(): sent.append(lax.ppermute(arrived[1], axes, ccw_perm))]
    concatenate x3 -> x0, other arithmetic: 1.05 us -> none  [local_ring(): both = jnp.concatenate(arrived, axis=0)]
    ppermute x11 -> x14, starting transfers between devices: 7.63 us -> 8.4 us  [the longest x3 5.91 us: local_ring(): sent.append(lax.ppermute(arrived[1], axes, ccw_perm))]
    slice x12 -> x15, local copies, waits for them, and re-layouts: 1.25 us -> 1.24 us  [split(): keys_part = jnp.concatenate([ch[:rows] for ch in chunks], axis=0)]
  transfers between devices with their start and end apart: 12 -> 15, of which waited for: 8 -> 8; matrix products, arithmetic and copies ran while one was open for 19% -> 26% of each run, Pallas kernels for 0% -> 0%
where the time goes in v3:
time: 53.4 us; the launch traced here: 53.1 us
  waiting for transfers between devices  20.1 us (38%)
  matrix products  17.7 us (33%)
  starting transfers between devices  8.86 us (17%)
  other arithmetic  3.4 us (6%)
  local copies, waits for them, and re-layouts  2.73 us (5%)
    ppermute x3, waiting for transfers between devices, local_ring(): sent.append(lax.ppermute(arrived[1], axes, ccw_perm))  10.4 us
    ppermute x4, waiting for transfers between devices, local_ring(): sent = [lax.ppermute(arrived[0], axes, cw_perm)]  7.41 us
    ppermute x3, starting transfers between devices, local_ring(): sent.append(lax.ppermute(arrived[1], axes, ccw_perm))  5.91 us
    dot_general x5, matrix products, gradients(): lax.dot_general(activation, scaled, contract_first, preferred_element_typ...  3.79 us
    dot_general x5, matrix products, gradients(): lax.dot_general(scaled, w_out, contract_last, preferred_element_type=jnp....  3.33 us
    dot_general x5, matrix products, gradients(): lax.dot_general(keys, both_grads, contract_first, preferred_element_type=...  3.28 us
    dot_general x1, matrix products, apply(): jnp.dot(q_act, full_out_w, preferred_element_type=jnp.float32)  2.75 us
    ppermute x7, waiting for transfers between devices, local_ring(): from_sib = [lax.ppermute(chunk, axes, swap) for chunk in arrived]  2.3 us
  transfers between devices with their start and end apart: 15, of which 8 were waited for; matrix products, arithmetic and copies ran while one was open for 26% of the time, Pallas kernels for 0%

profile of v3, /device:TPU:0, one launch (start us, length us, event | category | flops | bytes accessed | tf_op | source)
XLA Modules:
  0.0 53.1 jit_solution(16253407479866851429)
XLA Ops:
  0.0 1.1 %multiply_convert_fusion.27 = bf16[128,512]{1,0:T(8,128)(2,1)S(1)} fusion(bf16[128,512]{1,0:T(8,128)(2,1)} %param.8, f32[128]{0:T(128)} %param.10), kind=kLoop, calls=%fused_computation.89 | loop fusion | flops 196608 | bytes 262656 | tf_op jit(solution)/shard_map/convert_element_type | solution.py:132
  1.1 1.6 %pad_maximum_fusion.6 = bf16[256,512]{1,0:T(8,128)(2,1)} fusion(bf16[128,512]{1,0:T(8,128)(2,1)} %param.7, bf16[128,512]{1,0:T(8,128)(2,1)S(1)} %multiply_convert_fusion.27), kind=kLoop, calls=%fused_computation.78 | loop fusion | flops 524288 | bytes 524288 | tf_op jit(solution)/shard_map/concatenate | solution.py:133
  3.2 2.5 %collective-permute-start.2 = (bf16[256,512]{1,0:T(8,128)(2,1)}, bf16[256,512]{1,0:T(8,128)(2,1)}, u32[]{:S(2)}, u32[]{:S(2)}) collective-permute-start(bf16[256,512]{1,0:T(8,128)(2,1)} %pad_maximum_fusion.6), channel_id=1, source_target_pairs={{0,2},{1,3},{4,0},{5,1},{8,4},{9,5},{12,8},{13,9},{14,12},{15,13},... | collective-permute-start | bytes 786440 | tf_op jit(solution)/shard_map/ppermute | solution.py:140
  5.8 1.3 %copy.8 = bf16[512,512]{0,1:T(8,128)(2,1)S(1)} copy(bf16[512,512]{1,0:T(8,128)(2,1)} %param.13) | data formatting | bytes 1048576 | tf_op args[6]
  9.0 4.1 %collective-permute-done.2 = bf16[256,512]{1,0:T(8,128)(2,1)} collective-permute-done((bf16[256,512]{1,0:T(8,128)(2,1)}, bf16[256,512]{1,0:T(8,128)(2,1)}, u32[]{:S(2)}, u32[]{:S(2)}) %collective-permute-start.2) | collective-permute-done | bytes 262176 | tf_op jit(solution)/shard_map/ppermute | solution.py:140
  13.1 1.0 %fusion.89 = (bf16[128,512]{1,0:T(8,128)(2,1)S(1)}, bf16[128,512]{1,0:T(8,128)(2,1)S(1)}) fusion(bf16[256,512]{1,0:T(8,128)(2,1)} %collective-permute-done.2), kind=kLoop, calls=%fused_computation.137 | loop fusion | bytes 524288 | tf_op jit(solution)/shard_map/slice | solution.py:126
  14.6 1.7 %collective-permute-start.6 = (bf16[256,512]{1,0:T(8,128)(2,1)}, bf16[256,512]{1,0:T(8,128)(2,1)S(1)}, u32[]{:S(2)}, u32[]{:S(2)}) collective-permute-start(bf16[256,512]{1,0:T(8,128)(2,1)} %collective-permute-done.2), channel_id=1, source_target_pairs={{0,2},{1,3},{4,0},{5,1},{8,4},{9,5},{12,8},{13,9},{14,12},{15,13},... | collective-permute-start | bytes 786440 | tf_op jit(solution)/shard_map/ppermute | solution.py:140
  16.5 0.5 collective-permute-start.5
  17.1 0.8 %collective-permute-done.3 = bf16[256,512]{1,0:T(8,128)(2,1)S(1)} collective-permute-done((bf16[256,512]{1,0:T(8,128)(2,1)S(1)}, bf16[256,512]{1,0:T(8,128)(2,1)S(1)}, u32[]{:S(2)}, u32[]{:S(2)}) %collective-permute-start.3) | collective-permute-done | bytes 262176 | tf_op jit(solution)/shard_map/ppermute | solution.py:142
  18.8 0.8 %multiply_convert_fusion.11 = (bf16[512,512]{0,1:T(8,128)(2,1)S(1)}, bf16[512,512]{0,1:T(8,128)(2,1)S(1)}) fusion(f32[512,512]{0,1:T(8,128)S(1)} %fusion.84, f32[512,512]{0,1:T(8,128)S(1)} %fusion.85, bf16[512,512]{1,0:T(8,128)(2,1)S(1)} %copy-done.4, bf16[128,512]{1,0:T(8,128)(2,1)S(1)} %get-tuple-element.30, bf16[128,512]{1,0:T(8,128)(2,1)S(1)} %get-tuple-element.28, ...), kind=kOutput, calls=%fused_computation.49 | convolution fusion | flops 273940480 | bytes 4194304 | tf_op jit(solution)/shard_map/dot_general | solution.py:31
  19.7 0.6 %convolution_add_fusion.2 = f32[512,512]{0,1:T(8,128)S(1)} fusion(f32[512,512]{0,1:T(8,128)S(1)} %fusion.34, f32[512,512]{0,1:T(8,128)S(1)} %fusion.85, f32[512,512]{0,1:T(8,128)S(1)} %fusion.84, bf16[128,512]{1,0:T(8,128)(2,1)S(1)} %get-tuple-element.30, bf16[128,512]{1,0:T(8,128)(2,1)S(1)} %get-tuple-element.28, ...), kind=kOutput, calls=%fused_computation.3 | convolution fusion | flops 272367616 | bytes 4718592 | tf_op jit(solution)/shard_map/dot_general | solution.py:37
  20.3 3.3 %collective-permute-done.6 = bf16[256,512]{1,0:T(8,128)(2,1)S(1)} collective-permute-done((bf16[256,512]{1,0:T(8,128)(2,1)}, bf16[256,512]{1,0:T(8,128)(2,1)S(1)}, u32[]{:S(2)}, u32[]{:S(2)}) %collective-permute-start.6) | collective-permute-done | bytes 262176 | tf_op jit(solution)/shard_map/ppermute | solution.py:140
  23.7 0.8 %fusion.6 = f32[512,1024]{1,0:T(8,128)S(1)} fusion(bf16[512,512]{0,1:T(8,128)(2,1)S(1)} %get-tuple-element.10, bf16[512,512]{0,1:T(8,128)(2,1)S(1)} %get-tuple-element.9, bf16[128,512]{1,0:T(8,128)(2,1)S(1)} %get-tuple-element.29, bf16[128,512]{1,0:T(8,128)(2,1)S(1)} %get-tuple-element.27, bf16[128,512]{1,0:T(8,128)(2,1)S(1)} %get-tuple-element.25, ...), kind=kOutput, calls=%fused_computation.19 | convolution fusion | flops 541065216 | bytes 3670016 | tf_op jit(solution)/shard_map/dot_general | solution.py:36
  24.4 1.7 %collective-permute-start.10 = (bf16[256,512]{1,0:T(8,128)(2,1)S(1)}, bf16[256,512]{1,0:T(8,128)(2,1)S(1)}, u32[]{:S(2)}, u32[]{:S(2)}) collective-permute-start(bf16[256,512]{1,0:T(8,128)(2,1)S(1)} %collective-permute-done.6), channel_id=1, source_target_pairs={{0,2},{1,3},{4,0},{5,1},{8,4},{9,5},{12,8},{13,9},{14,12},{15,13},... | collective-permute-start | bytes 786440 | tf_op jit(solution)/shard_map/ppermute | solution.py:140
  26.4 0.5 collective-permute-start.9
  26.9 0.8 %collective-permute-done.7 = bf16[256,512]{1,0:T(8,128)(2,1)S(1)} collective-permute-done((bf16[256,512]{1,0:T(8,128)(2,1)S(1)}, bf16[256,512]{1,0:T(8,128)(2,1)S(1)}, u32[]{:S(2)}, u32[]{:S(2)}) %collective-permute-start.7) | collective-permute-done | bytes 262176 | tf_op jit(solution)/shard_map/ppermute | solution.py:142
  28.7 0.8 %multiply_convert_fusion.9 = (bf16[512,512]{0,1:T(8,128)(2,1)S(1)}, bf16[512,512]{0,1:T(8,128)(2,1)S(1)}) fusion(f32[512,512]{0,1:T(8,128)S(1)} %fusion.82, f32[512,512]{0,1:T(8,128)S(1)} %fusion.83, bf16[512,512]{1,0:T(8,128)(2,1)S(1)} %copy-done.4, bf16[128,512]{1,0:T(8,128)(2,1)S(1)} %get-tuple-element.40, bf16[128,512]{1,0:T(8,128)(2,1)S(1)} %get-tuple-element.38, ...), kind=kOutput, calls=%fused_computation.45 | convolution fusion | flops 273940480 | bytes 4194304 | tf_op jit(solution)/shard_map/dot_general | solution.py:31
  29.5 0.6 %convolution_add_fusion.1 = f32[512,512]{0,1:T(8,128)S(1)} fusion(f32[512,512]{0,1:T(8,128)S(1)} %convolution_add_fusion.2, f32[512,512]{0,1:T(8,128)S(1)} %fusion.83, f32[512,512]{0,1:T(8,128)S(1)} %fusion.82, bf16[128,512]{1,0:T(8,128)(2,1)S(1)} %get-tuple-element.40, bf16[128,512]{1,0:T(8,128)(2,1)S(1)} %get-tuple-element.38, ...), kind=kOutput, calls=%fused_computation.2 | convolution fusion | flops 272367616 | bytes 4718592 | tf_op jit(solution)/shard_map/dot_general | solution.py:37
  30.1 3.1 %collective-permute-done.10 = bf16[256,512]{1,0:T(8,128)(2,1)S(1)} collective-permute-done((bf16[256,512]{1,0:T(8,128)(2,1)S(1)}, bf16[256,512]{1,0:T(8,128)(2,1)S(1)}, u32[]{:S(2)}, u32[]{:S(2)}) %collective-permute-start.10) | collective-permute-done | bytes 262176 | tf_op jit(solution)/shard_map/ppermute | solution.py:140
  33.2 1.7 %collective-permute-done.9 = bf16[256,512]{1,0:T(8,128)(2,1)S(1)} collective-permute-done((bf16[256,512]{1,0:T(8,128)(2,1)S(1)}, bf16[256,512]{1,0:T(8,128)(2,1)S(1)}, u32[]{:S(2)}, u32[]{:S(2)}) %collective-permute-start.9) | collective-permute-done | bytes 262176 | tf_op jit(solution)/shard_map/ppermute | solution.py:138
  35.0 0.8 %fusion.10 = f32[512,1024]{1,0:T(8,128)S(1)} fusion(bf16[512,512]{0,1:T(8,128)(2,1)S(1)} %get-tuple-element.12, bf16[512,512]{0,1:T(8,128)(2,1)S(1)} %get-tuple-element.11, bf16[128,512]{1,0:T(8,128)(2,1)S(1)} %get-tuple-element.39, bf16[128,512]{1,0:T(8,128)(2,1)S(1)} %get-tuple-element.37, bf16[128,512]{1,0:T(8,128)(2,1)S(1)} %get-tuple-element.35, ...), kind=kOutput, calls=%fused_computation.23 | convolution fusion | flops 541065216 | bytes 3670016 | tf_op jit(solution)/shard_map/dot_general | solution.py:36
  35.8 0.8 %collective-permute-start.13 = (bf16[256,512]{1,0:T(8,128)(2,1)S(1)}, bf16[256,512]{1,0:T(8,128)(2,1)S(1)}, u32[]{:S(2)}, u32[]{:S(2)}) collective-permute-start(bf16[256,512]{1,0:T(8,128)(2,1)S(1)} %collective-permute-done.9), channel_id=1, source_target_pairs={{0,4},{1,5},{4,8},{5,9},{8,12},{9,13},{12,14},{13,15},{14,10},{15,... | collective-permute-start | bytes 786440 | tf_op jit(solution)/shard_map/ppermute | solution.py:138
  37.1 0.5 fusion.81
  37.6 0.8 %multiply_convert_fusion.7 = (bf16[512,512]{0,1:T(8,128)(2,1)S(1)}, bf16[512,512]{0,1:T(8,128)(2,1)S(1)}) fusion(f32[512,512]{0,1:T(8,128)S(1)} %fusion.80, f32[512,512]{0,1:T(8,128)S(1)} %fusion.81, bf16[512,512]{1,0:T(8,128)(2,1)S(1)} %copy-done.4, bf16[128,512]{1,0:T(8,128)(2,1)S(1)} %get-tuple-element.48, bf16[128,512]{1,0:T(8,128)(2,1)S(1)} %get-tuple-element.46, ...), kind=kOutput, calls=%fused_computation.41 | convolution fusion | flops 273940480 | bytes 4194304 | tf_op jit(solution)/shard_map/dot_general | solution.py:31
  38.4 0.6 %convolution_add_fusion = f32[512,512]{0,1:T(8,128)S(1)} fusion(f32[512,512]{0,1:T(8,128)S(1)} %convolution_add_fusion.1, f32[512,512]{0,1:T(8,128)S(1)} %fusion.81, f32[512,512]{0,1:T(8,128)S(1)} %fusion.80, bf16[128,512]{1,0:T(8,128)(2,1)S(1)} %get-tuple-element.48, bf16[128,512]{1,0:T(8,128)(2,1)S(1)} %get-tuple-element.46, ...), kind=kOutput, calls=%fused_computation.1 | convolution fusion | flops 272367616 | bytes 4718592 | tf_op jit(solution)/shard_map/dot_general | solution.py:37
  39.0 5.7 %collective-permute-done.13 = bf16[256,512]{1,0:T(8,128)(2,1)S(1)} collective-permute-done((bf16[256,512]{1,0:T(8,128)(2,1)S(1)}, bf16[256,512]{1,0:T(8,128)(2,1)S(1)}, u32[]{:S(2)}, u32[]{:S(2)}) %collective-permute-start.13) | collective-permute-done | bytes 262176 | tf_op jit(solution)/shard_map/ppermute | solution.py:138
  44.7 0.8 %fusion.14 = f32[512,1024]{1,0:T(8,128)S(1)} fusion(bf16[512,512]{0,1:T(8,128)(2,1)S(1)} %get-tuple-element.14, bf16[512,512]{0,1:T(8,128)(2,1)S(1)} %get-tuple-element.13, bf16[128,512]{1,0:T(8,128)(2,1)S(1)} %get-tuple-element.47, bf16[128,512]{1,0:T(8,128)(2,1)S(1)} %get-tuple-element.45, bf16[128,512]{1,0:T(8,128)(2,1)S(1)} %get-tuple-element.43, ...), kind=kOutput, calls=%fused_computation.27 | convolution fusion | flops 541065216 | bytes 3670016 | tf_op jit(solution)/shard_map/dot_general | solution.py:36
  45.5 0.7 %collective-permute-done.14 = bf16[256,512]{1,0:T(8,128)(2,1)S(1)} collective-permute-done((bf16[256,512]{1,0:T(8,128)(2,1)S(1)}, bf16[256,512]{1,0:T(8,128)(2,1)S(1)}, u32[]{:S(2)}, u32[]{:S(2)}) %collective-permute-start.14) | collective-permute-done | bytes 262176 | tf_op jit(solution)/shard_map/ppermute | solution.py:142
  47.3 1.5 %multiply_reduce_fusion = (f32[512]{0:T(512)S(1)}, f32[512,512]{0,1:T(8,128)}) fusion(f32[512,512]{0,1:T(8,128)S(1)} %convolution_add_fusion, bf16[128,512]{1,0:T(8,128)(2,1)S(1)} %get-tuple-element.22, bf16[128,512]{1,0:T(8,128)(2,1)S(1)} %get-tuple-element.20, f32[256,512]{1,0:T(8,128)S(1)} %fusion.52, f32[256,512]{1,0:T(8,128)S(1)} %fusion.51, ...), kind=kOutput, calls=%fused_computation.32 | convolution fusion | flops 136838656 | bytes 3934208 | tf_op jit(solution)/shard_map/dot_general | solution.py:37
  48.8 0.6 %add_add_fusion = f32[512,1024]{1,0:T(8,128)S(1)} fusion(f32[512,1024]{1,0:T(8,128)S(1)} %fusion.14, f32[512,1024]{1,0:T(8,128)S(1)} %fusion.10, f32[512,1024]{1,0:T(8,128)S(1)} %fusion.21, f32[512,1024]{1,0:T(8,128)S(1)} %fusion.6, bf16[256,512]{1,0:T(8,128)(2,1)S(1)} %get-tuple-element.16, bf16[256,512]{1,0:T(8,128)(2,1)S(1)} %get-tuple-element.15, ...), kind=kOutput, calls=%fused_computation | convolution fusion | flops 272105472 | bytes 11272192 | tf_op jit(solution)/shard_map/dot_general | solution.py:36
  49.4 0.5 multiply_reduce_fusion.2
  50.4 2.7 %convolution_convert_fusion = bf16[128,512]{1,0:T(8,128)(2,1)} fusion(bf16[128,512]{1,0:T(8,128)(2,1)S(1)} %copy-done, f32[512,1024]{1,0:T(8,128)S(1)} %add_add_fusion, bf16[512,512]{1,0:T(8,128)(2,1)S(1)} %copy-done.2, f32[512,512]{0,1:T(8,128)} %get-tuple-element.50, f32[512]{0:T(512)S(1)} %rsqrt_multiply_fusion, f32[512]{0:T(512)S(1)} %get-tuple-element.51, ...), kind=kOutput, calls=%fused_computation.15 | convolution fusion | flops 136249344 | bytes 3149824 | tf_op jit(solution)/shard_map/dot_general | solution.py:45
  (57 shorter events, 7.7 us)
Async XLA Ops:
  0.0 49.9 %copy-start = (bf16[128,512]{1,0:T(8,128)(2,1)S(1)}, bf16[128,512]{1,0:T(8,128)(2,1)}, u32[]{:S(2)}) copy-start(bf16[128,512]{1,0:T(8,128)(2,1)} %param.9) | copy-start | bytes 393220
  0.0 7.2 %copy-start.3 = (bf16[128,512]{1,0:T(8,128)(2,1)S(1)}, bf16[128,512]{1,0:T(8,128)(2,1)}, u32[]{:S(2)}) copy-start(bf16[128,512]{1,0:T(8,128)(2,1)} %param.7) | copy-start | bytes 393220
  0.0 7.2 %copy-start.1 = (bf16[512,512]{1,0:T(8,128)(2,1)S(1)}, bf16[512,512]{1,0:T(8,128)(2,1)}, u32[]{:S(2)}) copy-start(bf16[512,512]{1,0:T(8,128)(2,1)} %param.11) | copy-start | bytes 1572868
  0.0 7.5 %copy-start.2 = (bf16[512,512]{1,0:T(8,128)(2,1)S(1)}, bf16[512,512]{1,0:T(8,128)(2,1)}, u32[]{:S(2)}) copy-start(bf16[512,512]{1,0:T(8,128)(2,1)} %param.12) | copy-start | bytes 1572868
  2.7 4.5 %collective-permute-start = (bf16[256,512]{1,0:T(8,128)(2,1)}, bf16[256,512]{1,0:T(8,128)(2,1)S(1)}, u32[]{:S(2)}, u32[]{:S(2)}) collective-permute-start(bf16[256,512]{1,0:T(8,128)(2,1)} %pad_maximum_fusion.6), channel_id=1, source_target_pairs={{0,1},{1,0},{2,3},{3,2},{4,5},{5,4},{6,7},{7,6},{8,9},{9,8},{10,11... | collective-permute-start | bytes 786440 | tf_op jit(solution)/shard_map/ppermute | solution.py:134
  3.2 9.9 %collective-permute-start.2 = (bf16[256,512]{1,0:T(8,128)(2,1)}, bf16[256,512]{1,0:T(8,128)(2,1)}, u32[]{:S(2)}, u32[]{:S(2)}) collective-permute-start(bf16[256,512]{1,0:T(8,128)(2,1)} %pad_maximum_fusion.6), channel_id=1, source_target_pairs={{0,2},{1,3},{4,0},{5,1},{8,4},{9,5},{12,8},{13,9},{14,12},{15,13},... | collective-permute-start | bytes 786440 | tf_op jit(solution)/shard_map/ppermute | solution.py:140
  5.7 10.6 %collective-permute-start.1 = (bf16[256,512]{1,0:T(8,128)(2,1)}, bf16[256,512]{1,0:T(8,128)(2,1)S(1)}, u32[]{:S(2)}, u32[]{:S(2)}) collective-permute-start(bf16[256,512]{1,0:T(8,128)(2,1)} %pad_maximum_fusion.6), channel_id=1, source_target_pairs={{0,4},{1,5},{4,8},{5,9},{8,12},{9,13},{12,14},{13,15},{14,10},{15,... | collective-permute-start | bytes 786440 | tf_op jit(solution)/shard_map/ppermute | solution.py:138
  7.0 1.0 %copy-start.4 = (bf16[512,512]{1,0:T(8,128)(2,1)S(1)}, bf16[512,512]{1,0:T(8,128)(2,1)}, u32[]{:S(2)}) copy-start(bf16[512,512]{1,0:T(8,128)(2,1)} %param.13) | copy-start | bytes 1572868
  14.1 3.0 %collective-permute-start.4 = (bf16[256,512]{1,0:T(8,128)(2,1)}, bf16[256,512]{1,0:T(8,128)(2,1)S(1)}, u32[]{:S(2)}, u32[]{:S(2)}) collective-permute-start(bf16[256,512]{1,0:T(8,128)(2,1)} %collective-permute-done.2), channel_id=1, source_target_pairs={{0,1},{1,0},{2,3},{3,2},{4,5},{5,4},{6,7},{7,6},{8,9},{9,8},{10,11... | collective-permute-start | bytes 786440 | tf_op jit(solution)/shard_map/ppermute | solution.py:142
  14.6 9.0 %collective-permute-start.6 = (bf16[256,512]{1,0:T(8,128)(2,1)}, bf16[256,512]{1,0:T(8,128)(2,1)S(1)}, u32[]{:S(2)}, u32[]{:S(2)}) collective-permute-start(bf16[256,512]{1,0:T(8,128)(2,1)} %collective-permute-done.2), channel_id=1, source_target_pairs={{0,2},{1,3},{4,0},{5,1},{8,4},{9,5},{12,8},{13,9},{14,12},{15,13},... | collective-permute-start | bytes 786440 | tf_op jit(solution)/shard_map/ppermute | solution.py:140
  16.3 1.5 %collective-permute-start.3 = (bf16[256,512]{1,0:T(8,128)(2,1)S(1)}, bf16[256,512]{1,0:T(8,128)(2,1)S(1)}, u32[]{:S(2)}, u32[]{:S(2)}) collective-permute-start(bf16[256,512]{1,0:T(8,128)(2,1)S(1)} %collective-permute-done.1), channel_id=1, source_target_pairs={{0,1},{1,0},{2,3},{3,2},{4,5},{5,4},{6,7},{7,6},{8,9},{9,8},{10,11... | collective-permute-start | bytes 786440 | tf_op jit(solution)/shard_map/ppermute | solution.py:142
  16.5 9.6 %collective-permute-start.5 = (bf16[256,512]{1,0:T(8,128)(2,1)S(1)}, bf16[256,512]{1,0:T(8,128)(2,1)S(1)}, u32[]{:S(2)}, u32[]{:S(2)}) collective-permute-start(bf16[256,512]{1,0:T(8,128)(2,1)S(1)} %collective-permute-done.1), channel_id=1, source_target_pairs={{0,4},{1,5},{4,8},{5,9},{8,12},{9,13},{12,14},{13,15},{14,10},{15,... | collective-permute-start | bytes 786440 | tf_op jit(solution)/shard_map/ppermute | solution.py:138
  23.6 3.3 %collective-permute-start.8 = (bf16[256,512]{1,0:T(8,128)(2,1)S(1)}, bf16[256,512]{1,0:T(8,128)(2,1)S(1)}, u32[]{:S(2)}, u32[]{:S(2)}) collective-permute-start(bf16[256,512]{1,0:T(8,128)(2,1)S(1)} %collective-permute-done.6), channel_id=1, source_target_pairs={{0,1},{1,0},{2,3},{3,2},{4,5},{5,4},{6,7},{7,6},{8,9},{9,8},{10,11... | collective-permute-start | bytes 786440 | tf_op jit(solution)/shard_map/ppermute | solution.py:142
  24.4 8.8 %collective-permute-start.10 = (bf16[256,512]{1,0:T(8,128)(2,1)S(1)}, bf16[256,512]{1,0:T(8,128)(2,1)S(1)}, u32[]{:S(2)}, u32[]{:S(2)}) collective-permute-start(bf16[256,512]{1,0:T(8,128)(2,1)S(1)} %collective-permute-done.6), channel_id=1, source_target_pairs={{0,2},{1,3},{4,0},{5,1},{8,4},{9,5},{12,8},{13,9},{14,12},{15,13},... | collective-permute-start | bytes 786440 | tf_op jit(solution)/shard_map/ppermute | solution.py:140
  26.1 1.5 %collective-permute-start.7 = (bf16[256,512]{1,0:T(8,128)(2,1)S(1)}, bf16[256,512]{1,0:T(8,128)(2,1)S(1)}, u32[]{:S(2)}, u32[]{:S(2)}) collective-permute-start(bf16[256,512]{1,0:T(8,128)(2,1)S(1)} %collective-permute-done.5), channel_id=1, source_target_pairs={{0,1},{1,0},{2,3},{3,2},{4,5},{5,4},{6,7},{7,6},{8,9},{9,8},{10,11... | collective-permute-start | bytes 786440 | tf_op jit(solution)/shard_map/ppermute | solution.py:142
  26.4 8.6 %collective-permute-start.9 = (bf16[256,512]{1,0:T(8,128)(2,1)S(1)}, bf16[256,512]{1,0:T(8,128)(2,1)S(1)}, u32[]{:S(2)}, u32[]{:S(2)}) collective-permute-start(bf16[256,512]{1,0:T(8,128)(2,1)S(1)} %collective-permute-done.5), channel_id=1, source_target_pairs={{0,4},{1,5},{4,8},{5,9},{8,12},{9,13},{12,14},{13,15},{14,10},{15,... | collective-permute-start | bytes 786440 | tf_op jit(solution)/shard_map/ppermute | solution.py:138
  33.2 3.4 %collective-permute-start.12 = (bf16[256,512]{1,0:T(8,128)(2,1)S(1)}, bf16[256,512]{1,0:T(8,128)(2,1)S(1)}, u32[]{:S(2)}, u32[]{:S(2)}) collective-permute-start(bf16[256,512]{1,0:T(8,128)(2,1)S(1)} %collective-permute-done.10), channel_id=1, source_target_pairs={{0,1},{1,0},{2,3},{3,2},{4,5},{5,4},{6,7},{7,6},{8,9},{9,8},{10,11... | collective-permute-start | bytes 786440 | tf_op jit(solution)/shard_map/ppermute | solution.py:142
  35.0 1.6 %collective-permute-start.11 = (bf16[256,512]{1,0:T(8,128)(2,1)S(1)}, bf16[256,512]{1,0:T(8,128)(2,1)S(1)}, u32[]{:S(2)}, u32[]{:S(2)}) collective-permute-start(bf16[256,512]{1,0:T(8,128)(2,1)S(1)} %collective-permute-done.9), channel_id=1, source_target_pairs={{0,1},{1,0},{2,3},{3,2},{4,5},{5,4},{6,7},{7,6},{8,9},{9,8},{10,11... | collective-permute-start | bytes 786440 | tf_op jit(solution)/shard_map/ppermute | solution.py:142
  35.8 8.9 %collective-permute-start.13 = (bf16[256,512]{1,0:T(8,128)(2,1)S(1)}, bf16[256,512]{1,0:T(8,128)(2,1)S(1)}, u32[]{:S(2)}, u32[]{:S(2)}) collective-permute-start(bf16[256,512]{1,0:T(8,128)(2,1)S(1)} %collective-permute-done.9), channel_id=1, source_target_pairs={{0,4},{1,5},{4,8},{5,9},{8,12},{9,13},{12,14},{13,15},{14,10},{15,... | collective-permute-start | bytes 786440 | tf_op jit(solution)/shard_map/ppermute | solution.py:138
  44.7 1.5 %collective-permute-start.14 = (bf16[256,512]{1,0:T(8,128)(2,1)S(1)}, bf16[256,512]{1,0:T(8,128)(2,1)S(1)}, u32[]{:S(2)}, u32[]{:S(2)}) collective-permute-start(bf16[256,512]{1,0:T(8,128)(2,1)S(1)} %collective-permute-done.13), channel_id=1, source_target_pairs={{0,1},{1,0},{2,3},{3,2},{4,5},{5,4},{6,7},{7,6},{8,9},{9,8},{10,11... | collective-permute-start | bytes 786440 | tf_op jit(solution)/shard_map/ppermute | solution.py:142

commit v4 on v3

--- a/solution.py
+++ b/solution.py
@@ -117,30 +117,44 @@
             cw_perm.append((ring[p] * 2 + c, ring[(p + 1) % chips] * 2 + c))
             ccw_perm.append((ring[p] * 2 + c, ring[(p - 1) % chips] * 2 + c))
     swap = [(i, i ^ 1) for i in range(chips * 2)]
-    cw_steps = chips // 2
-    ccw_steps = (chips - 1) // 2
+    steps = chips // 2
     axes = ("seq", "outer")
 
-    def split(chunks):
-        rows = chunks[0].shape[0] // 2
-        keys_part = jnp.concatenate([ch[:rows] for ch in chunks], axis=0)
-        scaled_part = jnp.concatenate([ch[rows:] for ch in chunks], axis=0)
-        return keys_part, scaled_part
+    def split(chunks, half):
+        keys_parts = []
+        scaled_parts = []
+        for ch in chunks:
+            for j in range(ch.shape[0] // (2 * half)):
+                keys_parts.append(ch[2 * j * half:(2 * j + 1) * half])
+                scaled_parts.append(ch[(2 * j + 1) * half:(2 * j + 2) * half])
+        return jnp.concatenate(keys_parts, axis=0), jnp.concatenate(scaled_parts, axis=0)
 
     def local_ring(keys, values, queries, learn_rate, w_gate, w_up, w_out):
         hidden = w_gate.shape[1]
+        rows = keys.shape[0]
+        halves = 2 if rows % 16 == 0 else 1
+        half = rows // halves
         scaled = (learn_rate[:, None] * values.astype(jnp.float32)).astype(jnp.bfloat16)
-        own = jnp.concatenate([keys, scaled], axis=0)
+        pieces = []
+        for j in range(halves):
+            pieces += [keys[j * half:(j + 1) * half], scaled[j * half:(j + 1) * half]]
+        own = jnp.concatenate(pieces, axis=0)
         sib = lax.ppermute(own, axes, swap)
-        total = add_grads(None, *split([own, sib]), w_gate, w_up, w_out)
+        total = add_grads(None, *split([own, sib], half), w_gate, w_up, w_out)
         arrived = [own, own]
-        for step in range(1, cw_steps + 1):
-            sent = [lax.ppermute(arrived[0], axes, cw_perm)]
-            if step <= ccw_steps:
-                sent.append(lax.ppermute(arrived[1], axes, ccw_perm))
+        for step in range(1, steps + 1):
+            last = step == steps and chips % 2 == 0
+            if last and halves == 2:
+                sent = [lax.ppermute(arrived[0][:2 * half], axes, cw_perm),
+                        lax.ppermute(arrived[1][2 * half:], axes, ccw_perm)]
+            elif last:
+                sent = [lax.ppermute(arrived[0], axes, cw_perm)]
+            else:
+                sent = [lax.ppermute(arrived[0], axes, cw_perm),
+                        lax.ppermute(arrived[1], axes, ccw_perm)]
             arrived = sent
             from_sib = [lax.ppermute(chunk, axes, swap) for chunk in arrived]
-            total = add_grads(total, *split(arrived + from_sib), w_gate, w_up, w_out)
+            total = add_grads(total, *split(arrived + from_sib, half), w_gate, w_up, w_out)
         full_in, full_out = total
         new_gate = renorm(w_gate, full_in[:, :hidden])
         new_up = renorm(w_up, full_in[:, hidden:])

time: 53.4 us -> 51.3 us (0.961)
  waiting for transfers between devices: 20.1 us -> 14.2 us
  local copies, waits for them, and re-layouts: 2.73 us -> 5.2 us
  starting transfers between devices: 8.86 us -> 10.7 us
  other arithmetic: 3.4 us -> 2.47 us
    ppermute x7 -> x8, waiting for transfers between devices: 17.8 us -> 12.8 us  [the longest x3 11.3 us: local_ring(): lax.ppermute(arrived[1], axes, ccw_perm)]
    unnamed x11 -> x36, local copies, waits for them, and re-layouts: 1.49 us -> 4.19 us
    ppermute x7 -> x8, starting transfers between devices: 7.75 us -> 8.94 us  [the longest x3 5.81 us: local_ring(): lax.ppermute(arrived[1], axes, ccw_perm)]
    ppermute x7 -> x8, waiting for transfers between devices: 2.3 us -> 1.32 us  [local_ring(): from_sib = [lax.ppermute(chunk, axes, swap) for chunk in arrived]]
    concatenate x1, other arithmetic: 1.62 us -> 0.72 us  [local_ring(): own = jnp.concatenate(pieces, axis=0)]
    ppermute x7 -> x8, starting transfers between devices: 0.65 us -> 1.3 us  [local_ring(): from_sib = [lax.ppermute(chunk, axes, swap) for chunk in arrived]]
    slice x15 -> x8, local copies, waits for them, and re-layouts: 1.24 us -> 0.97 us  [the longest x1 0.89 us: local_ring(): pieces += [keys[j * half:(j + 1) * half], scaled[j * half:(j + 1) * half]]]
  transfers between devices with their start and end apart: 15 -> 17, of which waited for: 8 -> 5; matrix products, arithmetic and copies ran while one was open for 26% -> 27% of each run, Pallas kernels for 0% -> 0%
where the time goes in v4:
time: 51.3 us; the launch traced here: 50.9 us
  matrix products  17.8 us (35%)
  waiting for transfers between devices  14.2 us (28%)
  starting transfers between devices  10.7 us (21%)
  local copies, waits for them, and re-layouts  5.2 us (10%)
  other arithmetic  2.47 us (5%)
  between operations  0.57 us (1%)
    ppermute x3, waiting for transfers between devices, local_ring(): lax.ppermute(arrived[1], axes, ccw_perm)  11.3 us
    ppermute x3, starting transfers between devices, local_ring(): lax.ppermute(arrived[1], axes, ccw_perm)  5.81 us
    unnamed x36, local copies, waits for them, and re-layouts  4.19 us
    dot_general x5, matrix products, gradients(): lax.dot_general(activation, scaled, contract_first, preferred_element_typ...  3.87 us
    dot_general x5, matrix products, gradients(): lax.dot_general(keys, both_grads, contract_first, preferred_element_type=...  3.34 us
    dot_general x5, matrix products, gradients(): lax.dot_general(scaled, w_out, contract_last, preferred_element_type=jnp....  3.31 us
    dot_general x1, matrix products, apply(): jnp.dot(q_act, full_out_w, preferred_element_type=jnp.float32)  2.75 us
    dot_general x5, matrix products, gradients(): gate_pre = jnp.dot(keys, w_gate, preferred_element_type=jnp.float32)  2.03 us
  transfers between devices with their start and end apart: 17, of which 5 were waited for; matrix products, arithmetic and copies ran while one was open for 27% of the time, Pallas kernels for 0%

profile of v4, /device:TPU:0, one launch (start us, length us, event | category | flops | bytes accessed | tf_op | source)
XLA Modules:
  0.0 50.9 jit_solution(10999027689153393517)
XLA Ops:
  0.0 1.1 %multiply_convert_fusion.27 = bf16[128,512]{1,0:T(8,128)(2,1)S(1)} fusion(bf16[128,512]{1,0:T(8,128)(2,1)} %param.8, f32[128]{0:T(128)} %param.10), kind=kLoop, calls=%fused_computation.84 | loop fusion | flops 196608 | bytes 262656 | tf_op jit(solution)/shard_map/convert_element_type | solution.py:137
  1.1 0.9 %fusion.74 = (bf16[64,512]{1,0:T(8,128)(2,1)S(1)}, bf16[64,512]{1,0:T(8,128)(2,1)S(1)}, bf16[64,512]{1,0:T(8,128)(2,1)S(1)}, bf16[64,512]{1,0:T(8,128)(2,1)S(1)}) fusion(bf16[128,512]{1,0:T(8,128)(2,1)} %param.7, bf16[128,512]{1,0:T(8,128)(2,1)S(1)} %multiply_convert_fusion.27), kind=kLoop, calls=%fused_computation.163 | loop fusion | bytes 524288 | tf_op jit(solution)/shard_map/slice | solution.py:140
  2.0 0.7 %pad_maximum_fusion = bf16[256,512]{1,0:T(8,128)(2,1)} fusion(bf16[64,512]{1,0:T(8,128)(2,1)S(1)} %get-tuple-element.85, bf16[64,512]{1,0:T(8,128)(2,1)S(1)} %get-tuple-element.80, bf16[64,512]{1,0:T(8,128)(2,1)S(1)} %get-tuple-element.86, bf16[64,512]{1,0:T(8,128)(2,1)S(1)} %get-tuple-element.79), kind=kLoop, calls=%fused_computation.74 | loop fusion | flops 1048576 | bytes 524288 | tf_op jit(solution)/shard_map/concatenate | solution.py:141
  3.2 2.5 %collective-permute-start.2 = (bf16[256,512]{1,0:T(8,128)(2,1)}, bf16[256,512]{1,0:T(8,128)(2,1)}, u32[]{:S(2)}, u32[]{:S(2)}) collective-permute-start(bf16[256,512]{1,0:T(8,128)(2,1)} %pad_maximum_fusion), channel_id=1, source_target_pairs={{0,2},{1,3},{4,0},{5,1},{8,4},{9,5},{12,8},{13,9},{14,12},{15,13},... | collective-permute-start | bytes 786440 | tf_op jit(solution)/shard_map/ppermute | solution.py:154
  5.7 1.3 %copy.8 = bf16[512,512]{0,1:T(8,128)(2,1)S(1)} copy(bf16[512,512]{1,0:T(8,128)(2,1)} %param.13) | data formatting | bytes 1048576 | tf_op args[6]
  8.7 4.3 %collective-permute-done.2 = bf16[256,512]{1,0:T(8,128)(2,1)} collective-permute-done((bf16[256,512]{1,0:T(8,128)(2,1)}, bf16[256,512]{1,0:T(8,128)(2,1)}, u32[]{:S(2)}, u32[]{:S(2)}) %collective-permute-start.2) | collective-permute-done | bytes 262176 | tf_op jit(solution)/shard_map/ppermute | solution.py:154
  13.0 1.7 %collective-permute-start.6 = (bf16[256,512]{1,0:T(8,128)(2,1)}, bf16[256,512]{1,0:T(8,128)(2,1)S(1)}, u32[]{:S(2)}, u32[]{:S(2)}) collective-permute-start(bf16[256,512]{1,0:T(8,128)(2,1)} %collective-permute-done.2), channel_id=1, source_target_pairs={{0,2},{1,3},{4,0},{5,1},{8,4},{9,5},{12,8},{13,9},{14,12},{15,13},... | collective-permute-start | bytes 786440 | tf_op jit(solution)/shard_map/ppermute | solution.py:154
  15.9 0.9 %constant_dynamic-update-slice_fusion.13 = (bf16[512,512]{1,0:T(8,128)(2,1)S(1)}, bf16[512,512]{1,0:T(8,128)(2,1)S(1)}) fusion(bf16[512,512]{1,0:T(8,128)(2,1)S(1)} %get-tuple-element.47, bf16[256,512]{1,0:T(8,128)(2,1)} %collective-permute-done.2, bf16[512,512]{1,0:T(8,128)(2,1)S(1)} %get-tuple-element.48), kind=kLoop, calls=%fused_computation.100 | loop fusion | bytes 262144
  16.8 0.9 %constant_dynamic-update-slice_fusion.12 = (bf16[512,512]{1,0:T(8,128)(2,1)S(1)}, bf16[512,512]{1,0:T(8,128)(2,1)S(1)}) fusion(bf16[512,512]{1,0:T(8,128)(2,1)S(1)} %get-tuple-element.45, bf16[256,512]{1,0:T(8,128)(2,1)} %collective-permute-done.2, bf16[512,512]{1,0:T(8,128)(2,1)S(1)} %get-tuple-element.46), kind=kLoop, calls=%fused_computation.99 | loop fusion | bytes 262144
  18.2 0.5 fusion.77
  19.2 0.8 %multiply_convert_fusion.11 = (bf16[512,512]{0,1:T(8,128)(2,1)S(1)}, bf16[512,512]{0,1:T(8,128)(2,1)S(1)}) fusion(f32[512,512]{0,1:T(8,128)S(1)} %fusion.77, f32[512,512]{0,1:T(8,128)S(1)} %fusion.76, bf16[512,512]{1,0:T(8,128)(2,1)S(1)} %get-tuple-element.35, bf16[512,512]{1,0:T(8,128)(2,1)S(1)} %copy-done.6), kind=kOutput, calls=%fused_computation.48 | convolution fusion | flops 271843328 | bytes 4194304 | tf_op jit(solution)/shard_map/dot_general | solution.py:31
  20.0 2.0 %collective-permute-done.6 = bf16[256,512]{1,0:T(8,128)(2,1)S(1)} collective-permute-done((bf16[256,512]{1,0:T(8,128)(2,1)}, bf16[256,512]{1,0:T(8,128)(2,1)S(1)}, u32[]{:S(2)}, u32[]{:S(2)}) %collective-permute-start.6) | collective-permute-done | bytes 262176 | tf_op jit(solution)/shard_map/ppermute | solution.py:154
  22.0 1.7 %collective-permute-start.10 = (bf16[256,512]{1,0:T(8,128)(2,1)S(1)}, bf16[256,512]{1,0:T(8,128)(2,1)S(1)}, u32[]{:S(2)}, u32[]{:S(2)}) collective-permute-start(bf16[256,512]{1,0:T(8,128)(2,1)S(1)} %collective-permute-done.6), channel_id=1, source_target_pairs={{0,2},{1,3},{4,0},{5,1},{8,4},{9,5},{12,8},{13,9},{14,12},{15,13},... | collective-permute-start | bytes 786440 | tf_op jit(solution)/shard_map/ppermute | solution.py:154
  23.6 0.6 %convolution_add_fusion.2 = f32[512,512]{0,1:T(8,128)S(1)} fusion(f32[512,512]{0,1:T(8,128)S(1)} %fusion.35, bf16[512,512]{1,0:T(8,128)(2,1)S(1)} %get-tuple-element.35, f32[512,512]{0,1:T(8,128)S(1)} %fusion.76, f32[512,512]{0,1:T(8,128)S(1)} %fusion.77), kind=kOutput, calls=%fused_computation.5 | convolution fusion | flops 270270464 | bytes 4718592 | tf_op jit(solution)/shard_map/dot_general | solution.py:37
  25.0 0.8 %fusion.7 = f32[512,1024]{1,0:T(8,128)S(1)} fusion(bf16[512,512]{1,0:T(8,128)(2,1)S(1)} %get-tuple-element.36, bf16[512,512]{0,1:T(8,128)(2,1)S(1)} %get-tuple-element.12, bf16[512,512]{0,1:T(8,128)(2,1)S(1)} %get-tuple-element.11), kind=kOutput, calls=%fused_computation.19 | convolution fusion | flops 538968064 | bytes 3670016 | tf_op jit(solution)/shard_map/dot_general | solution.py:36
  25.8 4.9 %collective-permute-done.10 = bf16[256,512]{1,0:T(8,128)(2,1)S(1)} collective-permute-done((bf16[256,512]{1,0:T(8,128)(2,1)S(1)}, bf16[256,512]{1,0:T(8,128)(2,1)S(1)}, u32[]{:S(2)}, u32[]{:S(2)}) %collective-permute-start.10) | collective-permute-done | bytes 262176 | tf_op jit(solution)/shard_map/ppermute | solution.py:154
  30.7 1.7 %collective-permute-start.14 = (bf16[128,512]{1,0:T(8,128)(2,1)S(1)}, bf16[128,512]{1,0:T(8,128)(2,1)S(1)}, u32[]{:S(2)}, u32[]{:S(2)}) collective-permute-start(bf16[128,512]{1,0:T(8,128)(2,1)S(1)} %slice.330), channel_id=1, source_target_pairs={{0,2},{1,3},{4,0},{5,1},{8,4},{9,5},{12,8},{13,9},{14,12},{15,13},... | collective-permute-start | bytes 393224 | tf_op jit(solution)/shard_map/ppermute | solution.py:149
  32.5 0.5 fusion.79
  33.0 0.5 fusion.78
  33.5 0.6 %collective-permute-start.13 = (bf16[128,512]{1,0:T(8,128)(2,1)S(1)}, bf16[128,512]{1,0:T(8,128)(2,1)S(1)}, u32[]{:S(2)}, u32[]{:S(2)}) collective-permute-start(bf16[128,512]{1,0:T(8,128)(2,1)S(1)} %slice.328), channel_id=1, source_target_pairs={{0,4},{1,5},{4,8},{5,9},{8,12},{9,13},{12,14},{13,15},{14,10},{15,... | collective-permute-start | bytes 393224 | tf_op jit(solution)/shard_map/ppermute | solution.py:148
  34.1 0.8 %multiply_convert_fusion.9 = (bf16[512,512]{0,1:T(8,128)(2,1)S(1)}, bf16[512,512]{0,1:T(8,128)(2,1)S(1)}) fusion(f32[512,512]{0,1:T(8,128)S(1)} %fusion.79, f32[512,512]{0,1:T(8,128)S(1)} %fusion.78, bf16[512,512]{1,0:T(8,128)(2,1)S(1)} %get-tuple-element.55, bf16[512,512]{1,0:T(8,128)(2,1)S(1)} %copy-done.6), kind=kOutput, calls=%fused_computation.44 | convolution fusion | flops 271843328 | bytes 4194304 | tf_op jit(solution)/shard_map/dot_general | solution.py:31
  34.9 0.6 %convolution_add_fusion.1 = f32[512,512]{0,1:T(8,128)S(1)} fusion(f32[512,512]{0,1:T(8,128)S(1)} %convolution_add_fusion.2, bf16[512,512]{1,0:T(8,128)(2,1)S(1)} %get-tuple-element.55, f32[512,512]{0,1:T(8,128)S(1)} %fusion.78, f32[512,512]{0,1:T(8,128)S(1)} %fusion.79), kind=kOutput, calls=%fused_computation.4 | convolution fusion | flops 270270464 | bytes 4718592 | tf_op jit(solution)/shard_map/dot_general | solution.py:37
  35.6 0.8 %fusion.11 = f32[512,1024]{1,0:T(8,128)S(1)} fusion(bf16[512,512]{1,0:T(8,128)(2,1)S(1)} %get-tuple-element.56, bf16[512,512]{0,1:T(8,128)(2,1)S(1)} %get-tuple-element.14, bf16[512,512]{0,1:T(8,128)(2,1)S(1)} %get-tuple-element.13), kind=kOutput, calls=%fused_computation.23 | convolution fusion | flops 538968064 | bytes 3670016 | tf_op jit(solution)/shard_map/dot_general | solution.py:36
  36.4 0.5 collective-permute-start.11
  37.1 1.6 %collective-permute-done.13 = bf16[128,512]{1,0:T(8,128)(2,1)S(1)} collective-permute-done((bf16[128,512]{1,0:T(8,128)(2,1)S(1)}, bf16[128,512]{1,0:T(8,128)(2,1)S(1)}, u32[]{:S(2)}, u32[]{:S(2)}) %collective-permute-start.13) | collective-permute-done | bytes 131104 | tf_op jit(solution)/shard_map/ppermute | solution.py:148
  38.8 1.3 %collective-permute-done.15 = bf16[128,512]{1,0:T(8,128)(2,1)S(1)} collective-permute-done((bf16[128,512]{1,0:T(8,128)(2,1)S(1)}, bf16[128,512]{1,0:T(8,128)(2,1)S(1)}, u32[]{:S(2)}, u32[]{:S(2)}) %collective-permute-start.15) | collective-permute-done | bytes 131104 | tf_op jit(solution)/shard_map/ppermute | solution.py:156
  43.1 0.8 %multiply_convert_fusion.7 = (bf16[512,512]{0,1:T(8,128)(2,1)S(1)}, bf16[512,512]{0,1:T(8,128)(2,1)S(1)}) fusion(f32[512,512]{0,1:T(8,128)S(1)} %fusion.81, f32[512,512]{0,1:T(8,128)S(1)} %fusion.80, bf16[512,512]{1,0:T(8,128)(2,1)S(1)} %get-tuple-element.19, bf16[512,512]{1,0:T(8,128)(2,1)S(1)} %copy-done.6), kind=kOutput, calls=%fused_computation.40 | convolution fusion | flops 271843328 | bytes 4194304 | tf_op jit(solution)/shard_map/dot_general | solution.py:31
  43.9 0.9 %add_add_fusion = f32[512,1024]{1,0:T(8,128)S(1)} fusion(f32[512,1024]{1,0:T(8,128)S(1)} %fusion.25, f32[512,1024]{1,0:T(8,128)S(1)} %fusion.11, f32[512,1024]{1,0:T(8,128)S(1)} %fusion.21, f32[512,1024]{1,0:T(8,128)S(1)} %fusion.7, bf16[512,512]{1,0:T(8,128)(2,1)S(1)} %get-tuple-element.20, bf16[512,512]{0,1:T(8,128)(2,1)S(1)} %get-tuple-element.10, ...), kind=kOutput, calls=%fused_computation | convolution fusion | flops 541065216 | bytes 12058624 | tf_op jit(solution)/shard_map/dot_general | solution.py:36
  44.9 0.5 multiply_reduce_fusion.2
  45.4 0.5 %copy-done.5 = bf16[512,512]{0,1:T(8,128)(2,1)S(1)} copy-done((bf16[512,512]{0,1:T(8,128)(2,1)S(1)}, bf16[512,512]{0,1:T(8,128)(2,1)}, u32[]{:S(2)}) %copy-start.5) | copy-done | bytes 524312
  45.9 1.7 %multiply_reduce_fusion = (f32[512]{0:T(512)S(1)}, f32[512,512]{0,1:T(8,128)}) fusion(f32[512,512]{0,1:T(8,128)S(1)} %fusion.36, f32[512,512]{0,1:T(8,128)S(1)} %convolution_add_fusion.1, bf16[512,512]{1,0:T(8,128)(2,1)S(1)} %get-tuple-element.19, f32[512,512]{0,1:T(8,128)S(1)} %fusion.80, f32[512,512]{0,1:T(8,128)S(1)} %fusion.81, ...), kind=kOutput, calls=%fused_computation.31 | convolution fusion | flops 271580672 | bytes 6293504 | tf_op jit(solution)/shard_map/dot_general | solution.py:37
  48.1 2.7 %convolution_convert_fusion = bf16[128,512]{1,0:T(8,128)(2,1)} fusion(bf16[128,512]{1,0:T(8,128)(2,1)S(1)} %copy-done, f32[512,1024]{1,0:T(8,128)S(1)} %add_add_fusion, bf16[512,512]{1,0:T(8,128)(2,1)S(1)} %copy-done.2, f32[512,512]{0,1:T(8,128)} %get-tuple-element.84, f32[512]{0:T(512)S(1)} %rsqrt_multiply_fusion, f32[512]{0:T(512)S(1)} %rsqrt_multiply_fusion.1, ...), kind=kOutput, calls=%fused_computation.15 | convolution fusion | flops 136249344 | bytes 3149824 | tf_op jit(solution)/shard_map/dot_general | solution.py:45
  (83 shorter events, 8.8 us)
Async XLA Ops:
  0.0 47.7 %copy-start = (bf16[128,512]{1,0:T(8,128)(2,1)S(1)}, bf16[128,512]{1,0:T(8,128)(2,1)}, u32[]{:S(2)}) copy-start(bf16[128,512]{1,0:T(8,128)(2,1)} %param.9) | copy-start | bytes 393220
  0.0 7.2 %copy-start.3 = (bf16[128,512]{1,0:T(8,128)(2,1)S(1)}, bf16[128,512]{1,0:T(8,128)(2,1)}, u32[]{:S(2)}) copy-start(bf16[128,512]{1,0:T(8,128)(2,1)} %param.7) | copy-start | bytes 393220
  0.0 7.2 %copy-start.1 = (bf16[512,512]{1,0:T(8,128)(2,1)S(1)}, bf16[512,512]{1,0:T(8,128)(2,1)}, u32[]{:S(2)}) copy-start(bf16[512,512]{1,0:T(8,128)(2,1)} %param.11) | copy-start | bytes 1572868
  2.0 5.6 %copy-start.2 = (bf16[512,512]{1,0:T(8,128)(2,1)S(1)}, bf16[512,512]{1,0:T(8,128)(2,1)}, u32[]{:S(2)}) copy-start(bf16[512,512]{1,0:T(8,128)(2,1)} %param.12) | copy-start | bytes 1572868
  2.7 4.5 %collective-permute-start = (bf16[256,512]{1,0:T(8,128)(2,1)}, bf16[256,512]{1,0:T(8,128)(2,1)S(1)}, u32[]{:S(2)}, u32[]{:S(2)}) collective-permute-start(bf16[256,512]{1,0:T(8,128)(2,1)} %pad_maximum_fusion), channel_id=1, source_target_pairs={{0,1},{1,0},{2,3},{3,2},{4,5},{5,4},{6,7},{7,6},{8,9},{9,8},{10,11... | collective-permute-start | bytes 786440 | tf_op jit(solution)/shard_map/ppermute | solution.py:142
  3.2 9.9 %collective-permute-start.2 = (bf16[256,512]{1,0:T(8,128)(2,1)}, bf16[256,512]{1,0:T(8,128)(2,1)}, u32[]{:S(2)}, u32[]{:S(2)}) collective-permute-start(bf16[256,512]{1,0:T(8,128)(2,1)} %pad_maximum_fusion), channel_id=1, source_target_pairs={{0,2},{1,3},{4,0},{5,1},{8,4},{9,5},{12,8},{13,9},{14,12},{15,13},... | collective-permute-start | bytes 786440 | tf_op jit(solution)/shard_map/ppermute | solution.py:154
  5.7 9.5 %collective-permute-start.1 = (bf16[256,512]{1,0:T(8,128)(2,1)}, bf16[256,512]{1,0:T(8,128)(2,1)S(1)}, u32[]{:S(2)}, u32[]{:S(2)}) collective-permute-start(bf16[256,512]{1,0:T(8,128)(2,1)} %pad_maximum_fusion), channel_id=1, source_target_pairs={{0,4},{1,5},{4,8},{5,9},{8,12},{9,13},{12,14},{13,15},{14,10},{15,... | collective-permute-start | bytes 786440 | tf_op jit(solution)/shard_map/ppermute | solution.py:153
  7.0 1.7 %copy-start.4 = (bf16[512,512]{0,1:T(8,128)(2,1)}, bf16[512,512]{0,1:T(8,128)(2,1)S(1)}, u32[]{:S(2)}) copy-start(bf16[512,512]{0,1:T(8,128)(2,1)S(1)} %copy.8) | copy-start | bytes 1572868
  7.0 1.2 %copy-start.6 = (bf16[512,512]{1,0:T(8,128)(2,1)S(1)}, bf16[512,512]{1,0:T(8,128)(2,1)}, u32[]{:S(2)}) copy-start(bf16[512,512]{1,0:T(8,128)(2,1)} %param.13) | copy-start | bytes 1572868
  13.0 5.1 %collective-permute-start.4 = (bf16[256,512]{1,0:T(8,128)(2,1)}, bf16[256,512]{1,0:T(8,128)(2,1)S(1)}, u32[]{:S(2)}, u32[]{:S(2)}) collective-permute-start(bf16[256,512]{1,0:T(8,128)(2,1)} %collective-permute-done.2), channel_id=1, source_target_pairs={{0,1},{1,0},{2,3},{3,2},{4,5},{5,4},{6,7},{7,6},{8,9},{9,8},{10,11... | collective-permute-start | bytes 786440 | tf_op jit(solution)/shard_map/ppermute | solution.py:156
  13.0 8.9 %collective-permute-start.6 = (bf16[256,512]{1,0:T(8,128)(2,1)}, bf16[256,512]{1,0:T(8,128)(2,1)S(1)}, u32[]{:S(2)}, u32[]{:S(2)}) collective-permute-start(bf16[256,512]{1,0:T(8,128)(2,1)} %collective-permute-done.2), channel_id=1, source_target_pairs={{0,2},{1,3},{4,0},{5,1},{8,4},{9,5},{12,8},{13,9},{14,12},{15,13},... | collective-permute-start | bytes 786440 | tf_op jit(solution)/shard_map/ppermute | solution.py:154
  15.2 2.9 %collective-permute-start.3 = (bf16[256,512]{1,0:T(8,128)(2,1)S(1)}, bf16[256,512]{1,0:T(8,128)(2,1)S(1)}, u32[]{:S(2)}, u32[]{:S(2)}) collective-permute-start(bf16[256,512]{1,0:T(8,128)(2,1)S(1)} %collective-permute-done.1), channel_id=1, source_target_pairs={{0,1},{1,0},{2,3},{3,2},{4,5},{5,4},{6,7},{7,6},{8,9},{9,8},{10,11... | collective-permute-start | bytes 786440 | tf_op jit(solution)/shard_map/ppermute | solution.py:156
  15.5 8.8 %collective-permute-start.5 = (bf16[256,512]{1,0:T(8,128)(2,1)S(1)}, bf16[256,512]{1,0:T(8,128)(2,1)S(1)}, u32[]{:S(2)}, u32[]{:S(2)}) collective-permute-start(bf16[256,512]{1,0:T(8,128)(2,1)S(1)} %collective-permute-done.1), channel_id=1, source_target_pairs={{0,4},{1,5},{4,8},{5,9},{8,12},{9,13},{12,14},{13,15},{14,10},{15,... | collective-permute-start | bytes 786440 | tf_op jit(solution)/shard_map/ppermute | solution.py:153
  22.0 10.5 %collective-permute-start.8 = (bf16[256,512]{1,0:T(8,128)(2,1)S(1)}, bf16[256,512]{1,0:T(8,128)(2,1)S(1)}, u32[]{:S(2)}, u32[]{:S(2)}) collective-permute-start(bf16[256,512]{1,0:T(8,128)(2,1)S(1)} %collective-permute-done.6), channel_id=1, source_target_pairs={{0,1},{1,0},{2,3},{3,2},{4,5},{5,4},{6,7},{7,6},{8,9},{9,8},{10,11... | collective-permute-start | bytes 786440 | tf_op jit(solution)/shard_map/ppermute | solution.py:156
  22.0 8.7 %collective-permute-start.10 = (bf16[256,512]{1,0:T(8,128)(2,1)S(1)}, bf16[256,512]{1,0:T(8,128)(2,1)S(1)}, u32[]{:S(2)}, u32[]{:S(2)}) collective-permute-start(bf16[256,512]{1,0:T(8,128)(2,1)S(1)} %collective-permute-done.6), channel_id=1, source_target_pairs={{0,2},{1,3},{4,0},{5,1},{8,4},{9,5},{12,8},{13,9},{14,12},{15,13},... | collective-permute-start | bytes 786440 | tf_op jit(solution)/shard_map/ppermute | solution.py:154
  24.3 8.1 %collective-permute-start.7 = (bf16[256,512]{1,0:T(8,128)(2,1)S(1)}, bf16[256,512]{1,0:T(8,128)(2,1)S(1)}, u32[]{:S(2)}, u32[]{:S(2)}) collective-permute-start(bf16[256,512]{1,0:T(8,128)(2,1)S(1)} %collective-permute-done.5), channel_id=1, source_target_pairs={{0,1},{1,0},{2,3},{3,2},{4,5},{5,4},{6,7},{7,6},{8,9},{9,8},{10,11... | collective-permute-start | bytes 786440 | tf_op jit(solution)/shard_map/ppermute | solution.py:156
  24.6 8.9 %collective-permute-start.9 = (bf16[256,512]{1,0:T(8,128)(2,1)S(1)}, bf16[256,512]{1,0:T(8,128)(2,1)S(1)}, u32[]{:S(2)}, u32[]{:S(2)}) collective-permute-start(bf16[256,512]{1,0:T(8,128)(2,1)S(1)} %collective-permute-done.5), channel_id=1, source_target_pairs={{0,4},{1,5},{4,8},{5,9},{8,12},{9,13},{12,14},{13,15},{14,10},{15,... | collective-permute-start | bytes 786440 | tf_op jit(solution)/shard_map/ppermute | solution.py:153
  30.7 6.3 %collective-permute-start.14 = (bf16[128,512]{1,0:T(8,128)(2,1)S(1)}, bf16[128,512]{1,0:T(8,128)(2,1)S(1)}, u32[]{:S(2)}, u32[]{:S(2)}) collective-permute-start(bf16[128,512]{1,0:T(8,128)(2,1)S(1)} %slice.330), channel_id=1, source_target_pairs={{0,2},{1,3},{4,0},{5,1},{8,4},{9,5},{12,8},{13,9},{14,12},{15,13},... | collective-permute-start | bytes 393224 | tf_op jit(solution)/shard_map/ppermute | solution.py:149
  33.5 5.2 %collective-permute-start.13 = (bf16[128,512]{1,0:T(8,128)(2,1)S(1)}, bf16[128,512]{1,0:T(8,128)(2,1)S(1)}, u32[]{:S(2)}, u32[]{:S(2)}) collective-permute-start(bf16[128,512]{1,0:T(8,128)(2,1)S(1)} %slice.328), channel_id=1, source_target_pairs={{0,4},{1,5},{4,8},{5,9},{8,12},{9,13},{12,14},{13,15},{14,10},{15,... | collective-permute-start | bytes 393224 | tf_op jit(solution)/shard_map/ppermute | solution.py:148
  36.3 5.8 %collective-permute-start.12 = (bf16[256,512]{1,0:T(8,128)(2,1)S(1)}, bf16[256,512]{1,0:T(8,128)(2,1)S(1)}, u32[]{:S(2)}, u32[]{:S(2)}) collective-permute-start(bf16[256,512]{1,0:T(8,128)(2,1)S(1)} %collective-permute-done.10), channel_id=1, source_target_pairs={{0,1},{1,0},{2,3},{3,2},{4,5},{5,4},{6,7},{7,6},{8,9},{9,8},{10,11... | collective-permute-start | bytes 786440 | tf_op jit(solution)/shard_map/ppermute | solution.py:156
  36.4 5.7 %collective-permute-start.11 = (bf16[256,512]{1,0:T(8,128)(2,1)S(1)}, bf16[256,512]{1,0:T(8,128)(2,1)S(1)}, u32[]{:S(2)}, u32[]{:S(2)}) collective-permute-start(bf16[256,512]{1,0:T(8,128)(2,1)S(1)} %collective-permute-done.9), channel_id=1, source_target_pairs={{0,1},{1,0},{2,3},{3,2},{4,5},{5,4},{6,7},{7,6},{8,9},{9,8},{10,11... | collective-permute-start | bytes 786440 | tf_op jit(solution)/shard_map/ppermute | solution.py:156
  37.0 1.8 %collective-permute-start.16 = (bf16[128,512]{1,0:T(8,128)(2,1)S(1)}, bf16[128,512]{1,0:T(8,128)(2,1)S(1)}, u32[]{:S(2)}, u32[]{:S(2)}) collective-permute-start(bf16[128,512]{1,0:T(8,128)(2,1)S(1)} %collective-permute-done.14), channel_id=1, source_target_pairs={{0,1},{1,0},{2,3},{3,2},{4,5},{5,4},{6,7},{7,6},{8,9},{9,8},{10,11... | collective-permute-start | bytes 393224 | tf_op jit(solution)/shard_map/ppermute | solution.py:156
  38.7 1.3 %collective-permute-start.15 = (bf16[128,512]{1,0:T(8,128)(2,1)S(1)}, bf16[128,512]{1,0:T(8,128)(2,1)S(1)}, u32[]{:S(2)}, u32[]{:S(2)}) collective-permute-start(bf16[128,512]{1,0:T(8,128)(2,1)S(1)} %collective-permute-done.13), channel_id=1, source_target_pairs={{0,1},{1,0},{2,3},{3,2},{4,5},{5,4},{6,7},{7,6},{8,9},{9,8},{10,11... | collective-permute-start | bytes 393224 | tf_op jit(solution)/shard_map/ppermute | solution.py:156
  44.8 1.0 %copy-start.5 = (bf16[512,512]{0,1:T(8,128)(2,1)S(1)}, bf16[512,512]{0,1:T(8,128)(2,1)}, u32[]{:S(2)}) copy-start(bf16[512,512]{0,1:T(8,128)(2,1)} %copy-done.4) | copy-start | bytes 1572868

commit v5 on v4

--- a/solution.py
+++ b/solution.py
@@ -135,10 +135,10 @@
         halves = 2 if rows % 16 == 0 else 1
         half = rows // halves
         scaled = (learn_rate[:, None] * values.astype(jnp.float32)).astype(jnp.bfloat16)
-        pieces = []
-        for j in range(halves):
-            pieces += [keys[j * half:(j + 1) * half], scaled[j * half:(j + 1) * half]]
-        own = jnp.concatenate(pieces, axis=0)
+        width = keys.shape[1]
+        own = jnp.stack(
+            [keys.reshape(halves, half, width), scaled.reshape(halves, half, width)], axis=1
+        ).reshape(2 * rows, width)
         sib = lax.ppermute(own, axes, swap)
         total = add_grads(None, *split([own, sib], half), w_gate, w_up, w_out)
         arrived = [own, own]
@@ -159,6 +159,7 @@
         new_gate = renorm(w_gate, full_in[:, :hidden])
         new_up = renorm(w_up, full_in[:, hidden:])
         new_out = renorm(w_out, full_out)
+        new_gate, new_up, new_out = lax.optimization_barrier((new_gate, new_up, new_out))
         return apply(queries, new_gate, new_up, new_out)
 
     return local_ring

time: 51.3 us -> 47.3 us (0.922)
  local copies, waits for them, and re-layouts: 5.2 us -> 1.9 us
  matrix products: 17.8 us -> 15.3 us
  waiting for transfers between devices: 14.2 us -> 15.4 us
  other arithmetic: 2.47 us -> 3.16 us
    ppermute x3, waiting for transfers between devices: 11.3 us -> 0.08 us  [local_ring(): lax.ppermute(arrived[1], axes, ccw_perm)]
    ppermute x3, waiting for transfers between devices: 0.01 us -> 9.92 us  [local_ring(): lax.ppermute(arrived[0], axes, cw_perm)]
    ppermute x3, starting transfers between devices: 0.82 us -> 6.73 us  [local_ring(): lax.ppermute(arrived[0], axes, cw_perm)]
    ppermute x3, starting transfers between devices: 5.81 us -> 0.42 us  [local_ring(): lax.ppermute(arrived[1], axes, ccw_perm)]
    ppermute x1, waiting for transfers between devices: 0.01 us -> 3.19 us  [local_ring(): lax.ppermute(arrived[1][2 * half:], axes, ccw_perm)]
    unnamed x36 -> x30, local copies, waits for them, and re-layouts: 4.19 us -> 1.77 us
    ppermute x1, waiting for transfers between devices: 1.57 us -> 0.01 us  [local_ring(): lax.ppermute(arrived[0][:2 * half], axes, cw_perm)]
    dot_general x1, matrix products: 2.75 us -> 1.43 us  [apply(): jnp.dot(q_act, full_out_w, preferred_element_type=jnp.float32)]
  transfers between devices with their start and end apart: 17 -> 17, of which waited for: 5 -> 9; matrix products, arithmetic and copies ran while one was open for 27% -> 25% of each run, Pallas kernels for 0% -> 0%
where the time goes in v5:
time: 47.3 us; the launch traced here: 47 us
  waiting for transfers between devices  15.4 us (33%)
  matrix products  15.3 us (32%)
  starting transfers between devices  10.7 us (23%)
  other arithmetic  3.16 us (7%)
  local copies, waits for them, and re-layouts  1.9 us (4%)
  between operations  0.52 us (1%)
    ppermute x3, waiting for transfers between devices, local_ring(): lax.ppermute(arrived[0], axes, cw_perm)  9.92 us
    ppermute x3, starting transfers between devices, local_ring(): lax.ppermute(arrived[0], axes, cw_perm)  6.73 us
    dot_general x5, matrix products, gradients(): lax.dot_general(keys, both_grads, contract_first, preferred_element_type=...  3.34 us
    dot_general x5, matrix products, gradients(): lax.dot_general(scaled, w_out, contract_last, preferred_element_type=jnp....  3.33 us
    ppermute x1, waiting for transfers between devices, local_ring(): lax.ppermute(arrived[1][2 * half:], axes, ccw_perm)  3.19 us
    dot_general x5, matrix products, gradients(): lax.dot_general(activation, scaled, contract_first, preferred_element_typ...  2.84 us
    ppermute x8, waiting for transfers between devices, local_ring(): from_sib = [lax.ppermute(chunk, axes, swap) for chunk in arrived]  2.11 us
    dot_general x5, matrix products, gradients(): gate_pre = jnp.dot(keys, w_gate, preferred_element_type=jnp.float32)  2.03 us
  transfers between devices with their start and end apart: 17, of which 9 were waited for; matrix products, arithmetic and copies ran while one was open for 25% of the time, Pallas kernels for 0%

profile of v5, /device:TPU:0, one launch (start us, length us, event | category | flops | bytes accessed | tf_op | source)
XLA Modules:
  0.0 47.0 jit_solution(5156158378631801697)
XLA Ops:
  0.0 1.1 %multiply_convert_fusion.23 = bf16[128,512]{1,0:T(8,128)(2,1)S(1)} fusion(bf16[128,512]{1,0:T(8,128)(2,1)} %param.8, f32[128]{0:T(128)} %param.10), kind=kLoop, calls=%fused_computation.81 | loop fusion | flops 196608 | bytes 262656 | tf_op jit(solution)/shard_map/convert_element_type | solution.py:137
  1.1 0.9 %pad_maximum_fusion = bf16[2,2,64,512]{3,2,1,0:T(8,128)(2,1)S(1)} fusion(bf16[2,1,64,512]{3,2,1,0:T(8,128)(2,1)S(1)} %bitcast.52, bf16[2,1,64,512]{3,2,1,0:T(8,128)(2,1)} %bitcast.53), kind=kLoop, calls=%fused_computation.71 | loop fusion | flops 131072 | bytes 524288 | tf_op jit(solution)/shard_map/stack | solution.py:139
  2.0 3.1 %collective-permute-start.1 = (bf16[256,512]{1,0:T(8,128)(2,1)S(1)}, bf16[256,512]{1,0:T(8,128)(2,1)S(1)}, u32[]{:S(2)}, u32[]{:S(2)}) collective-permute-start(bf16[256,512]{1,0:T(8,128)(2,1)S(1)} %bitcast.48), channel_id=1, source_target_pairs={{0,4},{1,5},{4,8},{5,9},{8,12},{9,13},{12,14},{13,15},{14,10},{15,... | collective-permute-start | bytes 786440 | tf_op jit(solution)/shard_map/ppermute | solution.py:153
  5.1 1.3 %copy.9 = bf16[512,512]{0,1:T(8,128)(2,1)S(1)} copy(bf16[512,512]{1,0:T(8,128)(2,1)} %param.13) | data formatting | bytes 1048576 | tf_op args[6]
  8.5 2.8 %collective-permute-done.1 = bf16[256,512]{1,0:T(8,128)(2,1)S(1)} collective-permute-done((bf16[256,512]{1,0:T(8,128)(2,1)S(1)}, bf16[256,512]{1,0:T(8,128)(2,1)S(1)}, u32[]{:S(2)}, u32[]{:S(2)}) %collective-permute-start.1) | collective-permute-done | bytes 262176 | tf_op jit(solution)/shard_map/ppermute | solution.py:153
  11.3 1.8 %collective-permute-start.5 = (bf16[256,512]{1,0:T(8,128)(2,1)S(1)}, bf16[256,512]{1,0:T(8,128)(2,1)S(1)}, u32[]{:S(2)}, u32[]{:S(2)}) collective-permute-start(bf16[256,512]{1,0:T(8,128)(2,1)S(1)} %collective-permute-done.1), channel_id=1, source_target_pairs={{0,4},{1,5},{4,8},{5,9},{8,12},{9,13},{12,14},{13,15},{14,10},{15,... | collective-permute-start | bytes 786440 | tf_op jit(solution)/shard_map/ppermute | solution.py:153
  14.2 0.6 %collective-permute-done.4 = bf16[256,512]{1,0:T(8,128)(2,1)S(1)} collective-permute-done((bf16[256,512]{1,0:T(8,128)(2,1)S(1)}, bf16[256,512]{1,0:T(8,128)(2,1)S(1)}, u32[]{:S(2)}, u32[]{:S(2)}) %collective-permute-start.4) | collective-permute-done | bytes 262176 | tf_op jit(solution)/shard_map/ppermute | solution.py:156
  14.8 0.5 %fusion.71 = f32[512,512]{0,1:T(8,128)S(1)} fusion(bf16[512,512]{1,0:T(8,128)(2,1)S(1)} %get-tuple-element.44, bf16[512,512]{1,0:T(8,128)(2,1)S(1)} %copy-done.1), kind=kOutput, calls=%fused_computation.161 | convolution fusion | flops 268435456 | bytes 2097152 | tf_op jit(solution)/shard_map/dot_general | solution.py:30
  15.3 0.5 %fusion.72 = f32[512,512]{0,1:T(8,128)S(1)} fusion(bf16[512,512]{1,0:T(8,128)(2,1)S(1)} %get-tuple-element.44, bf16[512,512]{1,0:T(8,128)(2,1)S(1)} %copy-done.2), kind=kOutput, calls=%fused_computation.162 | convolution fusion | flops 268435456 | bytes 2097152 | tf_op jit(solution)/shard_map/dot_general | solution.py:29
  15.8 0.8 %multiply_convert_fusion.11 = (bf16[512,512]{0,1:T(8,128)(2,1)S(1)}, bf16[512,512]{0,1:T(8,128)(2,1)S(1)}) fusion(f32[512,512]{0,1:T(8,128)S(1)} %fusion.72, f32[512,512]{0,1:T(8,128)S(1)} %fusion.71, bf16[512,512]{1,0:T(8,128)(2,1)S(1)} %get-tuple-element.43, bf16[512,512]{1,0:T(8,128)(2,1)S(1)} %copy-done.3), kind=kOutput, calls=%fused_computation.48 | convolution fusion | flops 271843328 | bytes 4194304 | tf_op jit(solution)/shard_map/dot_general | solution.py:31
  16.6 0.6 %convolution_add_fusion.2 = f32[512,512]{0,1:T(8,128)S(1)} fusion(f32[512,512]{0,1:T(8,128)S(1)} %fusion.31, bf16[512,512]{1,0:T(8,128)(2,1)S(1)} %get-tuple-element.43, f32[512,512]{0,1:T(8,128)S(1)} %fusion.71, f32[512,512]{0,1:T(8,128)S(1)} %fusion.72), kind=kOutput, calls=%fused_computation.5 | convolution fusion | flops 270270464 | bytes 4718592 | tf_op jit(solution)/shard_map/dot_general | solution.py:37
  17.2 2.8 %collective-permute-done.5 = bf16[256,512]{1,0:T(8,128)(2,1)S(1)} collective-permute-done((bf16[256,512]{1,0:T(8,128)(2,1)S(1)}, bf16[256,512]{1,0:T(8,128)(2,1)S(1)}, u32[]{:S(2)}, u32[]{:S(2)}) %collective-permute-start.5) | collective-permute-done | bytes 262176 | tf_op jit(solution)/shard_map/ppermute | solution.py:153
  20.0 1.8 %collective-permute-start.9 = (bf16[256,512]{1,0:T(8,128)(2,1)S(1)}, bf16[256,512]{1,0:T(8,128)(2,1)S(1)}, u32[]{:S(2)}, u32[]{:S(2)}) collective-permute-start(bf16[256,512]{1,0:T(8,128)(2,1)S(1)} %collective-permute-done.5), channel_id=1, source_target_pairs={{0,4},{1,5},{4,8},{5,9},{8,12},{9,13},{12,14},{13,15},{14,10},{15,... | collective-permute-start | bytes 786440 | tf_op jit(solution)/shard_map/ppermute | solution.py:153
  22.4 0.8 %fusion.7 = f32[512,1024]{1,0:T(8,128)S(1)} fusion(bf16[512,512]{1,0:T(8,128)(2,1)S(1)} %get-tuple-element.44, bf16[512,512]{0,1:T(8,128)(2,1)S(1)} %get-tuple-element.20, bf16[512,512]{0,1:T(8,128)(2,1)S(1)} %get-tuple-element.19), kind=kOutput, calls=%fused_computation.19 | convolution fusion | flops 538968064 | bytes 3670016 | tf_op jit(solution)/shard_map/dot_general | solution.py:36
  23.5 0.5 %fusion.73 = f32[512,512]{0,1:T(8,128)S(1)} fusion(bf16[512,512]{1,0:T(8,128)(2,1)S(1)} %get-tuple-element.68, bf16[512,512]{1,0:T(8,128)(2,1)S(1)} %copy-done.1), kind=kOutput, calls=%fused_computation.163 | convolution fusion | flops 268435456 | bytes 2097152 | tf_op jit(solution)/shard_map/dot_general | solution.py:30
  24.0 0.5 %fusion.74 = f32[512,512]{0,1:T(8,128)S(1)} fusion(bf16[512,512]{1,0:T(8,128)(2,1)S(1)} %get-tuple-element.68, bf16[512,512]{1,0:T(8,128)(2,1)S(1)} %copy-done.2), kind=kOutput, calls=%fused_computation.164 | convolution fusion | flops 268435456 | bytes 2097152 | tf_op jit(solution)/shard_map/dot_general | solution.py:29
  24.5 4.3 %collective-permute-done.9 = bf16[256,512]{1,0:T(8,128)(2,1)S(1)} collective-permute-done((bf16[256,512]{1,0:T(8,128)(2,1)S(1)}, bf16[256,512]{1,0:T(8,128)(2,1)S(1)}, u32[]{:S(2)}, u32[]{:S(2)}) %collective-permute-start.9) | collective-permute-done | bytes 262176 | tf_op jit(solution)/shard_map/ppermute | solution.py:153
  28.8 1.9 %collective-permute-start.13 = (bf16[128,512]{1,0:T(8,128)(2,1)S(1)}, bf16[128,512]{1,0:T(8,128)(2,1)S(1)}, u32[]{:S(2)}, u32[]{:S(2)}) collective-permute-start(bf16[128,512]{1,0:T(8,128)(2,1)S(1)} %slice.328), channel_id=1, source_target_pairs={{0,4},{1,5},{4,8},{5,9},{8,12},{9,13},{12,14},{13,15},{14,10},{15,... | collective-permute-start | bytes 393224 | tf_op jit(solution)/shard_map/ppermute | solution.py:148
  30.6 0.8 %multiply_convert_fusion.9 = (bf16[512,512]{0,1:T(8,128)(2,1)S(1)}, bf16[512,512]{0,1:T(8,128)(2,1)S(1)}) fusion(f32[512,512]{0,1:T(8,128)S(1)} %fusion.74, f32[512,512]{0,1:T(8,128)S(1)} %fusion.73, bf16[512,512]{1,0:T(8,128)(2,1)S(1)} %get-tuple-element.67, bf16[512,512]{1,0:T(8,128)(2,1)S(1)} %copy-done.3), kind=kOutput, calls=%fused_computation.44 | convolution fusion | flops 271843328 | bytes 4194304 | tf_op jit(solution)/shard_map/dot_general | solution.py:31
  31.5 0.6 %convolution_add_fusion.1 = f32[512,512]{0,1:T(8,128)S(1)} fusion(f32[512,512]{0,1:T(8,128)S(1)} %convolution_add_fusion.2, bf16[512,512]{1,0:T(8,128)(2,1)S(1)} %get-tuple-element.67, f32[512,512]{0,1:T(8,128)S(1)} %fusion.73, f32[512,512]{0,1:T(8,128)S(1)} %fusion.74), kind=kOutput, calls=%fused_computation.4 | convolution fusion | flops 270270464 | bytes 4718592 | tf_op jit(solution)/shard_map/dot_general | solution.py:37
  32.5 0.8 %fusion.11 = f32[512,1024]{1,0:T(8,128)S(1)} fusion(bf16[512,512]{1,0:T(8,128)(2,1)S(1)} %get-tuple-element.68, bf16[512,512]{0,1:T(8,128)(2,1)S(1)} %get-tuple-element.22, bf16[512,512]{0,1:T(8,128)(2,1)S(1)} %get-tuple-element.21), kind=kOutput, calls=%fused_computation.23 | convolution fusion | flops 538968064 | bytes 3670016 | tf_op jit(solution)/shard_map/dot_general | solution.py:36
  33.4 0.5 %collective-permute-start.12 = (bf16[256,512]{1,0:T(8,128)(2,1)S(1)}, bf16[256,512]{1,0:T(8,128)(2,1)S(1)}, u32[]{:S(2)}, u32[]{:S(2)}) collective-permute-start(bf16[256,512]{1,0:T(8,128)(2,1)S(1)} %collective-permute-done.10), channel_id=1, source_target_pairs={{0,1},{1,0},{2,3},{3,2},{4,5},{5,4},{6,7},{7,6},{8,9},{9,8},{10,11... | collective-permute-start | bytes 786440 | tf_op jit(solution)/shard_map/ppermute | solution.py:156
  34.1 3.2 %collective-permute-done.14 = bf16[128,512]{1,0:T(8,128)(2,1)S(1)} collective-permute-done((bf16[128,512]{1,0:T(8,128)(2,1)S(1)}, bf16[128,512]{1,0:T(8,128)(2,1)S(1)}, u32[]{:S(2)}, u32[]{:S(2)}) %collective-permute-start.14) | collective-permute-done | bytes 131104 | tf_op jit(solution)/shard_map/ppermute | solution.py:149
  37.3 1.3 %collective-permute-done.16 = bf16[128,512]{1,0:T(8,128)(2,1)S(1)} collective-permute-done((bf16[128,512]{1,0:T(8,128)(2,1)S(1)}, bf16[128,512]{1,0:T(8,128)(2,1)S(1)}, u32[]{:S(2)}, u32[]{:S(2)}) %collective-permute-start.16) | collective-permute-done | bytes 131104 | tf_op jit(solution)/shard_map/ppermute | solution.py:156
  39.3 0.5 multiply_convert_fusion.18
  40.8 0.5 %fusion.75 = f32[512,512]{0,1:T(8,128)S(1)} fusion(bf16[512,512]{1,0:T(8,128)(2,1)S(1)} %get-tuple-element.28, bf16[512,512]{1,0:T(8,128)(2,1)S(1)} %copy-done.1), kind=kOutput, calls=%fused_computation.165 | convolution fusion | flops 268435456 | bytes 2097152 | tf_op jit(solution)/shard_map/dot_general | solution.py:30
  41.2 0.5 %fusion.76 = f32[512,512]{0,1:T(8,128)S(1)} fusion(bf16[512,512]{1,0:T(8,128)(2,1)S(1)} %get-tuple-element.28, bf16[512,512]{1,0:T(8,128)(2,1)S(1)} %copy-done.2), kind=kOutput, calls=%fused_computation.166 | convolution fusion | flops 268435456 | bytes 2097152 | tf_op jit(solution)/shard_map/dot_general | solution.py:29
  41.7 0.8 %multiply_convert_fusion.7 = (bf16[512,512]{0,1:T(8,128)(2,1)S(1)}, bf16[512,512]{0,1:T(8,128)(2,1)S(1)}) fusion(f32[512,512]{0,1:T(8,128)S(1)} %fusion.76, f32[512,512]{0,1:T(8,128)S(1)} %fusion.75, bf16[512,512]{1,0:T(8,128)(2,1)S(1)} %get-tuple-element.27, bf16[512,512]{1,0:T(8,128)(2,1)S(1)} %copy-done.3), kind=kOutput, calls=%fused_computation.40 | convolution fusion | flops 271843328 | bytes 4194304 | tf_op jit(solution)/shard_map/dot_general | solution.py:31
  42.5 0.9 %add_add_fusion = f32[512,1024]{1,0:T(8,128)S(1)} fusion(f32[512,1024]{1,0:T(8,128)S(1)} %fusion.25, f32[512,1024]{1,0:T(8,128)S(1)} %fusion.11, f32[512,1024]{1,0:T(8,128)S(1)} %fusion.21, f32[512,1024]{1,0:T(8,128)S(1)} %fusion.7, bf16[512,512]{1,0:T(8,128)(2,1)S(1)} %get-tuple-element.28, bf16[512,512]{0,1:T(8,128)(2,1)S(1)} %get-tuple-element.18, ...), kind=kOutput, calls=%fused_computation | convolution fusion | flops 541065216 | bytes 12058624 | tf_op jit(solution)/shard_map/dot_general | solution.py:36
  43.4 0.5 %multiply_reduce_fusion.1 = (f32[512]{0:T(512)S(1)}, f32[512]{0:T(512)S(1)}, f32[512]{0:T(512)S(1)}, f32[512]{0:T(512)S(1)}) fusion(f32[512,1024]{1,0:T(8,128)S(1)} %add_add_fusion, bf16[512,512]{1,0:T(8,128)(2,1)S(1)} %copy-done.1, bf16[512,512]{1,0:T(8,128)(2,1)S(1)} %copy-done.2), kind=kLoop, calls=%fused_computation.36 | loop fusion | flops 3143680 | bytes 3153920 | tf_op jit(solution)/shard_map/reduce_sum | solution.py:19
  44.0 0.7 %multiply_reduce_fusion = (f32[512]{0:T(512)S(1)}, f32[512,512]{0,1:T(8,128)S(1)}) fusion(f32[512,512]{0,1:T(8,128)S(1)} %fusion.32, f32[512,512]{0,1:T(8,128)S(1)} %convolution_add_fusion.1, bf16[512,512]{1,0:T(8,128)(2,1)S(1)} %get-tuple-element.27, f32[512,512]{0,1:T(8,128)S(1)} %fusion.75, f32[512,512]{0,1:T(8,128)S(1)} %fusion.76, ...), kind=kOutput, calls=%fused_computation.31 | convolution fusion | flops 271580672 | bytes 6293504 | tf_op jit(solution)/shard_map/dot_general | solution.py:37
  45.6 1.4 %convolution_convert_fusion = bf16[128,512]{1,0:T(8,128)(2,1)} fusion(bf16[512,512]{0,1:T(8,128)(2,1)S(1)} %multiply_convert_fusion, bf16[512,512]{1,0:T(8,128)(2,1)S(1)} %get-tuple-element.9, bf16[128,512]{1,0:T(8,128)(2,1)S(1)} %copy-done, f32[128,512]{0,1:T(8,128)S(1)} %convolution_bitcast_fusion.1), kind=kOutput, calls=%fused_computation.15 | convolution fusion | flops 134676480 | bytes 1572864 | tf_op jit(solution)/shard_map/dot_general | solution.py:45
  (78 shorter events, 7.1 us)
Async XLA Ops:
  0.0 45.2 %copy-start = (bf16[128,512]{1,0:T(8,128)(2,1)S(1)}, bf16[128,512]{1,0:T(8,128)(2,1)}, u32[]{:S(2)}) copy-start(bf16[128,512]{1,0:T(8,128)(2,1)} %param.9) | copy-start | bytes 393220
  0.0 6.7 %copy-start.2 = (bf16[512,512]{1,0:T(8,128)(2,1)S(1)}, bf16[512,512]{1,0:T(8,128)(2,1)}, u32[]{:S(2)}) copy-start(bf16[512,512]{1,0:T(8,128)(2,1)} %param.11) | copy-start | bytes 1572868
  2.0 5.0 %copy-start.1 = (bf16[512,512]{1,0:T(8,128)(2,1)S(1)}, bf16[512,512]{1,0:T(8,128)(2,1)}, u32[]{:S(2)}) copy-start(bf16[512,512]{1,0:T(8,128)(2,1)} %param.12) | copy-start | bytes 1572868
  2.0 9.3 %collective-permute-start.1 = (bf16[256,512]{1,0:T(8,128)(2,1)S(1)}, bf16[256,512]{1,0:T(8,128)(2,1)S(1)}, u32[]{:S(2)}, u32[]{:S(2)}) collective-permute-start(bf16[256,512]{1,0:T(8,128)(2,1)S(1)} %bitcast.48), channel_id=1, source_target_pairs={{0,4},{1,5},{4,8},{5,9},{8,12},{9,13},{12,14},{13,15},{14,10},{15,... | collective-permute-start | bytes 786440 | tf_op jit(solution)/shard_map/ppermute | solution.py:153
  5.1 8.1 %collective-permute-start.2 = (bf16[256,512]{1,0:T(8,128)(2,1)S(1)}, bf16[256,512]{1,0:T(8,128)(2,1)S(1)}, u32[]{:S(2)}, u32[]{:S(2)}) collective-permute-start(bf16[256,512]{1,0:T(8,128)(2,1)S(1)} %bitcast.49), channel_id=1, source_target_pairs={{0,2},{1,3},{4,0},{5,1},{8,4},{9,5},{12,8},{13,9},{14,12},{15,13},... | collective-permute-start | bytes 786440 | tf_op jit(solution)/shard_map/ppermute | solution.py:154
  5.1 1.5 %collective-permute-start = (bf16[256,512]{1,0:T(8,128)(2,1)S(1)}, bf16[256,512]{1,0:T(8,128)(2,1)S(1)}, u32[]{:S(2)}, u32[]{:S(2)}) collective-permute-start(bf16[256,512]{1,0:T(8,128)(2,1)S(1)} %bitcast.50), channel_id=1, source_target_pairs={{0,1},{1,0},{2,3},{3,2},{4,5},{5,4},{6,7},{7,6},{8,9},{9,8},{10,11... | collective-permute-start | bytes 786440 | tf_op jit(solution)/shard_map/ppermute | solution.py:142
  6.5 1.0 %copy-start.3 = (bf16[512,512]{1,0:T(8,128)(2,1)S(1)}, bf16[512,512]{1,0:T(8,128)(2,1)}, u32[]{:S(2)}) copy-start(bf16[512,512]{1,0:T(8,128)(2,1)} %param.13) | copy-start | bytes 1572868
  11.3 2.8 %collective-permute-start.3 = (bf16[256,512]{1,0:T(8,128)(2,1)S(1)}, bf16[256,512]{1,0:T(8,128)(2,1)S(1)}, u32[]{:S(2)}, u32[]{:S(2)}) collective-permute-start(bf16[256,512]{1,0:T(8,128)(2,1)S(1)} %collective-permute-done.1), channel_id=1, source_target_pairs={{0,1},{1,0},{2,3},{3,2},{4,5},{5,4},{6,7},{7,6},{8,9},{9,8},{10,11... | collective-permute-start | bytes 786440 | tf_op jit(solution)/shard_map/ppermute | solution.py:156
  11.3 8.7 %collective-permute-start.5 = (bf16[256,512]{1,0:T(8,128)(2,1)S(1)}, bf16[256,512]{1,0:T(8,128)(2,1)S(1)}, u32[]{:S(2)}, u32[]{:S(2)}) collective-permute-start(bf16[256,512]{1,0:T(8,128)(2,1)S(1)} %collective-permute-done.1), channel_id=1, source_target_pairs={{0,4},{1,5},{4,8},{5,9},{8,12},{9,13},{12,14},{13,15},{14,10},{15,... | collective-permute-start | bytes 786440 | tf_op jit(solution)/shard_map/ppermute | solution.py:153
  13.2 1.6 %collective-permute-start.4 = (bf16[256,512]{1,0:T(8,128)(2,1)S(1)}, bf16[256,512]{1,0:T(8,128)(2,1)S(1)}, u32[]{:S(2)}, u32[]{:S(2)}) collective-permute-start(bf16[256,512]{1,0:T(8,128)(2,1)S(1)} %collective-permute-done.2), channel_id=1, source_target_pairs={{0,1},{1,0},{2,3},{3,2},{4,5},{5,4},{6,7},{7,6},{8,9},{9,8},{10,11... | collective-permute-start | bytes 786440 | tf_op jit(solution)/shard_map/ppermute | solution.py:156
  13.5 8.5 %collective-permute-start.6 = (bf16[256,512]{1,0:T(8,128)(2,1)S(1)}, bf16[256,512]{1,0:T(8,128)(2,1)S(1)}, u32[]{:S(2)}, u32[]{:S(2)}) collective-permute-start(bf16[256,512]{1,0:T(8,128)(2,1)S(1)} %collective-permute-done.2), channel_id=1, source_target_pairs={{0,2},{1,3},{4,0},{5,1},{8,4},{9,5},{12,8},{13,9},{14,12},{15,13},... | collective-permute-start | bytes 786440 | tf_op jit(solution)/shard_map/ppermute | solution.py:154
  20.0 3.2 %collective-permute-start.7 = (bf16[256,512]{1,0:T(8,128)(2,1)S(1)}, bf16[256,512]{1,0:T(8,128)(2,1)S(1)}, u32[]{:S(2)}, u32[]{:S(2)}) collective-permute-start(bf16[256,512]{1,0:T(8,128)(2,1)S(1)} %collective-permute-done.5), channel_id=1, source_target_pairs={{0,1},{1,0},{2,3},{3,2},{4,5},{5,4},{6,7},{7,6},{8,9},{9,8},{10,11... | collective-permute-start | bytes 786440 | tf_op jit(solution)/shard_map/ppermute | solution.py:156
  20.0 8.7 %collective-permute-start.9 = (bf16[256,512]{1,0:T(8,128)(2,1)S(1)}, bf16[256,512]{1,0:T(8,128)(2,1)S(1)}, u32[]{:S(2)}, u32[]{:S(2)}) collective-permute-start(bf16[256,512]{1,0:T(8,128)(2,1)S(1)} %collective-permute-done.5), channel_id=1, source_target_pairs={{0,4},{1,5},{4,8},{5,9},{8,12},{9,13},{12,14},{13,15},{14,10},{15,... | collective-permute-start | bytes 786440 | tf_op jit(solution)/shard_map/ppermute | solution.py:153
  22.0 1.5 %collective-permute-start.8 = (bf16[256,512]{1,0:T(8,128)(2,1)S(1)}, bf16[256,512]{1,0:T(8,128)(2,1)S(1)}, u32[]{:S(2)}, u32[]{:S(2)}) collective-permute-start(bf16[256,512]{1,0:T(8,128)(2,1)S(1)} %collective-permute-done.6), channel_id=1, source_target_pairs={{0,1},{1,0},{2,3},{3,2},{4,5},{5,4},{6,7},{7,6},{8,9},{9,8},{10,11... | collective-permute-start | bytes 786440 | tf_op jit(solution)/shard_map/ppermute | solution.py:156
  22.2 9.9 %collective-permute-start.10 = (bf16[256,512]{1,0:T(8,128)(2,1)S(1)}, bf16[256,512]{1,0:T(8,128)(2,1)S(1)}, u32[]{:S(2)}, u32[]{:S(2)}) collective-permute-start(bf16[256,512]{1,0:T(8,128)(2,1)S(1)} %collective-permute-done.6), channel_id=1, source_target_pairs={{0,2},{1,3},{4,0},{5,1},{8,4},{9,5},{12,8},{13,9},{14,12},{15,13},... | collective-permute-start | bytes 786440 | tf_op jit(solution)/shard_map/ppermute | solution.py:154
  28.8 5.2 %collective-permute-start.13 = (bf16[128,512]{1,0:T(8,128)(2,1)S(1)}, bf16[128,512]{1,0:T(8,128)(2,1)S(1)}, u32[]{:S(2)}, u32[]{:S(2)}) collective-permute-start(bf16[128,512]{1,0:T(8,128)(2,1)S(1)} %slice.328), channel_id=1, source_target_pairs={{0,4},{1,5},{4,8},{5,9},{8,12},{9,13},{12,14},{13,15},{14,10},{15,... | collective-permute-start | bytes 393224 | tf_op jit(solution)/shard_map/ppermute | solution.py:148
  32.1 5.2 %collective-permute-start.14 = (bf16[128,512]{1,0:T(8,128)(2,1)S(1)}, bf16[128,512]{1,0:T(8,128)(2,1)S(1)}, u32[]{:S(2)}, u32[]{:S(2)}) collective-permute-start(bf16[128,512]{1,0:T(8,128)(2,1)S(1)} %slice.330), channel_id=1, source_target_pairs={{0,2},{1,3},{4,0},{5,1},{8,4},{9,5},{12,8},{13,9},{14,12},{15,13},... | collective-permute-start | bytes 393224 | tf_op jit(solution)/shard_map/ppermute | solution.py:149
  33.3 7.3 %collective-permute-start.11 = (bf16[256,512]{1,0:T(8,128)(2,1)S(1)}, bf16[256,512]{1,0:T(8,128)(2,1)S(1)}, u32[]{:S(2)}, u32[]{:S(2)}) collective-permute-start(bf16[256,512]{1,0:T(8,128)(2,1)S(1)} %collective-permute-done.9), channel_id=1, source_target_pairs={{0,1},{1,0},{2,3},{3,2},{4,5},{5,4},{6,7},{7,6},{8,9},{9,8},{10,11... | collective-permute-start | bytes 786440 | tf_op jit(solution)/shard_map/ppermute | solution.py:156
  33.4 7.3 %collective-permute-start.12 = (bf16[256,512]{1,0:T(8,128)(2,1)S(1)}, bf16[256,512]{1,0:T(8,128)(2,1)S(1)}, u32[]{:S(2)}, u32[]{:S(2)}) collective-permute-start(bf16[256,512]{1,0:T(8,128)(2,1)S(1)} %collective-permute-done.10), channel_id=1, source_target_pairs={{0,1},{1,0},{2,3},{3,2},{4,5},{5,4},{6,7},{7,6},{8,9},{9,8},{10,11... | collective-permute-start | bytes 786440 | tf_op jit(solution)/shard_map/ppermute | solution.py:156
  34.0 3.4 %collective-permute-start.15 = (bf16[128,512]{1,0:T(8,128)(2,1)S(1)}, bf16[128,512]{1,0:T(8,128)(2,1)S(1)}, u32[]{:S(2)}, u32[]{:S(2)}) collective-permute-start(bf16[128,512]{1,0:T(8,128)(2,1)S(1)} %collective-permute-done.13), channel_id=1, source_target_pairs={{0,1},{1,0},{2,3},{3,2},{4,5},{5,4},{6,7},{7,6},{8,9},{9,8},{10,11... | collective-permute-start | bytes 393224 | tf_op jit(solution)/shard_map/ppermute | solution.py:156
  37.3 1.3 %collective-permute-start.16 = (bf16[128,512]{1,0:T(8,128)(2,1)S(1)}, bf16[128,512]{1,0:T(8,128)(2,1)S(1)}, u32[]{:S(2)}, u32[]{:S(2)}) collective-permute-start(bf16[128,512]{1,0:T(8,128)(2,1)S(1)} %collective-permute-done.14), channel_id=1, source_target_pairs={{0,1},{1,0},{2,3},{3,2},{4,5},{5,4},{6,7},{7,6},{8,9},{9,8},{10,11... | collective-permute-start | bytes 393224 | tf_op jit(solution)/shard_map/ppermute | solution.py:156

commit v6 on v5

--- a/solution.py
+++ b/solution.py
@@ -153,6 +153,8 @@
                 sent = [lax.ppermute(arrived[0], axes, cw_perm),
                         lax.ppermute(arrived[1], axes, ccw_perm)]
             arrived = sent
+            if step == steps:
+                total, arrived = lax.optimization_barrier((total, arrived))
             from_sib = [lax.ppermute(chunk, axes, swap) for chunk in arrived]
             total = add_grads(total, *split(arrived + from_sib, half), w_gate, w_up, w_out)
         full_in, full_out = total

time: 47.3 us -> 45.3 us (0.958)
  local copies, waits for them, and re-layouts: 1.9 us -> 0.37 us
  waiting for transfers between devices: 15.4 us -> 13.9 us
  starting transfers between devices: 10.7 us -> 11.2 us
    ppermute x1, waiting for transfers between devices: 3.19 us -> 0.01 us  [local_ring(): lax.ppermute(arrived[1][2 * half:], axes, ccw_perm)]
    unnamed x30 -> x29, local copies, waits for them, and re-layouts: 1.77 us -> 0.24 us
    ppermute x3, waiting for transfers between devices: 9.92 us -> 11.4 us  [local_ring(): lax.ppermute(arrived[0], axes, cw_perm)]
    dot_general x5, matrix products: 2.03 us -> 3.08 us  [gradients(): gate_pre = jnp.dot(keys, w_gate, preferred_element_type=jnp.float32)]
    add x0 -> x1, other arithmetic: none -> 0.55 us  [add_grads(): return (total[0] + full_in, total[1] + full_out)]
    dot_general x5, matrix products: 2.84 us -> 2.29 us  [gradients(): lax.dot_general(activation, scaled, contract_first, preferred_element_typ...]
    ppermute x1, starting transfers between devices: 0.01 us -> 0.52 us  [local_ring(): sib = lax.ppermute(own, axes, swap)]
  transfers between devices with their start and end apart: 17 -> 17, of which waited for: 9 -> 10; matrix products, arithmetic and copies ran while one was open for 25% -> 27% of each run, Pallas kernels for 0% -> 0%
where the time goes in v6:
time: 45.3 us; the launch traced here: 45.1 us
  matrix products  15.6 us (34%)
  waiting for transfers between devices  13.9 us (31%)
  starting transfers between devices  11.2 us (25%)
  other arithmetic  3.59 us (8%)
  between operations  0.49 us (1%)
    ppermute x3, waiting for transfers between devices, local_ring(): lax.ppermute(arrived[0], axes, cw_perm)  11.4 us
    ppermute x3, starting transfers between devices, local_ring(): lax.ppermute(arrived[0], axes, cw_perm)  6.29 us
    dot_general x5, matrix products, gradients(): lax.dot_general(scaled, w_out, contract_last, preferred_element_type=jnp....  3.34 us
    dot_general x5, matrix products, gradients(): lax.dot_general(keys, both_grads, contract_first, preferred_element_type=...  3.22 us
    dot_general x5, matrix products, gradients(): gate_pre = jnp.dot(keys, w_gate, preferred_element_type=jnp.float32)  3.08 us
    ppermute x8, waiting for transfers between devices, local_ring(): from_sib = [lax.ppermute(chunk, axes, swap) for chunk in arrived]  2.4 us
    dot_general x5, matrix products, gradients(): lax.dot_general(activation, scaled, contract_first, preferred_element_typ...  2.29 us
    dot_general x5, matrix products, gradients(): up_pre = jnp.dot(keys, w_up, preferred_element_type=jnp.float32)  2.04 us
  transfers between devices with their start and end apart: 17, of which 10 were waited for; matrix products, arithmetic and copies ran while one was open for 27% of the time, Pallas kernels for 0%

profile of v6, /device:TPU:0, one launch (start us, length us, event | category | flops | bytes accessed | tf_op | source)
XLA Modules:
  0.0 45.1 jit_solution(5619692883520811182)
XLA Ops:
  0.0 1.1 %multiply_convert_fusion.23 = bf16[128,512]{1,0:T(8,128)(2,1)S(1)} fusion(bf16[128,512]{1,0:T(8,128)(2,1)} %param.8, f32[128]{0:T(128)} %param.10), kind=kLoop, calls=%fused_computation.80 | loop fusion | flops 196608 | bytes 262656 | tf_op jit(solution)/shard_map/convert_element_type | solution.py:137
  1.1 0.9 %pad_maximum_fusion = bf16[2,2,64,512]{3,2,1,0:T(8,128)(2,1)S(1)} fusion(bf16[2,1,64,512]{3,2,1,0:T(8,128)(2,1)S(1)} %bitcast.52, bf16[2,1,64,512]{3,2,1,0:T(8,128)(2,1)} %bitcast.53), kind=kLoop, calls=%fused_computation.70 | loop fusion | flops 131072 | bytes 524288 | tf_op jit(solution)/shard_map/stack | solution.py:139
  2.0 0.5 %collective-permute-start = (bf16[256,512]{1,0:T(8,128)(2,1)S(1)}, bf16[256,512]{1,0:T(8,128)(2,1)S(1)}, u32[]{:S(2)}, u32[]{:S(2)}) collective-permute-start(bf16[256,512]{1,0:T(8,128)(2,1)S(1)} %bitcast.48), channel_id=1, source_target_pairs={{0,1},{1,0},{2,3},{3,2},{4,5},{5,4},{6,7},{7,6},{8,9},{9,8},{10,11... | collective-permute-start | bytes 786440 | tf_op jit(solution)/shard_map/ppermute | solution.py:142
  2.5 2.6 %collective-permute-start.1 = (bf16[256,512]{1,0:T(8,128)(2,1)S(1)}, bf16[256,512]{1,0:T(8,128)(2,1)S(1)}, u32[]{:S(2)}, u32[]{:S(2)}) collective-permute-start(bf16[256,512]{1,0:T(8,128)(2,1)S(1)} %bitcast.49), channel_id=1, source_target_pairs={{0,4},{1,5},{4,8},{5,9},{8,12},{9,13},{12,14},{13,15},{14,10},{15,... | collective-permute-start | bytes 786440 | tf_op jit(solution)/shard_map/ppermute | solution.py:153
  5.2 1.3 %fusion.61 = f32[256,512]{1,0:T(8,128)S(1)} fusion(bf16[512,512]{1,0:T(8,128)(2,1)} %param.11, bf16[64,512]{1,0:T(8,128)(2,1)S(1)} %get-tuple-element.76, bf16[64,512]{1,0:T(8,128)(2,1)S(1)} %get-tuple-element.73, bf16[64,512]{1,0:T(8,128)(2,1)S(1)} %get-tuple-element.72, bf16[64,512]{1,0:T(8,128)(2,1)S(1)} %get-tuple-element.69), kind=kOutput, calls=%fused_computation.152 | convolution fusion | flops 135266304 | bytes 1310720 | tf_op jit(solution)/shard_map/dot_general | solution.py:29
  6.9 0.5 %multiply_convert_fusion.20 = (bf16[256,512]{1,0:T(8,128)(2,1)S(1)}, bf16[256,512]{1,0:T(8,128)(2,1)S(1)}) fusion(f32[256,512]{1,0:T(8,128)S(1)} %fusion.61, f32[256,512]{1,0:T(8,128)S(1)} %fusion.62, bf16[512,512]{1,0:T(8,128)(2,1)S(1)} %copy-done.3, bf16[64,512]{1,0:T(8,128)(2,1)S(1)} %get-tuple-element.74, bf16[64,512]{1,0:T(8,128)(2,1)S(1)} %get-tuple-element.75, ...), kind=kOutput, calls=%fused_computation.65 | convolution fusion | flops 136970240 | bytes 2359296 | tf_op jit(solution)/shard_map/dot_general | solution.py:31
  7.8 4.2 %collective-permute-done.1 = bf16[256,512]{1,0:T(8,128)(2,1)S(1)} collective-permute-done((bf16[256,512]{1,0:T(8,128)(2,1)S(1)}, bf16[256,512]{1,0:T(8,128)(2,1)S(1)}, u32[]{:S(2)}, u32[]{:S(2)}) %collective-permute-start.1) | collective-permute-done | bytes 262176 | tf_op jit(solution)/shard_map/ppermute | solution.py:153
  12.0 1.8 %collective-permute-start.5 = (bf16[256,512]{1,0:T(8,128)(2,1)S(1)}, bf16[256,512]{1,0:T(8,128)(2,1)S(1)}, u32[]{:S(2)}, u32[]{:S(2)}) collective-permute-start(bf16[256,512]{1,0:T(8,128)(2,1)S(1)} %collective-permute-done.1), channel_id=1, source_target_pairs={{0,4},{1,5},{4,8},{5,9},{8,12},{9,13},{12,14},{13,15},{14,10},{15,... | collective-permute-start | bytes 786440 | tf_op jit(solution)/shard_map/ppermute | solution.py:153
  14.8 0.6 %collective-permute-done.4 = bf16[256,512]{1,0:T(8,128)(2,1)S(1)} collective-permute-done((bf16[256,512]{1,0:T(8,128)(2,1)S(1)}, bf16[256,512]{1,0:T(8,128)(2,1)S(1)}, u32[]{:S(2)}, u32[]{:S(2)}) %collective-permute-start.4) | collective-permute-done | bytes 262176 | tf_op jit(solution)/shard_map/ppermute | solution.py:158
  15.5 0.5 %fusion.69 = f32[512,512]{0,1:T(8,128)S(1)} fusion(bf16[512,512]{1,0:T(8,128)(2,1)S(1)} %get-tuple-element.54, bf16[512,512]{1,0:T(8,128)(2,1)S(1)} %copy-done.1), kind=kOutput, calls=%fused_computation.160 | convolution fusion | flops 268435456 | bytes 2097152 | tf_op jit(solution)/shard_map/dot_general | solution.py:30
  16.0 0.5 %fusion.70 = f32[512,512]{0,1:T(8,128)S(1)} fusion(bf16[512,512]{1,0:T(8,128)(2,1)S(1)} %get-tuple-element.54, bf16[512,512]{1,0:T(8,128)(2,1)S(1)} %copy-done.2), kind=kOutput, calls=%fused_computation.161 | convolution fusion | flops 268435456 | bytes 2097152 | tf_op jit(solution)/shard_map/dot_general | solution.py:29
  16.5 0.8 %multiply_convert_fusion.11 = (bf16[512,512]{0,1:T(8,128)(2,1)S(1)}, bf16[512,512]{0,1:T(8,128)(2,1)S(1)}) fusion(f32[512,512]{0,1:T(8,128)S(1)} %fusion.70, f32[512,512]{0,1:T(8,128)S(1)} %fusion.69, bf16[512,512]{1,0:T(8,128)(2,1)S(1)} %get-tuple-element.53, bf16[512,512]{1,0:T(8,128)(2,1)S(1)} %copy-done.3), kind=kOutput, calls=%fused_computation.47 | convolution fusion | flops 271843328 | bytes 4194304 | tf_op jit(solution)/shard_map/dot_general | solution.py:31
  17.8 3.0 %collective-permute-done.5 = bf16[256,512]{1,0:T(8,128)(2,1)S(1)} collective-permute-done((bf16[256,512]{1,0:T(8,128)(2,1)S(1)}, bf16[256,512]{1,0:T(8,128)(2,1)S(1)}, u32[]{:S(2)}, u32[]{:S(2)}) %collective-permute-start.5) | collective-permute-done | bytes 262176 | tf_op jit(solution)/shard_map/ppermute | solution.py:153
  20.7 1.8 %collective-permute-start.9 = (bf16[256,512]{1,0:T(8,128)(2,1)S(1)}, bf16[256,512]{1,0:T(8,128)(2,1)S(1)}, u32[]{:S(2)}, u32[]{:S(2)}) collective-permute-start(bf16[256,512]{1,0:T(8,128)(2,1)S(1)} %collective-permute-done.5), channel_id=1, source_target_pairs={{0,4},{1,5},{4,8},{5,9},{8,12},{9,13},{12,14},{13,15},{14,10},{15,... | collective-permute-start | bytes 786440 | tf_op jit(solution)/shard_map/ppermute | solution.py:153
  23.1 0.8 %fusion.5 = f32[512,1024]{1,0:T(8,128)S(1)} fusion(bf16[512,512]{1,0:T(8,128)(2,1)S(1)} %get-tuple-element.54, bf16[512,512]{0,1:T(8,128)(2,1)S(1)} %get-tuple-element.30, bf16[512,512]{0,1:T(8,128)(2,1)S(1)} %get-tuple-element.29), kind=kOutput, calls=%fused_computation.18 | convolution fusion | flops 538968064 | bytes 3670016 | tf_op jit(solution)/shard_map/dot_general | solution.py:36
  24.2 0.5 %fusion.71 = f32[512,512]{0,1:T(8,128)S(1)} fusion(bf16[512,512]{1,0:T(8,128)(2,1)S(1)} %get-tuple-element.78, bf16[512,512]{1,0:T(8,128)(2,1)S(1)} %copy-done.1), kind=kOutput, calls=%fused_computation.162 | convolution fusion | flops 268435456 | bytes 2097152 | tf_op jit(solution)/shard_map/dot_general | solution.py:30
  24.7 0.5 %fusion.72 = f32[512,512]{0,1:T(8,128)S(1)} fusion(bf16[512,512]{1,0:T(8,128)(2,1)S(1)} %get-tuple-element.78, bf16[512,512]{1,0:T(8,128)(2,1)S(1)} %copy-done.2), kind=kOutput, calls=%fused_computation.163 | convolution fusion | flops 268435456 | bytes 2097152 | tf_op jit(solution)/shard_map/dot_general | solution.py:29
  25.2 4.2 %collective-permute-done.9 = bf16[256,512]{1,0:T(8,128)(2,1)S(1)} collective-permute-done((bf16[256,512]{1,0:T(8,128)(2,1)S(1)}, bf16[256,512]{1,0:T(8,128)(2,1)S(1)}, u32[]{:S(2)}, u32[]{:S(2)}) %collective-permute-start.9) | collective-permute-done | bytes 262176 | tf_op jit(solution)/shard_map/ppermute | solution.py:153
  29.5 1.9 %collective-permute-start.13 = (bf16[128,512]{1,0:T(8,128)(2,1)S(1)}, bf16[128,512]{1,0:T(8,128)(2,1)S(1)}, u32[]{:S(2)}, u32[]{:S(2)}) collective-permute-start(bf16[128,512]{1,0:T(8,128)(2,1)S(1)} %slice.328), channel_id=1, source_target_pairs={{0,4},{1,5},{4,8},{5,9},{8,12},{9,13},{12,14},{13,15},{14,10},{15,... | collective-permute-start | bytes 393224 | tf_op jit(solution)/shard_map/ppermute | solution.py:148
  31.3 0.8 %multiply_convert_fusion.9 = (bf16[512,512]{0,1:T(8,128)(2,1)S(1)}, bf16[512,512]{0,1:T(8,128)(2,1)S(1)}) fusion(f32[512,512]{0,1:T(8,128)S(1)} %fusion.72, f32[512,512]{0,1:T(8,128)S(1)} %fusion.71, bf16[512,512]{1,0:T(8,128)(2,1)S(1)} %get-tuple-element.77, bf16[512,512]{1,0:T(8,128)(2,1)S(1)} %copy-done.3), kind=kOutput, calls=%fused_computation.43 | convolution fusion | flops 271843328 | bytes 4194304 | tf_op jit(solution)/shard_map/dot_general | solution.py:31
  33.2 0.5 %collective-permute-start.12 = (bf16[256,512]{1,0:T(8,128)(2,1)S(1)}, bf16[256,512]{1,0:T(8,128)(2,1)S(1)}, u32[]{:S(2)}, u32[]{:S(2)}) collective-permute-start(bf16[256,512]{1,0:T(8,128)(2,1)S(1)} %collective-permute-done.10), channel_id=1, source_target_pairs={{0,1},{1,0},{2,3},{3,2},{4,5},{5,4},{6,7},{7,6},{8,9},{9,8},{10,11... | collective-permute-start | bytes 786440 | tf_op jit(solution)/shard_map/ppermute | solution.py:158
  33.7 0.8 %fusion.9 = f32[512,1024]{1,0:T(8,128)S(1)} fusion(bf16[512,512]{1,0:T(8,128)(2,1)S(1)} %get-tuple-element.78, bf16[512,512]{0,1:T(8,128)(2,1)S(1)} %get-tuple-element.32, bf16[512,512]{0,1:T(8,128)(2,1)S(1)} %get-tuple-element.31), kind=kOutput, calls=%fused_computation.22 | convolution fusion | flops 538968064 | bytes 3670016 | tf_op jit(solution)/shard_map/dot_general | solution.py:36
  35.1 0.5 %fusion.73 = f32[512,512]{0,1:T(8,128)S(1)} fusion(bf16[512,512]{1,0:T(8,128)(2,1)S(1)} %get-tuple-element.38, bf16[512,512]{1,0:T(8,128)(2,1)S(1)} %copy-done.1), kind=kOutput, calls=%fused_computation.164 | convolution fusion | flops 268435456 | bytes 2097152 | tf_op jit(solution)/shard_map/dot_general | solution.py:30
  35.6 0.5 %fusion.74 = f32[512,512]{0,1:T(8,128)S(1)} fusion(bf16[512,512]{1,0:T(8,128)(2,1)S(1)} %get-tuple-element.38, bf16[512,512]{1,0:T(8,128)(2,1)S(1)} %copy-done.2), kind=kOutput, calls=%fused_computation.165 | convolution fusion | flops 268435456 | bytes 2097152 | tf_op jit(solution)/shard_map/dot_general | solution.py:29
  36.1 0.8 %multiply_convert_fusion.7 = (bf16[512,512]{0,1:T(8,128)(2,1)S(1)}, bf16[512,512]{0,1:T(8,128)(2,1)S(1)}) fusion(f32[512,512]{0,1:T(8,128)S(1)} %fusion.74, f32[512,512]{0,1:T(8,128)S(1)} %fusion.73, bf16[512,512]{1,0:T(8,128)(2,1)S(1)} %get-tuple-element.37, bf16[512,512]{1,0:T(8,128)(2,1)S(1)} %copy-done.3), kind=kOutput, calls=%fused_computation.39 | convolution fusion | flops 271843328 | bytes 4194304 | tf_op jit(solution)/shard_map/dot_general | solution.py:31
  36.9 0.8 %add_add_fusion = f32[512,1024]{1,0:T(8,128)S(1)} fusion(f32[512,1024]{1,0:T(8,128)S(1)} %fusion.9, f32[512,1024]{1,0:T(8,128)S(1)} %fusion.19, f32[512,1024]{1,0:T(8,128)S(1)} %fusion.5, bf16[512,512]{1,0:T(8,128)(2,1)S(1)} %get-tuple-element.38, bf16[512,512]{0,1:T(8,128)(2,1)S(1)} %get-tuple-element.28, bf16[512,512]{0,1:T(8,128)(2,1)S(1)} %get-tuple-element.27), kind=kOutput, calls=%fused_computation | convolution fusion | flops 540540928 | bytes 9961472 | tf_op jit(solution)/shard_map/dot_general | solution.py:36
  37.7 0.5 %convolution_add_fusion = f32[512,512]{1,0:T(8,128)S(1)} fusion(f32[512,512]{1,0:T(8,128)S(1)} %convolution_add_fusion.1, bf16[512,512]{1,0:T(8,128)(2,1)S(1)} %get-tuple-element.37, f32[512,512]{0,1:T(8,128)S(1)} %fusion.73, f32[512,512]{0,1:T(8,128)S(1)} %fusion.74), kind=kOutput, calls=%fused_computation.1 | convolution fusion | flops 270270464 | bytes 4718592 | tf_op jit(solution)/shard_map/dot_general | solution.py:37
  38.8 0.8 %collective-permute-done.15 = bf16[128,512]{1,0:T(8,128)(2,1)S(1)} collective-permute-done((bf16[128,512]{1,0:T(8,128)(2,1)S(1)}, bf16[128,512]{1,0:T(8,128)(2,1)S(1)}, u32[]{:S(2)}, u32[]{:S(2)}) %collective-permute-start.15) | collective-permute-done | bytes 131104 | tf_op jit(solution)/shard_map/ppermute | solution.py:158
  40.9 0.5 %fusion.4 = (f32[512]{0:T(512)S(1)}, f32[512]{0:T(512)S(1)}, f32[512,512]{1,0:T(8,128)S(1)}) fusion(bf16[512,512]{1,0:T(8,128)(2,1)S(1)} %copy-done.3, f32[512,512]{1,0:T(8,128)S(1)} %convolution_add_fusion, bf16[64,512]{1,0:T(8,128)(2,1)S(1)} %get-tuple-element.100, bf16[64,512]{1,0:T(8,128)(2,1)S(1)} %get-tuple-element.98, ...), kind=kOutput, calls=%fused_computation.17 | convolution fusion | flops 137886720 | bytes 3936256 | tf_op jit(solution)/shard_map/dot_general | solution.py:37
  41.8 0.6 %add.143 = f32[512,1024]{1,0:T(8,128)S(1)} add(f32[512,1024]{1,0:T(8,128)S(1)} %add_add_fusion, f32[512,1024]{1,0:T(8,128)S(1)} %fusion.23) | non-fusion elementwise | flops 524288 | bytes 6291456 | tf_op jit(solution)/shard_map/add | solution.py:108
  42.4 0.5 %multiply_reduce_fusion.1 = (f32[512]{0:T(512)S(1)}, f32[512]{0:T(512)S(1)}, f32[512]{0:T(512)S(1)}, f32[512]{0:T(512)S(1)}) fusion(f32[512,1024]{1,0:T(8,128)S(1)} %add.143, bf16[512,512]{1,0:T(8,128)(2,1)S(1)} %copy-done.1, bf16[512,512]{1,0:T(8,128)(2,1)S(1)} %copy-done.2), kind=kLoop, calls=%fused_computation.32 | loop fusion | flops 3143680 | bytes 3153920 | tf_op jit(solution)/shard_map/reduce_sum | solution.py:19
  43.8 1.3 %convolution_convert_fusion = bf16[128,512]{1,0:T(8,128)(2,1)} fusion(bf16[512,512]{1,0:T(8,128)(2,1)S(1)} %multiply_convert_fusion, bf16[512,512]{1,0:T(8,128)(2,1)S(1)} %get-tuple-element.17, bf16[128,512]{1,0:T(8,128)(2,1)S(1)} %copy-done, f32[128,512]{0,1:T(8,128)S(1)} %convolution_bitcast_fusion.1), kind=kOutput, calls=%fused_computation.14 | convolution fusion | flops 134676480 | bytes 1572864 | tf_op jit(solution)/shard_map/dot_general | solution.py:45
  (77 shorter events, 7.9 us)
Async XLA Ops:
  0.0 43.5 %copy-start = (bf16[128,512]{1,0:T(8,128)(2,1)S(1)}, bf16[128,512]{1,0:T(8,128)(2,1)}, u32[]{:S(2)}) copy-start(bf16[128,512]{1,0:T(8,128)(2,1)} %param.9) | copy-start | bytes 393220
  0.0 6.6 %copy-start.1 = (bf16[512,512]{1,0:T(8,128)(2,1)S(1)}, bf16[512,512]{1,0:T(8,128)(2,1)}, u32[]{:S(2)}) copy-start(bf16[512,512]{1,0:T(8,128)(2,1)} %param.12) | copy-start | bytes 1572868
  2.0 4.9 %copy-start.3 = (bf16[512,512]{1,0:T(8,128)(2,1)S(1)}, bf16[512,512]{1,0:T(8,128)(2,1)}, u32[]{:S(2)}) copy-start(bf16[512,512]{1,0:T(8,128)(2,1)} %param.13) | copy-start | bytes 1572868
  2.0 3.2 %collective-permute-start = (bf16[256,512]{1,0:T(8,128)(2,1)S(1)}, bf16[256,512]{1,0:T(8,128)(2,1)S(1)}, u32[]{:S(2)}, u32[]{:S(2)}) collective-permute-start(bf16[256,512]{1,0:T(8,128)(2,1)S(1)} %bitcast.48), channel_id=1, source_target_pairs={{0,1},{1,0},{2,3},{3,2},{4,5},{5,4},{6,7},{7,6},{8,9},{9,8},{10,11... | collective-permute-start | bytes 786440 | tf_op jit(solution)/shard_map/ppermute | solution.py:142
  2.5 9.5 %collective-permute-start.1 = (bf16[256,512]{1,0:T(8,128)(2,1)S(1)}, bf16[256,512]{1,0:T(8,128)(2,1)S(1)}, u32[]{:S(2)}, u32[]{:S(2)}) collective-permute-start(bf16[256,512]{1,0:T(8,128)(2,1)S(1)} %bitcast.49), channel_id=1, source_target_pairs={{0,4},{1,5},{4,8},{5,9},{8,12},{9,13},{12,14},{13,15},{14,10},{15,... | collective-permute-start | bytes 786440 | tf_op jit(solution)/shard_map/ppermute | solution.py:153
  5.2 8.7 %collective-permute-start.2 = (bf16[256,512]{1,0:T(8,128)(2,1)S(1)}, bf16[256,512]{1,0:T(8,128)(2,1)S(1)}, u32[]{:S(2)}, u32[]{:S(2)}) collective-permute-start(bf16[256,512]{1,0:T(8,128)(2,1)S(1)} %bitcast.50), channel_id=1, source_target_pairs={{0,2},{1,3},{4,0},{5,1},{8,4},{9,5},{12,8},{13,9},{14,12},{15,13},... | collective-permute-start | bytes 786440 | tf_op jit(solution)/shard_map/ppermute | solution.py:154
  12.0 2.8 %collective-permute-start.3 = (bf16[256,512]{1,0:T(8,128)(2,1)S(1)}, bf16[256,512]{1,0:T(8,128)(2,1)S(1)}, u32[]{:S(2)}, u32[]{:S(2)}) collective-permute-start(bf16[256,512]{1,0:T(8,128)(2,1)S(1)} %collective-permute-done.1), channel_id=1, source_target_pairs={{0,1},{1,0},{2,3},{3,2},{4,5},{5,4},{6,7},{7,6},{8,9},{9,8},{10,11... | collective-permute-start | bytes 786440 | tf_op jit(solution)/shard_map/ppermute | solution.py:158
  12.0 8.7 %collective-permute-start.5 = (bf16[256,512]{1,0:T(8,128)(2,1)S(1)}, bf16[256,512]{1,0:T(8,128)(2,1)S(1)}, u32[]{:S(2)}, u32[]{:S(2)}) collective-permute-start(bf16[256,512]{1,0:T(8,128)(2,1)S(1)} %collective-permute-done.1), channel_id=1, source_target_pairs={{0,4},{1,5},{4,8},{5,9},{8,12},{9,13},{12,14},{13,15},{14,10},{15,... | collective-permute-start | bytes 786440 | tf_op jit(solution)/shard_map/ppermute | solution.py:153
  13.9 1.6 %collective-permute-start.4 = (bf16[256,512]{1,0:T(8,128)(2,1)S(1)}, bf16[256,512]{1,0:T(8,128)(2,1)S(1)}, u32[]{:S(2)}, u32[]{:S(2)}) collective-permute-start(bf16[256,512]{1,0:T(8,128)(2,1)S(1)} %collective-permute-done.2), channel_id=1, source_target_pairs={{0,1},{1,0},{2,3},{3,2},{4,5},{5,4},{6,7},{7,6},{8,9},{9,8},{10,11... | collective-permute-start | bytes 786440 | tf_op jit(solution)/shard_map/ppermute | solution.py:158
  14.1 8.5 %collective-permute-start.6 = (bf16[256,512]{1,0:T(8,128)(2,1)S(1)}, bf16[256,512]{1,0:T(8,128)(2,1)S(1)}, u32[]{:S(2)}, u32[]{:S(2)}) collective-permute-start(bf16[256,512]{1,0:T(8,128)(2,1)S(1)} %collective-permute-done.2), channel_id=1, source_target_pairs={{0,2},{1,3},{4,0},{5,1},{8,4},{9,5},{12,8},{13,9},{14,12},{15,13},... | collective-permute-start | bytes 786440 | tf_op jit(solution)/shard_map/ppermute | solution.py:154
  14.8 1.2 %copy-start.2 = (bf16[512,512]{1,0:T(8,128)(2,1)S(1)}, bf16[512,512]{1,0:T(8,128)(2,1)}, u32[]{:S(2)}) copy-start(bf16[512,512]{1,0:T(8,128)(2,1)} %param.11) | copy-start | bytes 1572868
  20.7 3.2 %collective-permute-start.7 = (bf16[256,512]{1,0:T(8,128)(2,1)S(1)}, bf16[256,512]{1,0:T(8,128)(2,1)S(1)}, u32[]{:S(2)}, u32[]{:S(2)}) collective-permute-start(bf16[256,512]{1,0:T(8,128)(2,1)S(1)} %collective-permute-done.5), channel_id=1, source_target_pairs={{0,1},{1,0},{2,3},{3,2},{4,5},{5,4},{6,7},{7,6},{8,9},{9,8},{10,11... | collective-permute-start | bytes 786440 | tf_op jit(solution)/shard_map/ppermute | solution.py:158
  20.7 8.7 %collective-permute-start.9 = (bf16[256,512]{1,0:T(8,128)(2,1)S(1)}, bf16[256,512]{1,0:T(8,128)(2,1)S(1)}, u32[]{:S(2)}, u32[]{:S(2)}) collective-permute-start(bf16[256,512]{1,0:T(8,128)(2,1)S(1)} %collective-permute-done.5), channel_id=1, source_target_pairs={{0,4},{1,5},{4,8},{5,9},{8,12},{9,13},{12,14},{13,15},{14,10},{15,... | collective-permute-start | bytes 786440 | tf_op jit(solution)/shard_map/ppermute | solution.py:153
  22.6 1.5 %collective-permute-start.8 = (bf16[256,512]{1,0:T(8,128)(2,1)S(1)}, bf16[256,512]{1,0:T(8,128)(2,1)S(1)}, u32[]{:S(2)}, u32[]{:S(2)}) collective-permute-start(bf16[256,512]{1,0:T(8,128)(2,1)S(1)} %collective-permute-done.6), channel_id=1, source_target_pairs={{0,1},{1,0},{2,3},{3,2},{4,5},{5,4},{6,7},{7,6},{8,9},{9,8},{10,11... | collective-permute-start | bytes 786440 | tf_op jit(solution)/shard_map/ppermute | solution.py:158
  22.9 9.7 %collective-permute-start.10 = (bf16[256,512]{1,0:T(8,128)(2,1)S(1)}, bf16[256,512]{1,0:T(8,128)(2,1)S(1)}, u32[]{:S(2)}, u32[]{:S(2)}) collective-permute-start(bf16[256,512]{1,0:T(8,128)(2,1)S(1)} %collective-permute-done.6), channel_id=1, source_target_pairs={{0,2},{1,3},{4,0},{5,1},{8,4},{9,5},{12,8},{13,9},{14,12},{15,13},... | collective-permute-start | bytes 786440 | tf_op jit(solution)/shard_map/ppermute | solution.py:154
  29.5 8.7 %collective-permute-start.13 = (bf16[128,512]{1,0:T(8,128)(2,1)S(1)}, bf16[128,512]{1,0:T(8,128)(2,1)S(1)}, u32[]{:S(2)}, u32[]{:S(2)}) collective-permute-start(bf16[128,512]{1,0:T(8,128)(2,1)S(1)} %slice.328), channel_id=1, source_target_pairs={{0,4},{1,5},{4,8},{5,9},{8,12},{9,13},{12,14},{13,15},{14,10},{15,... | collective-permute-start | bytes 393224 | tf_op jit(solution)/shard_map/ppermute | solution.py:148
  32.6 5.5 %collective-permute-start.14 = (bf16[128,512]{1,0:T(8,128)(2,1)S(1)}, bf16[128,512]{1,0:T(8,128)(2,1)S(1)}, u32[]{:S(2)}, u32[]{:S(2)}) collective-permute-start(bf16[128,512]{1,0:T(8,128)(2,1)S(1)} %slice.329), channel_id=1, source_target_pairs={{0,2},{1,3},{4,0},{5,1},{8,4},{9,5},{12,8},{13,9},{14,12},{15,13},... | collective-permute-start | bytes 393224 | tf_op jit(solution)/shard_map/ppermute | solution.py:149
  33.1 1.6 %collective-permute-start.11 = (bf16[256,512]{1,0:T(8,128)(2,1)S(1)}, bf16[256,512]{1,0:T(8,128)(2,1)S(1)}, u32[]{:S(2)}, u32[]{:S(2)}) collective-permute-start(bf16[256,512]{1,0:T(8,128)(2,1)S(1)} %collective-permute-done.9), channel_id=1, source_target_pairs={{0,1},{1,0},{2,3},{3,2},{4,5},{5,4},{6,7},{7,6},{8,9},{9,8},{10,11... | collective-permute-start | bytes 786440 | tf_op jit(solution)/shard_map/ppermute | solution.py:158
  33.2 1.9 %collective-permute-start.12 = (bf16[256,512]{1,0:T(8,128)(2,1)S(1)}, bf16[256,512]{1,0:T(8,128)(2,1)S(1)}, u32[]{:S(2)}, u32[]{:S(2)}) collective-permute-start(bf16[256,512]{1,0:T(8,128)(2,1)S(1)} %collective-permute-done.10), channel_id=1, source_target_pairs={{0,1},{1,0},{2,3},{3,2},{4,5},{5,4},{6,7},{7,6},{8,9},{9,8},{10,11... | collective-permute-start | bytes 786440 | tf_op jit(solution)/shard_map/ppermute | solution.py:158
  38.2 1.4 %collective-permute-start.15 = (bf16[128,512]{1,0:T(8,128)(2,1)S(1)}, bf16[128,512]{1,0:T(8,128)(2,1)S(1)}, u32[]{:S(2)}, u32[]{:S(2)}) collective-permute-start(bf16[128,512]{1,0:T(8,128)(2,1)S(1)} %collective-permute-done.13), channel_id=1, source_target_pairs={{0,1},{1,0},{2,3},{3,2},{4,5},{5,4},{6,7},{7,6},{8,9},{9,8},{10,11... | collective-permute-start | bytes 393224 | tf_op jit(solution)/shard_map/ppermute | solution.py:158
  38.4 1.4 %collective-permute-start.16 = (bf16[128,512]{1,0:T(8,128)(2,1)S(1)}, bf16[128,512]{1,0:T(8,128)(2,1)S(1)}, u32[]{:S(2)}, u32[]{:S(2)}) collective-permute-start(bf16[128,512]{1,0:T(8,128)(2,1)S(1)} %collective-permute-done.14), channel_id=1, source_target_pairs={{0,1},{1,0},{2,3},{3,2},{4,5},{5,4},{6,7},{7,6},{8,9},{9,8},{10,11... | collective-permute-start | bytes 393224 | tf_op jit(solution)/shard_map/ppermute | solution.py:158

commit v7 on v5

--- a/solution.py
+++ b/solution.py
@@ -112,10 +112,12 @@
     chips = len(ring)
     cw_perm = []
     ccw_perm = []
+    cross_perm = []
     for p in range(chips):
         for c in range(2):
             cw_perm.append((ring[p] * 2 + c, ring[(p + 1) % chips] * 2 + c))
             ccw_perm.append((ring[p] * 2 + c, ring[(p - 1) % chips] * 2 + c))
+            cross_perm.append((ring[p] * 2 + c, ring[(p - 1) % chips] * 2 + 1 - c))
     swap = [(i, i ^ 1) for i in range(chips * 2)]
     steps = chips // 2
     axes = ("seq", "outer")
@@ -143,15 +145,15 @@
         total = add_grads(None, *split([own, sib], half), w_gate, w_up, w_out)
         arrived = [own, own]
         for step in range(1, steps + 1):
-            last = step == steps and chips % 2 == 0
-            if last and halves == 2:
-                sent = [lax.ppermute(arrived[0][:2 * half], axes, cw_perm),
-                        lax.ppermute(arrived[1][2 * half:], axes, ccw_perm)]
-            elif last:
-                sent = [lax.ppermute(arrived[0], axes, cw_perm)]
-            else:
-                sent = [lax.ppermute(arrived[0], axes, cw_perm),
-                        lax.ppermute(arrived[1], axes, ccw_perm)]
+            if step == steps and chips % 2 == 0:
+                arrived = [lax.ppermute(arrived[0], axes, cw_perm),
+                           lax.ppermute(arrived[1], axes, cross_perm)]
+                total, arrived = lax.optimization_barrier((total, arrived))
+                total = add_grads(total, *split(arrived, half), w_gate, w_up, w_out)
+                continue
+            sent = [lax.ppermute(arrived[0], axes, cw_perm)]
+            if step < steps or chips % 2:
+                sent.append(lax.ppermute(arrived[1], axes, ccw_perm))
             arrived = sent
             from_sib = [lax.ppermute(chunk, axes, swap) for chunk in arrived]
             total = add_grads(total, *split(arrived + from_sib, half), w_gate, w_up, w_out)

time: 47.3 us -> 45.5 us (0.962)
  local copies, waits for them, and re-layouts: 1.9 us -> 0.35 us
  starting transfers between devices: 10.7 us -> 9.98 us
    ppermute x5 -> x7, waiting for transfers between devices: 3.28 us -> 11.9 us  [the longest x3 10.1 us: local_ring(): sent = [lax.ppermute(arrived[0], axes, cw_perm)]]
    ppermute x3 -> x1, waiting for transfers between devices: 9.92 us -> 2.19 us  [local_ring(): lax.ppermute(arrived[0], axes, cw_perm)]
    ppermute x3 -> x1, starting transfers between devices: 6.73 us -> 1.83 us  [local_ring(): lax.ppermute(arrived[0], axes, cw_perm)]
    ppermute x5 -> x7, starting transfers between devices: 2.73 us -> 6.88 us  [the longest x3 6.29 us: local_ring(): sent = [lax.ppermute(arrived[0], axes, cw_perm)]]
    unnamed x30 -> x29, local copies, waits for them, and re-layouts: 1.77 us -> 0.24 us
    dot_general x5, matrix products: 2.03 us -> 3.29 us  [gradients(): gate_pre = jnp.dot(keys, w_gate, preferred_element_type=jnp.float32)]
    ppermute x8 -> x6, waiting for transfers between devices: 2.11 us -> 1.13 us  [local_ring(): from_sib = [lax.ppermute(chunk, axes, swap) for chunk in arrived]]
    add x0 -> x1, other arithmetic: none -> 0.55 us  [add_grads(): return (total[0] + full_in, total[1] + full_out)]
  transfers between devices with their start and end apart: 17 -> 15, of which waited for: 9 -> 10; matrix products, arithmetic and copies ran while one was open for 25% -> 27% of each run, Pallas kernels for 0% -> 0%
where the time goes in v7:
time: 45.5 us; the launch traced here: 45.3 us
  matrix products  15.6 us (34%)
  waiting for transfers between devices  15.3 us (34%)
  starting transfers between devices  9.98 us (22%)
  other arithmetic  3.6 us (8%)
    ppermute x3, waiting for transfers between devices, local_ring(): sent = [lax.ppermute(arrived[0], axes, cw_perm)]  10.1 us
    ppermute x3, starting transfers between devices, local_ring(): sent = [lax.ppermute(arrived[0], axes, cw_perm)]  6.29 us
    dot_general x5, matrix products, gradients(): gate_pre = jnp.dot(keys, w_gate, preferred_element_type=jnp.float32)  3.29 us
    dot_general x5, matrix products, gradients(): lax.dot_general(keys, both_grads, contract_first, preferred_element_type=...  3.22 us
    dot_general x5, matrix products, gradients(): lax.dot_general(scaled, w_out, contract_last, preferred_element_type=jnp....  3.21 us
    dot_general x5, matrix products, gradients(): lax.dot_general(activation, scaled, contract_first, preferred_element_typ...  2.3 us
    ppermute x1, waiting for transfers between devices, local_ring(): lax.ppermute(arrived[0], axes, cw_perm)  2.19 us
    dot_general x5, matrix products, gradients(): up_pre = jnp.dot(keys, w_up, preferred_element_type=jnp.float32)  2.04 us
  transfers between devices with their start and end apart: 15, of which 10 were waited for; matrix products, arithmetic and copies ran while one was open for 27% of the time, Pallas kernels for 0%

profile of v7, /device:TPU:0, one launch (start us, length us, event | category | flops | bytes accessed | tf_op | source)
XLA Modules:
  0.0 45.3 jit_solution(9117369477293689460)
XLA Ops:
  0.0 1.1 %multiply_convert_fusion.23 = bf16[128,512]{1,0:T(8,128)(2,1)S(1)} fusion(bf16[128,512]{1,0:T(8,128)(2,1)} %param.8, f32[128]{0:T(128)} %param.10), kind=kLoop, calls=%fused_computation.80 | loop fusion | flops 196608 | bytes 262656 | tf_op jit(solution)/shard_map/convert_element_type | solution.py:139
  1.1 0.9 %pad_maximum_fusion = bf16[2,2,64,512]{3,2,1,0:T(8,128)(2,1)S(1)} fusion(bf16[2,1,64,512]{3,2,1,0:T(8,128)(2,1)S(1)} %bitcast.52, bf16[2,1,64,512]{3,2,1,0:T(8,128)(2,1)} %bitcast.53), kind=kLoop, calls=%fused_computation.70 | loop fusion | flops 131072 | bytes 524288 | tf_op jit(solution)/shard_map/stack | solution.py:141
  2.0 0.5 %collective-permute-start = (bf16[256,512]{1,0:T(8,128)(2,1)S(1)}, bf16[256,512]{1,0:T(8,128)(2,1)S(1)}, u32[]{:S(2)}, u32[]{:S(2)}) collective-permute-start(bf16[256,512]{1,0:T(8,128)(2,1)S(1)} %bitcast.48), channel_id=1, source_target_pairs={{0,1},{1,0},{2,3},{3,2},{4,5},{5,4},{6,7},{7,6},{8,9},{9,8},{10,11... | collective-permute-start | bytes 786440 | tf_op jit(solution)/shard_map/ppermute | solution.py:144
  2.5 2.6 %collective-permute-start.1 = (bf16[256,512]{1,0:T(8,128)(2,1)S(1)}, bf16[256,512]{1,0:T(8,128)(2,1)S(1)}, u32[]{:S(2)}, u32[]{:S(2)}) collective-permute-start(bf16[256,512]{1,0:T(8,128)(2,1)S(1)} %bitcast.49), channel_id=1, source_target_pairs={{0,4},{1,5},{4,8},{5,9},{8,12},{9,13},{12,14},{13,15},{14,10},{15,... | collective-permute-start | bytes 786440 | tf_op jit(solution)/shard_map/ppermute | solution.py:154
  5.2 1.3 %fusion.61 = f32[256,512]{1,0:T(8,128)S(1)} fusion(bf16[512,512]{1,0:T(8,128)(2,1)} %param.11, bf16[64,512]{1,0:T(8,128)(2,1)S(1)} %get-tuple-element.84, bf16[64,512]{1,0:T(8,128)(2,1)S(1)} %get-tuple-element.81, bf16[64,512]{1,0:T(8,128)(2,1)S(1)} %get-tuple-element.80, bf16[64,512]{1,0:T(8,128)(2,1)S(1)} %get-tuple-element.77), kind=kOutput, calls=%fused_computation.152 | convolution fusion | flops 135266304 | bytes 1310720 | tf_op jit(solution)/shard_map/dot_general | solution.py:29
  7.8 4.2 %collective-permute-done.1 = bf16[256,512]{1,0:T(8,128)(2,1)S(1)} collective-permute-done((bf16[256,512]{1,0:T(8,128)(2,1)S(1)}, bf16[256,512]{1,0:T(8,128)(2,1)S(1)}, u32[]{:S(2)}, u32[]{:S(2)}) %collective-permute-start.1) | collective-permute-done | bytes 262176 | tf_op jit(solution)/shard_map/ppermute | solution.py:154
  12.0 1.8 %collective-permute-start.5 = (bf16[256,512]{1,0:T(8,128)(2,1)S(1)}, bf16[256,512]{1,0:T(8,128)(2,1)S(1)}, u32[]{:S(2)}, u32[]{:S(2)}) collective-permute-start(bf16[256,512]{1,0:T(8,128)(2,1)S(1)} %collective-permute-done.1), channel_id=1, source_target_pairs={{0,4},{1,5},{4,8},{5,9},{8,12},{9,13},{12,14},{13,15},{14,10},{15,... | collective-permute-start | bytes 786440 | tf_op jit(solution)/shard_map/ppermute | solution.py:154
  14.8 0.6 %collective-permute-done.4 = bf16[256,512]{1,0:T(8,128)(2,1)S(1)} collective-permute-done((bf16[256,512]{1,0:T(8,128)(2,1)S(1)}, bf16[256,512]{1,0:T(8,128)(2,1)S(1)}, u32[]{:S(2)}, u32[]{:S(2)}) %collective-permute-start.4) | collective-permute-done | bytes 262176 | tf_op jit(solution)/shard_map/ppermute | solution.py:158
  15.5 0.5 %fusion.67 = f32[512,512]{0,1:T(8,128)S(1)} fusion(bf16[512,512]{1,0:T(8,128)(2,1)S(1)} %get-tuple-element.62, bf16[512,512]{1,0:T(8,128)(2,1)S(1)} %copy-done.1), kind=kOutput, calls=%fused_computation.158 | convolution fusion | flops 268435456 | bytes 2097152 | tf_op jit(solution)/shard_map/dot_general | solution.py:30
  16.0 0.5 %fusion.68 = f32[512,512]{0,1:T(8,128)S(1)} fusion(bf16[512,512]{1,0:T(8,128)(2,1)S(1)} %get-tuple-element.62, bf16[512,512]{1,0:T(8,128)(2,1)S(1)} %copy-done.2), kind=kOutput, calls=%fused_computation.159 | convolution fusion | flops 268435456 | bytes 2097152 | tf_op jit(solution)/shard_map/dot_general | solution.py:29
  16.5 0.8 %multiply_convert_fusion.11 = (bf16[512,512]{0,1:T(8,128)(2,1)S(1)}, bf16[512,512]{0,1:T(8,128)(2,1)S(1)}) fusion(f32[512,512]{0,1:T(8,128)S(1)} %fusion.68, f32[512,512]{0,1:T(8,128)S(1)} %fusion.67, bf16[512,512]{1,0:T(8,128)(2,1)S(1)} %get-tuple-element.61, bf16[512,512]{1,0:T(8,128)(2,1)S(1)} %copy-done.3), kind=kOutput, calls=%fused_computation.47 | convolution fusion | flops 271843328 | bytes 4194304 | tf_op jit(solution)/shard_map/dot_general | solution.py:31
  17.8 3.0 %collective-permute-done.5 = bf16[256,512]{1,0:T(8,128)(2,1)S(1)} collective-permute-done((bf16[256,512]{1,0:T(8,128)(2,1)S(1)}, bf16[256,512]{1,0:T(8,128)(2,1)S(1)}, u32[]{:S(2)}, u32[]{:S(2)}) %collective-permute-start.5) | collective-permute-done | bytes 262176 | tf_op jit(solution)/shard_map/ppermute | solution.py:154
  20.7 1.8 %collective-permute-start.9 = (bf16[256,512]{1,0:T(8,128)(2,1)S(1)}, bf16[256,512]{1,0:T(8,128)(2,1)S(1)}, u32[]{:S(2)}, u32[]{:S(2)}) collective-permute-start(bf16[256,512]{1,0:T(8,128)(2,1)S(1)} %collective-permute-done.5), channel_id=1, source_target_pairs={{0,4},{1,5},{4,8},{5,9},{8,12},{9,13},{12,14},{13,15},{14,10},{15,... | collective-permute-start | bytes 786440 | tf_op jit(solution)/shard_map/ppermute | solution.py:154
  23.1 0.8 %fusion.5 = f32[512,1024]{1,0:T(8,128)S(1)} fusion(bf16[512,512]{1,0:T(8,128)(2,1)S(1)} %get-tuple-element.62, bf16[512,512]{0,1:T(8,128)(2,1)S(1)} %get-tuple-element.30, bf16[512,512]{0,1:T(8,128)(2,1)S(1)} %get-tuple-element.29), kind=kOutput, calls=%fused_computation.18 | convolution fusion | flops 538968064 | bytes 3670016 | tf_op jit(solution)/shard_map/dot_general | solution.py:36
  24.2 0.5 %fusion.69 = f32[512,512]{0,1:T(8,128)S(1)} fusion(bf16[512,512]{1,0:T(8,128)(2,1)S(1)} %get-tuple-element.86, bf16[512,512]{1,0:T(8,128)(2,1)S(1)} %copy-done.1), kind=kOutput, calls=%fused_computation.160 | convolution fusion | flops 268435456 | bytes 2097152 | tf_op jit(solution)/shard_map/dot_general | solution.py:30
  24.7 0.5 %fusion.70 = f32[512,512]{0,1:T(8,128)S(1)} fusion(bf16[512,512]{1,0:T(8,128)(2,1)S(1)} %get-tuple-element.86, bf16[512,512]{1,0:T(8,128)(2,1)S(1)} %copy-done.2), kind=kOutput, calls=%fused_computation.161 | convolution fusion | flops 268435456 | bytes 2097152 | tf_op jit(solution)/shard_map/dot_general | solution.py:29
  25.2 0.8 %multiply_convert_fusion.9 = (bf16[512,512]{0,1:T(8,128)(2,1)S(1)}, bf16[512,512]{0,1:T(8,128)(2,1)S(1)}) fusion(f32[512,512]{0,1:T(8,128)S(1)} %fusion.70, f32[512,512]{0,1:T(8,128)S(1)} %fusion.69, bf16[512,512]{1,0:T(8,128)(2,1)S(1)} %get-tuple-element.85, bf16[512,512]{1,0:T(8,128)(2,1)S(1)} %copy-done.3), kind=kOutput, calls=%fused_computation.43 | convolution fusion | flops 271843328 | bytes 4194304 | tf_op jit(solution)/shard_map/dot_general | solution.py:31
  26.0 0.5 %convolution_add_fusion.1 = f32[512,512]{1,0:T(8,128)S(1)} fusion(f32[512,512]{1,0:T(8,128)S(1)} %convolution_add_fusion.2, bf16[512,512]{1,0:T(8,128)(2,1)S(1)} %get-tuple-element.85, f32[512,512]{0,1:T(8,128)S(1)} %fusion.69, f32[512,512]{0,1:T(8,128)S(1)} %fusion.70), kind=kOutput, calls=%fused_computation.2 | convolution fusion | flops 270270464 | bytes 4718592 | tf_op jit(solution)/shard_map/dot_general | solution.py:37
  26.5 3.0 %collective-permute-done.9 = bf16[256,512]{1,0:T(8,128)(2,1)S(1)} collective-permute-done((bf16[256,512]{1,0:T(8,128)(2,1)S(1)}, bf16[256,512]{1,0:T(8,128)(2,1)S(1)}, u32[]{:S(2)}, u32[]{:S(2)}) %collective-permute-start.9) | collective-permute-done | bytes 262176 | tf_op jit(solution)/shard_map/ppermute | solution.py:154
  29.4 1.8 %collective-permute-start.13 = (bf16[256,512]{1,0:T(8,128)(2,1)S(1)}, bf16[256,512]{1,0:T(8,128)(2,1)S(1)}, u32[]{:S(2)}, u32[]{:S(2)}) collective-permute-start(bf16[256,512]{1,0:T(8,128)(2,1)S(1)} %collective-permute-done.9), channel_id=1, source_target_pairs={{0,4},{1,5},{4,8},{5,9},{8,12},{9,13},{12,14},{13,15},{14,10},{15,... | collective-permute-start | bytes 786440 | tf_op jit(solution)/shard_map/ppermute | solution.py:149
  31.8 0.8 %fusion.9 = f32[512,1024]{1,0:T(8,128)S(1)} fusion(bf16[512,512]{1,0:T(8,128)(2,1)S(1)} %get-tuple-element.86, bf16[512,512]{0,1:T(8,128)(2,1)S(1)} %get-tuple-element.32, bf16[512,512]{0,1:T(8,128)(2,1)S(1)} %get-tuple-element.31), kind=kOutput, calls=%fused_computation.22 | convolution fusion | flops 538968064 | bytes 3670016 | tf_op jit(solution)/shard_map/dot_general | solution.py:36
  32.9 0.5 %fusion.71 = f32[512,512]{0,1:T(8,128)S(1)} fusion(bf16[512,512]{1,0:T(8,128)(2,1)S(1)} %get-tuple-element.46, bf16[512,512]{1,0:T(8,128)(2,1)S(1)} %copy-done.1), kind=kOutput, calls=%fused_computation.162 | convolution fusion | flops 268435456 | bytes 2097152 | tf_op jit(solution)/shard_map/dot_general | solution.py:30
  33.4 0.5 %fusion.72 = f32[512,512]{0,1:T(8,128)S(1)} fusion(bf16[512,512]{1,0:T(8,128)(2,1)S(1)} %get-tuple-element.46, bf16[512,512]{1,0:T(8,128)(2,1)S(1)} %copy-done.2), kind=kOutput, calls=%fused_computation.163 | convolution fusion | flops 268435456 | bytes 2097152 | tf_op jit(solution)/shard_map/dot_general | solution.py:29
  33.9 0.8 %multiply_convert_fusion.7 = (bf16[512,512]{0,1:T(8,128)(2,1)S(1)}, bf16[512,512]{0,1:T(8,128)(2,1)S(1)}) fusion(f32[512,512]{0,1:T(8,128)S(1)} %fusion.72, f32[512,512]{0,1:T(8,128)S(1)} %fusion.71, bf16[512,512]{1,0:T(8,128)(2,1)S(1)} %get-tuple-element.45, bf16[512,512]{1,0:T(8,128)(2,1)S(1)} %copy-done.3), kind=kOutput, calls=%fused_computation.39 | convolution fusion | flops 271843328 | bytes 4194304 | tf_op jit(solution)/shard_map/dot_general | solution.py:31
  34.7 0.8 %add_add_fusion = f32[512,1024]{1,0:T(8,128)S(1)} fusion(f32[512,1024]{1,0:T(8,128)S(1)} %fusion.9, f32[512,1024]{1,0:T(8,128)S(1)} %fusion.19, f32[512,1024]{1,0:T(8,128)S(1)} %fusion.5, bf16[512,512]{1,0:T(8,128)(2,1)S(1)} %get-tuple-element.46, bf16[512,512]{0,1:T(8,128)(2,1)S(1)} %get-tuple-element.28, bf16[512,512]{0,1:T(8,128)(2,1)S(1)} %get-tuple-element.27), kind=kOutput, calls=%fused_computation | convolution fusion | flops 540540928 | bytes 9961472 | tf_op jit(solution)/shard_map/dot_general | solution.py:36
  36.0 2.2 %collective-permute-done.13 = bf16[256,512]{1,0:T(8,128)(2,1)S(1)} collective-permute-done((bf16[256,512]{1,0:T(8,128)(2,1)S(1)}, bf16[256,512]{1,0:T(8,128)(2,1)S(1)}, u32[]{:S(2)}, u32[]{:S(2)}) %collective-permute-start.13) | collective-permute-done | bytes 262176 | tf_op jit(solution)/shard_map/ppermute | solution.py:149
  38.2 1.7 %collective-permute-done.14 = bf16[256,512]{1,0:T(8,128)(2,1)S(1)} collective-permute-done((bf16[256,512]{1,0:T(8,128)(2,1)S(1)}, bf16[256,512]{1,0:T(8,128)(2,1)S(1)}, u32[]{:S(2)}, u32[]{:S(2)}) %collective-permute-start.14) | collective-permute-done | bytes 262176 | tf_op jit(solution)/shard_map/ppermute | solution.py:150
  40.5 0.5 %multiply_convert_fusion.17 = (bf16[256,512]{1,0:T(8,128)(2,1)S(1)}, bf16[256,512]{1,0:T(8,128)(2,1)S(1)}, f32[256,512]{1,0:T(8,128)S(1)}) fusion(f32[256,512]{1,0:T(8,128)S(1)} %fusion.42, f32[256,512]{1,0:T(8,128)S(1)} %fusion.60, bf16[512,512]{1,0:T(8,128)(2,1)S(1)} %copy-done.2, bf16[64,512]{1,0:T(8,128)(2,1)S(1)} %get-tuple-element.103, ...), kind=kOutput, calls=%fused_computation.60 | convolution fusion | flops 136970240 | bytes 2883584 | tf_op jit(solution)/shard_map/dot_general | solution.py:29
  41.5 0.6 %add.143 = f32[512,1024]{1,0:T(8,128)S(1)} add(f32[512,1024]{1,0:T(8,128)S(1)} %add_add_fusion, f32[512,1024]{1,0:T(8,128)S(1)} %fusion.23) | non-fusion elementwise | flops 524288 | bytes 6291456 | tf_op jit(solution)/shard_map/add | solution.py:108
  42.1 0.5 %multiply_reduce_fusion.1 = (f32[512]{0:T(512)S(1)}, f32[512]{0:T(512)S(1)}, f32[512]{0:T(512)S(1)}, f32[512]{0:T(512)S(1)}) fusion(f32[512,1024]{1,0:T(8,128)S(1)} %add.143, bf16[512,512]{1,0:T(8,128)(2,1)S(1)} %copy-done.1, bf16[512,512]{1,0:T(8,128)(2,1)S(1)} %copy-done.2), kind=kLoop, calls=%fused_computation.32 | loop fusion | flops 3143680 | bytes 3153920 | tf_op jit(solution)/shard_map/reduce_sum | solution.py:19
  42.6 0.5 %fusion.4 = (f32[512]{0:T(512)S(1)}, f32[512]{0:T(512)S(1)}, f32[512,512]{1,0:T(8,128)S(1)}) fusion(bf16[512,512]{1,0:T(8,128)(2,1)S(1)} %copy-done.3, f32[512,512]{1,0:T(8,128)S(1)} %convolution_add_fusion, bf16[64,512]{1,0:T(8,128)(2,1)S(1)} %get-tuple-element.105, bf16[64,512]{1,0:T(8,128)(2,1)S(1)} %get-tuple-element.104, ...), kind=kOutput, calls=%fused_computation.17 | convolution fusion | flops 137886720 | bytes 3936256 | tf_op jit(solution)/shard_map/dot_general | solution.py:37
  44.0 1.3 %convolution_convert_fusion = bf16[128,512]{1,0:T(8,128)(2,1)} fusion(bf16[512,512]{1,0:T(8,128)(2,1)S(1)} %multiply_convert_fusion, bf16[512,512]{1,0:T(8,128)(2,1)S(1)} %get-tuple-element.17, bf16[128,512]{1,0:T(8,128)(2,1)S(1)} %copy-done, f32[128,512]{0,1:T(8,128)S(1)} %convolution_bitcast_fusion.1), kind=kOutput, calls=%fused_computation.14 | convolution fusion | flops 134676480 | bytes 1572864 | tf_op jit(solution)/shard_map/dot_general | solution.py:45
  (69 shorter events, 6.8 us)
Async XLA Ops:
  0.0 43.7 %copy-start = (bf16[128,512]{1,0:T(8,128)(2,1)S(1)}, bf16[128,512]{1,0:T(8,128)(2,1)}, u32[]{:S(2)}) copy-start(bf16[128,512]{1,0:T(8,128)(2,1)} %param.9) | copy-start | bytes 393220
  0.0 6.6 %copy-start.1 = (bf16[512,512]{1,0:T(8,128)(2,1)S(1)}, bf16[512,512]{1,0:T(8,128)(2,1)}, u32[]{:S(2)}) copy-start(bf16[512,512]{1,0:T(8,128)(2,1)} %param.12) | copy-start | bytes 1572868
  2.0 4.9 %copy-start.3 = (bf16[512,512]{1,0:T(8,128)(2,1)S(1)}, bf16[512,512]{1,0:T(8,128)(2,1)}, u32[]{:S(2)}) copy-start(bf16[512,512]{1,0:T(8,128)(2,1)} %param.13) | copy-start | bytes 1572868
  2.0 3.2 %collective-permute-start = (bf16[256,512]{1,0:T(8,128)(2,1)S(1)}, bf16[256,512]{1,0:T(8,128)(2,1)S(1)}, u32[]{:S(2)}, u32[]{:S(2)}) collective-permute-start(bf16[256,512]{1,0:T(8,128)(2,1)S(1)} %bitcast.48), channel_id=1, source_target_pairs={{0,1},{1,0},{2,3},{3,2},{4,5},{5,4},{6,7},{7,6},{8,9},{9,8},{10,11... | collective-permute-start | bytes 786440 | tf_op jit(solution)/shard_map/ppermute | solution.py:144
  2.5 9.5 %collective-permute-start.1 = (bf16[256,512]{1,0:T(8,128)(2,1)S(1)}, bf16[256,512]{1,0:T(8,128)(2,1)S(1)}, u32[]{:S(2)}, u32[]{:S(2)}) collective-permute-start(bf16[256,512]{1,0:T(8,128)(2,1)S(1)} %bitcast.49), channel_id=1, source_target_pairs={{0,4},{1,5},{4,8},{5,9},{8,12},{9,13},{12,14},{13,15},{14,10},{15,... | collective-permute-start | bytes 786440 | tf_op jit(solution)/shard_map/ppermute | solution.py:154
  5.2 8.7 %collective-permute-start.2 = (bf16[256,512]{1,0:T(8,128)(2,1)S(1)}, bf16[256,512]{1,0:T(8,128)(2,1)S(1)}, u32[]{:S(2)}, u32[]{:S(2)}) collective-permute-start(bf16[256,512]{1,0:T(8,128)(2,1)S(1)} %bitcast.50), channel_id=1, source_target_pairs={{0,2},{1,3},{4,0},{5,1},{8,4},{9,5},{12,8},{13,9},{14,12},{15,13},... | collective-permute-start | bytes 786440 | tf_op jit(solution)/shard_map/ppermute | solution.py:156
  12.0 2.8 %collective-permute-start.3 = (bf16[256,512]{1,0:T(8,128)(2,1)S(1)}, bf16[256,512]{1,0:T(8,128)(2,1)S(1)}, u32[]{:S(2)}, u32[]{:S(2)}) collective-permute-start(bf16[256,512]{1,0:T(8,128)(2,1)S(1)} %collective-permute-done.1), channel_id=1, source_target_pairs={{0,1},{1,0},{2,3},{3,2},{4,5},{5,4},{6,7},{7,6},{8,9},{9,8},{10,11... | collective-permute-start | bytes 786440 | tf_op jit(solution)/shard_map/ppermute | solution.py:158
  12.0 8.7 %collective-permute-start.5 = (bf16[256,512]{1,0:T(8,128)(2,1)S(1)}, bf16[256,512]{1,0:T(8,128)(2,1)S(1)}, u32[]{:S(2)}, u32[]{:S(2)}) collective-permute-start(bf16[256,512]{1,0:T(8,128)(2,1)S(1)} %collective-permute-done.1), channel_id=1, source_target_pairs={{0,4},{1,5},{4,8},{5,9},{8,12},{9,13},{12,14},{13,15},{14,10},{15,... | collective-permute-start | bytes 786440 | tf_op jit(solution)/shard_map/ppermute | solution.py:154
  13.9 1.6 %collective-permute-start.4 = (bf16[256,512]{1,0:T(8,128)(2,1)S(1)}, bf16[256,512]{1,0:T(8,128)(2,1)S(1)}, u32[]{:S(2)}, u32[]{:S(2)}) collective-permute-start(bf16[256,512]{1,0:T(8,128)(2,1)S(1)} %collective-permute-done.2), channel_id=1, source_target_pairs={{0,1},{1,0},{2,3},{3,2},{4,5},{5,4},{6,7},{7,6},{8,9},{9,8},{10,11... | collective-permute-start | bytes 786440 | tf_op jit(solution)/shard_map/ppermute | solution.py:158
  14.1 8.5 %collective-permute-start.6 = (bf16[256,512]{1,0:T(8,128)(2,1)S(1)}, bf16[256,512]{1,0:T(8,128)(2,1)S(1)}, u32[]{:S(2)}, u32[]{:S(2)}) collective-permute-start(bf16[256,512]{1,0:T(8,128)(2,1)S(1)} %collective-permute-done.2), channel_id=1, source_target_pairs={{0,2},{1,3},{4,0},{5,1},{8,4},{9,5},{12,8},{13,9},{14,12},{15,13},... | collective-permute-start | bytes 786440 | tf_op jit(solution)/shard_map/ppermute | solution.py:156
  14.8 1.2 %copy-start.2 = (bf16[512,512]{1,0:T(8,128)(2,1)S(1)}, bf16[512,512]{1,0:T(8,128)(2,1)}, u32[]{:S(2)}) copy-start(bf16[512,512]{1,0:T(8,128)(2,1)} %param.11) | copy-start | bytes 1572868
  20.7 3.2 %collective-permute-start.7 = (bf16[256,512]{1,0:T(8,128)(2,1)S(1)}, bf16[256,512]{1,0:T(8,128)(2,1)S(1)}, u32[]{:S(2)}, u32[]{:S(2)}) collective-permute-start(bf16[256,512]{1,0:T(8,128)(2,1)S(1)} %collective-permute-done.5), channel_id=1, source_target_pairs={{0,1},{1,0},{2,3},{3,2},{4,5},{5,4},{6,7},{7,6},{8,9},{9,8},{10,11... | collective-permute-start | bytes 786440 | tf_op jit(solution)/shard_map/ppermute | solution.py:158
  20.7 8.7 %collective-permute-start.9 = (bf16[256,512]{1,0:T(8,128)(2,1)S(1)}, bf16[256,512]{1,0:T(8,128)(2,1)S(1)}, u32[]{:S(2)}, u32[]{:S(2)}) collective-permute-start(bf16[256,512]{1,0:T(8,128)(2,1)S(1)} %collective-permute-done.5), channel_id=1, source_target_pairs={{0,4},{1,5},{4,8},{5,9},{8,12},{9,13},{12,14},{13,15},{14,10},{15,... | collective-permute-start | bytes 786440 | tf_op jit(solution)/shard_map/ppermute | solution.py:154
  22.6 1.5 %collective-permute-start.8 = (bf16[256,512]{1,0:T(8,128)(2,1)S(1)}, bf16[256,512]{1,0:T(8,128)(2,1)S(1)}, u32[]{:S(2)}, u32[]{:S(2)}) collective-permute-start(bf16[256,512]{1,0:T(8,128)(2,1)S(1)} %collective-permute-done.6), channel_id=1, source_target_pairs={{0,1},{1,0},{2,3},{3,2},{4,5},{5,4},{6,7},{7,6},{8,9},{9,8},{10,11... | collective-permute-start | bytes 786440 | tf_op jit(solution)/shard_map/ppermute | solution.py:158
  22.9 8.5 %collective-permute-start.10 = (bf16[256,512]{1,0:T(8,128)(2,1)S(1)}, bf16[256,512]{1,0:T(8,128)(2,1)S(1)}, u32[]{:S(2)}, u32[]{:S(2)}) collective-permute-start(bf16[256,512]{1,0:T(8,128)(2,1)S(1)} %collective-permute-done.6), channel_id=1, source_target_pairs={{0,2},{1,3},{4,0},{5,1},{8,4},{9,5},{12,8},{13,9},{14,12},{15,13},... | collective-permute-start | bytes 786440 | tf_op jit(solution)/shard_map/ppermute | solution.py:156
  29.4 3.1 %collective-permute-start.11 = (bf16[256,512]{1,0:T(8,128)(2,1)S(1)}, bf16[256,512]{1,0:T(8,128)(2,1)S(1)}, u32[]{:S(2)}, u32[]{:S(2)}) collective-permute-start(bf16[256,512]{1,0:T(8,128)(2,1)S(1)} %collective-permute-done.9), channel_id=1, source_target_pairs={{0,1},{1,0},{2,3},{3,2},{4,5},{5,4},{6,7},{7,6},{8,9},{9,8},{10,11... | collective-permute-start | bytes 786440 | tf_op jit(solution)/shard_map/ppermute | solution.py:158
  29.4 8.7 %collective-permute-start.13 = (bf16[256,512]{1,0:T(8,128)(2,1)S(1)}, bf16[256,512]{1,0:T(8,128)(2,1)S(1)}, u32[]{:S(2)}, u32[]{:S(2)}) collective-permute-start(bf16[256,512]{1,0:T(8,128)(2,1)S(1)} %collective-permute-done.9), channel_id=1, source_target_pairs={{0,4},{1,5},{4,8},{5,9},{8,12},{9,13},{12,14},{13,15},{14,10},{15,... | collective-permute-start | bytes 786440 | tf_op jit(solution)/shard_map/ppermute | solution.py:149
  31.4 1.5 %collective-permute-start.12 = (bf16[256,512]{1,0:T(8,128)(2,1)S(1)}, bf16[256,512]{1,0:T(8,128)(2,1)S(1)}, u32[]{:S(2)}, u32[]{:S(2)}) collective-permute-start(bf16[256,512]{1,0:T(8,128)(2,1)S(1)} %collective-permute-done.10), channel_id=1, source_target_pairs={{0,1},{1,0},{2,3},{3,2},{4,5},{5,4},{6,7},{7,6},{8,9},{9,8},{10,11... | collective-permute-start | bytes 786440 | tf_op jit(solution)/shard_map/ppermute | solution.py:158
  31.6 8.3 %collective-permute-start.14 = (bf16[256,512]{1,0:T(8,128)(2,1)S(1)}, bf16[256,512]{1,0:T(8,128)(2,1)S(1)}, u32[]{:S(2)}, u32[]{:S(2)}) collective-permute-start(bf16[256,512]{1,0:T(8,128)(2,1)S(1)} %collective-permute-done.10), channel_id=1, source_target_pairs={{0,3},{1,2},{4,1},{5,0},{8,5},{9,4},{12,9},{13,8},{14,13},{15,12},... | collective-permute-start | bytes 786440 | tf_op jit(solution)/shard_map/ppermute | solution.py:150

commit v8 on v6

--- a/solution.py
+++ b/solution.py
@@ -141,18 +141,19 @@
         ).reshape(2 * rows, width)
         sib = lax.ppermute(own, axes, swap)
         total = add_grads(None, *split([own, sib], half), w_gate, w_up, w_out)
-        arrived = [own, own]
+        subs = [own[j * 2 * half:(j + 1) * 2 * half] for j in range(halves)]
+        cws = list(subs)
+        ccws = list(subs)
         for step in range(1, steps + 1):
             last = step == steps and chips % 2 == 0
-            if last and halves == 2:
-                sent = [lax.ppermute(arrived[0][:2 * half], axes, cw_perm),
-                        lax.ppermute(arrived[1][2 * half:], axes, ccw_perm)]
-            elif last:
-                sent = [lax.ppermute(arrived[0], axes, cw_perm)]
-            else:
-                sent = [lax.ppermute(arrived[0], axes, cw_perm),
-                        lax.ppermute(arrived[1], axes, ccw_perm)]
-            arrived = sent
+            arrived = []
+            for j in range(halves):
+                if not last or halves == 1 or j == 0:
+                    cws[j] = lax.ppermute(cws[j], axes, cw_perm)
+                    arrived.append(cws[j])
+                if not last or (halves == 2 and j == 1):
+                    ccws[j] = lax.ppermute(ccws[j], axes, ccw_perm)
+                    arrived.append(ccws[j])
             if step == steps:
                 total, arrived = lax.optimization_barrier((total, arrived))
             from_sib = [lax.ppermute(chunk, axes, swap) for chunk in arrived]

time: 45.3 us -> 47.3 us (1.044)
  starting transfers between devices: 11.2 us -> 18.4 us
  waiting for transfers between devices: 13.9 us -> 8.14 us
  matrix products: 15.6 us -> 14.5 us
  other arithmetic: 3.59 us -> 4.48 us
  local copies, waits for them, and re-layouts: 0.37 us -> 0.9 us
    ppermute x8 -> x14, starting transfers between devices: 9.02 us -> 15.9 us  [the longest x7 13.3 us: local_ring(): cws[j] = lax.ppermute(cws[j], axes, cw_perm)]
    ppermute x8 -> x14, waiting for transfers between devices: 11.5 us -> 6.59 us  [the longest x7 5.41 us: local_ring(): ccws[j] = lax.ppermute(ccws[j], axes, ccw_perm)]
    dot_general x5, matrix products: 3.08 us -> 2.04 us  [gradients(): gate_pre = jnp.dot(keys, w_gate, preferred_element_type=jnp.float32)]
    another operation x1 -> x2, other arithmetic: 0.94 us -> 1.83 us  [local_ring(): jnp.stack([keys.reshape(halves, half, width), scaled.reshape(halves, half...]
    ppermute x8 -> x14, waiting for transfers between devices: 2.4 us -> 1.55 us  [local_ring(): from_sib = [lax.ppermute(chunk, axes, swap) for chunk in arrived]]
    ppermute x8 -> x14, starting transfers between devices: 1.67 us -> 2.42 us  [local_ring(): from_sib = [lax.ppermute(chunk, axes, swap) for chunk in arrived]]
    unnamed x29, local copies, waits for them, and re-layouts: 0.24 us -> 0.79 us
  transfers between devices with their start and end apart: 17 -> 29, of which waited for: 10 -> 8; matrix products, arithmetic and copies ran while one was open for 27% -> 26% of each run, Pallas kernels for 0% -> 0%
where the time goes in v8:
time: 47.3 us; the launch traced here: 47 us
  starting transfers between devices  18.4 us (39%)
  matrix products  14.5 us (31%)
  waiting for transfers between devices  8.14 us (17%)
  other arithmetic  4.48 us (9%)
  local copies, waits for them, and re-layouts  0.9 us (2%)
  between operations  0.54 us (1%)
    ppermute x7, starting transfers between devices, local_ring(): cws[j] = lax.ppermute(cws[j], axes, cw_perm)  13.3 us
    ppermute x7, waiting for transfers between devices, local_ring(): ccws[j] = lax.ppermute(ccws[j], axes, ccw_perm)  5.41 us
    dot_general x5, matrix products, gradients(): lax.dot_general(scaled, w_out, contract_last, preferred_element_type=jnp....  3.33 us
    dot_general x5, matrix products, gradients(): lax.dot_general(keys, both_grads, contract_first, preferred_element_type=...  3.22 us
    ppermute x7, starting transfers between devices, local_ring(): ccws[j] = lax.ppermute(ccws[j], axes, ccw_perm)  2.69 us
    ppermute x14, starting transfers between devices, local_ring(): from_sib = [lax.ppermute(chunk, axes, swap) for chunk in arrived]  2.42 us
    dot_general x5, matrix products, gradients(): lax.dot_general(activation, scaled, contract_first, preferred_element_typ...  2.3 us
    dot_general x5, matrix products, gradients(): gate_pre = jnp.dot(keys, w_gate, preferred_element_type=jnp.float32)  2.04 us
  transfers between devices with their start and end apart: 29, of which 8 were waited for; matrix products, arithmetic and copies ran while one was open for 26% of the time, Pallas kernels for 0%

profile of v8, /device:TPU:0, one launch (start us, length us, event | category | flops | bytes accessed | tf_op | source)
XLA Modules:
  0.0 47.0 jit_solution(11419650914110643340)
XLA Ops:
  0.0 1.1 %multiply_convert_fusion.23 = bf16[128,512]{1,0:T(8,128)(2,1)S(1)} fusion(bf16[128,512]{1,0:T(8,128)(2,1)} %param.8, f32[128]{0:T(128)} %param.10), kind=kLoop, calls=%fused_computation.84 | loop fusion | flops 196608 | bytes 262656 | tf_op jit(solution)/shard_map/convert_element_type | solution.py:137
  1.1 0.9 %fusion.40 = (bf16[1,2,64,512]{3,2,1,0:T(8,128)(2,1)S(1)}, bf16[1,2,64,512]{3,2,1,0:T(8,128)(2,1)S(1)}) fusion(bf16[2,1,64,512]{3,2,1,0:T(8,128)(2,1)} %bitcast.54, bf16[2,1,64,512]{3,2,1,0:T(8,128)(2,1)S(1)} %bitcast.50), kind=kLoop, calls=%fused_computation.86 | loop fusion | flops 131072 | bytes 524288 | tf_op jit(solution)/shard_map/stack | solution.py:139
  2.0 3.1 %collective-permute-start.1 = (bf16[128,512]{1,0:T(8,128)(2,1)S(1)}, bf16[128,512]{1,0:T(8,128)(2,1)S(1)}, u32[]{:S(2)}, u32[]{:S(2)}) collective-permute-start(bf16[128,512]{1,0:T(8,128)(2,1)S(1)} %bitcast.58), channel_id=1, source_target_pairs={{0,4},{1,5},{4,8},{5,9},{8,12},{9,13},{12,14},{13,15},{14,10},{15,... | collective-permute-start | bytes 393224 | tf_op jit(solution)/shard_map/ppermute | solution.py:152
  5.0 2.0 %collective-permute-start.3 = (bf16[128,512]{1,0:T(8,128)(2,1)S(1)}, bf16[128,512]{1,0:T(8,128)(2,1)S(1)}, u32[]{:S(2)}, u32[]{:S(2)}) collective-permute-start(bf16[128,512]{1,0:T(8,128)(2,1)S(1)} %bitcast.56), channel_id=1, source_target_pairs={{0,4},{1,5},{4,8},{5,9},{8,12},{9,13},{12,14},{13,15},{14,10},{15,... | collective-permute-start | bytes 393224 | tf_op jit(solution)/shard_map/ppermute | solution.py:152
  7.1 0.9 %pad_maximum_fusion = bf16[2,2,64,512]{3,2,1,0:T(8,128)(2,1)S(1)} fusion(bf16[2,1,64,512]{3,2,1,0:T(8,128)(2,1)S(1)} %bitcast.51, bf16[2,1,64,512]{3,2,1,0:T(8,128)(2,1)} %bitcast.55), kind=kLoop, calls=%fused_computation.70 | loop fusion | flops 131072 | bytes 524288 | tf_op jit(solution)/shard_map/stack | solution.py:139
  8.1 1.2 %collective-permute-done.1 = bf16[128,512]{1,0:T(8,128)(2,1)S(1)} collective-permute-done((bf16[128,512]{1,0:T(8,128)(2,1)S(1)}, bf16[128,512]{1,0:T(8,128)(2,1)S(1)}, u32[]{:S(2)}, u32[]{:S(2)}) %collective-permute-start.1) | collective-permute-done | bytes 131104 | tf_op jit(solution)/shard_map/ppermute | solution.py:152
  9.3 2.1 %collective-permute-done.2 = bf16[128,512]{1,0:T(8,128)(2,1)S(1)} collective-permute-done((bf16[128,512]{1,0:T(8,128)(2,1)S(1)}, bf16[128,512]{1,0:T(8,128)(2,1)S(1)}, u32[]{:S(2)}, u32[]{:S(2)}) %collective-permute-start.2) | collective-permute-done | bytes 131104 | tf_op jit(solution)/shard_map/ppermute | solution.py:155
  11.4 0.5 %collective-permute-start.7 = (bf16[128,512]{1,0:T(8,128)(2,1)S(1)}, bf16[128,512]{1,0:T(8,128)(2,1)S(1)}, u32[]{:S(2)}, u32[]{:S(2)}) collective-permute-start(bf16[128,512]{1,0:T(8,128)(2,1)S(1)} %collective-permute-done.3), channel_id=1, source_target_pairs={{0,1},{1,0},{2,3},{3,2},{4,5},{5,4},{6,7},{7,6},{8,9},{9,8},{10,11... | collective-permute-start | bytes 393224 | tf_op jit(solution)/shard_map/ppermute | solution.py:159
  11.9 0.9 %collective-permute-done.4 = bf16[128,512]{1,0:T(8,128)(2,1)S(1)} collective-permute-done((bf16[128,512]{1,0:T(8,128)(2,1)S(1)}, bf16[128,512]{1,0:T(8,128)(2,1)S(1)}, u32[]{:S(2)}, u32[]{:S(2)}) %collective-permute-start.4) | collective-permute-done | bytes 131104 | tf_op jit(solution)/shard_map/ppermute | solution.py:155
  12.9 1.6 %collective-permute-start.9 = (bf16[128,512]{1,0:T(8,128)(2,1)S(1)}, bf16[128,512]{1,0:T(8,128)(2,1)S(1)}, u32[]{:S(2)}, u32[]{:S(2)}) collective-permute-start(bf16[128,512]{1,0:T(8,128)(2,1)S(1)} %collective-permute-done.1), channel_id=1, source_target_pairs={{0,4},{1,5},{4,8},{5,9},{8,12},{9,13},{12,14},{13,15},{14,10},{15,... | collective-permute-start | bytes 393224 | tf_op jit(solution)/shard_map/ppermute | solution.py:152
  15.1 1.6 %collective-permute-start.11 = (bf16[128,512]{1,0:T(8,128)(2,1)S(1)}, bf16[128,512]{1,0:T(8,128)(2,1)S(1)}, u32[]{:S(2)}, u32[]{:S(2)}) collective-permute-start(bf16[128,512]{1,0:T(8,128)(2,1)S(1)} %collective-permute-done.3), channel_id=1, source_target_pairs={{0,4},{1,5},{4,8},{5,9},{8,12},{9,13},{12,14},{13,15},{14,10},{15,... | collective-permute-start | bytes 393224 | tf_op jit(solution)/shard_map/ppermute | solution.py:152
  16.7 0.5 %collective-permute-start.12 = (bf16[128,512]{1,0:T(8,128)(2,1)S(1)}, bf16[128,512]{1,0:T(8,128)(2,1)S(1)}, u32[]{:S(2)}, u32[]{:S(2)}) collective-permute-start(bf16[128,512]{1,0:T(8,128)(2,1)S(1)} %collective-permute-done.4), channel_id=1, source_target_pairs={{0,2},{1,3},{4,0},{5,1},{8,4},{9,5},{12,8},{13,9},{14,12},{15,13},... | collective-permute-start | bytes 393224 | tf_op jit(solution)/shard_map/ppermute | solution.py:155
  19.7 0.6 %copy-done.3 = bf16[512,512]{1,0:T(8,128)(2,1)S(1)} copy-done((bf16[512,512]{1,0:T(8,128)(2,1)S(1)}, bf16[512,512]{1,0:T(8,128)(2,1)}, u32[]{:S(2)}) %copy-start.3) | copy-done | bytes 524312
  20.3 0.8 %multiply_convert_fusion.11 = (bf16[512,512]{0,1:T(8,128)(2,1)S(1)}, bf16[512,512]{0,1:T(8,128)(2,1)S(1)}) fusion(f32[512,512]{0,1:T(8,128)S(1)} %fusion.72, f32[512,512]{0,1:T(8,128)S(1)} %fusion.71, bf16[512,512]{1,0:T(8,128)(2,1)S(1)} %get-tuple-element.71, bf16[512,512]{1,0:T(8,128)(2,1)S(1)} %copy-done.3), kind=kOutput, calls=%fused_computation.47 | convolution fusion | flops 271843328 | bytes 4194304 | tf_op jit(solution)/shard_map/dot_general | solution.py:31
  21.1 0.8 %fusion.5 = f32[512,1024]{1,0:T(8,128)S(1)} fusion(bf16[512,512]{1,0:T(8,128)(2,1)S(1)} %get-tuple-element.72, bf16[512,512]{0,1:T(8,128)(2,1)S(1)} %get-tuple-element.30, bf16[512,512]{0,1:T(8,128)(2,1)S(1)} %get-tuple-element.29), kind=kOutput, calls=%fused_computation.18 | convolution fusion | flops 538968064 | bytes 3670016 | tf_op jit(solution)/shard_map/dot_general | solution.py:36
  22.4 1.6 %collective-permute-start.17 = (bf16[128,512]{1,0:T(8,128)(2,1)S(1)}, bf16[128,512]{1,0:T(8,128)(2,1)S(1)}, u32[]{:S(2)}, u32[]{:S(2)}) collective-permute-start(bf16[128,512]{1,0:T(8,128)(2,1)S(1)} %collective-permute-done.9), channel_id=1, source_target_pairs={{0,4},{1,5},{4,8},{5,9},{8,12},{9,13},{12,14},{13,15},{14,10},{15,... | collective-permute-start | bytes 393224 | tf_op jit(solution)/shard_map/ppermute | solution.py:152
  25.9 1.6 %collective-permute-start.19 = (bf16[128,512]{1,0:T(8,128)(2,1)S(1)}, bf16[128,512]{1,0:T(8,128)(2,1)S(1)}, u32[]{:S(2)}, u32[]{:S(2)}) collective-permute-start(bf16[128,512]{1,0:T(8,128)(2,1)S(1)} %collective-permute-done.11), channel_id=1, source_target_pairs={{0,4},{1,5},{4,8},{5,9},{8,12},{9,13},{12,14},{13,15},{14,10},{15,... | collective-permute-start | bytes 393224 | tf_op jit(solution)/shard_map/ppermute | solution.py:152
  29.1 0.8 %multiply_convert_fusion.9 = (bf16[512,512]{0,1:T(8,128)(2,1)S(1)}, bf16[512,512]{0,1:T(8,128)(2,1)S(1)}) fusion(f32[512,512]{0,1:T(8,128)S(1)} %fusion.74, f32[512,512]{0,1:T(8,128)S(1)} %fusion.73, bf16[512,512]{1,0:T(8,128)(2,1)S(1)} %get-tuple-element.87, bf16[512,512]{1,0:T(8,128)(2,1)S(1)} %copy-done.3), kind=kOutput, calls=%fused_computation.43 | convolution fusion | flops 271843328 | bytes 4194304 | tf_op jit(solution)/shard_map/dot_general | solution.py:31
  30.3 0.8 %fusion.9 = f32[512,1024]{1,0:T(8,128)S(1)} fusion(bf16[512,512]{1,0:T(8,128)(2,1)S(1)} %get-tuple-element.88, bf16[512,512]{0,1:T(8,128)(2,1)S(1)} %get-tuple-element.32, bf16[512,512]{0,1:T(8,128)(2,1)S(1)} %get-tuple-element.31), kind=kOutput, calls=%fused_computation.22 | convolution fusion | flops 538968064 | bytes 3670016 | tf_op jit(solution)/shard_map/dot_general | solution.py:36
  31.2 1.6 %collective-permute-start.25 = (bf16[128,512]{1,0:T(8,128)(2,1)S(1)}, bf16[128,512]{1,0:T(8,128)(2,1)S(1)}, u32[]{:S(2)}, u32[]{:S(2)}) collective-permute-start(bf16[128,512]{1,0:T(8,128)(2,1)S(1)} %collective-permute-done.17), channel_id=1, source_target_pairs={{0,4},{1,5},{4,8},{5,9},{8,12},{9,13},{12,14},{13,15},{14,10},{15,... | collective-permute-start | bytes 393224 | tf_op jit(solution)/shard_map/ppermute | solution.py:152
  33.3 0.6 %collective-permute-done.20 = bf16[128,512]{1,0:T(8,128)(2,1)S(1)} collective-permute-done((bf16[128,512]{1,0:T(8,128)(2,1)S(1)}, bf16[128,512]{1,0:T(8,128)(2,1)S(1)}, u32[]{:S(2)}, u32[]{:S(2)}) %collective-permute-start.20) | collective-permute-done | bytes 131104 | tf_op jit(solution)/shard_map/ppermute | solution.py:155
  34.0 0.7 %collective-permute-start.26 = (bf16[128,512]{1,0:T(8,128)(2,1)S(1)}, bf16[128,512]{1,0:T(8,128)(2,1)S(1)}, u32[]{:S(2)}, u32[]{:S(2)}) collective-permute-start(bf16[128,512]{1,0:T(8,128)(2,1)S(1)} %collective-permute-done.20), channel_id=1, source_target_pairs={{0,2},{1,3},{4,0},{5,1},{8,4},{9,5},{12,8},{13,9},{14,12},{15,13},... | collective-permute-start | bytes 393224 | tf_op jit(solution)/shard_map/ppermute | solution.py:155
  34.8 0.5 %collective-permute-done.24 = bf16[128,512]{1,0:T(8,128)(2,1)S(1)} collective-permute-done((bf16[128,512]{1,0:T(8,128)(2,1)S(1)}, bf16[128,512]{1,0:T(8,128)(2,1)S(1)}, u32[]{:S(2)}, u32[]{:S(2)}) %collective-permute-start.24) | collective-permute-done | bytes 131104 | tf_op jit(solution)/shard_map/ppermute | solution.py:159
  36.3 0.8 %multiply_convert_fusion.7 = (bf16[512,512]{0,1:T(8,128)(2,1)S(1)}, bf16[512,512]{0,1:T(8,128)(2,1)S(1)}) fusion(f32[512,512]{0,1:T(8,128)S(1)} %fusion.76, f32[512,512]{0,1:T(8,128)S(1)} %fusion.75, bf16[512,512]{1,0:T(8,128)(2,1)S(1)} %get-tuple-element.55, bf16[512,512]{1,0:T(8,128)(2,1)S(1)} %copy-done.3), kind=kOutput, calls=%fused_computation.39 | convolution fusion | flops 271843328 | bytes 4194304 | tf_op jit(solution)/shard_map/dot_general | solution.py:31
  37.1 0.8 %add_add_fusion = f32[512,1024]{1,0:T(8,128)S(1)} fusion(f32[512,1024]{1,0:T(8,128)S(1)} %fusion.9, f32[512,1024]{1,0:T(8,128)S(1)} %fusion.19, f32[512,1024]{1,0:T(8,128)S(1)} %fusion.5, bf16[512,512]{1,0:T(8,128)(2,1)S(1)} %get-tuple-element.56, bf16[512,512]{0,1:T(8,128)(2,1)S(1)} %get-tuple-element.28, bf16[512,512]{0,1:T(8,128)(2,1)S(1)} %get-tuple-element.27), kind=kOutput, calls=%fused_computation | convolution fusion | flops 540540928 | bytes 9961472 | tf_op jit(solution)/shard_map/dot_general | solution.py:36
  38.4 1.8 %collective-permute-done.26 = bf16[128,512]{1,0:T(8,128)(2,1)S(1)} collective-permute-done((bf16[128,512]{1,0:T(8,128)(2,1)S(1)}, bf16[128,512]{1,0:T(8,128)(2,1)S(1)}, u32[]{:S(2)}, u32[]{:S(2)}) %collective-permute-start.26) | collective-permute-done | bytes 131104 | tf_op jit(solution)/shard_map/ppermute | solution.py:155
  40.2 0.5 %collective-permute-start.28 = (bf16[128,512]{1,0:T(8,128)(2,1)S(1)}, bf16[128,512]{1,0:T(8,128)(2,1)S(1)}, u32[]{:S(2)}, u32[]{:S(2)}) collective-permute-start(bf16[128,512]{1,0:T(8,128)(2,1)S(1)} %collective-permute-done.26), channel_id=1, source_target_pairs={{0,1},{1,0},{2,3},{3,2},{4,5},{5,4},{6,7},{7,6},{8,9},{9,8},{10,11... | collective-permute-start | bytes 393224 | tf_op jit(solution)/shard_map/ppermute | solution.py:159
  40.7 0.8 %collective-permute-done.27 = bf16[128,512]{1,0:T(8,128)(2,1)S(1)} collective-permute-done((bf16[128,512]{1,0:T(8,128)(2,1)S(1)}, bf16[128,512]{1,0:T(8,128)(2,1)S(1)}, u32[]{:S(2)}, u32[]{:S(2)}) %collective-permute-start.27) | collective-permute-done | bytes 131104 | tf_op jit(solution)/shard_map/ppermute | solution.py:159
  42.8 0.5 %fusion.4 = (f32[512]{0:T(512)S(1)}, f32[512]{0:T(512)S(1)}, f32[512,512]{1,0:T(8,128)S(1)}) fusion(bf16[512,512]{1,0:T(8,128)(2,1)S(1)} %copy-done.3, f32[512,512]{1,0:T(8,128)S(1)} %convolution_add_fusion, bf16[64,512]{1,0:T(8,128)(2,1)S(1)} %get-tuple-element.54, bf16[64,512]{1,0:T(8,128)(2,1)S(1)} %get-tuple-element.52, ...), kind=kOutput, calls=%fused_computation.17 | convolution fusion | flops 137886720 | bytes 3936256 | tf_op jit(solution)/shard_map/dot_general | solution.py:37
  43.8 0.6 %add.143 = f32[512,1024]{1,0:T(8,128)S(1)} add(f32[512,1024]{1,0:T(8,128)S(1)} %add_add_fusion, f32[512,1024]{1,0:T(8,128)S(1)} %fusion.23) | non-fusion elementwise | flops 524288 | bytes 6291456 | tf_op jit(solution)/shard_map/add | solution.py:108
  44.3 0.5 %multiply_reduce_fusion.1 = (f32[512]{0:T(512)S(1)}, f32[512]{0:T(512)S(1)}, f32[512]{0:T(512)S(1)}, f32[512]{0:T(512)S(1)}) fusion(f32[512,1024]{1,0:T(8,128)S(1)} %add.143, bf16[512,512]{1,0:T(8,128)(2,1)S(1)} %copy-done.1, bf16[512,512]{1,0:T(8,128)(2,1)S(1)} %copy-done.2), kind=kLoop, calls=%fused_computation.32 | loop fusion | flops 3143680 | bytes 3153920 | tf_op jit(solution)/shard_map/reduce_sum | solution.py:19
  45.8 1.3 %convolution_convert_fusion = bf16[128,512]{1,0:T(8,128)(2,1)} fusion(bf16[512,512]{1,0:T(8,128)(2,1)S(1)} %multiply_convert_fusion, bf16[512,512]{1,0:T(8,128)(2,1)S(1)} %get-tuple-element.17, bf16[128,512]{1,0:T(8,128)(2,1)S(1)} %copy-done, f32[128,512]{0,1:T(8,128)S(1)} %convolution_bitcast_fusion.1), kind=kOutput, calls=%fused_computation.14 | convolution fusion | flops 134676480 | bytes 1572864 | tf_op jit(solution)/shard_map/dot_general | solution.py:45
  (100 shorter events, 12.1 us)
Async XLA Ops:
  0.0 45.4 %copy-start = (bf16[128,512]{1,0:T(8,128)(2,1)S(1)}, bf16[128,512]{1,0:T(8,128)(2,1)}, u32[]{:S(2)}) copy-start(bf16[128,512]{1,0:T(8,128)(2,1)} %param.9) | copy-start | bytes 393220
  0.0 17.2 %copy-start.1 = (bf16[512,512]{1,0:T(8,128)(2,1)S(1)}, bf16[512,512]{1,0:T(8,128)(2,1)}, u32[]{:S(2)}) copy-start(bf16[512,512]{1,0:T(8,128)(2,1)} %param.12) | copy-start | bytes 1572868
  2.0 7.3 %collective-permute-start.1 = (bf16[128,512]{1,0:T(8,128)(2,1)S(1)}, bf16[128,512]{1,0:T(8,128)(2,1)S(1)}, u32[]{:S(2)}, u32[]{:S(2)}) collective-permute-start(bf16[128,512]{1,0:T(8,128)(2,1)S(1)} %bitcast.58), channel_id=1, source_target_pairs={{0,4},{1,5},{4,8},{5,9},{8,12},{9,13},{12,14},{13,15},{14,10},{15,... | collective-permute-start | bytes 393224 | tf_op jit(solution)/shard_map/ppermute | solution.py:152
  5.0 6.3 %collective-permute-start.2 = (bf16[128,512]{1,0:T(8,128)(2,1)S(1)}, bf16[128,512]{1,0:T(8,128)(2,1)S(1)}, u32[]{:S(2)}, u32[]{:S(2)}) collective-permute-start(bf16[128,512]{1,0:T(8,128)(2,1)S(1)} %bitcast.59), channel_id=1, source_target_pairs={{0,2},{1,3},{4,0},{5,1},{8,4},{9,5},{12,8},{13,9},{14,12},{15,13},... | collective-permute-start | bytes 393224 | tf_op jit(solution)/shard_map/ppermute | solution.py:155
  5.0 6.3 %collective-permute-start.3 = (bf16[128,512]{1,0:T(8,128)(2,1)S(1)}, bf16[128,512]{1,0:T(8,128)(2,1)S(1)}, u32[]{:S(2)}, u32[]{:S(2)}) collective-permute-start(bf16[128,512]{1,0:T(8,128)(2,1)S(1)} %bitcast.56), channel_id=1, source_target_pairs={{0,4},{1,5},{4,8},{5,9},{8,12},{9,13},{12,14},{13,15},{14,10},{15,... | collective-permute-start | bytes 393224 | tf_op jit(solution)/shard_map/ppermute | solution.py:152
  7.1 5.8 %collective-permute-start.4 = (bf16[128,512]{1,0:T(8,128)(2,1)S(1)}, bf16[128,512]{1,0:T(8,128)(2,1)S(1)}, u32[]{:S(2)}, u32[]{:S(2)}) collective-permute-start(bf16[128,512]{1,0:T(8,128)(2,1)S(1)} %bitcast.57), channel_id=1, source_target_pairs={{0,2},{1,3},{4,0},{5,1},{8,4},{9,5},{12,8},{13,9},{14,12},{15,13},... | collective-permute-start | bytes 393224 | tf_op jit(solution)/shard_map/ppermute | solution.py:155
  8.0 10.2 %collective-permute-start = (bf16[256,512]{1,0:T(8,128)(2,1)S(1)}, bf16[256,512]{1,0:T(8,128)(2,1)S(1)}, u32[]{:S(2)}, u32[]{:S(2)}) collective-permute-start(bf16[256,512]{1,0:T(8,128)(2,1)S(1)} %bitcast.52), channel_id=1, source_target_pairs={{0,1},{1,0},{2,3},{3,2},{4,5},{5,4},{6,7},{7,6},{8,9},{9,8},{10,11... | collective-permute-start | bytes 786440 | tf_op jit(solution)/shard_map/ppermute | solution.py:142
  8.1 9.6 %copy-start.2 = (bf16[512,512]{1,0:T(8,128)(2,1)S(1)}, bf16[512,512]{1,0:T(8,128)(2,1)}, u32[]{:S(2)}) copy-start(bf16[512,512]{1,0:T(8,128)(2,1)} %param.11) | copy-start | bytes 1572868
  9.3 3.6 %collective-permute-start.5 = (bf16[128,512]{1,0:T(8,128)(2,1)S(1)}, bf16[128,512]{1,0:T(8,128)(2,1)S(1)}, u32[]{:S(2)}, u32[]{:S(2)}) collective-permute-start(bf16[128,512]{1,0:T(8,128)(2,1)S(1)} %collective-permute-done.1), channel_id=1, source_target_pairs={{0,1},{1,0},{2,3},{3,2},{4,5},{5,4},{6,7},{7,6},{8,9},{9,8},{10,11... | collective-permute-start | bytes 393224 | tf_op jit(solution)/shard_map/ppermute | solution.py:159
  11.4 3.2 %collective-permute-start.6 = (bf16[128,512]{1,0:T(8,128)(2,1)S(1)}, bf16[128,512]{1,0:T(8,128)(2,1)S(1)}, u32[]{:S(2)}, u32[]{:S(2)}) collective-permute-start(bf16[128,512]{1,0:T(8,128)(2,1)S(1)} %collective-permute-done.2), channel_id=1, source_target_pairs={{0,1},{1,0},{2,3},{3,2},{4,5},{5,4},{6,7},{7,6},{8,9},{9,8},{10,11... | collective-permute-start | bytes 393224 | tf_op jit(solution)/shard_map/ppermute | solution.py:159
  11.4 3.7 %collective-permute-start.7 = (bf16[128,512]{1,0:T(8,128)(2,1)S(1)}, bf16[128,512]{1,0:T(8,128)(2,1)S(1)}, u32[]{:S(2)}, u32[]{:S(2)}) collective-permute-start(bf16[128,512]{1,0:T(8,128)(2,1)S(1)} %collective-permute-done.3), channel_id=1, source_target_pairs={{0,1},{1,0},{2,3},{3,2},{4,5},{5,4},{6,7},{7,6},{8,9},{9,8},{10,11... | collective-permute-start | bytes 393224 | tf_op jit(solution)/shard_map/ppermute | solution.py:159
  12.8 3.9 %collective-permute-start.8 = (bf16[128,512]{1,0:T(8,128)(2,1)S(1)}, bf16[128,512]{1,0:T(8,128)(2,1)S(1)}, u32[]{:S(2)}, u32[]{:S(2)}) collective-permute-start(bf16[128,512]{1,0:T(8,128)(2,1)S(1)} %collective-permute-done.4), channel_id=1, source_target_pairs={{0,1},{1,0},{2,3},{3,2},{4,5},{5,4},{6,7},{7,6},{8,9},{9,8},{10,11... | collective-permute-start | bytes 393224 | tf_op jit(solution)/shard_map/ppermute | solution.py:159
  12.9 9.4 %collective-permute-start.9 = (bf16[128,512]{1,0:T(8,128)(2,1)S(1)}, bf16[128,512]{1,0:T(8,128)(2,1)S(1)}, u32[]{:S(2)}, u32[]{:S(2)}) collective-permute-start(bf16[128,512]{1,0:T(8,128)(2,1)S(1)} %collective-permute-done.1), channel_id=1, source_target_pairs={{0,4},{1,5},{4,8},{5,9},{8,12},{9,13},{12,14},{13,15},{14,10},{15,... | collective-permute-start | bytes 393224 | tf_op jit(solution)/shard_map/ppermute | solution.py:152
  14.5 9.5 %collective-permute-start.10 = (bf16[128,512]{1,0:T(8,128)(2,1)S(1)}, bf16[128,512]{1,0:T(8,128)(2,1)S(1)}, u32[]{:S(2)}, u32[]{:S(2)}) collective-permute-start(bf16[128,512]{1,0:T(8,128)(2,1)S(1)} %collective-permute-done.2), channel_id=1, source_target_pairs={{0,2},{1,3},{4,0},{5,1},{8,4},{9,5},{12,8},{13,9},{14,12},{15,13},... | collective-permute-start | bytes 393224 | tf_op jit(solution)/shard_map/ppermute | solution.py:155
  15.1 9.2 %collective-permute-start.11 = (bf16[128,512]{1,0:T(8,128)(2,1)S(1)}, bf16[128,512]{1,0:T(8,128)(2,1)S(1)}, u32[]{:S(2)}, u32[]{:S(2)}) collective-permute-start(bf16[128,512]{1,0:T(8,128)(2,1)S(1)} %collective-permute-done.3), channel_id=1, source_target_pairs={{0,4},{1,5},{4,8},{5,9},{8,12},{9,13},{12,14},{13,15},{14,10},{15,... | collective-permute-start | bytes 393224 | tf_op jit(solution)/shard_map/ppermute | solution.py:152
  16.7 7.9 %collective-permute-start.12 = (bf16[128,512]{1,0:T(8,128)(2,1)S(1)}, bf16[128,512]{1,0:T(8,128)(2,1)S(1)}, u32[]{:S(2)}, u32[]{:S(2)}) collective-permute-start(bf16[128,512]{1,0:T(8,128)(2,1)S(1)} %collective-permute-done.4), channel_id=1, source_target_pairs={{0,2},{1,3},{4,0},{5,1},{8,4},{9,5},{12,8},{13,9},{14,12},{15,13},... | collective-permute-start | bytes 393224 | tf_op jit(solution)/shard_map/ppermute | solution.py:155
  22.3 3.0 %collective-permute-start.13 = (bf16[128,512]{1,0:T(8,128)(2,1)S(1)}, bf16[128,512]{1,0:T(8,128)(2,1)S(1)}, u32[]{:S(2)}, u32[]{:S(2)}) collective-permute-start(bf16[128,512]{1,0:T(8,128)(2,1)S(1)} %collective-permute-done.9), channel_id=1, source_target_pairs={{0,1},{1,0},{2,3},{3,2},{4,5},{5,4},{6,7},{7,6},{8,9},{9,8},{10,11... | collective-permute-start | bytes 393224 | tf_op jit(solution)/shard_map/ppermute | solution.py:159
  22.4 8.7 %collective-permute-start.17 = (bf16[128,512]{1,0:T(8,128)(2,1)S(1)}, bf16[128,512]{1,0:T(8,128)(2,1)S(1)}, u32[]{:S(2)}, u32[]{:S(2)}) collective-permute-start(bf16[128,512]{1,0:T(8,128)(2,1)S(1)} %collective-permute-done.9), channel_id=1, source_target_pairs={{0,4},{1,5},{4,8},{5,9},{8,12},{9,13},{12,14},{13,15},{14,10},{15,... | collective-permute-start | bytes 393224 | tf_op jit(solution)/shard_map/ppermute | solution.py:152
  24.1 1.8 %collective-permute-start.14 = (bf16[128,512]{1,0:T(8,128)(2,1)S(1)}, bf16[128,512]{1,0:T(8,128)(2,1)S(1)}, u32[]{:S(2)}, u32[]{:S(2)}) collective-permute-start(bf16[128,512]{1,0:T(8,128)(2,1)S(1)} %collective-permute-done.10), channel_id=1, source_target_pairs={{0,1},{1,0},{2,3},{3,2},{4,5},{5,4},{6,7},{7,6},{8,9},{9,8},{10,11... | collective-permute-start | bytes 393224 | tf_op jit(solution)/shard_map/ppermute | solution.py:159
  24.2 3.3 %collective-permute-start.15 = (bf16[128,512]{1,0:T(8,128)(2,1)S(1)}, bf16[128,512]{1,0:T(8,128)(2,1)S(1)}, u32[]{:S(2)}, u32[]{:S(2)}) collective-permute-start(bf16[128,512]{1,0:T(8,128)(2,1)S(1)} %collective-permute-done.11), channel_id=1, source_target_pairs={{0,1},{1,0},{2,3},{3,2},{4,5},{5,4},{6,7},{7,6},{8,9},{9,8},{10,11... | collective-permute-start | bytes 393224 | tf_op jit(solution)/shard_map/ppermute | solution.py:159
  24.6 3.4 %collective-permute-start.16 = (bf16[128,512]{1,0:T(8,128)(2,1)S(1)}, bf16[128,512]{1,0:T(8,128)(2,1)S(1)}, u32[]{:S(2)}, u32[]{:S(2)}) collective-permute-start(bf16[128,512]{1,0:T(8,128)(2,1)S(1)} %collective-permute-done.12), channel_id=1, source_target_pairs={{0,1},{1,0},{2,3},{3,2},{4,5},{5,4},{6,7},{7,6},{8,9},{9,8},{10,11... | collective-permute-start | bytes 393224 | tf_op jit(solution)/shard_map/ppermute | solution.py:159
  25.3 7.5 %collective-permute-start.18 = (bf16[128,512]{1,0:T(8,128)(2,1)S(1)}, bf16[128,512]{1,0:T(8,128)(2,1)S(1)}, u32[]{:S(2)}, u32[]{:S(2)}) collective-permute-start(bf16[128,512]{1,0:T(8,128)(2,1)S(1)} %collective-permute-done.10), channel_id=1, source_target_pairs={{0,2},{1,3},{4,0},{5,1},{8,4},{9,5},{12,8},{13,9},{14,12},{15,13},... | collective-permute-start | bytes 393224 | tf_op jit(solution)/shard_map/ppermute | solution.py:155
  25.9 7.1 %collective-permute-start.19 = (bf16[128,512]{1,0:T(8,128)(2,1)S(1)}, bf16[128,512]{1,0:T(8,128)(2,1)S(1)}, u32[]{:S(2)}, u32[]{:S(2)}) collective-permute-start(bf16[128,512]{1,0:T(8,128)(2,1)S(1)} %collective-permute-done.11), channel_id=1, source_target_pairs={{0,4},{1,5},{4,8},{5,9},{8,12},{9,13},{12,14},{13,15},{14,10},{15,... | collective-permute-start | bytes 393224 | tf_op jit(solution)/shard_map/ppermute | solution.py:152
  27.5 6.4 %collective-permute-start.20 = (bf16[128,512]{1,0:T(8,128)(2,1)S(1)}, bf16[128,512]{1,0:T(8,128)(2,1)S(1)}, u32[]{:S(2)}, u32[]{:S(2)}) collective-permute-start(bf16[128,512]{1,0:T(8,128)(2,1)S(1)} %collective-permute-done.12), channel_id=1, source_target_pairs={{0,2},{1,3},{4,0},{5,1},{8,4},{9,5},{12,8},{13,9},{14,12},{15,13},... | collective-permute-start | bytes 393224 | tf_op jit(solution)/shard_map/ppermute | solution.py:155
  31.1 2.9 %collective-permute-start.21 = (bf16[128,512]{1,0:T(8,128)(2,1)S(1)}, bf16[128,512]{1,0:T(8,128)(2,1)S(1)}, u32[]{:S(2)}, u32[]{:S(2)}) collective-permute-start(bf16[128,512]{1,0:T(8,128)(2,1)S(1)} %collective-permute-done.17), channel_id=1, source_target_pairs={{0,1},{1,0},{2,3},{3,2},{4,5},{5,4},{6,7},{7,6},{8,9},{9,8},{10,11... | collective-permute-start | bytes 393224 | tf_op jit(solution)/shard_map/ppermute | solution.py:159
  31.2 7.2 %collective-permute-start.25 = (bf16[128,512]{1,0:T(8,128)(2,1)S(1)}, bf16[128,512]{1,0:T(8,128)(2,1)S(1)}, u32[]{:S(2)}, u32[]{:S(2)}) collective-permute-start(bf16[128,512]{1,0:T(8,128)(2,1)S(1)} %collective-permute-done.17), channel_id=1, source_target_pairs={{0,4},{1,5},{4,8},{5,9},{8,12},{9,13},{12,14},{13,15},{14,10},{15,... | collective-permute-start | bytes 393224 | tf_op jit(solution)/shard_map/ppermute | solution.py:152
  32.8 1.9 %collective-permute-start.22 = (bf16[128,512]{1,0:T(8,128)(2,1)S(1)}, bf16[128,512]{1,0:T(8,128)(2,1)S(1)}, u32[]{:S(2)}, u32[]{:S(2)}) collective-permute-start(bf16[128,512]{1,0:T(8,128)(2,1)S(1)} %collective-permute-done.18), channel_id=1, source_target_pairs={{0,1},{1,0},{2,3},{3,2},{4,5},{5,4},{6,7},{7,6},{8,9},{9,8},{10,11... | collective-permute-start | bytes 393224 | tf_op jit(solution)/shard_map/ppermute | solution.py:159
  33.0 1.8 %collective-permute-start.23 = (bf16[128,512]{1,0:T(8,128)(2,1)S(1)}, bf16[128,512]{1,0:T(8,128)(2,1)S(1)}, u32[]{:S(2)}, u32[]{:S(2)}) collective-permute-start(bf16[128,512]{1,0:T(8,128)(2,1)S(1)} %collective-permute-done.19), channel_id=1, source_target_pairs={{0,1},{1,0},{2,3},{3,2},{4,5},{5,4},{6,7},{7,6},{8,9},{9,8},{10,11... | collective-permute-start | bytes 393224 | tf_op jit(solution)/shard_map/ppermute | solution.py:159
  34.0 1.3 %collective-permute-start.24 = (bf16[128,512]{1,0:T(8,128)(2,1)S(1)}, bf16[128,512]{1,0:T(8,128)(2,1)S(1)}, u32[]{:S(2)}, u32[]{:S(2)}) collective-permute-start(bf16[128,512]{1,0:T(8,128)(2,1)S(1)} %collective-permute-done.20), channel_id=1, source_target_pairs={{0,1},{1,0},{2,3},{3,2},{4,5},{5,4},{6,7},{7,6},{8,9},{9,8},{10,11... | collective-permute-start | bytes 393224 | tf_op jit(solution)/shard_map/ppermute | solution.py:159
  34.0 6.1 %collective-permute-start.26 = (bf16[128,512]{1,0:T(8,128)(2,1)S(1)}, bf16[128,512]{1,0:T(8,128)(2,1)S(1)}, u32[]{:S(2)}, u32[]{:S(2)}) collective-permute-start(bf16[128,512]{1,0:T(8,128)(2,1)S(1)} %collective-permute-done.20), channel_id=1, source_target_pairs={{0,2},{1,3},{4,0},{5,1},{8,4},{9,5},{12,8},{13,9},{14,12},{15,13},... | collective-permute-start | bytes 393224 | tf_op jit(solution)/shard_map/ppermute | solution.py:155
  40.2 1.3 %collective-permute-start.27 = (bf16[128,512]{1,0:T(8,128)(2,1)S(1)}, bf16[128,512]{1,0:T(8,128)(2,1)S(1)}, u32[]{:S(2)}, u32[]{:S(2)}) collective-permute-start(bf16[128,512]{1,0:T(8,128)(2,1)S(1)} %collective-permute-done.25), channel_id=1, source_target_pairs={{0,1},{1,0},{2,3},{3,2},{4,5},{5,4},{6,7},{7,6},{8,9},{9,8},{10,11... | collective-permute-start | bytes 393224 | tf_op jit(solution)/shard_map/ppermute | solution.py:159
  40.2 1.5 %collective-permute-start.28 = (bf16[128,512]{1,0:T(8,128)(2,1)S(1)}, bf16[128,512]{1,0:T(8,128)(2,1)S(1)}, u32[]{:S(2)}, u32[]{:S(2)}) collective-permute-start(bf16[128,512]{1,0:T(8,128)(2,1)S(1)} %collective-permute-done.26), channel_id=1, source_target_pairs={{0,1},{1,0},{2,3},{3,2},{4,5},{5,4},{6,7},{7,6},{8,9},{9,8},{10,11... | collective-permute-start | bytes 393224 | tf_op jit(solution)/shard_map/ppermute | solution.py:159
  (1 other events, 1.0 us)

commit v9 on v6

--- a/solution.py
+++ b/solution.py
@@ -39,8 +39,10 @@
 
 
 def apply(queries, full_gate, full_up, full_out_w):
-    q_gate = jnp.dot(queries, full_gate, preferred_element_type=jnp.float32)
-    q_up = jnp.dot(queries, full_up, preferred_element_type=jnp.float32)
+    hidden = full_gate.shape[1]
+    q_both = jnp.dot(queries, jnp.concatenate([full_gate, full_up], axis=1), preferred_element_type=jnp.float32)
+    q_gate = q_both[:, :hidden]
+    q_up = q_both[:, hidden:]
     q_act = (jax.nn.silu(q_gate) * q_up).astype(jnp.bfloat16)
     return jnp.dot(q_act, full_out_w, preferred_element_type=jnp.float32).astype(jnp.bfloat16)
 
@@ -134,8 +136,8 @@
         rows = keys.shape[0]
         halves = 2 if rows % 16 == 0 else 1
         half = rows // halves
+        width = keys.shape[1]
         scaled = (learn_rate[:, None] * values.astype(jnp.float32)).astype(jnp.bfloat16)
-        width = keys.shape[1]
         own = jnp.stack(
             [keys.reshape(halves, half, width), scaled.reshape(halves, half, width)], axis=1
         ).reshape(2 * rows, width)

time: 45.3 us -> 45.1 us (level)
  no operation moved by 1% of the time
where the time goes in v9:
time: 45.1 us; the launch traced here: 44.9 us
  matrix products  15.4 us (34%)
  waiting for transfers between devices  13.9 us (31%)
  starting transfers between devices  11.2 us (25%)
  other arithmetic  3.59 us (8%)
  between operations  0.48 us (1%)
    ppermute x3, waiting for transfers between devices, local_ring(): lax.ppermute(arrived[0], axes, cw_perm)  11.4 us
    ppermute x3, starting transfers between devices, local_ring(): lax.ppermute(arrived[0], axes, cw_perm)  6.29 us
    dot_general x5, matrix products, gradients(): lax.dot_general(scaled, w_out, contract_last, preferred_element_type=jnp....  3.34 us
    dot_general x5, matrix products, gradients(): lax.dot_general(keys, both_grads, contract_first, preferred_element_type=...  3.22 us
    dot_general x5, matrix products, gradients(): gate_pre = jnp.dot(keys, w_gate, preferred_element_type=jnp.float32)  3.08 us
    ppermute x8, waiting for transfers between devices, local_ring(): from_sib = [lax.ppermute(chunk, axes, swap) for chunk in arrived]  2.4 us
    dot_general x5, matrix products, gradients(): lax.dot_general(activation, scaled, contract_first, preferred_element_typ...  2.29 us
    dot_general x5, matrix products, gradients(): up_pre = jnp.dot(keys, w_up, preferred_element_type=jnp.float32)  2.04 us
  transfers between devices with their start and end apart: 17, of which 10 were waited for; matrix products, arithmetic and copies ran while one was open for 27% of the time, Pallas kernels for 0%

profile of v9, /device:TPU:0, one launch (start us, length us, event | category | flops | bytes accessed | tf_op | source)
XLA Modules:
  0.0 44.9 jit_solution(1603429120868366795)
XLA Ops:
  0.0 1.1 %multiply_convert_fusion.23 = bf16[128,512]{1,0:T(8,128)(2,1)S(1)} fusion(bf16[128,512]{1,0:T(8,128)(2,1)} %param.8, f32[128]{0:T(128)} %param.10), kind=kLoop, calls=%fused_computation.77 | loop fusion | flops 196608 | bytes 262656 | tf_op jit(solution)/shard_map/convert_element_type | solution.py:140
  1.1 0.9 %pad_maximum_fusion = bf16[2,2,64,512]{3,2,1,0:T(8,128)(2,1)S(1)} fusion(bf16[2,1,64,512]{3,2,1,0:T(8,128)(2,1)S(1)} %bitcast.41, bf16[2,1,64,512]{3,2,1,0:T(8,128)(2,1)} %bitcast.42), kind=kLoop, calls=%fused_computation.72 | loop fusion | flops 131072 | bytes 524288 | tf_op jit(solution)/shard_map/stack | solution.py:141
  2.0 0.5 %collective-permute-start = (bf16[256,512]{1,0:T(8,128)(2,1)S(1)}, bf16[256,512]{1,0:T(8,128)(2,1)S(1)}, u32[]{:S(2)}, u32[]{:S(2)}) collective-permute-start(bf16[256,512]{1,0:T(8,128)(2,1)S(1)} %bitcast.37), channel_id=1, source_target_pairs={{0,1},{1,0},{2,3},{3,2},{4,5},{5,4},{6,7},{7,6},{8,9},{9,8},{10,11... | collective-permute-start | bytes 786440 | tf_op jit(solution)/shard_map/ppermute | solution.py:144
  2.5 2.6 %collective-permute-start.1 = (bf16[256,512]{1,0:T(8,128)(2,1)S(1)}, bf16[256,512]{1,0:T(8,128)(2,1)S(1)}, u32[]{:S(2)}, u32[]{:S(2)}) collective-permute-start(bf16[256,512]{1,0:T(8,128)(2,1)S(1)} %bitcast.38), channel_id=1, source_target_pairs={{0,4},{1,5},{4,8},{5,9},{8,12},{9,13},{12,14},{13,15},{14,10},{15,... | collective-permute-start | bytes 786440 | tf_op jit(solution)/shard_map/ppermute | solution.py:155
  5.2 1.3 %fusion.60 = f32[256,512]{1,0:T(8,128)S(1)} fusion(bf16[512,512]{1,0:T(8,128)(2,1)} %param.11, bf16[64,512]{1,0:T(8,128)(2,1)S(1)} %get-tuple-element.76, bf16[64,512]{1,0:T(8,128)(2,1)S(1)} %get-tuple-element.73, bf16[64,512]{1,0:T(8,128)(2,1)S(1)} %get-tuple-element.72, bf16[64,512]{1,0:T(8,128)(2,1)S(1)} %get-tuple-element.69), kind=kOutput, calls=%fused_computation.150 | convolution fusion | flops 135266304 | bytes 1310720 | tf_op jit(solution)/shard_map/dot_general | solution.py:29
  7.8 4.2 %collective-permute-done.1 = bf16[256,512]{1,0:T(8,128)(2,1)S(1)} collective-permute-done((bf16[256,512]{1,0:T(8,128)(2,1)S(1)}, bf16[256,512]{1,0:T(8,128)(2,1)S(1)}, u32[]{:S(2)}, u32[]{:S(2)}) %collective-permute-start.1) | collective-permute-done | bytes 262176 | tf_op jit(solution)/shard_map/ppermute | solution.py:155
  12.0 1.8 %collective-permute-start.5 = (bf16[256,512]{1,0:T(8,128)(2,1)S(1)}, bf16[256,512]{1,0:T(8,128)(2,1)S(1)}, u32[]{:S(2)}, u32[]{:S(2)}) collective-permute-start(bf16[256,512]{1,0:T(8,128)(2,1)S(1)} %collective-permute-done.1), channel_id=1, source_target_pairs={{0,4},{1,5},{4,8},{5,9},{8,12},{9,13},{12,14},{13,15},{14,10},{15,... | collective-permute-start | bytes 786440 | tf_op jit(solution)/shard_map/ppermute | solution.py:155
  14.8 0.6 %collective-permute-done.4 = bf16[256,512]{1,0:T(8,128)(2,1)S(1)} collective-permute-done((bf16[256,512]{1,0:T(8,128)(2,1)S(1)}, bf16[256,512]{1,0:T(8,128)(2,1)S(1)}, u32[]{:S(2)}, u32[]{:S(2)}) %collective-permute-start.4) | collective-permute-done | bytes 262176 | tf_op jit(solution)/shard_map/ppermute | solution.py:160
  15.5 0.5 %fusion.68 = f32[512,512]{0,1:T(8,128)S(1)} fusion(bf16[512,512]{1,0:T(8,128)(2,1)S(1)} %get-tuple-element.54, bf16[512,512]{1,0:T(8,128)(2,1)S(1)} %copy-done.1), kind=kOutput, calls=%fused_computation.158 | convolution fusion | flops 268435456 | bytes 2097152 | tf_op jit(solution)/shard_map/dot_general | solution.py:30
  16.0 0.5 %fusion.69 = f32[512,512]{0,1:T(8,128)S(1)} fusion(bf16[512,512]{1,0:T(8,128)(2,1)S(1)} %get-tuple-element.54, bf16[512,512]{1,0:T(8,128)(2,1)S(1)} %copy-done.2), kind=kOutput, calls=%fused_computation.159 | convolution fusion | flops 268435456 | bytes 2097152 | tf_op jit(solution)/shard_map/dot_general | solution.py:29
  16.5 0.8 %multiply_convert_fusion.11 = (bf16[512,512]{0,1:T(8,128)(2,1)S(1)}, bf16[512,512]{0,1:T(8,128)(2,1)S(1)}) fusion(f32[512,512]{0,1:T(8,128)S(1)} %fusion.69, f32[512,512]{0,1:T(8,128)S(1)} %fusion.68, bf16[512,512]{1,0:T(8,128)(2,1)S(1)} %get-tuple-element.53, bf16[512,512]{1,0:T(8,128)(2,1)S(1)} %copy-done.3), kind=kOutput, calls=%fused_computation.47 | convolution fusion | flops 271843328 | bytes 4194304 | tf_op jit(solution)/shard_map/dot_general | solution.py:31
  17.8 3.0 %collective-permute-done.5 = bf16[256,512]{1,0:T(8,128)(2,1)S(1)} collective-permute-done((bf16[256,512]{1,0:T(8,128)(2,1)S(1)}, bf16[256,512]{1,0:T(8,128)(2,1)S(1)}, u32[]{:S(2)}, u32[]{:S(2)}) %collective-permute-start.5) | collective-permute-done | bytes 262176 | tf_op jit(solution)/shard_map/ppermute | solution.py:155
  20.7 1.8 %collective-permute-start.9 = (bf16[256,512]{1,0:T(8,128)(2,1)S(1)}, bf16[256,512]{1,0:T(8,128)(2,1)S(1)}, u32[]{:S(2)}, u32[]{:S(2)}) collective-permute-start(bf16[256,512]{1,0:T(8,128)(2,1)S(1)} %collective-permute-done.5), channel_id=1, source_target_pairs={{0,4},{1,5},{4,8},{5,9},{8,12},{9,13},{12,14},{13,15},{14,10},{15,... | collective-permute-start | bytes 786440 | tf_op jit(solution)/shard_map/ppermute | solution.py:155
  23.1 0.8 %fusion.3 = f32[512,1024]{1,0:T(8,128)S(1)} fusion(bf16[512,512]{1,0:T(8,128)(2,1)S(1)} %get-tuple-element.54, bf16[512,512]{0,1:T(8,128)(2,1)S(1)} %get-tuple-element.30, bf16[512,512]{0,1:T(8,128)(2,1)S(1)} %get-tuple-element.29), kind=kOutput, calls=%fused_computation.15 | convolution fusion | flops 538968064 | bytes 3670016 | tf_op jit(solution)/shard_map/dot_general | solution.py:36
  24.2 0.5 %fusion.70 = f32[512,512]{0,1:T(8,128)S(1)} fusion(bf16[512,512]{1,0:T(8,128)(2,1)S(1)} %get-tuple-element.78, bf16[512,512]{1,0:T(8,128)(2,1)S(1)} %copy-done.1), kind=kOutput, calls=%fused_computation.160 | convolution fusion | flops 268435456 | bytes 2097152 | tf_op jit(solution)/shard_map/dot_general | solution.py:30
  24.7 0.5 %fusion.71 = f32[512,512]{0,1:T(8,128)S(1)} fusion(bf16[512,512]{1,0:T(8,128)(2,1)S(1)} %get-tuple-element.78, bf16[512,512]{1,0:T(8,128)(2,1)S(1)} %copy-done.2), kind=kOutput, calls=%fused_computation.161 | convolution fusion | flops 268435456 | bytes 2097152 | tf_op jit(solution)/shard_map/dot_general | solution.py:29
  25.2 4.2 %collective-permute-done.9 = bf16[256,512]{1,0:T(8,128)(2,1)S(1)} collective-permute-done((bf16[256,512]{1,0:T(8,128)(2,1)S(1)}, bf16[256,512]{1,0:T(8,128)(2,1)S(1)}, u32[]{:S(2)}, u32[]{:S(2)}) %collective-permute-start.9) | collective-permute-done | bytes 262176 | tf_op jit(solution)/shard_map/ppermute | solution.py:155
  29.5 1.9 %collective-permute-start.13 = (bf16[128,512]{1,0:T(8,128)(2,1)S(1)}, bf16[128,512]{1,0:T(8,128)(2,1)S(1)}, u32[]{:S(2)}, u32[]{:S(2)}) collective-permute-start(bf16[128,512]{1,0:T(8,128)(2,1)S(1)} %slice.336), channel_id=1, source_target_pairs={{0,4},{1,5},{4,8},{5,9},{8,12},{9,13},{12,14},{13,15},{14,10},{15,... | collective-permute-start | bytes 393224 | tf_op jit(solution)/shard_map/ppermute | solution.py:150
  31.3 0.8 %multiply_convert_fusion.9 = (bf16[512,512]{0,1:T(8,128)(2,1)S(1)}, bf16[512,512]{0,1:T(8,128)(2,1)S(1)}) fusion(f32[512,512]{0,1:T(8,128)S(1)} %fusion.71, f32[512,512]{0,1:T(8,128)S(1)} %fusion.70, bf16[512,512]{1,0:T(8,128)(2,1)S(1)} %get-tuple-element.77, bf16[512,512]{1,0:T(8,128)(2,1)S(1)} %copy-done.3), kind=kOutput, calls=%fused_computation.43 | convolution fusion | flops 271843328 | bytes 4194304 | tf_op jit(solution)/shard_map/dot_general | solution.py:31
  33.2 0.5 %collective-permute-start.12 = (bf16[256,512]{1,0:T(8,128)(2,1)S(1)}, bf16[256,512]{1,0:T(8,128)(2,1)S(1)}, u32[]{:S(2)}, u32[]{:S(2)}) collective-permute-start(bf16[256,512]{1,0:T(8,128)(2,1)S(1)} %collective-permute-done.10), channel_id=1, source_target_pairs={{0,1},{1,0},{2,3},{3,2},{4,5},{5,4},{6,7},{7,6},{8,9},{9,8},{10,11... | collective-permute-start | bytes 786440 | tf_op jit(solution)/shard_map/ppermute | solution.py:160
  33.7 0.8 %fusion.7 = f32[512,1024]{1,0:T(8,128)S(1)} fusion(bf16[512,512]{1,0:T(8,128)(2,1)S(1)} %get-tuple-element.78, bf16[512,512]{0,1:T(8,128)(2,1)S(1)} %get-tuple-element.32, bf16[512,512]{0,1:T(8,128)(2,1)S(1)} %get-tuple-element.31), kind=kOutput, calls=%fused_computation.19 | convolution fusion | flops 538968064 | bytes 3670016 | tf_op jit(solution)/shard_map/dot_general | solution.py:36
  35.1 0.5 %fusion.72 = f32[512,512]{0,1:T(8,128)S(1)} fusion(bf16[512,512]{1,0:T(8,128)(2,1)S(1)} %get-tuple-element.38, bf16[512,512]{1,0:T(8,128)(2,1)S(1)} %copy-done.1), kind=kOutput, calls=%fused_computation.162 | convolution fusion | flops 268435456 | bytes 2097152 | tf_op jit(solution)/shard_map/dot_general | solution.py:30
  35.6 0.5 %fusion.73 = f32[512,512]{0,1:T(8,128)S(1)} fusion(bf16[512,512]{1,0:T(8,128)(2,1)S(1)} %get-tuple-element.38, bf16[512,512]{1,0:T(8,128)(2,1)S(1)} %copy-done.2), kind=kOutput, calls=%fused_computation.163 | convolution fusion | flops 268435456 | bytes 2097152 | tf_op jit(solution)/shard_map/dot_general | solution.py:29
  36.1 0.8 %multiply_convert_fusion.7 = (bf16[512,512]{0,1:T(8,128)(2,1)S(1)}, bf16[512,512]{0,1:T(8,128)(2,1)S(1)}) fusion(f32[512,512]{0,1:T(8,128)S(1)} %fusion.73, f32[512,512]{0,1:T(8,128)S(1)} %fusion.72, bf16[512,512]{1,0:T(8,128)(2,1)S(1)} %get-tuple-element.37, bf16[512,512]{1,0:T(8,128)(2,1)S(1)} %copy-done.3), kind=kOutput, calls=%fused_computation.39 | convolution fusion | flops 271843328 | bytes 4194304 | tf_op jit(solution)/shard_map/dot_general | solution.py:31
  36.9 0.8 %add_add_fusion = f32[512,1024]{1,0:T(8,128)S(1)} fusion(f32[512,1024]{1,0:T(8,128)S(1)} %fusion.7, f32[512,1024]{1,0:T(8,128)S(1)} %fusion.20, f32[512,1024]{1,0:T(8,128)S(1)} %fusion.3, bf16[512,512]{1,0:T(8,128)(2,1)S(1)} %get-tuple-element.38, bf16[512,512]{0,1:T(8,128)(2,1)S(1)} %get-tuple-element.28, bf16[512,512]{0,1:T(8,128)(2,1)S(1)} %get-tuple-element.27), kind=kOutput, calls=%fused_computation | convolution fusion | flops 540540928 | bytes 9961472 | tf_op jit(solution)/shard_map/dot_general | solution.py:36
  37.7 0.5 %convolution_add_fusion = f32[512,512]{1,0:T(8,128)S(1)} fusion(f32[512,512]{1,0:T(8,128)S(1)} %convolution_add_fusion.1, bf16[512,512]{1,0:T(8,128)(2,1)S(1)} %get-tuple-element.37, f32[512,512]{0,1:T(8,128)S(1)} %fusion.72, f32[512,512]{0,1:T(8,128)S(1)} %fusion.73), kind=kOutput, calls=%fused_computation.1 | convolution fusion | flops 270270464 | bytes 4718592 | tf_op jit(solution)/shard_map/dot_general | solution.py:37
  38.8 0.8 %collective-permute-done.15 = bf16[128,512]{1,0:T(8,128)(2,1)S(1)} collective-permute-done((bf16[128,512]{1,0:T(8,128)(2,1)S(1)}, bf16[128,512]{1,0:T(8,128)(2,1)S(1)}, u32[]{:S(2)}, u32[]{:S(2)}) %collective-permute-start.15) | collective-permute-done | bytes 131104 | tf_op jit(solution)/shard_map/ppermute | solution.py:160
  40.9 0.5 %fusion.2 = (f32[512]{0:T(512)S(1)}, f32[512]{0:T(512)S(1)}, f32[512,512]{1,0:T(8,128)S(1)}) fusion(bf16[512,512]{1,0:T(8,128)(2,1)S(1)} %copy-done.3, f32[512,512]{1,0:T(8,128)S(1)} %convolution_add_fusion, bf16[64,512]{1,0:T(8,128)(2,1)S(1)} %get-tuple-element.100, bf16[64,512]{1,0:T(8,128)(2,1)S(1)} %get-tuple-element.98, ...), kind=kOutput, calls=%fused_computation.14 | convolution fusion | flops 137886720 | bytes 3936256 | tf_op jit(solution)/shard_map/dot_general | solution.py:37
  41.8 0.6 %add.143 = f32[512,1024]{1,0:T(8,128)S(1)} add(f32[512,1024]{1,0:T(8,128)S(1)} %add_add_fusion, f32[512,1024]{1,0:T(8,128)S(1)} %fusion.24) | non-fusion elementwise | flops 524288 | bytes 6291456 | tf_op jit(solution)/shard_map/add | solution.py:110
  42.4 0.5 %multiply_reduce_fusion.1 = (f32[512]{0:T(512)S(1)}, f32[512]{0:T(512)S(1)}, f32[512]{0:T(512)S(1)}, f32[512]{0:T(512)S(1)}) fusion(f32[512,1024]{1,0:T(8,128)S(1)} %add.143, bf16[512,512]{1,0:T(8,128)(2,1)S(1)} %copy-done.1, bf16[512,512]{1,0:T(8,128)(2,1)S(1)} %copy-done.2), kind=kLoop, calls=%fused_computation.32 | loop fusion | flops 3143680 | bytes 3153920 | tf_op jit(solution)/shard_map/reduce_sum | solution.py:19
  43.5 0.5 %convolution_bitcast_fusion = f32[128,1024]{0,1:T(8,128)S(1)} fusion(bf16[128,512]{1,0:T(8,128)(2,1)S(1)} %copy-done, bf16[512,512]{1,0:T(8,128)(2,1)S(1)} %get-tuple-element.17, bf16[512,512]{1,0:T(8,128)(2,1)S(1)} %get-tuple-element.16), kind=kOutput, calls=%fused_computation.10 | convolution fusion | flops 136314880 | bytes 1703936 | tf_op jit(solution)/shard_map/dot_general | solution.py:43
  44.0 0.9 %convolution_convert_fusion = bf16[128,512]{1,0:T(8,128)(2,1)} fusion(bf16[512,512]{1,0:T(8,128)(2,1)S(1)} %multiply_convert_fusion, f32[128,1024]{0,1:T(8,128)S(1)} %convolution_bitcast_fusion), kind=kOutput, calls=%fused_computation.11 | convolution fusion | flops 67567616 | bytes 1179648 | tf_op jit(solution)/shard_map/dot_general | solution.py:47
  (77 shorter events, 8.0 us)
Async XLA Ops:
  0.0 43.5 %copy-start = (bf16[128,512]{1,0:T(8,128)(2,1)S(1)}, bf16[128,512]{1,0:T(8,128)(2,1)}, u32[]{:S(2)}) copy-start(bf16[128,512]{1,0:T(8,128)(2,1)} %param.9) | copy-start | bytes 393220
  0.0 6.6 %copy-start.1 = (bf16[512,512]{1,0:T(8,128)(2,1)S(1)}, bf16[512,512]{1,0:T(8,128)(2,1)}, u32[]{:S(2)}) copy-start(bf16[512,512]{1,0:T(8,128)(2,1)} %param.12) | copy-start | bytes 1572868
  2.0 4.9 %copy-start.3 = (bf16[512,512]{1,0:T(8,128)(2,1)S(1)}, bf16[512,512]{1,0:T(8,128)(2,1)}, u32[]{:S(2)}) copy-start(bf16[512,512]{1,0:T(8,128)(2,1)} %param.13) | copy-start | bytes 1572868
  2.0 3.2 %collective-permute-start = (bf16[256,512]{1,0:T(8,128)(2,1)S(1)}, bf16[256,512]{1,0:T(8,128)(2,1)S(1)}, u32[]{:S(2)}, u32[]{:S(2)}) collective-permute-start(bf16[256,512]{1,0:T(8,128)(2,1)S(1)} %bitcast.37), channel_id=1, source_target_pairs={{0,1},{1,0},{2,3},{3,2},{4,5},{5,4},{6,7},{7,6},{8,9},{9,8},{10,11... | collective-permute-start | bytes 786440 | tf_op jit(solution)/shard_map/ppermute | solution.py:144
  2.5 9.5 %collective-permute-start.1 = (bf16[256,512]{1,0:T(8,128)(2,1)S(1)}, bf16[256,512]{1,0:T(8,128)(2,1)S(1)}, u32[]{:S(2)}, u32[]{:S(2)}) collective-permute-start(bf16[256,512]{1,0:T(8,128)(2,1)S(1)} %bitcast.38), channel_id=1, source_target_pairs={{0,4},{1,5},{4,8},{5,9},{8,12},{9,13},{12,14},{13,15},{14,10},{15,... | collective-permute-start | bytes 786440 | tf_op jit(solution)/shard_map/ppermute | solution.py:155
  5.2 8.7 %collective-permute-start.2 = (bf16[256,512]{1,0:T(8,128)(2,1)S(1)}, bf16[256,512]{1,0:T(8,128)(2,1)S(1)}, u32[]{:S(2)}, u32[]{:S(2)}) collective-permute-start(bf16[256,512]{1,0:T(8,128)(2,1)S(1)} %bitcast.39), channel_id=1, source_target_pairs={{0,2},{1,3},{4,0},{5,1},{8,4},{9,5},{12,8},{13,9},{14,12},{15,13},... | collective-permute-start | bytes 786440 | tf_op jit(solution)/shard_map/ppermute | solution.py:156
  12.0 2.8 %collective-permute-start.3 = (bf16[256,512]{1,0:T(8,128)(2,1)S(1)}, bf16[256,512]{1,0:T(8,128)(2,1)S(1)}, u32[]{:S(2)}, u32[]{:S(2)}) collective-permute-start(bf16[256,512]{1,0:T(8,128)(2,1)S(1)} %collective-permute-done.1), channel_id=1, source_target_pairs={{0,1},{1,0},{2,3},{3,2},{4,5},{5,4},{6,7},{7,6},{8,9},{9,8},{10,11... | collective-permute-start | bytes 786440 | tf_op jit(solution)/shard_map/ppermute | solution.py:160
  12.0 8.7 %collective-permute-start.5 = (bf16[256,512]{1,0:T(8,128)(2,1)S(1)}, bf16[256,512]{1,0:T(8,128)(2,1)S(1)}, u32[]{:S(2)}, u32[]{:S(2)}) collective-permute-start(bf16[256,512]{1,0:T(8,128)(2,1)S(1)} %collective-permute-done.1), channel_id=1, source_target_pairs={{0,4},{1,5},{4,8},{5,9},{8,12},{9,13},{12,14},{13,15},{14,10},{15,... | collective-permute-start | bytes 786440 | tf_op jit(solution)/shard_map/ppermute | solution.py:155
  13.9 1.6 %collective-permute-start.4 = (bf16[256,512]{1,0:T(8,128)(2,1)S(1)}, bf16[256,512]{1,0:T(8,128)(2,1)S(1)}, u32[]{:S(2)}, u32[]{:S(2)}) collective-permute-start(bf16[256,512]{1,0:T(8,128)(2,1)S(1)} %collective-permute-done.2), channel_id=1, source_target_pairs={{0,1},{1,0},{2,3},{3,2},{4,5},{5,4},{6,7},{7,6},{8,9},{9,8},{10,11... | collective-permute-start | bytes 786440 | tf_op jit(solution)/shard_map/ppermute | solution.py:160
  14.1 8.5 %collective-permute-start.6 = (bf16[256,512]{1,0:T(8,128)(2,1)S(1)}, bf16[256,512]{1,0:T(8,128)(2,1)S(1)}, u32[]{:S(2)}, u32[]{:S(2)}) collective-permute-start(bf16[256,512]{1,0:T(8,128)(2,1)S(1)} %collective-permute-done.2), channel_id=1, source_target_pairs={{0,2},{1,3},{4,0},{5,1},{8,4},{9,5},{12,8},{13,9},{14,12},{15,13},... | collective-permute-start | bytes 786440 | tf_op jit(solution)/shard_map/ppermute | solution.py:156
  14.8 1.2 %copy-start.2 = (bf16[512,512]{1,0:T(8,128)(2,1)S(1)}, bf16[512,512]{1,0:T(8,128)(2,1)}, u32[]{:S(2)}) copy-start(bf16[512,512]{1,0:T(8,128)(2,1)} %param.11) | copy-start | bytes 1572868
  20.7 3.2 %collective-permute-start.7 = (bf16[256,512]{1,0:T(8,128)(2,1)S(1)}, bf16[256,512]{1,0:T(8,128)(2,1)S(1)}, u32[]{:S(2)}, u32[]{:S(2)}) collective-permute-start(bf16[256,512]{1,0:T(8,128)(2,1)S(1)} %collective-permute-done.5), channel_id=1, source_target_pairs={{0,1},{1,0},{2,3},{3,2},{4,5},{5,4},{6,7},{7,6},{8,9},{9,8},{10,11... | collective-permute-start | bytes 786440 | tf_op jit(solution)/shard_map/ppermute | solution.py:160
  20.7 8.7 %collective-permute-start.9 = (bf16[256,512]{1,0:T(8,128)(2,1)S(1)}, bf16[256,512]{1,0:T(8,128)(2,1)S(1)}, u32[]{:S(2)}, u32[]{:S(2)}) collective-permute-start(bf16[256,512]{1,0:T(8,128)(2,1)S(1)} %collective-permute-done.5), channel_id=1, source_target_pairs={{0,4},{1,5},{4,8},{5,9},{8,12},{9,13},{12,14},{13,15},{14,10},{15,... | collective-permute-start | bytes 786440 | tf_op jit(solution)/shard_map/ppermute | solution.py:155
  22.6 1.5 %collective-permute-start.8 = (bf16[256,512]{1,0:T(8,128)(2,1)S(1)}, bf16[256,512]{1,0:T(8,128)(2,1)S(1)}, u32[]{:S(2)}, u32[]{:S(2)}) collective-permute-start(bf16[256,512]{1,0:T(8,128)(2,1)S(1)} %collective-permute-done.6), channel_id=1, source_target_pairs={{0,1},{1,0},{2,3},{3,2},{4,5},{5,4},{6,7},{7,6},{8,9},{9,8},{10,11... | collective-permute-start | bytes 786440 | tf_op jit(solution)/shard_map/ppermute | solution.py:160
  22.9 9.7 %collective-permute-start.10 = (bf16[256,512]{1,0:T(8,128)(2,1)S(1)}, bf16[256,512]{1,0:T(8,128)(2,1)S(1)}, u32[]{:S(2)}, u32[]{:S(2)}) collective-permute-start(bf16[256,512]{1,0:T(8,128)(2,1)S(1)} %collective-permute-done.6), channel_id=1, source_target_pairs={{0,2},{1,3},{4,0},{5,1},{8,4},{9,5},{12,8},{13,9},{14,12},{15,13},... | collective-permute-start | bytes 786440 | tf_op jit(solution)/shard_map/ppermute | solution.py:156
  29.5 8.7 %collective-permute-start.13 = (bf16[128,512]{1,0:T(8,128)(2,1)S(1)}, bf16[128,512]{1,0:T(8,128)(2,1)S(1)}, u32[]{:S(2)}, u32[]{:S(2)}) collective-permute-start(bf16[128,512]{1,0:T(8,128)(2,1)S(1)} %slice.336), channel_id=1, source_target_pairs={{0,4},{1,5},{4,8},{5,9},{8,12},{9,13},{12,14},{13,15},{14,10},{15,... | collective-permute-start | bytes 393224 | tf_op jit(solution)/shard_map/ppermute | solution.py:150
  32.6 5.5 %collective-permute-start.14 = (bf16[128,512]{1,0:T(8,128)(2,1)S(1)}, bf16[128,512]{1,0:T(8,128)(2,1)S(1)}, u32[]{:S(2)}, u32[]{:S(2)}) collective-permute-start(bf16[128,512]{1,0:T(8,128)(2,1)S(1)} %slice.337), channel_id=1, source_target_pairs={{0,2},{1,3},{4,0},{5,1},{8,4},{9,5},{12,8},{13,9},{14,12},{15,13},... | collective-permute-start | bytes 393224 | tf_op jit(solution)/shard_map/ppermute | solution.py:151
  33.1 1.6 %collective-permute-start.11 = (bf16[256,512]{1,0:T(8,128)(2,1)S(1)}, bf16[256,512]{1,0:T(8,128)(2,1)S(1)}, u32[]{:S(2)}, u32[]{:S(2)}) collective-permute-start(bf16[256,512]{1,0:T(8,128)(2,1)S(1)} %collective-permute-done.9), channel_id=1, source_target_pairs={{0,1},{1,0},{2,3},{3,2},{4,5},{5,4},{6,7},{7,6},{8,9},{9,8},{10,11... | collective-permute-start | bytes 786440 | tf_op jit(solution)/shard_map/ppermute | solution.py:160
  33.2 1.9 %collective-permute-start.12 = (bf16[256,512]{1,0:T(8,128)(2,1)S(1)}, bf16[256,512]{1,0:T(8,128)(2,1)S(1)}, u32[]{:S(2)}, u32[]{:S(2)}) collective-permute-start(bf16[256,512]{1,0:T(8,128)(2,1)S(1)} %collective-permute-done.10), channel_id=1, source_target_pairs={{0,1},{1,0},{2,3},{3,2},{4,5},{5,4},{6,7},{7,6},{8,9},{9,8},{10,11... | collective-permute-start | bytes 786440 | tf_op jit(solution)/shard_map/ppermute | solution.py:160
  38.2 1.4 %collective-permute-start.15 = (bf16[128,512]{1,0:T(8,128)(2,1)S(1)}, bf16[128,512]{1,0:T(8,128)(2,1)S(1)}, u32[]{:S(2)}, u32[]{:S(2)}) collective-permute-start(bf16[128,512]{1,0:T(8,128)(2,1)S(1)} %collective-permute-done.13), channel_id=1, source_target_pairs={{0,1},{1,0},{2,3},{3,2},{4,5},{5,4},{6,7},{7,6},{8,9},{9,8},{10,11... | collective-permute-start | bytes 393224 | tf_op jit(solution)/shard_map/ppermute | solution.py:160
  38.4 1.4 %collective-permute-start.16 = (bf16[128,512]{1,0:T(8,128)(2,1)S(1)}, bf16[128,512]{1,0:T(8,128)(2,1)S(1)}, u32[]{:S(2)}, u32[]{:S(2)}) collective-permute-start(bf16[128,512]{1,0:T(8,128)(2,1)S(1)} %collective-permute-done.14), channel_id=1, source_target_pairs={{0,1},{1,0},{2,3},{3,2},{4,5},{5,4},{6,7},{7,6},{8,9},{9,8},{10,11... | collective-permute-start | bytes 393224 | tf_op jit(solution)/shard_map/ppermute | solution.py:160

commit v10 on v9

--- a/solution.py
+++ b/solution.py
@@ -1,6 +1,7 @@
 import jax
 import jax.numpy as jnp
 from jax import lax
+from jax.experimental import pallas as pl
 from jax.sharding import PartitionSpec as P
 
 epsilon = 1e-06
@@ -45,6 +46,22 @@
     q_up = q_both[:, hidden:]
     q_act = (jax.nn.silu(q_gate) * q_up).astype(jnp.bfloat16)
     return jnp.dot(q_act, full_out_w, preferred_element_type=jnp.float32).astype(jnp.bfloat16)
+
+
+def _tail_kernel(in_a, in_b, out_a, out_b, wg, wu, wo, q, o):
+    hidden = wg.shape[1]
+    grad_in = in_a[...] + in_b[...]
+    new_gate = renorm(wg[...], grad_in[:, :hidden])
+    new_up = renorm(wu[...], grad_in[:, hidden:])
+    new_out = renorm(wo[...], out_a[...] + out_b[...])
+    o[...] = apply(q[...], new_gate, new_up, new_out)
+
+
+def tail(total, last, w_gate, w_up, w_out, queries):
+    return pl.pallas_call(
+        _tail_kernel,
+        out_shape=jax.ShapeDtypeStruct((queries.shape[0], w_out.shape[1]), jnp.bfloat16),
+    )(total[0], last[0], total[1], last[1], w_gate, w_up, w_out, queries)
 
 
 def local_gather(keys, values, queries, learn_rate, w_gate, w_up, w_out):
@@ -158,13 +175,11 @@
             if step == steps:
                 total, arrived = lax.optimization_barrier((total, arrived))
             from_sib = [lax.ppermute(chunk, axes, swap) for chunk in arrived]
+            if step == steps:
+                last = gradients(*split(arrived + from_sib, half), w_gate, w_up, w_out)
+                return tail(total, last, w_gate, w_up, w_out, queries)
             total = add_grads(total, *split(arrived + from_sib, half), w_gate, w_up, w_out)
-        full_in, full_out = total
-        new_gate = renorm(w_gate, full_in[:, :hidden])
-        new_up = renorm(w_up, full_in[:, hidden:])
-        new_out = renorm(w_out, full_out)
-        new_gate, new_up, new_out = lax.optimization_barrier((new_gate, new_up, new_out))
-        return apply(queries, new_gate, new_up, new_out)
+        del hidden
 
     return local_ring
 

time: 45.1 us -> 51.8 us (1.15)
  Pallas kernels: 0 us -> 5.44 us
  matrix products: 15.4 us -> 18.5 us
  other arithmetic: 3.59 us -> 1.98 us
    pallas_call x0 -> x1, Pallas kernels: none -> 5.44 us  [tail(): pl.pallas_call(_tail_kernel, out_shape=jax.ShapeDtypeStruct((queries.shap...]
    dot_general x5, matrix products: 3.22 us -> 5.9 us  [gradients(): lax.dot_general(keys, both_grads, contract_first, preferred_element_type=...]
    dot_general x5, matrix products: 2.29 us -> 4.16 us  [gradients(): lax.dot_general(activation, scaled, contract_first, preferred_element_typ...]
    dot_general x2 -> x0, matrix products: 1.42 us -> none  [the longest x1 0.95 us: apply(): jnp.dot(q_act, full_out_w, preferred_element_type=jnp.float32)]
    add x1 -> x0, other arithmetic: 0.55 us -> none  [add_grads(): return (total[0] + full_in, total[1] + full_out)]
  transfers between devices with their start and end apart: 17 -> 17, of which waited for: 10 -> 10; matrix products, arithmetic and copies ran while one was open for 27% -> 28% of each run, Pallas kernels for 0% -> 0%
where the time goes in v10:
time: 51.8 us; the launch traced here: 51.7 us
  matrix products  18.5 us (36%)
  waiting for transfers between devices  13.9 us (27%)
  starting transfers between devices  11.1 us (21%)
  Pallas kernels  5.44 us (11%)
  other arithmetic  1.98 us (4%)
    ppermute x3, waiting for transfers between devices, local_ring(): lax.ppermute(arrived[0], axes, cw_perm)  11.4 us
    ppermute x3, starting transfers between devices, local_ring(): lax.ppermute(arrived[0], axes, cw_perm)  6.29 us
    dot_general x5, matrix products, gradients(): lax.dot_general(keys, both_grads, contract_first, preferred_element_type=...  5.9 us
    pallas_call x1, Pallas kernels, tail(): pl.pallas_call(_tail_kernel, out_shape=jax.ShapeDtypeStruct((queries.shap...  5.44 us
    dot_general x5, matrix products, gradients(): lax.dot_general(activation, scaled, contract_first, preferred_element_typ...  4.16 us
    dot_general x5, matrix products, gradients(): lax.dot_general(scaled, w_out, contract_last, preferred_element_type=jnp....  3.31 us
    dot_general x5, matrix products, gradients(): gate_pre = jnp.dot(keys, w_gate, preferred_element_type=jnp.float32)  3.07 us
    ppermute x8, waiting for transfers between devices, local_ring(): from_sib = [lax.ppermute(chunk, axes, swap) for chunk in arrived]  2.39 us
  transfers between devices with their start and end apart: 17, of which 10 were waited for; matrix products, arithmetic and copies ran while one was open for 28% of the time, Pallas kernels for 0%

profile of v10, /device:TPU:0, one launch (start us, length us, event | category | flops | bytes accessed | tf_op | source)
XLA Modules:
  0.0 51.7 jit_solution(10676183208223860359)
XLA Ops:
  0.0 1.0 %multiply_convert_fusion.20 = bf16[128,512]{1,0:T(8,128)(2,1)S(1)} fusion(bf16[128,512]{1,0:T(8,128)(2,1)} %param.8, f32[128]{0:T(128)} %param.10), kind=kLoop, calls=%fused_computation.55 | loop fusion | flops 196608 | bytes 262656 | tf_op jit(solution)/shard_map/convert_element_type | solution.py:157
  1.1 0.9 %pad_maximum_fusion = bf16[2,2,64,512]{3,2,1,0:T(8,128)(2,1)S(1)} fusion(bf16[2,1,64,512]{3,2,1,0:T(8,128)(2,1)S(1)} %bitcast.37, bf16[2,1,64,512]{3,2,1,0:T(8,128)(2,1)} %bitcast.38), kind=kLoop, calls=%fused_computation.50 | loop fusion | flops 131072 | bytes 524288 | tf_op jit(solution)/shard_map/stack | solution.py:158
  2.0 0.5 %collective-permute-start = (bf16[256,512]{1,0:T(8,128)(2,1)S(1)}, bf16[256,512]{1,0:T(8,128)(2,1)S(1)}, u32[]{:S(2)}, u32[]{:S(2)}) collective-permute-start(bf16[256,512]{1,0:T(8,128)(2,1)S(1)} %bitcast.33), channel_id=1, source_target_pairs={{0,1},{1,0},{2,3},{3,2},{4,5},{5,4},{6,7},{7,6},{8,9},{9,8},{10,11... | collective-permute-start | bytes 786440 | tf_op jit(solution)/shard_map/ppermute | solution.py:161
  2.5 2.6 %collective-permute-start.1 = (bf16[256,512]{1,0:T(8,128)(2,1)S(1)}, bf16[256,512]{1,0:T(8,128)(2,1)S(1)}, u32[]{:S(2)}, u32[]{:S(2)}) collective-permute-start(bf16[256,512]{1,0:T(8,128)(2,1)S(1)} %bitcast.34), channel_id=1, source_target_pairs={{0,4},{1,5},{4,8},{5,9},{8,12},{9,13},{12,14},{13,15},{14,10},{15,... | collective-permute-start | bytes 786440 | tf_op jit(solution)/shard_map/ppermute | solution.py:172
  5.2 1.3 %fusion.49 = f32[256,512]{1,0:T(8,128)S(1)} fusion(bf16[512,512]{1,0:T(8,128)(2,1)} %wg.1, bf16[64,512]{1,0:T(8,128)(2,1)S(1)} %get-tuple-element.62, bf16[64,512]{1,0:T(8,128)(2,1)S(1)} %get-tuple-element.59, bf16[64,512]{1,0:T(8,128)(2,1)S(1)} %get-tuple-element.58, bf16[64,512]{1,0:T(8,128)(2,1)S(1)} %get-tuple-element.55), kind=kOutput, calls=%fused_computation.122 | convolution fusion | flops 135266304 | bytes 1310720 | tf_op jit(solution)/shard_map/dot_general | solution.py:30
  7.8 4.2 %collective-permute-done.1 = bf16[256,512]{1,0:T(8,128)(2,1)S(1)} collective-permute-done((bf16[256,512]{1,0:T(8,128)(2,1)S(1)}, bf16[256,512]{1,0:T(8,128)(2,1)S(1)}, u32[]{:S(2)}, u32[]{:S(2)}) %collective-permute-start.1) | collective-permute-done | bytes 262176 | tf_op jit(solution)/shard_map/ppermute | solution.py:172
  12.0 1.8 %collective-permute-start.5 = (bf16[256,512]{1,0:T(8,128)(2,1)S(1)}, bf16[256,512]{1,0:T(8,128)(2,1)S(1)}, u32[]{:S(2)}, u32[]{:S(2)}) collective-permute-start(bf16[256,512]{1,0:T(8,128)(2,1)S(1)} %collective-permute-done.1), channel_id=1, source_target_pairs={{0,4},{1,5},{4,8},{5,9},{8,12},{9,13},{12,14},{13,15},{14,10},{15,... | collective-permute-start | bytes 786440 | tf_op jit(solution)/shard_map/ppermute | solution.py:172
  14.8 0.6 %collective-permute-done.4 = bf16[256,512]{1,0:T(8,128)(2,1)S(1)} collective-permute-done((bf16[256,512]{1,0:T(8,128)(2,1)S(1)}, bf16[256,512]{1,0:T(8,128)(2,1)S(1)}, u32[]{:S(2)}, u32[]{:S(2)}) %collective-permute-start.4) | collective-permute-done | bytes 262176 | tf_op jit(solution)/shard_map/ppermute | solution.py:177
  15.5 0.5 fusion.57
  16.0 0.5 fusion.58
  16.5 0.8 %multiply_convert_fusion.8 = (bf16[512,512]{0,1:T(8,128)(2,1)S(1)}, bf16[512,512]{0,1:T(8,128)(2,1)S(1)}) fusion(f32[512,512]{0,1:T(8,128)S(1)} %fusion.58, f32[512,512]{0,1:T(8,128)S(1)} %fusion.57, bf16[512,512]{1,0:T(8,128)(2,1)S(1)} %get-tuple-element.39, bf16[512,512]{1,0:T(8,128)(2,1)S(1)} %copy-done.2), kind=kOutput, calls=%fused_computation.27 | convolution fusion | flops 271843328 | bytes 4194304 | tf_op jit(solution)/shard_map/dot_general | solution.py:32
  17.3 0.5 convolution_add_fusion.2
  17.7 3.0 %collective-permute-done.5 = bf16[256,512]{1,0:T(8,128)(2,1)S(1)} collective-permute-done((bf16[256,512]{1,0:T(8,128)(2,1)S(1)}, bf16[256,512]{1,0:T(8,128)(2,1)S(1)}, u32[]{:S(2)}, u32[]{:S(2)}) %collective-permute-start.5) | collective-permute-done | bytes 262176 | tf_op jit(solution)/shard_map/ppermute | solution.py:172
  20.7 1.8 %collective-permute-start.9 = (bf16[256,512]{1,0:T(8,128)(2,1)S(1)}, bf16[256,512]{1,0:T(8,128)(2,1)S(1)}, u32[]{:S(2)}, u32[]{:S(2)}) collective-permute-start(bf16[256,512]{1,0:T(8,128)(2,1)S(1)} %collective-permute-done.5), channel_id=1, source_target_pairs={{0,4},{1,5},{4,8},{5,9},{8,12},{9,13},{12,14},{13,15},{14,10},{15,... | collective-permute-start | bytes 786440 | tf_op jit(solution)/shard_map/ppermute | solution.py:172
  23.1 0.8 %fusion = f32[512,1024]{1,0:T(8,128)S(1)} fusion(bf16[512,512]{1,0:T(8,128)(2,1)S(1)} %get-tuple-element.40, bf16[512,512]{0,1:T(8,128)(2,1)S(1)} %get-tuple-element.16, bf16[512,512]{0,1:T(8,128)(2,1)S(1)} %get-tuple-element.15), kind=kOutput, calls=%fused_computation.4 | convolution fusion | flops 538968064 | bytes 3670016 | tf_op jit(solution)/shard_map/dot_general | solution.py:37
  24.2 0.5 fusion.59
  24.7 0.5 fusion.60
  25.2 4.3 %collective-permute-done.9 = bf16[256,512]{1,0:T(8,128)(2,1)S(1)} collective-permute-done((bf16[256,512]{1,0:T(8,128)(2,1)S(1)}, bf16[256,512]{1,0:T(8,128)(2,1)S(1)}, u32[]{:S(2)}, u32[]{:S(2)}) %collective-permute-start.9) | collective-permute-done | bytes 262176 | tf_op jit(solution)/shard_map/ppermute | solution.py:172
  29.4 1.9 %collective-permute-start.13 = (bf16[128,512]{1,0:T(8,128)(2,1)S(1)}, bf16[128,512]{1,0:T(8,128)(2,1)S(1)}, u32[]{:S(2)}, u32[]{:S(2)}) collective-permute-start(bf16[128,512]{1,0:T(8,128)(2,1)S(1)} %slice.320), channel_id=1, source_target_pairs={{0,4},{1,5},{4,8},{5,9},{8,12},{9,13},{12,14},{13,15},{14,10},{15,... | collective-permute-start | bytes 393224 | tf_op jit(solution)/shard_map/ppermute | solution.py:167
  31.3 0.8 %multiply_convert_fusion.6 = (bf16[512,512]{0,1:T(8,128)(2,1)S(1)}, bf16[512,512]{0,1:T(8,128)(2,1)S(1)}) fusion(f32[512,512]{0,1:T(8,128)S(1)} %fusion.60, f32[512,512]{0,1:T(8,128)S(1)} %fusion.59, bf16[512,512]{1,0:T(8,128)(2,1)S(1)} %get-tuple-element.63, bf16[512,512]{1,0:T(8,128)(2,1)S(1)} %copy-done.2), kind=kOutput, calls=%fused_computation.23 | convolution fusion | flops 271843328 | bytes 4194304 | tf_op jit(solution)/shard_map/dot_general | solution.py:32
  32.1 0.5 convolution_add_fusion.1
  33.1 0.5 collective-permute-start.12
  33.7 0.8 %fusion.4 = f32[512,1024]{1,0:T(8,128)S(1)} fusion(bf16[512,512]{1,0:T(8,128)(2,1)S(1)} %get-tuple-element.64, bf16[512,512]{0,1:T(8,128)(2,1)S(1)} %get-tuple-element.18, bf16[512,512]{0,1:T(8,128)(2,1)S(1)} %get-tuple-element.17), kind=kOutput, calls=%fused_computation.8 | convolution fusion | flops 538968064 | bytes 3670016 | tf_op jit(solution)/shard_map/dot_general | solution.py:37
  35.1 0.5 fusion.61
  35.6 0.5 fusion.62
  36.1 0.8 %multiply_convert_fusion.4 = (bf16[512,512]{0,1:T(8,128)(2,1)S(1)}, bf16[512,512]{0,1:T(8,128)(2,1)S(1)}) fusion(f32[512,512]{0,1:T(8,128)S(1)} %fusion.62, f32[512,512]{0,1:T(8,128)S(1)} %fusion.61, bf16[512,512]{1,0:T(8,128)(2,1)S(1)} %get-tuple-element.23, bf16[512,512]{1,0:T(8,128)(2,1)S(1)} %copy-done.2), kind=kOutput, calls=%fused_computation.19 | convolution fusion | flops 271843328 | bytes 4194304 | tf_op jit(solution)/shard_map/dot_general | solution.py:32
  36.9 2.1 %add_add_fusion.in_a = f32[512,1024]{1,0:T(8,128)} fusion(f32[512,1024]{1,0:T(8,128)S(1)} %fusion.4, f32[512,1024]{1,0:T(8,128)S(1)} %fusion.14, f32[512,1024]{1,0:T(8,128)S(1)} %fusion, bf16[512,512]{1,0:T(8,128)(2,1)S(1)} %get-tuple-element.24, bf16[512,512]{0,1:T(8,128)(2,1)S(1)} %get-tuple-element.14, bf16[512,512]{0,1:T(8,128)(2,1)S(1)} %get-tuple-element.13), kind=kOutput, calls=%fused_computation | convolution fusion | flops 540540928 | bytes 9961472 | tf_op jit(solution)/shard_map/dot_general | solution.py:37
  39.0 1.5 %convolution_add_fusion.out_a = f32[512,512]{1,0:T(8,128)} fusion(f32[512,512]{1,0:T(8,128)S(1)} %convolution_add_fusion.1, bf16[512,512]{1,0:T(8,128)(2,1)S(1)} %get-tuple-element.23, f32[512,512]{0,1:T(8,128)S(1)} %fusion.61, f32[512,512]{0,1:T(8,128)S(1)} %fusion.62), kind=kOutput, calls=%fused_computation.1 | convolution fusion | flops 270270464 | bytes 4718592 | tf_op jit(solution)/shard_map/dot_general | solution.py:38
  41.0 0.8 %collective-permute-done.15 = bf16[128,512]{1,0:T(8,128)(2,1)S(1)} collective-permute-done((bf16[128,512]{1,0:T(8,128)(2,1)S(1)}, bf16[128,512]{1,0:T(8,128)(2,1)S(1)}, u32[]{:S(2)}, u32[]{:S(2)}) %collective-permute-start.15) | collective-permute-done | bytes 131104 | tf_op jit(solution)/shard_map/ppermute | solution.py:177
  42.6 1.4 %fusion.25.out_b = f32[512,512]{1,0:T(8,128)} fusion(f32[256,512]{1,0:T(8,128)S(1)} %fusion.48, f32[256,512]{1,0:T(8,128)S(1)} %fusion.47, bf16[64,512]{1,0:T(8,128)(2,1)S(1)} %get-tuple-element.86, bf16[64,512]{1,0:T(8,128)(2,1)S(1)} %get-tuple-element.84, bf16[64,512]{1,0:T(8,128)(2,1)S(1)} %get-tuple-element.87, bf16[64,512]{1,0:T(8,128)(2,1)S(1)} %get-tuple-element.80), kind=kOutput, calls=%fused_computation.49 | convolution fusion | flops 136052736 | bytes 2359296 | tf_op jit(solution)/shard_map/dot_general | solution.py:38
  44.4 1.8 %fusion.18.in_b = f32[512,1024]{1,0:T(8,128)} fusion(bf16[256,512]{1,0:T(8,128)(2,1)S(1)} %get-tuple-element.20, bf16[256,512]{1,0:T(8,128)(2,1)S(1)} %get-tuple-element.19, bf16[64,512]{1,0:T(8,128)(2,1)S(1)} %get-tuple-element.85, bf16[64,512]{1,0:T(8,128)(2,1)S(1)} %get-tuple-element.83, bf16[64,512]{1,0:T(8,128)(2,1)S(1)} %get-tuple-element.88, ...), kind=kOutput, calls=%fused_computation.34 | convolution fusion | flops 270532608 | bytes 2883584 | tf_op jit(solution)/shard_map/dot_general | solution.py:37
  46.2 5.4 %shard_map.73 = bf16[128,512]{1,0:T(8,128)(2,1)} custom-call(f32[512,1024]{1,0:T(8,128)} %add_add_fusion.in_a, f32[512,1024]{1,0:T(8,128)} %fusion.18.in_b, f32[512,512]{1,0:T(8,128)} %convolution_add_fusion.out_a, f32[512,512]{1,0:T(8,128)} %fusion.25.out_b, bf16[512,512]{1,0:T(8,128)(2,1)} %wg.1, bf16[512,512]{1,0:T(8,128)(2,1)} %wu.1, ...), custom_call_target="tpu_custom_call" | custom-call | tf_op jit(solution)/shard_map/pallas_call | solution.py:61
  (67 shorter events, 6.0 us)
Async XLA Ops:
  0.0 6.6 %copy-start.1 = (bf16[512,512]{1,0:T(8,128)(2,1)S(1)}, bf16[512,512]{1,0:T(8,128)(2,1)}, u32[]{:S(2)}) copy-start(bf16[512,512]{1,0:T(8,128)(2,1)} %wu.1) | copy-start | bytes 1572868
  2.0 4.9 %copy-start.2 = (bf16[512,512]{1,0:T(8,128)(2,1)S(1)}, bf16[512,512]{1,0:T(8,128)(2,1)}, u32[]{:S(2)}) copy-start(bf16[512,512]{1,0:T(8,128)(2,1)} %wo.1) | copy-start | bytes 1572868
  2.0 3.2 %collective-permute-start = (bf16[256,512]{1,0:T(8,128)(2,1)S(1)}, bf16[256,512]{1,0:T(8,128)(2,1)S(1)}, u32[]{:S(2)}, u32[]{:S(2)}) collective-permute-start(bf16[256,512]{1,0:T(8,128)(2,1)S(1)} %bitcast.33), channel_id=1, source_target_pairs={{0,1},{1,0},{2,3},{3,2},{4,5},{5,4},{6,7},{7,6},{8,9},{9,8},{10,11... | collective-permute-start | bytes 786440 | tf_op jit(solution)/shard_map/ppermute | solution.py:161
  2.5 9.5 %collective-permute-start.1 = (bf16[256,512]{1,0:T(8,128)(2,1)S(1)}, bf16[256,512]{1,0:T(8,128)(2,1)S(1)}, u32[]{:S(2)}, u32[]{:S(2)}) collective-permute-start(bf16[256,512]{1,0:T(8,128)(2,1)S(1)} %bitcast.34), channel_id=1, source_target_pairs={{0,4},{1,5},{4,8},{5,9},{8,12},{9,13},{12,14},{13,15},{14,10},{15,... | collective-permute-start | bytes 786440 | tf_op jit(solution)/shard_map/ppermute | solution.py:172
  5.2 8.7 %collective-permute-start.2 = (bf16[256,512]{1,0:T(8,128)(2,1)S(1)}, bf16[256,512]{1,0:T(8,128)(2,1)S(1)}, u32[]{:S(2)}, u32[]{:S(2)}) collective-permute-start(bf16[256,512]{1,0:T(8,128)(2,1)S(1)} %bitcast.35), channel_id=1, source_target_pairs={{0,2},{1,3},{4,0},{5,1},{8,4},{9,5},{12,8},{13,9},{14,12},{15,13},... | collective-permute-start | bytes 786440 | tf_op jit(solution)/shard_map/ppermute | solution.py:173
  12.0 2.8 %collective-permute-start.3 = (bf16[256,512]{1,0:T(8,128)(2,1)S(1)}, bf16[256,512]{1,0:T(8,128)(2,1)S(1)}, u32[]{:S(2)}, u32[]{:S(2)}) collective-permute-start(bf16[256,512]{1,0:T(8,128)(2,1)S(1)} %collective-permute-done.1), channel_id=1, source_target_pairs={{0,1},{1,0},{2,3},{3,2},{4,5},{5,4},{6,7},{7,6},{8,9},{9,8},{10,11... | collective-permute-start | bytes 786440 | tf_op jit(solution)/shard_map/ppermute | solution.py:177
  12.0 8.7 %collective-permute-start.5 = (bf16[256,512]{1,0:T(8,128)(2,1)S(1)}, bf16[256,512]{1,0:T(8,128)(2,1)S(1)}, u32[]{:S(2)}, u32[]{:S(2)}) collective-permute-start(bf16[256,512]{1,0:T(8,128)(2,1)S(1)} %collective-permute-done.1), channel_id=1, source_target_pairs={{0,4},{1,5},{4,8},{5,9},{8,12},{9,13},{12,14},{13,15},{14,10},{15,... | collective-permute-start | bytes 786440 | tf_op jit(solution)/shard_map/ppermute | solution.py:172
  13.8 1.6 %collective-permute-start.4 = (bf16[256,512]{1,0:T(8,128)(2,1)S(1)}, bf16[256,512]{1,0:T(8,128)(2,1)S(1)}, u32[]{:S(2)}, u32[]{:S(2)}) collective-permute-start(bf16[256,512]{1,0:T(8,128)(2,1)S(1)} %collective-permute-done.2), channel_id=1, source_target_pairs={{0,1},{1,0},{2,3},{3,2},{4,5},{5,4},{6,7},{7,6},{8,9},{9,8},{10,11... | collective-permute-start | bytes 786440 | tf_op jit(solution)/shard_map/ppermute | solution.py:177
  14.1 8.5 %collective-permute-start.6 = (bf16[256,512]{1,0:T(8,128)(2,1)S(1)}, bf16[256,512]{1,0:T(8,128)(2,1)S(1)}, u32[]{:S(2)}, u32[]{:S(2)}) collective-permute-start(bf16[256,512]{1,0:T(8,128)(2,1)S(1)} %collective-permute-done.2), channel_id=1, source_target_pairs={{0,2},{1,3},{4,0},{5,1},{8,4},{9,5},{12,8},{13,9},{14,12},{15,13},... | collective-permute-start | bytes 786440 | tf_op jit(solution)/shard_map/ppermute | solution.py:173
  14.8 1.2 %copy-start = (bf16[512,512]{1,0:T(8,128)(2,1)S(1)}, bf16[512,512]{1,0:T(8,128)(2,1)}, u32[]{:S(2)}) copy-start(bf16[512,512]{1,0:T(8,128)(2,1)} %wg.1) | copy-start | bytes 1572868
  20.7 3.2 %collective-permute-start.7 = (bf16[256,512]{1,0:T(8,128)(2,1)S(1)}, bf16[256,512]{1,0:T(8,128)(2,1)S(1)}, u32[]{:S(2)}, u32[]{:S(2)}) collective-permute-start(bf16[256,512]{1,0:T(8,128)(2,1)S(1)} %collective-permute-done.5), channel_id=1, source_target_pairs={{0,1},{1,0},{2,3},{3,2},{4,5},{5,4},{6,7},{7,6},{8,9},{9,8},{10,11... | collective-permute-start | bytes 786440 | tf_op jit(solution)/shard_map/ppermute | solution.py:177
  20.7 8.7 %collective-permute-start.9 = (bf16[256,512]{1,0:T(8,128)(2,1)S(1)}, bf16[256,512]{1,0:T(8,128)(2,1)S(1)}, u32[]{:S(2)}, u32[]{:S(2)}) collective-permute-start(bf16[256,512]{1,0:T(8,128)(2,1)S(1)} %collective-permute-done.5), channel_id=1, source_target_pairs={{0,4},{1,5},{4,8},{5,9},{8,12},{9,13},{12,14},{13,15},{14,10},{15,... | collective-permute-start | bytes 786440 | tf_op jit(solution)/shard_map/ppermute | solution.py:172
  22.6 1.5 %collective-permute-start.8 = (bf16[256,512]{1,0:T(8,128)(2,1)S(1)}, bf16[256,512]{1,0:T(8,128)(2,1)S(1)}, u32[]{:S(2)}, u32[]{:S(2)}) collective-permute-start(bf16[256,512]{1,0:T(8,128)(2,1)S(1)} %collective-permute-done.6), channel_id=1, source_target_pairs={{0,1},{1,0},{2,3},{3,2},{4,5},{5,4},{6,7},{7,6},{8,9},{9,8},{10,11... | collective-permute-start | bytes 786440 | tf_op jit(solution)/shard_map/ppermute | solution.py:177
  22.9 9.8 %collective-permute-start.10 = (bf16[256,512]{1,0:T(8,128)(2,1)S(1)}, bf16[256,512]{1,0:T(8,128)(2,1)S(1)}, u32[]{:S(2)}, u32[]{:S(2)}) collective-permute-start(bf16[256,512]{1,0:T(8,128)(2,1)S(1)} %collective-permute-done.6), channel_id=1, source_target_pairs={{0,2},{1,3},{4,0},{5,1},{8,4},{9,5},{12,8},{13,9},{14,12},{15,13},... | collective-permute-start | bytes 786440 | tf_op jit(solution)/shard_map/ppermute | solution.py:173
  29.4 11.0 %collective-permute-start.13 = (bf16[128,512]{1,0:T(8,128)(2,1)S(1)}, bf16[128,512]{1,0:T(8,128)(2,1)S(1)}, u32[]{:S(2)}, u32[]{:S(2)}) collective-permute-start(bf16[128,512]{1,0:T(8,128)(2,1)S(1)} %slice.320), channel_id=1, source_target_pairs={{0,4},{1,5},{4,8},{5,9},{8,12},{9,13},{12,14},{13,15},{14,10},{15,... | collective-permute-start | bytes 393224 | tf_op jit(solution)/shard_map/ppermute | solution.py:167
  32.6 7.8 %collective-permute-start.14 = (bf16[128,512]{1,0:T(8,128)(2,1)S(1)}, bf16[128,512]{1,0:T(8,128)(2,1)S(1)}, u32[]{:S(2)}, u32[]{:S(2)}) collective-permute-start(bf16[128,512]{1,0:T(8,128)(2,1)S(1)} %slice.321), channel_id=1, source_target_pairs={{0,2},{1,3},{4,0},{5,1},{8,4},{9,5},{12,8},{13,9},{14,12},{15,13},... | collective-permute-start | bytes 393224 | tf_op jit(solution)/shard_map/ppermute | solution.py:168
  33.1 1.6 %collective-permute-start.11 = (bf16[256,512]{1,0:T(8,128)(2,1)S(1)}, bf16[256,512]{1,0:T(8,128)(2,1)S(1)}, u32[]{:S(2)}, u32[]{:S(2)}) collective-permute-start(bf16[256,512]{1,0:T(8,128)(2,1)S(1)} %collective-permute-done.9), channel_id=1, source_target_pairs={{0,1},{1,0},{2,3},{3,2},{4,5},{5,4},{6,7},{7,6},{8,9},{9,8},{10,11... | collective-permute-start | bytes 786440 | tf_op jit(solution)/shard_map/ppermute | solution.py:177
  33.1 1.9 %collective-permute-start.12 = (bf16[256,512]{1,0:T(8,128)(2,1)S(1)}, bf16[256,512]{1,0:T(8,128)(2,1)S(1)}, u32[]{:S(2)}, u32[]{:S(2)}) collective-permute-start(bf16[256,512]{1,0:T(8,128)(2,1)S(1)} %collective-permute-done.10), channel_id=1, source_target_pairs={{0,1},{1,0},{2,3},{3,2},{4,5},{5,4},{6,7},{7,6},{8,9},{9,8},{10,11... | collective-permute-start | bytes 786440 | tf_op jit(solution)/shard_map/ppermute | solution.py:177
  40.4 1.4 %collective-permute-start.15 = (bf16[128,512]{1,0:T(8,128)(2,1)S(1)}, bf16[128,512]{1,0:T(8,128)(2,1)S(1)}, u32[]{:S(2)}, u32[]{:S(2)}) collective-permute-start(bf16[128,512]{1,0:T(8,128)(2,1)S(1)} %collective-permute-done.13), channel_id=1, source_target_pairs={{0,1},{1,0},{2,3},{3,2},{4,5},{5,4},{6,7},{7,6},{8,9},{9,8},{10,11... | collective-permute-start | bytes 393224 | tf_op jit(solution)/shard_map/ppermute | solution.py:177
  40.6 1.4 %collective-permute-start.16 = (bf16[128,512]{1,0:T(8,128)(2,1)S(1)}, bf16[128,512]{1,0:T(8,128)(2,1)S(1)}, u32[]{:S(2)}, u32[]{:S(2)}) collective-permute-start(bf16[128,512]{1,0:T(8,128)(2,1)S(1)} %collective-permute-done.14), channel_id=1, source_target_pairs={{0,1},{1,0},{2,3},{3,2},{4,5},{5,4},{6,7},{7,6},{8,9},{9,8},{10,11... | collective-permute-start | bytes 393224 | tf_op jit(solution)/shard_map/ppermute | solution.py:177

commit v11 on v6

--- a/solution.py
+++ b/solution.py
@@ -112,10 +112,14 @@
     chips = len(ring)
     cw_perm = []
     ccw_perm = []
+    cw2_perm = []
+    ccw2_perm = []
     for p in range(chips):
         for c in range(2):
             cw_perm.append((ring[p] * 2 + c, ring[(p + 1) % chips] * 2 + c))
             ccw_perm.append((ring[p] * 2 + c, ring[(p - 1) % chips] * 2 + c))
+            cw2_perm.append((ring[p] * 2 + c, ring[(p + 2) % chips] * 2 + c))
+            ccw2_perm.append((ring[p] * 2 + c, ring[(p - 2) % chips] * 2 + c))
     swap = [(i, i ^ 1) for i in range(chips * 2)]
     steps = chips // 2
     axes = ("seq", "outer")
@@ -142,21 +146,29 @@
         sib = lax.ppermute(own, axes, swap)
         total = add_grads(None, *split([own, sib], half), w_gate, w_up, w_out)
         arrived = [own, own]
-        for step in range(1, steps + 1):
-            last = step == steps and chips % 2 == 0
-            if last and halves == 2:
+        jump = chips % 2 == 0 and chips >= 4 and halves == 2
+        last_step = steps - 1 if jump else steps
+        for step in range(1, last_step + 1):
+            final = step == last_step
+            if final and jump:
+                sent = [lax.ppermute(arrived[0], axes, cw_perm),
+                        lax.ppermute(arrived[1], axes, ccw_perm),
+                        lax.ppermute(arrived[0][:2 * half], axes, cw2_perm),
+                        lax.ppermute(arrived[1][2 * half:], axes, ccw2_perm)]
+            elif final and chips % 2 == 0 and halves == 2:
                 sent = [lax.ppermute(arrived[0][:2 * half], axes, cw_perm),
                         lax.ppermute(arrived[1][2 * half:], axes, ccw_perm)]
-            elif last:
+            elif final and chips % 2 == 0:
                 sent = [lax.ppermute(arrived[0], axes, cw_perm)]
             else:
                 sent = [lax.ppermute(arrived[0], axes, cw_perm),
                         lax.ppermute(arrived[1], axes, ccw_perm)]
             arrived = sent
-            if step == steps:
+            if final:
                 total, arrived = lax.optimization_barrier((total, arrived))
             from_sib = [lax.ppermute(chunk, axes, swap) for chunk in arrived]
             total = add_grads(total, *split(arrived + from_sib, half), w_gate, w_up, w_out)
+            arrived = arrived[:2]
         full_in, full_out = total
         new_gate = renorm(w_gate, full_in[:, :hidden])
         new_up = renorm(w_up, full_in[:, hidden:])

time: 45.3 us -> 48.1 us (1.062)
  waiting for transfers between devices: 13.9 us -> 17.1 us
  matrix products: 15.6 us -> 13.6 us
  starting transfers between devices: 11.2 us -> 12.4 us
    ppermute x3, waiting for transfers between devices: 0.08 us -> 3.24 us  [local_ring(): lax.ppermute(arrived[1], axes, ccw_perm)]
    ppermute x2, waiting for transfers between devices: 0.01 us -> 3.06 us  [the longest x1 3.05 us: local_ring(): lax.ppermute(arrived[1][2 * half:], axes, ccw2_perm)]
    ppermute x3, waiting for transfers between devices: 11.4 us -> 9.04 us  [local_ring(): lax.ppermute(arrived[0], axes, cw_perm)]
    ppermute x3, starting transfers between devices: 0.41 us -> 1.95 us  [local_ring(): lax.ppermute(arrived[1], axes, ccw_perm)]
    ppermute x3, starting transfers between devices: 6.29 us -> 4.97 us  [local_ring(): lax.ppermute(arrived[0], axes, cw_perm)]
    dot_general x5 -> x4, matrix products: 3.08 us -> 1.88 us  [gradients(): gate_pre = jnp.dot(keys, w_gate, preferred_element_type=jnp.float32)]
    ppermute x2, starting transfers between devices: 2.32 us -> 3.03 us  [the longest x1 2.89 us: local_ring(): lax.ppermute(arrived[0][:2 * half], axes, cw2_perm)]
    ppermute x8, waiting for transfers between devices: 2.4 us -> 1.73 us  [local_ring(): from_sib = [lax.ppermute(chunk, axes, swap) for chunk in arrived]]
  transfers between devices with their start and end apart: 17 -> 17, of which waited for: 10 -> 9; matrix products, arithmetic and copies ran while one was open for 27% -> 17% of each run, Pallas kernels for 0% -> 0%
where the time goes in v11:
time: 48.1 us; the launch traced here: 47.9 us
  waiting for transfers between devices  17.1 us (36%)
  matrix products  13.6 us (28%)
  starting transfers between devices  12.4 us (26%)
  other arithmetic  3.64 us (8%)
  local copies, waits for them, and re-layouts  0.79 us (2%)
    ppermute x3, waiting for transfers between devices, local_ring(): lax.ppermute(arrived[0], axes, cw_perm)  9.04 us
    ppermute x3, starting transfers between devices, local_ring(): lax.ppermute(arrived[0], axes, cw_perm)  4.97 us
    ppermute x3, waiting for transfers between devices, local_ring(): lax.ppermute(arrived[1], axes, ccw_perm)  3.24 us
    ppermute x1, waiting for transfers between devices, local_ring(): lax.ppermute(arrived[1][2 * half:], axes, ccw2_perm)  3.05 us
    dot_general x4, matrix products, gradients(): lax.dot_general(scaled, w_out, contract_last, preferred_element_type=jnp....  3.05 us
    dot_general x4, matrix products, gradients(): lax.dot_general(keys, both_grads, contract_first, preferred_element_type=...  3.01 us
    ppermute x1, starting transfers between devices, local_ring(): lax.ppermute(arrived[0][:2 * half], axes, cw2_perm)  2.89 us
    dot_general x4, matrix products, gradients(): lax.dot_general(activation, scaled, contract_first, preferred_element_typ...  2.13 us
  transfers between devices with their start and end apart: 17, of which 9 were waited for; matrix products, arithmetic and copies ran while one was open for 17% of the time, Pallas kernels for 0%

profile of v11, /device:TPU:0, one launch (start us, length us, event | category | flops | bytes accessed | tf_op | source)
XLA Modules:
  0.0 47.9 jit_solution(14103955616789013157)
XLA Ops:
  0.0 1.1 %multiply_convert_fusion.19 = bf16[128,512]{1,0:T(8,128)(2,1)S(1)} fusion(bf16[128,512]{1,0:T(8,128)(2,1)} %param.8, f32[128]{0:T(128)} %param.10), kind=kLoop, calls=%fused_computation.68 | loop fusion | flops 196608 | bytes 262656 | tf_op jit(solution)/shard_map/convert_element_type | solution.py:141
  1.1 1.0 %pad_maximum_fusion = bf16[2,2,64,512]{3,2,1,0:T(8,128)(2,1)S(1)} fusion(bf16[2,1,64,512]{3,2,1,0:T(8,128)(2,1)S(1)} %bitcast.49, bf16[2,1,64,512]{3,2,1,0:T(8,128)(2,1)} %bitcast.50), kind=kLoop, calls=%fused_computation.60 | loop fusion | flops 131072 | bytes 524288 | tf_op jit(solution)/shard_map/stack | solution.py:143
  2.1 0.5 %collective-permute-start = (bf16[256,512]{1,0:T(8,128)(2,1)S(1)}, bf16[256,512]{1,0:T(8,128)(2,1)S(1)}, u32[]{:S(2)}, u32[]{:S(2)}) collective-permute-start(bf16[256,512]{1,0:T(8,128)(2,1)S(1)} %bitcast.45), channel_id=1, source_target_pairs={{0,1},{1,0},{2,3},{3,2},{4,5},{5,4},{6,7},{7,6},{8,9},{9,8},{10,11... | collective-permute-start | bytes 786440 | tf_op jit(solution)/shard_map/ppermute | solution.py:146
  2.6 2.6 %collective-permute-start.1 = (bf16[256,512]{1,0:T(8,128)(2,1)S(1)}, bf16[256,512]{1,0:T(8,128)(2,1)S(1)}, u32[]{:S(2)}, u32[]{:S(2)}) collective-permute-start(bf16[256,512]{1,0:T(8,128)(2,1)S(1)} %bitcast.46), channel_id=1, source_target_pairs={{0,4},{1,5},{4,8},{5,9},{8,12},{9,13},{12,14},{13,15},{14,10},{15,... | collective-permute-start | bytes 786440 | tf_op jit(solution)/shard_map/ppermute | solution.py:164
  7.3 4.8 %collective-permute-done.1 = bf16[256,512]{1,0:T(8,128)(2,1)S(1)} collective-permute-done((bf16[256,512]{1,0:T(8,128)(2,1)S(1)}, bf16[256,512]{1,0:T(8,128)(2,1)S(1)}, u32[]{:S(2)}, u32[]{:S(2)}) %collective-permute-start.1) | collective-permute-done | bytes 262176 | tf_op jit(solution)/shard_map/ppermute | solution.py:164
  12.1 1.8 %collective-permute-start.5 = (bf16[256,512]{1,0:T(8,128)(2,1)S(1)}, bf16[256,512]{1,0:T(8,128)(2,1)S(1)}, u32[]{:S(2)}, u32[]{:S(2)}) collective-permute-start(bf16[256,512]{1,0:T(8,128)(2,1)S(1)} %collective-permute-done.1), channel_id=1, source_target_pairs={{0,4},{1,5},{4,8},{5,9},{8,12},{9,13},{12,14},{13,15},{14,10},{15,... | collective-permute-start | bytes 786440 | tf_op jit(solution)/shard_map/ppermute | solution.py:164
  14.9 0.6 %collective-permute-done.4 = bf16[256,512]{1,0:T(8,128)(2,1)S(1)} collective-permute-done((bf16[256,512]{1,0:T(8,128)(2,1)S(1)}, bf16[256,512]{1,0:T(8,128)(2,1)S(1)}, u32[]{:S(2)}, u32[]{:S(2)}) %collective-permute-start.4) | collective-permute-done | bytes 262176 | tf_op jit(solution)/shard_map/ppermute | solution.py:169
  15.5 0.5 %fusion.52 = f32[512,512]{0,1:T(8,128)S(1)} fusion(bf16[512,512]{1,0:T(8,128)(2,1)S(1)} %get-tuple-element.72, bf16[512,512]{1,0:T(8,128)(2,1)S(1)} %copy-done.1), kind=kOutput, calls=%fused_computation.145 | convolution fusion | flops 268435456 | bytes 2097152 | tf_op jit(solution)/shard_map/dot_general | solution.py:30
  16.0 0.5 %fusion.53 = f32[512,512]{0,1:T(8,128)S(1)} fusion(bf16[512,512]{1,0:T(8,128)(2,1)S(1)} %get-tuple-element.72, bf16[512,512]{1,0:T(8,128)(2,1)S(1)} %copy-done.2), kind=kOutput, calls=%fused_computation.146 | convolution fusion | flops 268435456 | bytes 2097152 | tf_op jit(solution)/shard_map/dot_general | solution.py:29
  16.5 4.2 %collective-permute-done.5 = bf16[256,512]{1,0:T(8,128)(2,1)S(1)} collective-permute-done((bf16[256,512]{1,0:T(8,128)(2,1)S(1)}, bf16[256,512]{1,0:T(8,128)(2,1)S(1)}, u32[]{:S(2)}, u32[]{:S(2)}) %collective-permute-start.5) | collective-permute-done | bytes 262176 | tf_op jit(solution)/shard_map/ppermute | solution.py:164
  20.8 2.9 %collective-permute-start.11 = (bf16[128,512]{1,0:T(8,128)(2,1)S(1)}, bf16[128,512]{1,0:T(8,128)(2,1)S(1)}, u32[]{:S(2)}, u32[]{:S(2)}) collective-permute-start(bf16[128,512]{1,0:T(8,128)(2,1)S(1)} %slice.312), channel_id=1, source_target_pairs={{0,8},{1,9},{4,12},{5,13},{8,14},{9,15},{12,10},{13,11},{14,6},{15... | collective-permute-start | bytes 393224 | tf_op jit(solution)/shard_map/ppermute | solution.py:156
  23.7 0.8 %multiply_convert_fusion.11 = (bf16[512,512]{0,1:T(8,128)(2,1)S(1)}, bf16[512,512]{0,1:T(8,128)(2,1)S(1)}) fusion(f32[512,512]{0,1:T(8,128)S(1)} %fusion.53, f32[512,512]{0,1:T(8,128)S(1)} %fusion.52, bf16[512,512]{1,0:T(8,128)(2,1)S(1)} %get-tuple-element.71, bf16[512,512]{1,0:T(8,128)(2,1)S(1)} %copy-done.3), kind=kOutput, calls=%fused_computation.46 | convolution fusion | flops 271843328 | bytes 4194304 | tf_op jit(solution)/shard_map/dot_general | solution.py:31
  24.5 0.5 convolution_add_fusion.1
  25.2 0.5 %collective-permute-start.8 = (bf16[256,512]{1,0:T(8,128)(2,1)S(1)}, bf16[256,512]{1,0:T(8,128)(2,1)S(1)}, u32[]{:S(2)}, u32[]{:S(2)}) collective-permute-start(bf16[256,512]{1,0:T(8,128)(2,1)S(1)} %collective-permute-done.6), channel_id=1, source_target_pairs={{0,1},{1,0},{2,3},{3,2},{4,5},{5,4},{6,7},{7,6},{8,9},{9,8},{10,11... | collective-permute-start | bytes 786440 | tf_op jit(solution)/shard_map/ppermute | solution.py:169
  25.7 1.7 %collective-permute-start.10 = (bf16[256,512]{1,0:T(8,128)(2,1)S(1)}, bf16[256,512]{1,0:T(8,128)(2,1)S(1)}, u32[]{:S(2)}, u32[]{:S(2)}) collective-permute-start(bf16[256,512]{1,0:T(8,128)(2,1)S(1)} %collective-permute-done.6), channel_id=1, source_target_pairs={{0,2},{1,3},{4,0},{5,1},{8,4},{9,5},{12,8},{13,9},{14,12},{15,13},... | collective-permute-start | bytes 786440 | tf_op jit(solution)/shard_map/ppermute | solution.py:155
  27.5 0.8 %fusion.10 = f32[512,1024]{1,0:T(8,128)S(1)} fusion(bf16[512,512]{1,0:T(8,128)(2,1)S(1)} %get-tuple-element.72, bf16[512,512]{0,1:T(8,128)(2,1)S(1)} %get-tuple-element.36, bf16[512,512]{0,1:T(8,128)(2,1)S(1)} %get-tuple-element.35), kind=kOutput, calls=%fused_computation.26 | convolution fusion | flops 538968064 | bytes 3670016 | tf_op jit(solution)/shard_map/dot_general | solution.py:36
  28.3 0.5 %collective-permute-start.9 = (bf16[256,512]{1,0:T(8,128)(2,1)S(1)}, bf16[256,512]{1,0:T(8,128)(2,1)S(1)}, u32[]{:S(2)}, u32[]{:S(2)}) collective-permute-start(bf16[256,512]{1,0:T(8,128)(2,1)S(1)} %collective-permute-done.5), channel_id=1, source_target_pairs={{0,4},{1,5},{4,8},{5,9},{8,12},{9,13},{12,14},{13,15},{14,10},{15,... | collective-permute-start | bytes 786440 | tf_op jit(solution)/shard_map/ppermute | solution.py:154
  28.9 0.5 %fusion.54 = f32[512,512]{0,1:T(8,128)S(1)} fusion(bf16[512,512]{1,0:T(8,128)(2,1)S(1)} %get-tuple-element.56, bf16[512,512]{1,0:T(8,128)(2,1)S(1)} %copy-done.1), kind=kOutput, calls=%fused_computation.147 | convolution fusion | flops 268435456 | bytes 2097152 | tf_op jit(solution)/shard_map/dot_general | solution.py:30
  29.4 0.5 %fusion.55 = f32[512,512]{0,1:T(8,128)S(1)} fusion(bf16[512,512]{1,0:T(8,128)(2,1)S(1)} %get-tuple-element.56, bf16[512,512]{1,0:T(8,128)(2,1)S(1)} %copy-done.2), kind=kOutput, calls=%fused_computation.148 | convolution fusion | flops 268435456 | bytes 2097152 | tf_op jit(solution)/shard_map/dot_general | solution.py:29
  29.9 0.8 %multiply_convert_fusion.9 = (bf16[512,512]{0,1:T(8,128)(2,1)S(1)}, bf16[512,512]{0,1:T(8,128)(2,1)S(1)}) fusion(f32[512,512]{0,1:T(8,128)S(1)} %fusion.55, f32[512,512]{0,1:T(8,128)S(1)} %fusion.54, bf16[512,512]{1,0:T(8,128)(2,1)S(1)} %get-tuple-element.55, bf16[512,512]{1,0:T(8,128)(2,1)S(1)} %copy-done.3), kind=kOutput, calls=%fused_computation.42 | convolution fusion | flops 271843328 | bytes 4194304 | tf_op jit(solution)/shard_map/dot_general | solution.py:31
  30.7 0.8 %add_add_fusion = f32[512,1024]{1,0:T(8,128)S(1)} fusion(f32[512,1024]{1,0:T(8,128)S(1)} %fusion.20, f32[512,1024]{1,0:T(8,128)S(1)} %fusion.10, bf16[512,512]{1,0:T(8,128)(2,1)S(1)} %get-tuple-element.56, bf16[512,512]{0,1:T(8,128)(2,1)S(1)} %get-tuple-element.34, bf16[512,512]{0,1:T(8,128)(2,1)S(1)} %get-tuple-element.33), kind=kOutput, calls=%fused_computation | convolution fusion | flops 540016640 | bytes 7864320 | tf_op jit(solution)/shard_map/dot_general | solution.py:36
  31.9 3.1 %collective-permute-done.12 = bf16[128,512]{1,0:T(8,128)(2,1)S(1)} collective-permute-done((bf16[128,512]{1,0:T(8,128)(2,1)S(1)}, bf16[128,512]{1,0:T(8,128)(2,1)S(1)}, u32[]{:S(2)}, u32[]{:S(2)}) %collective-permute-start.12) | collective-permute-done | bytes 131104 | tf_op jit(solution)/shard_map/ppermute | solution.py:157
  35.0 3.2 %collective-permute-done.10 = bf16[256,512]{1,0:T(8,128)(2,1)S(1)} collective-permute-done((bf16[256,512]{1,0:T(8,128)(2,1)S(1)}, bf16[256,512]{1,0:T(8,128)(2,1)S(1)}, u32[]{:S(2)}, u32[]{:S(2)}) %collective-permute-start.10) | collective-permute-done | bytes 262176 | tf_op jit(solution)/shard_map/ppermute | solution.py:155
  38.3 0.5 %collective-permute-start.14 = (bf16[256,512]{1,0:T(8,128)(2,1)S(1)}, bf16[256,512]{1,0:T(8,128)(2,1)S(1)}, u32[]{:S(2)}, u32[]{:S(2)}) collective-permute-start(bf16[256,512]{1,0:T(8,128)(2,1)S(1)} %collective-permute-done.10), channel_id=1, source_target_pairs={{0,1},{1,0},{2,3},{3,2},{4,5},{5,4},{6,7},{7,6},{8,9},{9,8},{10,11... | collective-permute-start | bytes 786440 | tf_op jit(solution)/shard_map/ppermute | solution.py:169
  40.6 0.6 %fusion.56 = f32[768,512]{0,1:T(8,128)S(1)} fusion(bf16[768,512]{1,0:T(8,128)(2,1)S(1)} %get-tuple-element.96, bf16[512,512]{1,0:T(8,128)(2,1)S(1)} %copy-done.1), kind=kOutput, calls=%fused_computation.149 | convolution fusion | flops 402653184 | bytes 2883584 | tf_op jit(solution)/shard_map/dot_general | solution.py:30
  41.2 0.6 %fusion.57 = f32[768,512]{0,1:T(8,128)S(1)} fusion(bf16[768,512]{1,0:T(8,128)(2,1)S(1)} %get-tuple-element.96, bf16[512,512]{1,0:T(8,128)(2,1)S(1)} %copy-done.2), kind=kOutput, calls=%fused_computation.150 | convolution fusion | flops 402653184 | bytes 2883584 | tf_op jit(solution)/shard_map/dot_general | solution.py:29
  41.8 1.0 %multiply_convert_fusion.2 = (bf16[768,512]{0,1:T(8,128)(2,1)S(1)}, bf16[768,512]{0,1:T(8,128)(2,1)S(1)}) fusion(f32[768,512]{0,1:T(8,128)S(1)} %fusion.57, f32[768,512]{0,1:T(8,128)S(1)} %fusion.56, bf16[768,512]{1,0:T(8,128)(2,1)S(1)} %get-tuple-element.95, bf16[512,512]{1,0:T(8,128)(2,1)S(1)} %copy-done.3), kind=kOutput, calls=%fused_computation.7 | convolution fusion | flops 407764992 | bytes 6029312 | tf_op jit(solution)/shard_map/dot_general | solution.py:31
  42.8 0.8 %fusion.9 = (f32[512]{0:T(512)S(1)}, f32[512]{0:T(512)S(1)}, f32[512,512]{1,0:T(8,128)S(1)}) fusion(bf16[512,512]{1,0:T(8,128)(2,1)S(1)} %copy-done.3, f32[512,512]{1,0:T(8,128)S(1)} %convolution_add_fusion, bf16[768,512]{1,0:T(8,128)(2,1)S(1)} %get-tuple-element.95, f32[768,512]{0,1:T(8,128)S(1)} %fusion.56, f32[768,512]{0,1:T(8,128)S(1)} %fusion.57), kind=kOutput, calls=%fused_computation.25 | convolution fusion | flops 406846464 | bytes 6557696 | tf_op jit(solution)/shard_map/dot_general | solution.py:37
  43.7 1.0 %fusion = f32[512,1024]{1,0:T(8,128)S(1)} fusion(bf16[768,512]{1,0:T(8,128)(2,1)S(1)} %get-tuple-element.96, bf16[768,512]{0,1:T(8,128)(2,1)S(1)} %get-tuple-element.30, bf16[768,512]{0,1:T(8,128)(2,1)S(1)} %get-tuple-element.29), kind=kOutput, calls=%fused_computation.1 | convolution fusion | flops 808452096 | bytes 4456448 | tf_op jit(solution)/shard_map/dot_general | solution.py:36
  44.7 0.6 %add.126 = f32[512,1024]{1,0:T(8,128)S(1)} add(f32[512,1024]{1,0:T(8,128)S(1)} %add_add_fusion, f32[512,1024]{1,0:T(8,128)S(1)} %fusion) | non-fusion elementwise | flops 524288 | bytes 6291456 | tf_op jit(solution)/shard_map/add | solution.py:108
  45.3 0.5 %multiply_reduce_fusion.1 = (f32[512]{0:T(512)S(1)}, f32[512]{0:T(512)S(1)}, f32[512]{0:T(512)S(1)}, f32[512]{0:T(512)S(1)}) fusion(f32[512,1024]{1,0:T(8,128)S(1)} %add.126, bf16[512,512]{1,0:T(8,128)(2,1)S(1)} %copy-done.1, bf16[512,512]{1,0:T(8,128)(2,1)S(1)} %copy-done.2), kind=kLoop, calls=%fused_computation.36 | loop fusion | flops 3143680 | bytes 3153920 | tf_op jit(solution)/shard_map/reduce_sum | solution.py:19
  46.7 1.3 %convolution_convert_fusion = bf16[128,512]{1,0:T(8,128)(2,1)} fusion(bf16[512,512]{1,0:T(8,128)(2,1)S(1)} %multiply_convert_fusion.3, bf16[512,512]{1,0:T(8,128)(2,1)S(1)} %get-tuple-element.21, bf16[128,512]{1,0:T(8,128)(2,1)S(1)} %copy-done, f32[128,512]{0,1:T(8,128)S(1)} %convolution_bitcast_fusion.1), kind=kOutput, calls=%fused_computation.22 | convolution fusion | flops 134676480 | bytes 1572864 | tf_op jit(solution)/shard_map/dot_general | solution.py:45
  (72 shorter events, 6.4 us)
Async XLA Ops:
  0.0 46.3 %copy-start = (bf16[128,512]{1,0:T(8,128)(2,1)S(1)}, bf16[128,512]{1,0:T(8,128)(2,1)}, u32[]{:S(2)}) copy-start(bf16[128,512]{1,0:T(8,128)(2,1)} %param.9) | copy-start | bytes 393220
  0.0 5.3 %copy-start.1 = (bf16[512,512]{1,0:T(8,128)(2,1)S(1)}, bf16[512,512]{1,0:T(8,128)(2,1)}, u32[]{:S(2)}) copy-start(bf16[512,512]{1,0:T(8,128)(2,1)} %param.12) | copy-start | bytes 1572868
  1.1 4.6 %copy-start.2 = (bf16[512,512]{1,0:T(8,128)(2,1)S(1)}, bf16[512,512]{1,0:T(8,128)(2,1)}, u32[]{:S(2)}) copy-start(bf16[512,512]{1,0:T(8,128)(2,1)} %param.11) | copy-start | bytes 1572868
  2.1 3.2 %collective-permute-start = (bf16[256,512]{1,0:T(8,128)(2,1)S(1)}, bf16[256,512]{1,0:T(8,128)(2,1)S(1)}, u32[]{:S(2)}, u32[]{:S(2)}) collective-permute-start(bf16[256,512]{1,0:T(8,128)(2,1)S(1)} %bitcast.45), channel_id=1, source_target_pairs={{0,1},{1,0},{2,3},{3,2},{4,5},{5,4},{6,7},{7,6},{8,9},{9,8},{10,11... | collective-permute-start | bytes 786440 | tf_op jit(solution)/shard_map/ppermute | solution.py:146
  2.6 9.5 %collective-permute-start.1 = (bf16[256,512]{1,0:T(8,128)(2,1)S(1)}, bf16[256,512]{1,0:T(8,128)(2,1)S(1)}, u32[]{:S(2)}, u32[]{:S(2)}) collective-permute-start(bf16[256,512]{1,0:T(8,128)(2,1)S(1)} %bitcast.46), channel_id=1, source_target_pairs={{0,4},{1,5},{4,8},{5,9},{8,12},{9,13},{12,14},{13,15},{14,10},{15,... | collective-permute-start | bytes 786440 | tf_op jit(solution)/shard_map/ppermute | solution.py:164
  5.2 8.7 %collective-permute-start.2 = (bf16[256,512]{1,0:T(8,128)(2,1)S(1)}, bf16[256,512]{1,0:T(8,128)(2,1)S(1)}, u32[]{:S(2)}, u32[]{:S(2)}) collective-permute-start(bf16[256,512]{1,0:T(8,128)(2,1)S(1)} %bitcast.47), channel_id=1, source_target_pairs={{0,2},{1,3},{4,0},{5,1},{8,4},{9,5},{12,8},{13,9},{14,12},{15,13},... | collective-permute-start | bytes 786440 | tf_op jit(solution)/shard_map/ppermute | solution.py:165
  5.3 1.0 %copy-start.3 = (bf16[512,512]{1,0:T(8,128)(2,1)S(1)}, bf16[512,512]{1,0:T(8,128)(2,1)}, u32[]{:S(2)}) copy-start(bf16[512,512]{1,0:T(8,128)(2,1)} %param.13) | copy-start | bytes 1572868
  12.1 2.8 %collective-permute-start.3 = (bf16[256,512]{1,0:T(8,128)(2,1)S(1)}, bf16[256,512]{1,0:T(8,128)(2,1)S(1)}, u32[]{:S(2)}, u32[]{:S(2)}) collective-permute-start(bf16[256,512]{1,0:T(8,128)(2,1)S(1)} %collective-permute-done.1), channel_id=1, source_target_pairs={{0,1},{1,0},{2,3},{3,2},{4,5},{5,4},{6,7},{7,6},{8,9},{9,8},{10,11... | collective-permute-start | bytes 786440 | tf_op jit(solution)/shard_map/ppermute | solution.py:169
  12.1 8.7 %collective-permute-start.5 = (bf16[256,512]{1,0:T(8,128)(2,1)S(1)}, bf16[256,512]{1,0:T(8,128)(2,1)S(1)}, u32[]{:S(2)}, u32[]{:S(2)}) collective-permute-start(bf16[256,512]{1,0:T(8,128)(2,1)S(1)} %collective-permute-done.1), channel_id=1, source_target_pairs={{0,4},{1,5},{4,8},{5,9},{8,12},{9,13},{12,14},{13,15},{14,10},{15,... | collective-permute-start | bytes 786440 | tf_op jit(solution)/shard_map/ppermute | solution.py:164
  13.9 1.6 %collective-permute-start.4 = (bf16[256,512]{1,0:T(8,128)(2,1)S(1)}, bf16[256,512]{1,0:T(8,128)(2,1)S(1)}, u32[]{:S(2)}, u32[]{:S(2)}) collective-permute-start(bf16[256,512]{1,0:T(8,128)(2,1)S(1)} %collective-permute-done.2), channel_id=1, source_target_pairs={{0,1},{1,0},{2,3},{3,2},{4,5},{5,4},{6,7},{7,6},{8,9},{9,8},{10,11... | collective-permute-start | bytes 786440 | tf_op jit(solution)/shard_map/ppermute | solution.py:169
  14.2 10.8 %collective-permute-start.6 = (bf16[256,512]{1,0:T(8,128)(2,1)S(1)}, bf16[256,512]{1,0:T(8,128)(2,1)S(1)}, u32[]{:S(2)}, u32[]{:S(2)}) collective-permute-start(bf16[256,512]{1,0:T(8,128)(2,1)S(1)} %collective-permute-done.2), channel_id=1, source_target_pairs={{0,2},{1,3},{4,0},{5,1},{8,4},{9,5},{12,8},{13,9},{14,12},{15,13},... | collective-permute-start | bytes 786440 | tf_op jit(solution)/shard_map/ppermute | solution.py:165
  20.8 11.1 %collective-permute-start.11 = (bf16[128,512]{1,0:T(8,128)(2,1)S(1)}, bf16[128,512]{1,0:T(8,128)(2,1)S(1)}, u32[]{:S(2)}, u32[]{:S(2)}) collective-permute-start(bf16[128,512]{1,0:T(8,128)(2,1)S(1)} %slice.312), channel_id=1, source_target_pairs={{0,8},{1,9},{4,12},{5,13},{8,14},{9,15},{12,10},{13,11},{14,6},{15... | collective-permute-start | bytes 393224 | tf_op jit(solution)/shard_map/ppermute | solution.py:156
  25.0 10.0 %collective-permute-start.12 = (bf16[128,512]{1,0:T(8,128)(2,1)S(1)}, bf16[128,512]{1,0:T(8,128)(2,1)S(1)}, u32[]{:S(2)}, u32[]{:S(2)}) collective-permute-start(bf16[128,512]{1,0:T(8,128)(2,1)S(1)} %slice.313), channel_id=1, source_target_pairs={{0,6},{1,7},{4,2},{5,3},{8,0},{9,1},{12,4},{13,5},{14,8},{15,9},{1... | collective-permute-start | bytes 393224 | tf_op jit(solution)/shard_map/ppermute | solution.py:157
  25.1 3.1 %collective-permute-start.7 = (bf16[256,512]{1,0:T(8,128)(2,1)S(1)}, bf16[256,512]{1,0:T(8,128)(2,1)S(1)}, u32[]{:S(2)}, u32[]{:S(2)}) collective-permute-start(bf16[256,512]{1,0:T(8,128)(2,1)S(1)} %collective-permute-done.5), channel_id=1, source_target_pairs={{0,1},{1,0},{2,3},{3,2},{4,5},{5,4},{6,7},{7,6},{8,9},{9,8},{10,11... | collective-permute-start | bytes 786440 | tf_op jit(solution)/shard_map/ppermute | solution.py:169
  25.2 3.6 %collective-permute-start.8 = (bf16[256,512]{1,0:T(8,128)(2,1)S(1)}, bf16[256,512]{1,0:T(8,128)(2,1)S(1)}, u32[]{:S(2)}, u32[]{:S(2)}) collective-permute-start(bf16[256,512]{1,0:T(8,128)(2,1)S(1)} %collective-permute-done.6), channel_id=1, source_target_pairs={{0,1},{1,0},{2,3},{3,2},{4,5},{5,4},{6,7},{7,6},{8,9},{9,8},{10,11... | collective-permute-start | bytes 786440 | tf_op jit(solution)/shard_map/ppermute | solution.py:169
  25.7 12.5 %collective-permute-start.10 = (bf16[256,512]{1,0:T(8,128)(2,1)S(1)}, bf16[256,512]{1,0:T(8,128)(2,1)S(1)}, u32[]{:S(2)}, u32[]{:S(2)}) collective-permute-start(bf16[256,512]{1,0:T(8,128)(2,1)S(1)} %collective-permute-done.6), channel_id=1, source_target_pairs={{0,2},{1,3},{4,0},{5,1},{8,4},{9,5},{12,8},{13,9},{14,12},{15,13},... | collective-permute-start | bytes 786440 | tf_op jit(solution)/shard_map/ppermute | solution.py:155
  28.3 9.9 %collective-permute-start.9 = (bf16[256,512]{1,0:T(8,128)(2,1)S(1)}, bf16[256,512]{1,0:T(8,128)(2,1)S(1)}, u32[]{:S(2)}, u32[]{:S(2)}) collective-permute-start(bf16[256,512]{1,0:T(8,128)(2,1)S(1)} %collective-permute-done.5), channel_id=1, source_target_pairs={{0,4},{1,5},{4,8},{5,9},{8,12},{9,13},{12,14},{13,15},{14,10},{15,... | collective-permute-start | bytes 786440 | tf_op jit(solution)/shard_map/ppermute | solution.py:154
  38.2 1.6 %collective-permute-start.13 = (bf16[256,512]{1,0:T(8,128)(2,1)S(1)}, bf16[256,512]{1,0:T(8,128)(2,1)S(1)}, u32[]{:S(2)}, u32[]{:S(2)}) collective-permute-start(bf16[256,512]{1,0:T(8,128)(2,1)S(1)} %collective-permute-done.9), channel_id=1, source_target_pairs={{0,1},{1,0},{2,3},{3,2},{4,5},{5,4},{6,7},{7,6},{8,9},{9,8},{10,11... | collective-permute-start | bytes 786440 | tf_op jit(solution)/shard_map/ppermute | solution.py:169
  38.3 1.9 %collective-permute-start.14 = (bf16[256,512]{1,0:T(8,128)(2,1)S(1)}, bf16[256,512]{1,0:T(8,128)(2,1)S(1)}, u32[]{:S(2)}, u32[]{:S(2)}) collective-permute-start(bf16[256,512]{1,0:T(8,128)(2,1)S(1)} %collective-permute-done.10), channel_id=1, source_target_pairs={{0,1},{1,0},{2,3},{3,2},{4,5},{5,4},{6,7},{7,6},{8,9},{9,8},{10,11... | collective-permute-start | bytes 786440 | tf_op jit(solution)/shard_map/ppermute | solution.py:169
  38.8 1.6 %collective-permute-start.15 = (bf16[128,512]{1,0:T(8,128)(2,1)S(1)}, bf16[128,512]{1,0:T(8,128)(2,1)S(1)}, u32[]{:S(2)}, u32[]{:S(2)}) collective-permute-start(bf16[128,512]{1,0:T(8,128)(2,1)S(1)} %collective-permute-done.11), channel_id=1, source_target_pairs={{0,1},{1,0},{2,3},{3,2},{4,5},{5,4},{6,7},{7,6},{8,9},{9,8},{10,11... | collective-permute-start | bytes 393224 | tf_op jit(solution)/shard_map/ppermute | solution.py:169
  38.9 1.7 %collective-permute-start.16 = (bf16[128,512]{1,0:T(8,128)(2,1)S(1)}, bf16[128,512]{1,0:T(8,128)(2,1)S(1)}, u32[]{:S(2)}, u32[]{:S(2)}) collective-permute-start(bf16[128,512]{1,0:T(8,128)(2,1)S(1)} %collective-permute-done.12), channel_id=1, source_target_pairs={{0,1},{1,0},{2,3},{3,2},{4,5},{5,4},{6,7},{7,6},{8,9},{9,8},{10,11... | collective-permute-start | bytes 393224 | tf_op jit(solution)/shard_map/ppermute | solution.py:169

commit v12 on v6

--- a/solution.py
+++ b/solution.py
@@ -156,7 +156,11 @@
             if step == steps:
                 total, arrived = lax.optimization_barrier((total, arrived))
             from_sib = [lax.ppermute(chunk, axes, swap) for chunk in arrived]
-            total = add_grads(total, *split(arrived + from_sib, half), w_gate, w_up, w_out)
+            if step == steps:
+                total = add_grads(total, *split(arrived, half), w_gate, w_up, w_out)
+                total = add_grads(total, *split(from_sib, half), w_gate, w_up, w_out)
+            else:
+                total = add_grads(total, *split(arrived + from_sib, half), w_gate, w_up, w_out)
         full_in, full_out = total
         new_gate = renorm(w_gate, full_in[:, :hidden])
         new_up = renorm(w_up, full_in[:, hidden:])

time: 45.3 us -> 44.3 us (0.978)
  waiting for transfers between devices: 13.9 us -> 12 us
  other arithmetic: 3.59 us -> 4.29 us
    reduce_sum x0 -> x1, other arithmetic: none -> 1.22 us  [renorm(): jnp.mean(old * old, axis=1, keepdims=True) + epsilon]
    ppermute x3, waiting for transfers between devices: 11.4 us -> 10.3 us  [local_ring(): lax.ppermute(arrived[0], axes, cw_perm)]
    ppermute x8, waiting for transfers between devices: 2.4 us -> 1.42 us  [local_ring(): from_sib = [lax.ppermute(chunk, axes, swap) for chunk in arrived]]
    dot_general x5 -> x6, matrix products: 3.08 us -> 2.31 us  [gradients(): gate_pre = jnp.dot(keys, w_gate, preferred_element_type=jnp.float32)]
    add x1 -> x0, other arithmetic: 0.55 us -> none  [add_grads(): return (total[0] + full_in, total[1] + full_out)]
    ppermute x1, starting transfers between devices: 0.52 us -> 0.01 us  [local_ring(): sib = lax.ppermute(own, axes, swap)]
    dot_general x5 -> x6, matrix products: 3.22 us -> 3.67 us  [gradients(): lax.dot_general(keys, both_grads, contract_first, preferred_element_type=...]
    dot_general x5 -> x6, matrix products: 2.29 us -> 2.64 us  [gradients(): lax.dot_general(activation, scaled, contract_first, preferred_element_typ...]
  transfers between devices with their start and end apart: 17 -> 17, of which waited for: 10 -> 9; matrix products, arithmetic and copies ran while one was open for 27% -> 32% of each run, Pallas kernels for 0% -> 0%
where the time goes in v12:
time: 44.3 us; the launch traced here: 44.1 us
  matrix products  15.6 us (35%)
  waiting for transfers between devices  12 us (27%)
  starting transfers between devices  11.2 us (25%)
  other arithmetic  4.29 us (10%)
  between operations  0.5 us (1%)
  local copies, waits for them, and re-layouts  0.45 us (1%)
    ppermute x3, waiting for transfers between devices, local_ring(): lax.ppermute(arrived[0], axes, cw_perm)  10.3 us
    ppermute x3, starting transfers between devices, local_ring(): lax.ppermute(arrived[0], axes, cw_perm)  6.73 us
    dot_general x6, matrix products, gradients(): lax.dot_general(keys, both_grads, contract_first, preferred_element_type=...  3.67 us
    dot_general x6, matrix products, gradients(): lax.dot_general(scaled, w_out, contract_last, preferred_element_type=jnp....  3.51 us
    dot_general x6, matrix products, gradients(): lax.dot_general(activation, scaled, contract_first, preferred_element_typ...  2.64 us
    dot_general x6, matrix products, gradients(): gate_pre = jnp.dot(keys, w_gate, preferred_element_type=jnp.float32)  2.31 us
    dot_general x6, matrix products, gradients(): up_pre = jnp.dot(keys, w_up, preferred_element_type=jnp.float32)  2.19 us
    ppermute x1, starting transfers between devices, local_ring(): lax.ppermute(arrived[0][:2 * half], axes, cw_perm)  1.88 us
  transfers between devices with their start and end apart: 17, of which 9 were waited for; matrix products, arithmetic and copies ran while one was open for 32% of the time, Pallas kernels for 0%

profile of v12, /device:TPU:0, one launch (start us, length us, event | category | flops | bytes accessed | tf_op | source)
XLA Modules:
  0.0 44.1 jit_solution(13135549636914949959)
XLA Ops:
  0.0 1.1 %multiply_convert_fusion.25 = bf16[128,512]{1,0:T(8,128)(2,1)S(1)} fusion(bf16[128,512]{1,0:T(8,128)(2,1)} %param.8, f32[128]{0:T(128)} %param.10), kind=kLoop, calls=%fused_computation.87 | loop fusion | flops 196608 | bytes 262656 | tf_op jit(solution)/shard_map/convert_element_type | solution.py:137
  1.1 0.9 %pad_maximum_fusion = bf16[2,2,64,512]{3,2,1,0:T(8,128)(2,1)S(1)} fusion(bf16[2,1,64,512]{3,2,1,0:T(8,128)(2,1)S(1)} %bitcast.55, bf16[2,1,64,512]{3,2,1,0:T(8,128)(2,1)} %bitcast.56), kind=kLoop, calls=%fused_computation.61 | loop fusion | flops 131072 | bytes 524288 | tf_op jit(solution)/shard_map/stack | solution.py:139
  2.0 3.1 %collective-permute-start.1 = (bf16[256,512]{1,0:T(8,128)(2,1)S(1)}, bf16[256,512]{1,0:T(8,128)(2,1)S(1)}, u32[]{:S(2)}, u32[]{:S(2)}) collective-permute-start(bf16[256,512]{1,0:T(8,128)(2,1)S(1)} %bitcast.51), channel_id=1, source_target_pairs={{0,4},{1,5},{4,8},{5,9},{8,12},{9,13},{12,14},{13,15},{14,10},{15,... | collective-permute-start | bytes 786440 | tf_op jit(solution)/shard_map/ppermute | solution.py:153
  5.1 1.2 %fusion.4 = f32[512]{0:T(512)S(1)} fusion(bf16[512,512]{1,0:T(8,128)(2,1)} %param.13), kind=kLoop, calls=%fused_computation.18 | loop fusion | flops 785920 | bytes 526336 | tf_op jit(solution)/shard_map/reduce_sum | solution.py:18
  7.4 0.5 %multiply_convert_fusion.17 = (bf16[256,512]{1,0:T(8,128)(2,1)S(1)}, bf16[256,512]{1,0:T(8,128)(2,1)S(1)}) fusion(f32[256,512]{1,0:T(8,128)S(1)} %fusion.81, f32[256,512]{1,0:T(8,128)S(1)} %fusion.82, bf16[512,512]{1,0:T(8,128)(2,1)S(1)} %copy-done.3, bf16[64,512]{1,0:T(8,128)(2,1)S(1)} %get-tuple-element.74, bf16[64,512]{1,0:T(8,128)(2,1)S(1)} %get-tuple-element.75, ...), kind=kOutput, calls=%fused_computation.57 | convolution fusion | flops 136970240 | bytes 2359296 | tf_op jit(solution)/shard_map/dot_general | solution.py:31
  8.3 3.0 %collective-permute-done.1 = bf16[256,512]{1,0:T(8,128)(2,1)S(1)} collective-permute-done((bf16[256,512]{1,0:T(8,128)(2,1)S(1)}, bf16[256,512]{1,0:T(8,128)(2,1)S(1)}, u32[]{:S(2)}, u32[]{:S(2)}) %collective-permute-start.1) | collective-permute-done | bytes 262176 | tf_op jit(solution)/shard_map/ppermute | solution.py:153
  11.3 1.8 %collective-permute-start.5 = (bf16[256,512]{1,0:T(8,128)(2,1)S(1)}, bf16[256,512]{1,0:T(8,128)(2,1)S(1)}, u32[]{:S(2)}, u32[]{:S(2)}) collective-permute-start(bf16[256,512]{1,0:T(8,128)(2,1)S(1)} %collective-permute-done.1), channel_id=1, source_target_pairs={{0,4},{1,5},{4,8},{5,9},{8,12},{9,13},{12,14},{13,15},{14,10},{15,... | collective-permute-start | bytes 786440 | tf_op jit(solution)/shard_map/ppermute | solution.py:153
  14.2 0.6 %collective-permute-done.4 = bf16[256,512]{1,0:T(8,128)(2,1)S(1)} collective-permute-done((bf16[256,512]{1,0:T(8,128)(2,1)S(1)}, bf16[256,512]{1,0:T(8,128)(2,1)S(1)}, u32[]{:S(2)}, u32[]{:S(2)}) %collective-permute-start.4) | collective-permute-done | bytes 262176 | tf_op jit(solution)/shard_map/ppermute | solution.py:158
  14.8 0.5 %fusion.89 = f32[512,512]{0,1:T(8,128)S(1)} fusion(bf16[512,512]{1,0:T(8,128)(2,1)S(1)} %get-tuple-element.54, bf16[512,512]{1,0:T(8,128)(2,1)S(1)} %copy-done.1), kind=kOutput, calls=%fused_computation.184 | convolution fusion | flops 268435456 | bytes 2097152 | tf_op jit(solution)/shard_map/dot_general | solution.py:30
  15.3 0.5 %fusion.90 = f32[512,512]{0,1:T(8,128)S(1)} fusion(bf16[512,512]{1,0:T(8,128)(2,1)S(1)} %get-tuple-element.54, bf16[512,512]{1,0:T(8,128)(2,1)S(1)} %copy-done.2), kind=kOutput, calls=%fused_computation.185 | convolution fusion | flops 268435456 | bytes 2097152 | tf_op jit(solution)/shard_map/dot_general | solution.py:29
  15.8 0.8 %multiply_convert_fusion.11 = (bf16[512,512]{0,1:T(8,128)(2,1)S(1)}, bf16[512,512]{0,1:T(8,128)(2,1)S(1)}) fusion(f32[512,512]{0,1:T(8,128)S(1)} %fusion.90, f32[512,512]{0,1:T(8,128)S(1)} %fusion.89, bf16[512,512]{1,0:T(8,128)(2,1)S(1)} %get-tuple-element.53, bf16[512,512]{1,0:T(8,128)(2,1)S(1)} %copy-done.3), kind=kOutput, calls=%fused_computation.48 | convolution fusion | flops 271843328 | bytes 4194304 | tf_op jit(solution)/shard_map/dot_general | solution.py:31
  16.6 0.5 %convolution_add_fusion.2 = f32[512,512]{1,0:T(8,128)S(1)} fusion(f32[512,512]{1,0:T(8,128)S(1)} %fusion.24, bf16[512,512]{1,0:T(8,128)(2,1)S(1)} %get-tuple-element.53, f32[512,512]{0,1:T(8,128)S(1)} %fusion.89, f32[512,512]{0,1:T(8,128)S(1)} %fusion.90), kind=kOutput, calls=%fused_computation.4 | convolution fusion | flops 270270464 | bytes 4718592 | tf_op jit(solution)/shard_map/dot_general | solution.py:37
  17.1 3.0 %collective-permute-done.5 = bf16[256,512]{1,0:T(8,128)(2,1)S(1)} collective-permute-done((bf16[256,512]{1,0:T(8,128)(2,1)S(1)}, bf16[256,512]{1,0:T(8,128)(2,1)S(1)}, u32[]{:S(2)}, u32[]{:S(2)}) %collective-permute-start.5) | collective-permute-done | bytes 262176 | tf_op jit(solution)/shard_map/ppermute | solution.py:153
  20.1 1.8 %collective-permute-start.9 = (bf16[256,512]{1,0:T(8,128)(2,1)S(1)}, bf16[256,512]{1,0:T(8,128)(2,1)S(1)}, u32[]{:S(2)}, u32[]{:S(2)}) collective-permute-start(bf16[256,512]{1,0:T(8,128)(2,1)S(1)} %collective-permute-done.5), channel_id=1, source_target_pairs={{0,4},{1,5},{4,8},{5,9},{8,12},{9,13},{12,14},{13,15},{14,10},{15,... | collective-permute-start | bytes 786440 | tf_op jit(solution)/shard_map/ppermute | solution.py:153
  22.5 0.8 %fusion.5 = f32[512,1024]{1,0:T(8,128)S(1)} fusion(bf16[512,512]{1,0:T(8,128)(2,1)S(1)} %get-tuple-element.54, bf16[512,512]{0,1:T(8,128)(2,1)S(1)} %get-tuple-element.28, bf16[512,512]{0,1:T(8,128)(2,1)S(1)} %get-tuple-element.27), kind=kOutput, calls=%fused_computation.19 | convolution fusion | flops 538968064 | bytes 3670016 | tf_op jit(solution)/shard_map/dot_general | solution.py:36
  23.5 0.5 %fusion.91 = f32[512,512]{0,1:T(8,128)S(1)} fusion(bf16[512,512]{1,0:T(8,128)(2,1)S(1)} %get-tuple-element.78, bf16[512,512]{1,0:T(8,128)(2,1)S(1)} %copy-done.1), kind=kOutput, calls=%fused_computation.186 | convolution fusion | flops 268435456 | bytes 2097152 | tf_op jit(solution)/shard_map/dot_general | solution.py:30
  24.0 0.5 %fusion.92 = f32[512,512]{0,1:T(8,128)S(1)} fusion(bf16[512,512]{1,0:T(8,128)(2,1)S(1)} %get-tuple-element.78, bf16[512,512]{1,0:T(8,128)(2,1)S(1)} %copy-done.2), kind=kOutput, calls=%fused_computation.187 | convolution fusion | flops 268435456 | bytes 2097152 | tf_op jit(solution)/shard_map/dot_general | solution.py:29
  24.5 4.3 %collective-permute-done.9 = bf16[256,512]{1,0:T(8,128)(2,1)S(1)} collective-permute-done((bf16[256,512]{1,0:T(8,128)(2,1)S(1)}, bf16[256,512]{1,0:T(8,128)(2,1)S(1)}, u32[]{:S(2)}, u32[]{:S(2)}) %collective-permute-start.9) | collective-permute-done | bytes 262176 | tf_op jit(solution)/shard_map/ppermute | solution.py:153
  28.8 1.9 %collective-permute-start.13 = (bf16[128,512]{1,0:T(8,128)(2,1)S(1)}, bf16[128,512]{1,0:T(8,128)(2,1)S(1)}, u32[]{:S(2)}, u32[]{:S(2)}) collective-permute-start(bf16[128,512]{1,0:T(8,128)(2,1)S(1)} %slice.328), channel_id=1, source_target_pairs={{0,4},{1,5},{4,8},{5,9},{8,12},{9,13},{12,14},{13,15},{14,10},{15,... | collective-permute-start | bytes 393224 | tf_op jit(solution)/shard_map/ppermute | solution.py:148
  30.7 0.8 %multiply_convert_fusion.9 = (bf16[512,512]{0,1:T(8,128)(2,1)S(1)}, bf16[512,512]{0,1:T(8,128)(2,1)S(1)}) fusion(f32[512,512]{0,1:T(8,128)S(1)} %fusion.92, f32[512,512]{0,1:T(8,128)S(1)} %fusion.91, bf16[512,512]{1,0:T(8,128)(2,1)S(1)} %get-tuple-element.77, bf16[512,512]{1,0:T(8,128)(2,1)S(1)} %copy-done.3), kind=kOutput, calls=%fused_computation.44 | convolution fusion | flops 271843328 | bytes 4194304 | tf_op jit(solution)/shard_map/dot_general | solution.py:31
  31.5 0.5 %convolution_add_fusion.1 = f32[512,512]{1,0:T(8,128)S(1)} fusion(f32[512,512]{1,0:T(8,128)S(1)} %convolution_add_fusion.2, bf16[512,512]{1,0:T(8,128)(2,1)S(1)} %get-tuple-element.77, f32[512,512]{0,1:T(8,128)S(1)} %fusion.91, f32[512,512]{0,1:T(8,128)S(1)} %fusion.92), kind=kOutput, calls=%fused_computation.3 | convolution fusion | flops 270270464 | bytes 4718592 | tf_op jit(solution)/shard_map/dot_general | solution.py:37
  32.5 0.5 %collective-permute-start.12 = (bf16[256,512]{1,0:T(8,128)(2,1)S(1)}, bf16[256,512]{1,0:T(8,128)(2,1)S(1)}, u32[]{:S(2)}, u32[]{:S(2)}) collective-permute-start(bf16[256,512]{1,0:T(8,128)(2,1)S(1)} %collective-permute-done.10), channel_id=1, source_target_pairs={{0,1},{1,0},{2,3},{3,2},{4,5},{5,4},{6,7},{7,6},{8,9},{9,8},{10,11... | collective-permute-start | bytes 786440 | tf_op jit(solution)/shard_map/ppermute | solution.py:158
  33.0 0.8 %fusion.9 = f32[512,1024]{1,0:T(8,128)S(1)} fusion(bf16[512,512]{1,0:T(8,128)(2,1)S(1)} %get-tuple-element.78, bf16[512,512]{0,1:T(8,128)(2,1)S(1)} %get-tuple-element.30, bf16[512,512]{0,1:T(8,128)(2,1)S(1)} %get-tuple-element.29), kind=kOutput, calls=%fused_computation.23 | convolution fusion | flops 538968064 | bytes 3670016 | tf_op jit(solution)/shard_map/dot_general | solution.py:36
  34.4 0.5 %fusion.93 = f32[512,512]{0,1:T(8,128)S(1)} fusion(bf16[512,512]{1,0:T(8,128)(2,1)S(1)} %get-tuple-element.38, bf16[512,512]{1,0:T(8,128)(2,1)S(1)} %copy-done.1), kind=kOutput, calls=%fused_computation.188 | convolution fusion | flops 268435456 | bytes 2097152 | tf_op jit(solution)/shard_map/dot_general | solution.py:30
  34.9 0.5 %fusion.94 = f32[512,512]{0,1:T(8,128)S(1)} fusion(bf16[512,512]{1,0:T(8,128)(2,1)S(1)} %get-tuple-element.38, bf16[512,512]{1,0:T(8,128)(2,1)S(1)} %copy-done.2), kind=kOutput, calls=%fused_computation.189 | convolution fusion | flops 268435456 | bytes 2097152 | tf_op jit(solution)/shard_map/dot_general | solution.py:29
  35.4 0.8 %multiply_convert_fusion.7 = (bf16[512,512]{0,1:T(8,128)(2,1)S(1)}, bf16[512,512]{0,1:T(8,128)(2,1)S(1)}) fusion(f32[512,512]{0,1:T(8,128)S(1)} %fusion.94, f32[512,512]{0,1:T(8,128)S(1)} %fusion.93, bf16[512,512]{1,0:T(8,128)(2,1)S(1)} %get-tuple-element.37, bf16[512,512]{1,0:T(8,128)(2,1)S(1)} %copy-done.3), kind=kOutput, calls=%fused_computation.40 | convolution fusion | flops 271843328 | bytes 4194304 | tf_op jit(solution)/shard_map/dot_general | solution.py:31
  36.2 0.8 %add_add_fusion.1 = f32[512,1024]{1,0:T(8,128)S(1)} fusion(f32[512,1024]{1,0:T(8,128)S(1)} %fusion.9, f32[512,1024]{1,0:T(8,128)S(1)} %fusion.19, f32[512,1024]{1,0:T(8,128)S(1)} %fusion.5, bf16[512,512]{1,0:T(8,128)(2,1)S(1)} %get-tuple-element.38, bf16[512,512]{0,1:T(8,128)(2,1)S(1)} %get-tuple-element.26, bf16[512,512]{0,1:T(8,128)(2,1)S(1)} %get-tuple-element.25), kind=kOutput, calls=%fused_computation.1 | convolution fusion | flops 540540928 | bytes 9961472 | tf_op jit(solution)/shard_map/dot_general | solution.py:36
  37.0 0.5 %convolution_add_fusion = f32[512,512]{1,0:T(8,128)S(1)} fusion(f32[512,512]{1,0:T(8,128)S(1)} %convolution_add_fusion.1, bf16[512,512]{1,0:T(8,128)(2,1)S(1)} %get-tuple-element.37, f32[512,512]{0,1:T(8,128)S(1)} %fusion.93, f32[512,512]{0,1:T(8,128)S(1)} %fusion.94), kind=kOutput, calls=%fused_computation.2 | convolution fusion | flops 270270464 | bytes 4718592 | tf_op jit(solution)/shard_map/dot_general | solution.py:37
  40.7 0.5 %add_add_fusion = f32[512,1024]{1,0:T(8,128)S(1)} fusion(f32[512,1024]{1,0:T(8,128)S(1)} %add_add_fusion.1, f32[512,1024]{1,0:T(8,128)S(1)} %fusion.25, bf16[128,512]{1,0:T(8,128)(2,1)S(1)} %get-tuple-element.34, bf16[128,512]{1,0:T(8,128)(2,1)S(1)} %get-tuple-element.33, bf16[64,512]{1,0:T(8,128)(2,1)S(1)} %get-tuple-element.95, ...), kind=kOutput, calls=%fused_computation | convolution fusion | flops 136052736 | bytes 6684672 | tf_op jit(solution)/shard_map/dot_general | solution.py:36
  41.2 0.5 %multiply_reduce_fusion.1 = (f32[512]{0:T(512)S(1)}, f32[512]{0:T(512)S(1)}, f32[512]{0:T(512)S(1)}, f32[512]{0:T(512)S(1)}) fusion(f32[512,1024]{1,0:T(8,128)S(1)} %add_add_fusion, bf16[512,512]{1,0:T(8,128)(2,1)S(1)} %copy-done.1, bf16[512,512]{1,0:T(8,128)(2,1)S(1)} %copy-done.2), kind=kLoop, calls=%fused_computation.33 | loop fusion | flops 3143680 | bytes 3153920 | tf_op jit(solution)/shard_map/reduce_sum | solution.py:19
  41.7 0.5 %multiply_reduce_fusion = (f32[512]{0:T(512)S(1)}, f32[512,512]{1,0:T(8,128)S(1)}) fusion(bf16[64,512]{1,0:T(8,128)(2,1)S(1)} %get-tuple-element.96, bf16[64,512]{1,0:T(8,128)(2,1)S(1)} %get-tuple-element.94, f32[128,512]{1,0:T(8,128)S(1)} %fusion.55, f32[128,512]{1,0:T(8,128)S(1)} %fusion.54, f32[512,512]{1,0:T(8,128)S(1)} %convolution_add_fusion, ...), kind=kOutput, calls=%fused_computation.31 | convolution fusion | flops 69336576 | bytes 4327424 | tf_op jit(solution)/shard_map/dot_general | solution.py:37
  43.0 1.1 %convolution_convert_fusion = bf16[128,512]{1,0:T(8,128)(2,1)} fusion(bf16[512,512]{1,0:T(8,128)(2,1)S(1)} %multiply_convert_fusion, bf16[128,512]{1,0:T(8,128)(2,1)S(1)} %copy-done, bf16[512,512]{1,0:T(8,128)(2,1)S(1)} %get-tuple-element.17, f32[128,512]{1,0:T(8,128)S(1)} %convolution_bitcast_fusion.1), kind=kOutput, calls=%fused_computation.15 | convolution fusion | flops 134676480 | bytes 1572864 | tf_op jit(solution)/shard_map/dot_general | solution.py:45
  (82 shorter events, 8.3 us)
Async XLA Ops:
  0.0 42.8 %copy-start = (bf16[128,512]{1,0:T(8,128)(2,1)S(1)}, bf16[128,512]{1,0:T(8,128)(2,1)}, u32[]{:S(2)}) copy-start(bf16[128,512]{1,0:T(8,128)(2,1)} %param.9) | copy-start | bytes 393220
  0.0 6.7 %copy-start.2 = (bf16[512,512]{1,0:T(8,128)(2,1)S(1)}, bf16[512,512]{1,0:T(8,128)(2,1)}, u32[]{:S(2)}) copy-start(bf16[512,512]{1,0:T(8,128)(2,1)} %param.11) | copy-start | bytes 1572868
  0.0 7.0 %copy-start.1 = (bf16[512,512]{1,0:T(8,128)(2,1)S(1)}, bf16[512,512]{1,0:T(8,128)(2,1)}, u32[]{:S(2)}) copy-start(bf16[512,512]{1,0:T(8,128)(2,1)} %param.12) | copy-start | bytes 1572868
  2.0 9.3 %collective-permute-start.1 = (bf16[256,512]{1,0:T(8,128)(2,1)S(1)}, bf16[256,512]{1,0:T(8,128)(2,1)S(1)}, u32[]{:S(2)}, u32[]{:S(2)}) collective-permute-start(bf16[256,512]{1,0:T(8,128)(2,1)S(1)} %bitcast.51), channel_id=1, source_target_pairs={{0,4},{1,5},{4,8},{5,9},{8,12},{9,13},{12,14},{13,15},{14,10},{15,... | collective-permute-start | bytes 786440 | tf_op jit(solution)/shard_map/ppermute | solution.py:153
  5.1 8.1 %collective-permute-start.2 = (bf16[256,512]{1,0:T(8,128)(2,1)S(1)}, bf16[256,512]{1,0:T(8,128)(2,1)S(1)}, u32[]{:S(2)}, u32[]{:S(2)}) collective-permute-start(bf16[256,512]{1,0:T(8,128)(2,1)S(1)} %bitcast.52), channel_id=1, source_target_pairs={{0,2},{1,3},{4,0},{5,1},{8,4},{9,5},{12,8},{13,9},{14,12},{15,13},... | collective-permute-start | bytes 786440 | tf_op jit(solution)/shard_map/ppermute | solution.py:154
  5.1 1.5 %collective-permute-start = (bf16[256,512]{1,0:T(8,128)(2,1)S(1)}, bf16[256,512]{1,0:T(8,128)(2,1)S(1)}, u32[]{:S(2)}, u32[]{:S(2)}) collective-permute-start(bf16[256,512]{1,0:T(8,128)(2,1)S(1)} %bitcast.53), channel_id=1, source_target_pairs={{0,1},{1,0},{2,3},{3,2},{4,5},{5,4},{6,7},{7,6},{8,9},{9,8},{10,11... | collective-permute-start | bytes 786440 | tf_op jit(solution)/shard_map/ppermute | solution.py:142
  6.3 1.0 %copy-start.3 = (bf16[512,512]{1,0:T(8,128)(2,1)S(1)}, bf16[512,512]{1,0:T(8,128)(2,1)}, u32[]{:S(2)}) copy-start(bf16[512,512]{1,0:T(8,128)(2,1)} %param.13) | copy-start | bytes 1572868
  11.3 2.8 %collective-permute-start.3 = (bf16[256,512]{1,0:T(8,128)(2,1)S(1)}, bf16[256,512]{1,0:T(8,128)(2,1)S(1)}, u32[]{:S(2)}, u32[]{:S(2)}) collective-permute-start(bf16[256,512]{1,0:T(8,128)(2,1)S(1)} %collective-permute-done.1), channel_id=1, source_target_pairs={{0,1},{1,0},{2,3},{3,2},{4,5},{5,4},{6,7},{7,6},{8,9},{9,8},{10,11... | collective-permute-start | bytes 786440 | tf_op jit(solution)/shard_map/ppermute | solution.py:158
  11.3 8.7 %collective-permute-start.5 = (bf16[256,512]{1,0:T(8,128)(2,1)S(1)}, bf16[256,512]{1,0:T(8,128)(2,1)S(1)}, u32[]{:S(2)}, u32[]{:S(2)}) collective-permute-start(bf16[256,512]{1,0:T(8,128)(2,1)S(1)} %collective-permute-done.1), channel_id=1, source_target_pairs={{0,4},{1,5},{4,8},{5,9},{8,12},{9,13},{12,14},{13,15},{14,10},{15,... | collective-permute-start | bytes 786440 | tf_op jit(solution)/shard_map/ppermute | solution.py:153
  13.2 1.6 %collective-permute-start.4 = (bf16[256,512]{1,0:T(8,128)(2,1)S(1)}, bf16[256,512]{1,0:T(8,128)(2,1)S(1)}, u32[]{:S(2)}, u32[]{:S(2)}) collective-permute-start(bf16[256,512]{1,0:T(8,128)(2,1)S(1)} %collective-permute-done.2), channel_id=1, source_target_pairs={{0,1},{1,0},{2,3},{3,2},{4,5},{5,4},{6,7},{7,6},{8,9},{9,8},{10,11... | collective-permute-start | bytes 786440 | tf_op jit(solution)/shard_map/ppermute | solution.py:158
  13.5 8.5 %collective-permute-start.6 = (bf16[256,512]{1,0:T(8,128)(2,1)S(1)}, bf16[256,512]{1,0:T(8,128)(2,1)S(1)}, u32[]{:S(2)}, u32[]{:S(2)}) collective-permute-start(bf16[256,512]{1,0:T(8,128)(2,1)S(1)} %collective-permute-done.2), channel_id=1, source_target_pairs={{0,2},{1,3},{4,0},{5,1},{8,4},{9,5},{12,8},{13,9},{14,12},{15,13},... | collective-permute-start | bytes 786440 | tf_op jit(solution)/shard_map/ppermute | solution.py:154
  20.1 3.2 %collective-permute-start.7 = (bf16[256,512]{1,0:T(8,128)(2,1)S(1)}, bf16[256,512]{1,0:T(8,128)(2,1)S(1)}, u32[]{:S(2)}, u32[]{:S(2)}) collective-permute-start(bf16[256,512]{1,0:T(8,128)(2,1)S(1)} %collective-permute-done.5), channel_id=1, source_target_pairs={{0,1},{1,0},{2,3},{3,2},{4,5},{5,4},{6,7},{7,6},{8,9},{9,8},{10,11... | collective-permute-start | bytes 786440 | tf_op jit(solution)/shard_map/ppermute | solution.py:158
  20.1 8.7 %collective-permute-start.9 = (bf16[256,512]{1,0:T(8,128)(2,1)S(1)}, bf16[256,512]{1,0:T(8,128)(2,1)S(1)}, u32[]{:S(2)}, u32[]{:S(2)}) collective-permute-start(bf16[256,512]{1,0:T(8,128)(2,1)S(1)} %collective-permute-done.5), channel_id=1, source_target_pairs={{0,4},{1,5},{4,8},{5,9},{8,12},{9,13},{12,14},{13,15},{14,10},{15,... | collective-permute-start | bytes 786440 | tf_op jit(solution)/shard_map/ppermute | solution.py:153
  22.0 1.5 %collective-permute-start.8 = (bf16[256,512]{1,0:T(8,128)(2,1)S(1)}, bf16[256,512]{1,0:T(8,128)(2,1)S(1)}, u32[]{:S(2)}, u32[]{:S(2)}) collective-permute-start(bf16[256,512]{1,0:T(8,128)(2,1)S(1)} %collective-permute-done.6), channel_id=1, source_target_pairs={{0,1},{1,0},{2,3},{3,2},{4,5},{5,4},{6,7},{7,6},{8,9},{9,8},{10,11... | collective-permute-start | bytes 786440 | tf_op jit(solution)/shard_map/ppermute | solution.py:158
  22.2 9.7 %collective-permute-start.10 = (bf16[256,512]{1,0:T(8,128)(2,1)S(1)}, bf16[256,512]{1,0:T(8,128)(2,1)S(1)}, u32[]{:S(2)}, u32[]{:S(2)}) collective-permute-start(bf16[256,512]{1,0:T(8,128)(2,1)S(1)} %collective-permute-done.6), channel_id=1, source_target_pairs={{0,2},{1,3},{4,0},{5,1},{8,4},{9,5},{12,8},{13,9},{14,12},{15,13},... | collective-permute-start | bytes 786440 | tf_op jit(solution)/shard_map/ppermute | solution.py:154
  28.8 8.7 %collective-permute-start.13 = (bf16[128,512]{1,0:T(8,128)(2,1)S(1)}, bf16[128,512]{1,0:T(8,128)(2,1)S(1)}, u32[]{:S(2)}, u32[]{:S(2)}) collective-permute-start(bf16[128,512]{1,0:T(8,128)(2,1)S(1)} %slice.328), channel_id=1, source_target_pairs={{0,4},{1,5},{4,8},{5,9},{8,12},{9,13},{12,14},{13,15},{14,10},{15,... | collective-permute-start | bytes 393224 | tf_op jit(solution)/shard_map/ppermute | solution.py:148
  32.0 5.5 %collective-permute-start.14 = (bf16[128,512]{1,0:T(8,128)(2,1)S(1)}, bf16[128,512]{1,0:T(8,128)(2,1)S(1)}, u32[]{:S(2)}, u32[]{:S(2)}) collective-permute-start(bf16[128,512]{1,0:T(8,128)(2,1)S(1)} %slice.329), channel_id=1, source_target_pairs={{0,2},{1,3},{4,0},{5,1},{8,4},{9,5},{12,8},{13,9},{14,12},{15,13},... | collective-permute-start | bytes 393224 | tf_op jit(solution)/shard_map/ppermute | solution.py:149
  32.4 1.6 %collective-permute-start.11 = (bf16[256,512]{1,0:T(8,128)(2,1)S(1)}, bf16[256,512]{1,0:T(8,128)(2,1)S(1)}, u32[]{:S(2)}, u32[]{:S(2)}) collective-permute-start(bf16[256,512]{1,0:T(8,128)(2,1)S(1)} %collective-permute-done.9), channel_id=1, source_target_pairs={{0,1},{1,0},{2,3},{3,2},{4,5},{5,4},{6,7},{7,6},{8,9},{9,8},{10,11... | collective-permute-start | bytes 786440 | tf_op jit(solution)/shard_map/ppermute | solution.py:158
  32.5 1.9 %collective-permute-start.12 = (bf16[256,512]{1,0:T(8,128)(2,1)S(1)}, bf16[256,512]{1,0:T(8,128)(2,1)S(1)}, u32[]{:S(2)}, u32[]{:S(2)}) collective-permute-start(bf16[256,512]{1,0:T(8,128)(2,1)S(1)} %collective-permute-done.10), channel_id=1, source_target_pairs={{0,1},{1,0},{2,3},{3,2},{4,5},{5,4},{6,7},{7,6},{8,9},{9,8},{10,11... | collective-permute-start | bytes 786440 | tf_op jit(solution)/shard_map/ppermute | solution.py:158
  37.5 2.3 %collective-permute-start.15 = (bf16[128,512]{1,0:T(8,128)(2,1)S(1)}, bf16[128,512]{1,0:T(8,128)(2,1)S(1)}, u32[]{:S(2)}, u32[]{:S(2)}) collective-permute-start(bf16[128,512]{1,0:T(8,128)(2,1)S(1)} %collective-permute-done.13), channel_id=1, source_target_pairs={{0,1},{1,0},{2,3},{3,2},{4,5},{5,4},{6,7},{7,6},{8,9},{9,8},{10,11... | collective-permute-start | bytes 393224 | tf_op jit(solution)/shard_map/ppermute | solution.py:158
  37.7 2.2 %collective-permute-start.16 = (bf16[128,512]{1,0:T(8,128)(2,1)S(1)}, bf16[128,512]{1,0:T(8,128)(2,1)S(1)}, u32[]{:S(2)}, u32[]{:S(2)}) collective-permute-start(bf16[128,512]{1,0:T(8,128)(2,1)S(1)} %collective-permute-done.14), channel_id=1, source_target_pairs={{0,1},{1,0},{2,3},{3,2},{4,5},{5,4},{6,7},{7,6},{8,9},{9,8},{10,11... | collective-permute-start | bytes 393224 | tf_op jit(solution)/shard_map/ppermute | solution.py:158

commit v13 on v12

--- a/solution.py
+++ b/solution.py
@@ -17,6 +17,15 @@
     update = old + grads
     factor = jnp.sqrt(jnp.mean(old * old, axis=1, keepdims=True) + epsilon) / jnp.sqrt(
         jnp.mean(update * update, axis=1, keepdims=True) + epsilon
+    )
+    return (update * factor).astype(jnp.bfloat16)
+
+
+def renorm_rows(weight, grads):
+    old = weight.astype(jnp.float32)
+    update = old + grads
+    factor = jnp.sqrt(jnp.mean(old * old, axis=-1, keepdims=True) + epsilon) / jnp.sqrt(
+        jnp.mean(update * update, axis=-1, keepdims=True) + epsilon
     )
     return (update * factor).astype(jnp.bfloat16)
 
@@ -162,11 +171,10 @@
             else:
                 total = add_grads(total, *split(arrived + from_sib, half), w_gate, w_up, w_out)
         full_in, full_out = total
-        new_gate = renorm(w_gate, full_in[:, :hidden])
-        new_up = renorm(w_up, full_in[:, hidden:])
-        new_out = renorm(w_out, full_out)
-        new_gate, new_up, new_out = lax.optimization_barrier((new_gate, new_up, new_out))
-        return apply(queries, new_gate, new_up, new_out)
+        old_all = jnp.stack([w_gate, w_up, w_out], axis=1)
+        grads_all = jnp.stack([full_in[:, :hidden], full_in[:, hidden:], full_out], axis=1)
+        new_all = lax.optimization_barrier(renorm_rows(old_all, grads_all))
+        return apply(queries, new_all[:, 0], new_all[:, 1], new_all[:, 2])
 
     return local_ring
 

time: 44.3 us -> 45.3 us (1.023)
  matrix products: 15.6 us -> 16.5 us
  waiting for transfers between devices: 12 us -> 12.9 us
  other arithmetic: 4.29 us -> 3.45 us
    ppermute x3, waiting for transfers between devices: 10.3 us -> 11.4 us  [local_ring(): lax.ppermute(arrived[0], axes, cw_perm)]
    dot_general x6, matrix products: 2.31 us -> 3.36 us  [gradients(): gate_pre = jnp.dot(keys, w_gate, preferred_element_type=jnp.float32)]
    reduce_sum x2 -> x1, other arithmetic: 1.76 us -> 0.9 us  [renorm_rows(): jnp.mean(old * old, axis=-1, keepdims=True) + epsilon]
    ppermute x1, starting transfers between devices: 0.01 us -> 0.52 us  [local_ring(): sib = lax.ppermute(own, axes, swap)]
  transfers between devices with their start and end apart: 17 -> 17, of which waited for: 9 -> 8; matrix products, arithmetic and copies ran while one was open for 32% -> 31% of each run, Pallas kernels for 0% -> 0%
where the time goes in v13:
time: 45.3 us; the launch traced here: 45.1 us
  matrix products  16.5 us (36%)
  waiting for transfers between devices  12.9 us (28%)
  starting transfers between devices  11.2 us (25%)
  other arithmetic  3.45 us (8%)
  local copies, waits for them, and re-layouts  0.58 us (1%)
  between operations  0.53 us (1%)
    ppermute x3, waiting for transfers between devices, local_ring(): lax.ppermute(arrived[0], axes, cw_perm)  11.4 us
    ppermute x3, starting transfers between devices, local_ring(): lax.ppermute(arrived[0], axes, cw_perm)  6.29 us
    dot_general x6, matrix products, gradients(): lax.dot_general(keys, both_grads, contract_first, preferred_element_type=...  3.66 us
    dot_general x6, matrix products, gradients(): lax.dot_general(scaled, w_out, contract_last, preferred_element_type=jnp....  3.51 us
    dot_general x6, matrix products, gradients(): gate_pre = jnp.dot(keys, w_gate, preferred_element_type=jnp.float32)  3.36 us
    dot_general x6, matrix products, gradients(): lax.dot_general(activation, scaled, contract_first, preferred_element_typ...  2.44 us
    dot_general x6, matrix products, gradients(): up_pre = jnp.dot(keys, w_up, preferred_element_type=jnp.float32)  2.2 us
    ppermute x1, starting transfers between devices, local_ring(): lax.ppermute(arrived[0][:2 * half], axes, cw_perm)  1.88 us
  transfers between devices with their start and end apart: 17, of which 8 were waited for; matrix products, arithmetic and copies ran while one was open for 31% of the time, Pallas kernels for 0%

profile of v13, /device:TPU:0, one launch (start us, length us, event | category | flops | bytes accessed | tf_op | source)
XLA Modules:
  0.0 45.1 jit_solution(5201417311127225619)
XLA Ops:
  0.0 1.1 %multiply_convert_fusion.23 = bf16[128,512]{1,0:T(8,128)(2,1)S(1)} fusion(bf16[128,512]{1,0:T(8,128)(2,1)} %param.8, f32[128]{0:T(128)} %param.10), kind=kLoop, calls=%fused_computation.84 | loop fusion | flops 196608 | bytes 262656 | tf_op jit(solution)/shard_map/convert_element_type | solution.py:146
  1.1 0.9 %pad_maximum_fusion.1 = bf16[2,2,64,512]{3,2,1,0:T(8,128)(2,1)S(1)} fusion(bf16[2,1,64,512]{3,2,1,0:T(8,128)(2,1)S(1)} %bitcast.77, bf16[2,1,64,512]{3,2,1,0:T(8,128)(2,1)} %bitcast.78), kind=kLoop, calls=%fused_computation.58 | loop fusion | flops 131072 | bytes 524288 | tf_op jit(solution)/shard_map/stack | solution.py:148
  2.0 0.5 %collective-permute-start = (bf16[256,512]{1,0:T(8,128)(2,1)S(1)}, bf16[256,512]{1,0:T(8,128)(2,1)S(1)}, u32[]{:S(2)}, u32[]{:S(2)}) collective-permute-start(bf16[256,512]{1,0:T(8,128)(2,1)S(1)} %bitcast.73), channel_id=1, source_target_pairs={{0,1},{1,0},{2,3},{3,2},{4,5},{5,4},{6,7},{7,6},{8,9},{9,8},{10,11... | collective-permute-start | bytes 786440 | tf_op jit(solution)/shard_map/ppermute | solution.py:151
  2.5 2.6 %collective-permute-start.1 = (bf16[256,512]{1,0:T(8,128)(2,1)S(1)}, bf16[256,512]{1,0:T(8,128)(2,1)S(1)}, u32[]{:S(2)}, u32[]{:S(2)}) collective-permute-start(bf16[256,512]{1,0:T(8,128)(2,1)S(1)} %bitcast.74), channel_id=1, source_target_pairs={{0,4},{1,5},{4,8},{5,9},{8,12},{9,13},{12,14},{13,15},{14,10},{15,... | collective-permute-start | bytes 786440 | tf_op jit(solution)/shard_map/ppermute | solution.py:162
  5.2 1.3 %fusion.79 = f32[256,512]{1,0:T(8,128)S(1)} fusion(bf16[512,512]{1,0:T(8,128)(2,1)} %param.11, bf16[64,512]{1,0:T(8,128)(2,1)S(1)} %get-tuple-element.68, bf16[64,512]{1,0:T(8,128)(2,1)S(1)} %get-tuple-element.65, bf16[64,512]{1,0:T(8,128)(2,1)S(1)} %get-tuple-element.64, bf16[64,512]{1,0:T(8,128)(2,1)S(1)} %get-tuple-element.61), kind=kOutput, calls=%fused_computation.171 | convolution fusion | flops 135266304 | bytes 1310720 | tf_op jit(solution)/shard_map/dot_general | solution.py:38
  6.9 0.5 %multiply_convert_fusion.15 = (bf16[256,512]{1,0:T(8,128)(2,1)S(1)}, bf16[256,512]{1,0:T(8,128)(2,1)S(1)}) fusion(f32[256,512]{1,0:T(8,128)S(1)} %fusion.79, f32[256,512]{1,0:T(8,128)S(1)} %fusion.80, bf16[512,512]{1,0:T(8,128)(2,1)S(1)} %copy-done.3, bf16[64,512]{1,0:T(8,128)(2,1)S(1)} %get-tuple-element.66, bf16[64,512]{1,0:T(8,128)(2,1)S(1)} %get-tuple-element.67, ...), kind=kOutput, calls=%fused_computation.54 | convolution fusion | flops 136970240 | bytes 2359296 | tf_op jit(solution)/shard_map/dot_general | solution.py:40
  7.4 0.5 %fusion.17 = f32[512,1024]{1,0:T(8,128)S(1)} fusion(bf16[256,512]{1,0:T(8,128)(2,1)S(1)} %get-tuple-element.24, bf16[256,512]{1,0:T(8,128)(2,1)S(1)} %get-tuple-element.23, bf16[64,512]{1,0:T(8,128)(2,1)S(1)} %get-tuple-element.68, bf16[64,512]{1,0:T(8,128)(2,1)S(1)} %get-tuple-element.65, bf16[64,512]{1,0:T(8,128)(2,1)S(1)} %get-tuple-element.64, ...), kind=kOutput, calls=%fused_computation.48 | convolution fusion | flops 270532608 | bytes 2883584 | tf_op jit(solution)/shard_map/dot_general | solution.py:45
  7.8 4.2 %collective-permute-done.1 = bf16[256,512]{1,0:T(8,128)(2,1)S(1)} collective-permute-done((bf16[256,512]{1,0:T(8,128)(2,1)S(1)}, bf16[256,512]{1,0:T(8,128)(2,1)S(1)}, u32[]{:S(2)}, u32[]{:S(2)}) %collective-permute-start.1) | collective-permute-done | bytes 262176 | tf_op jit(solution)/shard_map/ppermute | solution.py:162
  12.0 1.8 %collective-permute-start.5 = (bf16[256,512]{1,0:T(8,128)(2,1)S(1)}, bf16[256,512]{1,0:T(8,128)(2,1)S(1)}, u32[]{:S(2)}, u32[]{:S(2)}) collective-permute-start(bf16[256,512]{1,0:T(8,128)(2,1)S(1)} %collective-permute-done.1), channel_id=1, source_target_pairs={{0,4},{1,5},{4,8},{5,9},{8,12},{9,13},{12,14},{13,15},{14,10},{15,... | collective-permute-start | bytes 786440 | tf_op jit(solution)/shard_map/ppermute | solution.py:162
  14.8 0.6 %collective-permute-done.4 = bf16[256,512]{1,0:T(8,128)(2,1)S(1)} collective-permute-done((bf16[256,512]{1,0:T(8,128)(2,1)S(1)}, bf16[256,512]{1,0:T(8,128)(2,1)S(1)}, u32[]{:S(2)}, u32[]{:S(2)}) %collective-permute-start.4) | collective-permute-done | bytes 262176 | tf_op jit(solution)/shard_map/ppermute | solution.py:167
  15.5 0.5 %fusion.87 = f32[512,512]{0,1:T(8,128)S(1)} fusion(bf16[512,512]{1,0:T(8,128)(2,1)S(1)} %get-tuple-element.46, bf16[512,512]{1,0:T(8,128)(2,1)S(1)} %copy-done.1), kind=kOutput, calls=%fused_computation.179 | convolution fusion | flops 268435456 | bytes 2097152 | tf_op jit(solution)/shard_map/dot_general | solution.py:39
  16.0 0.5 %fusion.88 = f32[512,512]{0,1:T(8,128)S(1)} fusion(bf16[512,512]{1,0:T(8,128)(2,1)S(1)} %get-tuple-element.46, bf16[512,512]{1,0:T(8,128)(2,1)S(1)} %copy-done.2), kind=kOutput, calls=%fused_computation.180 | convolution fusion | flops 268435456 | bytes 2097152 | tf_op jit(solution)/shard_map/dot_general | solution.py:38
  16.5 0.8 %multiply_convert_fusion.9 = (bf16[512,512]{0,1:T(8,128)(2,1)S(1)}, bf16[512,512]{0,1:T(8,128)(2,1)S(1)}) fusion(f32[512,512]{0,1:T(8,128)S(1)} %fusion.88, f32[512,512]{0,1:T(8,128)S(1)} %fusion.87, bf16[512,512]{1,0:T(8,128)(2,1)S(1)} %get-tuple-element.45, bf16[512,512]{1,0:T(8,128)(2,1)S(1)} %copy-done.3), kind=kOutput, calls=%fused_computation.42 | convolution fusion | flops 271843328 | bytes 4194304 | tf_op jit(solution)/shard_map/dot_general | solution.py:40
  17.3 0.5 %convolution_add_fusion.2 = f32[512,512]{1,0:T(8,128)S(1)} fusion(f32[512,512]{1,0:T(8,128)S(1)} %fusion.22, bf16[512,512]{1,0:T(8,128)(2,1)S(1)} %get-tuple-element.45, f32[512,512]{0,1:T(8,128)S(1)} %fusion.87, f32[512,512]{0,1:T(8,128)S(1)} %fusion.88), kind=kOutput, calls=%fused_computation.10 | convolution fusion | flops 270270464 | bytes 4718592 | tf_op jit(solution)/shard_map/dot_general | solution.py:46
  17.8 3.0 %collective-permute-done.5 = bf16[256,512]{1,0:T(8,128)(2,1)S(1)} collective-permute-done((bf16[256,512]{1,0:T(8,128)(2,1)S(1)}, bf16[256,512]{1,0:T(8,128)(2,1)S(1)}, u32[]{:S(2)}, u32[]{:S(2)}) %collective-permute-start.5) | collective-permute-done | bytes 262176 | tf_op jit(solution)/shard_map/ppermute | solution.py:162
  20.7 1.8 %collective-permute-start.9 = (bf16[256,512]{1,0:T(8,128)(2,1)S(1)}, bf16[256,512]{1,0:T(8,128)(2,1)S(1)}, u32[]{:S(2)}, u32[]{:S(2)}) collective-permute-start(bf16[256,512]{1,0:T(8,128)(2,1)S(1)} %collective-permute-done.5), channel_id=1, source_target_pairs={{0,4},{1,5},{4,8},{5,9},{8,12},{9,13},{12,14},{13,15},{14,10},{15,... | collective-permute-start | bytes 786440 | tf_op jit(solution)/shard_map/ppermute | solution.py:162
  23.1 0.8 %fusion.3 = f32[512,1024]{1,0:T(8,128)S(1)} fusion(bf16[512,512]{1,0:T(8,128)(2,1)S(1)} %get-tuple-element.46, bf16[512,512]{0,1:T(8,128)(2,1)S(1)} %get-tuple-element.20, bf16[512,512]{0,1:T(8,128)(2,1)S(1)} %get-tuple-element.19), kind=kOutput, calls=%fused_computation.18 | convolution fusion | flops 538968064 | bytes 3670016 | tf_op jit(solution)/shard_map/dot_general | solution.py:45
  24.2 0.5 %fusion.89 = f32[512,512]{0,1:T(8,128)S(1)} fusion(bf16[512,512]{1,0:T(8,128)(2,1)S(1)} %get-tuple-element.70, bf16[512,512]{1,0:T(8,128)(2,1)S(1)} %copy-done.1), kind=kOutput, calls=%fused_computation.181 | convolution fusion | flops 268435456 | bytes 2097152 | tf_op jit(solution)/shard_map/dot_general | solution.py:39
  24.7 0.5 %fusion.90 = f32[512,512]{0,1:T(8,128)S(1)} fusion(bf16[512,512]{1,0:T(8,128)(2,1)S(1)} %get-tuple-element.70, bf16[512,512]{1,0:T(8,128)(2,1)S(1)} %copy-done.2), kind=kOutput, calls=%fused_computation.182 | convolution fusion | flops 268435456 | bytes 2097152 | tf_op jit(solution)/shard_map/dot_general | solution.py:38
  25.2 4.2 %collective-permute-done.9 = bf16[256,512]{1,0:T(8,128)(2,1)S(1)} collective-permute-done((bf16[256,512]{1,0:T(8,128)(2,1)S(1)}, bf16[256,512]{1,0:T(8,128)(2,1)S(1)}, u32[]{:S(2)}, u32[]{:S(2)}) %collective-permute-start.9) | collective-permute-done | bytes 262176 | tf_op jit(solution)/shard_map/ppermute | solution.py:162
  29.5 1.9 %collective-permute-start.13 = (bf16[128,512]{1,0:T(8,128)(2,1)S(1)}, bf16[128,512]{1,0:T(8,128)(2,1)S(1)}, u32[]{:S(2)}, u32[]{:S(2)}) collective-permute-start(bf16[128,512]{1,0:T(8,128)(2,1)S(1)} %slice.340), channel_id=1, source_target_pairs={{0,4},{1,5},{4,8},{5,9},{8,12},{9,13},{12,14},{13,15},{14,10},{15,... | collective-permute-start | bytes 393224 | tf_op jit(solution)/shard_map/ppermute | solution.py:157
  31.3 0.8 %multiply_convert_fusion.7 = (bf16[512,512]{0,1:T(8,128)(2,1)S(1)}, bf16[512,512]{0,1:T(8,128)(2,1)S(1)}) fusion(f32[512,512]{0,1:T(8,128)S(1)} %fusion.90, f32[512,512]{0,1:T(8,128)S(1)} %fusion.89, bf16[512,512]{1,0:T(8,128)(2,1)S(1)} %get-tuple-element.69, bf16[512,512]{1,0:T(8,128)(2,1)S(1)} %copy-done.3), kind=kOutput, calls=%fused_computation.38 | convolution fusion | flops 271843328 | bytes 4194304 | tf_op jit(solution)/shard_map/dot_general | solution.py:40
  32.1 0.5 %convolution_add_fusion.1 = f32[512,512]{1,0:T(8,128)S(1)} fusion(f32[512,512]{1,0:T(8,128)S(1)} %convolution_add_fusion.2, bf16[512,512]{1,0:T(8,128)(2,1)S(1)} %get-tuple-element.69, f32[512,512]{0,1:T(8,128)S(1)} %fusion.89, f32[512,512]{0,1:T(8,128)S(1)} %fusion.90), kind=kOutput, calls=%fused_computation.9 | convolution fusion | flops 270270464 | bytes 4718592 | tf_op jit(solution)/shard_map/dot_general | solution.py:46
  33.2 0.5 %collective-permute-start.12 = (bf16[256,512]{1,0:T(8,128)(2,1)S(1)}, bf16[256,512]{1,0:T(8,128)(2,1)S(1)}, u32[]{:S(2)}, u32[]{:S(2)}) collective-permute-start(bf16[256,512]{1,0:T(8,128)(2,1)S(1)} %collective-permute-done.10), channel_id=1, source_target_pairs={{0,1},{1,0},{2,3},{3,2},{4,5},{5,4},{6,7},{7,6},{8,9},{9,8},{10,11... | collective-permute-start | bytes 786440 | tf_op jit(solution)/shard_map/ppermute | solution.py:167
  33.7 0.8 %fusion.7 = f32[512,1024]{1,0:T(8,128)S(1)} fusion(bf16[512,512]{1,0:T(8,128)(2,1)S(1)} %get-tuple-element.70, bf16[512,512]{0,1:T(8,128)(2,1)S(1)} %get-tuple-element.22, bf16[512,512]{0,1:T(8,128)(2,1)S(1)} %get-tuple-element.21), kind=kOutput, calls=%fused_computation.22 | convolution fusion | flops 538968064 | bytes 3670016 | tf_op jit(solution)/shard_map/dot_general | solution.py:45
  35.1 0.5 %fusion.91 = f32[512,512]{0,1:T(8,128)S(1)} fusion(bf16[512,512]{1,0:T(8,128)(2,1)S(1)} %get-tuple-element.30, bf16[512,512]{1,0:T(8,128)(2,1)S(1)} %copy-done.1), kind=kOutput, calls=%fused_computation.183 | convolution fusion | flops 268435456 | bytes 2097152 | tf_op jit(solution)/shard_map/dot_general | solution.py:39
  35.6 0.5 %fusion.92 = f32[512,512]{0,1:T(8,128)S(1)} fusion(bf16[512,512]{1,0:T(8,128)(2,1)S(1)} %get-tuple-element.30, bf16[512,512]{1,0:T(8,128)(2,1)S(1)} %copy-done.2), kind=kOutput, calls=%fused_computation.184 | convolution fusion | flops 268435456 | bytes 2097152 | tf_op jit(solution)/shard_map/dot_general | solution.py:38
  36.1 0.8 %multiply_convert_fusion.5 = (bf16[512,512]{0,1:T(8,128)(2,1)S(1)}, bf16[512,512]{0,1:T(8,128)(2,1)S(1)}) fusion(f32[512,512]{0,1:T(8,128)S(1)} %fusion.92, f32[512,512]{0,1:T(8,128)S(1)} %fusion.91, bf16[512,512]{1,0:T(8,128)(2,1)S(1)} %get-tuple-element.29, bf16[512,512]{1,0:T(8,128)(2,1)S(1)} %copy-done.3), kind=kOutput, calls=%fused_computation.34 | convolution fusion | flops 271843328 | bytes 4194304 | tf_op jit(solution)/shard_map/dot_general | solution.py:40
  36.9 0.8 %add_add_fusion.1 = f32[512,1024]{1,0:T(8,128)S(1)} fusion(f32[512,1024]{1,0:T(8,128)S(1)} %fusion.7, f32[512,1024]{1,0:T(8,128)S(1)} %fusion.17, f32[512,1024]{1,0:T(8,128)S(1)} %fusion.3, bf16[512,512]{1,0:T(8,128)(2,1)S(1)} %get-tuple-element.30, bf16[512,512]{0,1:T(8,128)(2,1)S(1)} %get-tuple-element.18, bf16[512,512]{0,1:T(8,128)(2,1)S(1)} %get-tuple-element.17), kind=kOutput, calls=%fused_computation.6 | convolution fusion | flops 540540928 | bytes 9961472 | tf_op jit(solution)/shard_map/dot_general | solution.py:45
  42.3 0.9 %fusion = (f32[512,3]{0,1:T(4,128)S(1)}, f32[512,3]{0,1:T(4,128)S(1)}) fusion(bf16[512,1,512]{2,0,1:T(8,128)(2,1)S(1)} %bitcast.71, bf16[512,1,512]{2,0,1:T(8,128)(2,1)S(1)} %bitcast.67, bf16[512,1,512]{2,0,1:T(8,128)(2,1)S(1)} %bitcast.69, f32[512,1,512]{2,0,1:T(8,128)S(1)} %add_bitcast_fusion, f32[512,1,512]{2,0,1:T(8,128)S(1)} %get-tuple-element.16, ...), kind=kLoop, calls=%fused_computation.2 | loop fusion | flops 7861248 | bytes 4730880 | tf_op jit(solution)/shard_map/reduce_sum | solution.py:27
  43.2 0.6 %multiply_convert_fusion = bf16[512,3,512]{2,0,1:T(8,128)(2,1)S(1)} fusion(f32[512,3]{0,1:T(4,128)S(1)} %rsqrt_multiply_fusion, f32[512,1,512]{2,0,1:T(8,128)S(1)} %add_bitcast_fusion, f32[512,1,512]{2,0,1:T(8,128)S(1)} %get-tuple-element.16, f32[512,1,512]{2,0,1:T(8,128)S(1)} %get-tuple-element.15, bf16[512,1,512]{2,0,1:T(8,128)(2,1)S(1)} %bitcast.72, ...), kind=kLoop, calls=%fused_computation.3 | loop fusion | flops 6291456 | bytes 6297600 | tf_op jit(solution)/shard_map/convert_element_type | solution.py:30
  44.0 1.1 %convolution_convert_fusion = bf16[128,512]{1,0:T(8,128)(2,1)} fusion(bf16[128,512]{1,0:T(8,128)(2,1)S(1)} %copy-done, bf16[512,3,512]{2,0,1:T(8,128)(2,1)S(1)} %multiply_convert_fusion, f32[128,512]{1,0:T(8,128)S(1)} %convolution_bitcast_fusion.1), kind=kOutput, calls=%fused_computation.15 | convolution fusion | flops 134676480 | bytes 1572864 | tf_op jit(solution)/shard_map/dot_general | solution.py:54
  (79 shorter events, 8.1 us)
Async XLA Ops:
  0.0 43.8 %copy-start = (bf16[128,512]{1,0:T(8,128)(2,1)S(1)}, bf16[128,512]{1,0:T(8,128)(2,1)}, u32[]{:S(2)}) copy-start(bf16[128,512]{1,0:T(8,128)(2,1)} %param.9) | copy-start | bytes 393220
  0.0 6.6 %copy-start.1 = (bf16[512,512]{1,0:T(8,128)(2,1)S(1)}, bf16[512,512]{1,0:T(8,128)(2,1)}, u32[]{:S(2)}) copy-start(bf16[512,512]{1,0:T(8,128)(2,1)} %param.12) | copy-start | bytes 1572868
  2.0 4.9 %copy-start.3 = (bf16[512,512]{1,0:T(8,128)(2,1)S(1)}, bf16[512,512]{1,0:T(8,128)(2,1)}, u32[]{:S(2)}) copy-start(bf16[512,512]{1,0:T(8,128)(2,1)} %param.13) | copy-start | bytes 1572868
  2.0 3.2 %collective-permute-start = (bf16[256,512]{1,0:T(8,128)(2,1)S(1)}, bf16[256,512]{1,0:T(8,128)(2,1)S(1)}, u32[]{:S(2)}, u32[]{:S(2)}) collective-permute-start(bf16[256,512]{1,0:T(8,128)(2,1)S(1)} %bitcast.73), channel_id=1, source_target_pairs={{0,1},{1,0},{2,3},{3,2},{4,5},{5,4},{6,7},{7,6},{8,9},{9,8},{10,11... | collective-permute-start | bytes 786440 | tf_op jit(solution)/shard_map/ppermute | solution.py:151
  2.5 9.5 %collective-permute-start.1 = (bf16[256,512]{1,0:T(8,128)(2,1)S(1)}, bf16[256,512]{1,0:T(8,128)(2,1)S(1)}, u32[]{:S(2)}, u32[]{:S(2)}) collective-permute-start(bf16[256,512]{1,0:T(8,128)(2,1)S(1)} %bitcast.74), channel_id=1, source_target_pairs={{0,4},{1,5},{4,8},{5,9},{8,12},{9,13},{12,14},{13,15},{14,10},{15,... | collective-permute-start | bytes 786440 | tf_op jit(solution)/shard_map/ppermute | solution.py:162
  5.2 8.7 %collective-permute-start.2 = (bf16[256,512]{1,0:T(8,128)(2,1)S(1)}, bf16[256,512]{1,0:T(8,128)(2,1)S(1)}, u32[]{:S(2)}, u32[]{:S(2)}) collective-permute-start(bf16[256,512]{1,0:T(8,128)(2,1)S(1)} %bitcast.75), channel_id=1, source_target_pairs={{0,2},{1,3},{4,0},{5,1},{8,4},{9,5},{12,8},{13,9},{14,12},{15,13},... | collective-permute-start | bytes 786440 | tf_op jit(solution)/shard_map/ppermute | solution.py:163
  12.0 2.8 %collective-permute-start.3 = (bf16[256,512]{1,0:T(8,128)(2,1)S(1)}, bf16[256,512]{1,0:T(8,128)(2,1)S(1)}, u32[]{:S(2)}, u32[]{:S(2)}) collective-permute-start(bf16[256,512]{1,0:T(8,128)(2,1)S(1)} %collective-permute-done.1), channel_id=1, source_target_pairs={{0,1},{1,0},{2,3},{3,2},{4,5},{5,4},{6,7},{7,6},{8,9},{9,8},{10,11... | collective-permute-start | bytes 786440 | tf_op jit(solution)/shard_map/ppermute | solution.py:167
  12.0 8.7 %collective-permute-start.5 = (bf16[256,512]{1,0:T(8,128)(2,1)S(1)}, bf16[256,512]{1,0:T(8,128)(2,1)S(1)}, u32[]{:S(2)}, u32[]{:S(2)}) collective-permute-start(bf16[256,512]{1,0:T(8,128)(2,1)S(1)} %collective-permute-done.1), channel_id=1, source_target_pairs={{0,4},{1,5},{4,8},{5,9},{8,12},{9,13},{12,14},{13,15},{14,10},{15,... | collective-permute-start | bytes 786440 | tf_op jit(solution)/shard_map/ppermute | solution.py:162
  13.9 1.6 %collective-permute-start.4 = (bf16[256,512]{1,0:T(8,128)(2,1)S(1)}, bf16[256,512]{1,0:T(8,128)(2,1)S(1)}, u32[]{:S(2)}, u32[]{:S(2)}) collective-permute-start(bf16[256,512]{1,0:T(8,128)(2,1)S(1)} %collective-permute-done.2), channel_id=1, source_target_pairs={{0,1},{1,0},{2,3},{3,2},{4,5},{5,4},{6,7},{7,6},{8,9},{9,8},{10,11... | collective-permute-start | bytes 786440 | tf_op jit(solution)/shard_map/ppermute | solution.py:167
  14.1 8.5 %collective-permute-start.6 = (bf16[256,512]{1,0:T(8,128)(2,1)S(1)}, bf16[256,512]{1,0:T(8,128)(2,1)S(1)}, u32[]{:S(2)}, u32[]{:S(2)}) collective-permute-start(bf16[256,512]{1,0:T(8,128)(2,1)S(1)} %collective-permute-done.2), channel_id=1, source_target_pairs={{0,2},{1,3},{4,0},{5,1},{8,4},{9,5},{12,8},{13,9},{14,12},{15,13},... | collective-permute-start | bytes 786440 | tf_op jit(solution)/shard_map/ppermute | solution.py:163
  14.8 1.2 %copy-start.2 = (bf16[512,512]{1,0:T(8,128)(2,1)S(1)}, bf16[512,512]{1,0:T(8,128)(2,1)}, u32[]{:S(2)}) copy-start(bf16[512,512]{1,0:T(8,128)(2,1)} %param.11) | copy-start | bytes 1572868
  20.7 3.2 %collective-permute-start.7 = (bf16[256,512]{1,0:T(8,128)(2,1)S(1)}, bf16[256,512]{1,0:T(8,128)(2,1)S(1)}, u32[]{:S(2)}, u32[]{:S(2)}) collective-permute-start(bf16[256,512]{1,0:T(8,128)(2,1)S(1)} %collective-permute-done.5), channel_id=1, source_target_pairs={{0,1},{1,0},{2,3},{3,2},{4,5},{5,4},{6,7},{7,6},{8,9},{9,8},{10,11... | collective-permute-start | bytes 786440 | tf_op jit(solution)/shard_map/ppermute | solution.py:167
  20.7 8.7 %collective-permute-start.9 = (bf16[256,512]{1,0:T(8,128)(2,1)S(1)}, bf16[256,512]{1,0:T(8,128)(2,1)S(1)}, u32[]{:S(2)}, u32[]{:S(2)}) collective-permute-start(bf16[256,512]{1,0:T(8,128)(2,1)S(1)} %collective-permute-done.5), channel_id=1, source_target_pairs={{0,4},{1,5},{4,8},{5,9},{8,12},{9,13},{12,14},{13,15},{14,10},{15,... | collective-permute-start | bytes 786440 | tf_op jit(solution)/shard_map/ppermute | solution.py:162
  22.6 1.5 %collective-permute-start.8 = (bf16[256,512]{1,0:T(8,128)(2,1)S(1)}, bf16[256,512]{1,0:T(8,128)(2,1)S(1)}, u32[]{:S(2)}, u32[]{:S(2)}) collective-permute-start(bf16[256,512]{1,0:T(8,128)(2,1)S(1)} %collective-permute-done.6), channel_id=1, source_target_pairs={{0,1},{1,0},{2,3},{3,2},{4,5},{5,4},{6,7},{7,6},{8,9},{9,8},{10,11... | collective-permute-start | bytes 786440 | tf_op jit(solution)/shard_map/ppermute | solution.py:167
  22.9 9.7 %collective-permute-start.10 = (bf16[256,512]{1,0:T(8,128)(2,1)S(1)}, bf16[256,512]{1,0:T(8,128)(2,1)S(1)}, u32[]{:S(2)}, u32[]{:S(2)}) collective-permute-start(bf16[256,512]{1,0:T(8,128)(2,1)S(1)} %collective-permute-done.6), channel_id=1, source_target_pairs={{0,2},{1,3},{4,0},{5,1},{8,4},{9,5},{12,8},{13,9},{14,12},{15,13},... | collective-permute-start | bytes 786440 | tf_op jit(solution)/shard_map/ppermute | solution.py:163
  29.5 8.7 %collective-permute-start.13 = (bf16[128,512]{1,0:T(8,128)(2,1)S(1)}, bf16[128,512]{1,0:T(8,128)(2,1)S(1)}, u32[]{:S(2)}, u32[]{:S(2)}) collective-permute-start(bf16[128,512]{1,0:T(8,128)(2,1)S(1)} %slice.340), channel_id=1, source_target_pairs={{0,4},{1,5},{4,8},{5,9},{8,12},{9,13},{12,14},{13,15},{14,10},{15,... | collective-permute-start | bytes 393224 | tf_op jit(solution)/shard_map/ppermute | solution.py:157
  32.6 5.5 %collective-permute-start.14 = (bf16[128,512]{1,0:T(8,128)(2,1)S(1)}, bf16[128,512]{1,0:T(8,128)(2,1)S(1)}, u32[]{:S(2)}, u32[]{:S(2)}) collective-permute-start(bf16[128,512]{1,0:T(8,128)(2,1)S(1)} %slice.341), channel_id=1, source_target_pairs={{0,2},{1,3},{4,0},{5,1},{8,4},{9,5},{12,8},{13,9},{14,12},{15,13},... | collective-permute-start | bytes 393224 | tf_op jit(solution)/shard_map/ppermute | solution.py:158
  33.1 1.6 %collective-permute-start.11 = (bf16[256,512]{1,0:T(8,128)(2,1)S(1)}, bf16[256,512]{1,0:T(8,128)(2,1)S(1)}, u32[]{:S(2)}, u32[]{:S(2)}) collective-permute-start(bf16[256,512]{1,0:T(8,128)(2,1)S(1)} %collective-permute-done.9), channel_id=1, source_target_pairs={{0,1},{1,0},{2,3},{3,2},{4,5},{5,4},{6,7},{7,6},{8,9},{9,8},{10,11... | collective-permute-start | bytes 786440 | tf_op jit(solution)/shard_map/ppermute | solution.py:167
  33.2 1.9 %collective-permute-start.12 = (bf16[256,512]{1,0:T(8,128)(2,1)S(1)}, bf16[256,512]{1,0:T(8,128)(2,1)S(1)}, u32[]{:S(2)}, u32[]{:S(2)}) collective-permute-start(bf16[256,512]{1,0:T(8,128)(2,1)S(1)} %collective-permute-done.10), channel_id=1, source_target_pairs={{0,1},{1,0},{2,3},{3,2},{4,5},{5,4},{6,7},{7,6},{8,9},{9,8},{10,11... | collective-permute-start | bytes 786440 | tf_op jit(solution)/shard_map/ppermute | solution.py:167
  38.1 2.3 %collective-permute-start.15 = (bf16[128,512]{1,0:T(8,128)(2,1)S(1)}, bf16[128,512]{1,0:T(8,128)(2,1)S(1)}, u32[]{:S(2)}, u32[]{:S(2)}) collective-permute-start(bf16[128,512]{1,0:T(8,128)(2,1)S(1)} %collective-permute-done.13), channel_id=1, source_target_pairs={{0,1},{1,0},{2,3},{3,2},{4,5},{5,4},{6,7},{7,6},{8,9},{9,8},{10,11... | collective-permute-start | bytes 393224 | tf_op jit(solution)/shard_map/ppermute | solution.py:167
  38.3 2.1 %collective-permute-start.16 = (bf16[128,512]{1,0:T(8,128)(2,1)S(1)}, bf16[128,512]{1,0:T(8,128)(2,1)S(1)}, u32[]{:S(2)}, u32[]{:S(2)}) collective-permute-start(bf16[128,512]{1,0:T(8,128)(2,1)S(1)} %collective-permute-done.14), channel_id=1, source_target_pairs={{0,1},{1,0},{2,3},{3,2},{4,5},{5,4},{6,7},{7,6},{8,9},{9,8},{10,11... | collective-permute-start | bytes 393224 | tf_op jit(solution)/shard_map/ppermute | solution.py:167

commit v14 on v12

--- a/solution.py
+++ b/solution.py
@@ -1,6 +1,7 @@
 import jax
 import jax.numpy as jnp
 from jax import lax
+from jax.experimental import pallas as pl
 from jax.sharding import PartitionSpec as P
 
 epsilon = 1e-06
@@ -43,6 +44,26 @@
     q_up = jnp.dot(queries, full_up, preferred_element_type=jnp.float32)
     q_act = (jax.nn.silu(q_gate) * q_up).astype(jnp.bfloat16)
     return jnp.dot(q_act, full_out_w, preferred_element_type=jnp.float32).astype(jnp.bfloat16)
+
+
+def _build_kernel(k_ref, v_ref, lr_ref, o_ref):
+    rows, width = v_ref.shape
+    half = rows // 2
+    rate = jnp.transpose(jnp.broadcast_to(lr_ref[...], (width, rows)))
+    scaled = (v_ref[...].astype(jnp.float32) * rate).astype(jnp.bfloat16)
+    keys = k_ref[...]
+    o_ref[0:half] = keys[0:half]
+    o_ref[half:2 * half] = scaled[0:half]
+    o_ref[2 * half:3 * half] = keys[half:]
+    o_ref[3 * half:] = scaled[half:]
+
+
+def build_block(keys, values, learn_rate):
+    rows, width = keys.shape
+    return pl.pallas_call(
+        _build_kernel,
+        out_shape=jax.ShapeDtypeStruct((2 * rows, width), keys.dtype),
+    )(keys, values, learn_rate.reshape(1, rows))
 
 
 def local_gather(keys, values, queries, learn_rate, w_gate, w_up, w_out):
@@ -134,11 +155,14 @@
         rows = keys.shape[0]
         halves = 2 if rows % 16 == 0 else 1
         half = rows // halves
-        scaled = (learn_rate[:, None] * values.astype(jnp.float32)).astype(jnp.bfloat16)
         width = keys.shape[1]
-        own = jnp.stack(
-            [keys.reshape(halves, half, width), scaled.reshape(halves, half, width)], axis=1
-        ).reshape(2 * rows, width)
+        if halves == 2 and rows % 128 == 0 and width % 128 == 0:
+            own = build_block(keys, values, learn_rate)
+        else:
+            scaled = (learn_rate[:, None] * values.astype(jnp.float32)).astype(jnp.bfloat16)
+            own = jnp.stack(
+                [keys.reshape(halves, half, width), scaled.reshape(halves, half, width)], axis=1
+            ).reshape(2 * rows, width)
         sib = lax.ppermute(own, axes, swap)
         total = add_grads(None, *split([own, sib], half), w_gate, w_up, w_out)
         arrived = [own, own]

time: 44.3 us -> 44.4 us (level)
  other arithmetic: 4.29 us -> 2.27 us
  Pallas kernels: 0 us -> 1.87 us
  local copies, waits for them, and re-layouts: 0.45 us -> 1.37 us
  waiting for transfers between devices: 12 us -> 11.3 us
    pallas_call x0 -> x1, Pallas kernels: none -> 1.87 us  [build_block(): pl.pallas_call(_build_kernel, out_shape=jax.ShapeDtypeStruct((2 * rows, w...]
    convert_element_type x1 -> x0, other arithmetic: 1.08 us -> none  [local_ring(): (learn_rate[:, None] * values.astype(jnp.float32)).astype(jnp.bfloat16)]
    slice x5, local copies, waits for them, and re-layouts: 0.08 us -> 1.07 us  [split(): keys_parts.append(ch[2 * j * half:(2 * j + 1) * half])]
    another operation x1 -> x0, other arithmetic: 0.94 us -> none  [local_ring(): jnp.stack([keys.reshape(halves, half, width), scaled.reshape(halves, half...]
  transfers between devices with their start and end apart: 17 -> 17, of which waited for: 9 -> 8; matrix products, arithmetic and copies ran while one was open for 32% -> 34% of each run, Pallas kernels for 0% -> 0%
where the time goes in v14:
time: 44.4 us; the launch traced here: 44.2 us
  matrix products  15.7 us (35%)
  waiting for transfers between devices  11.3 us (25%)
  starting transfers between devices  11.2 us (25%)
  other arithmetic  2.27 us (5%)
  Pallas kernels  1.87 us (4%)
  local copies, waits for them, and re-layouts  1.37 us (3%)
  between operations  0.51 us (1%)
    ppermute x3, waiting for transfers between devices, local_ring(): lax.ppermute(arrived[0], axes, cw_perm)  9.81 us
    ppermute x3, starting transfers between devices, local_ring(): lax.ppermute(arrived[0], axes, cw_perm)  6.69 us
    dot_general x6, matrix products, gradients(): lax.dot_general(keys, both_grads, contract_first, preferred_element_type=...  3.75 us
    dot_general x6, matrix products, gradients(): lax.dot_general(scaled, w_out, contract_last, preferred_element_type=jnp....  3.51 us
    dot_general x6, matrix products, gradients(): lax.dot_general(activation, scaled, contract_first, preferred_element_typ...  2.65 us
    dot_general x6, matrix products, gradients(): gate_pre = jnp.dot(keys, w_gate, preferred_element_type=jnp.float32)  2.31 us
    dot_general x6, matrix products, gradients(): up_pre = jnp.dot(keys, w_up, preferred_element_type=jnp.float32)  2.19 us
    ppermute x1, starting transfers between devices, local_ring(): lax.ppermute(arrived[0][:2 * half], axes, cw_perm)  1.88 us
  transfers between devices with their start and end apart: 17, of which 8 were waited for; matrix products, arithmetic and copies ran while one was open for 34% of the time, Pallas kernels for 0%

profile of v14, /device:TPU:0, one launch (start us, length us, event | category | flops | bytes accessed | tf_op | source)
XLA Modules:
  0.0 44.2 jit_solution(11920222825370402311)
XLA Ops:
  0.0 1.9 %shard_map.73 = bf16[256,512]{1,0:T(8,128)(2,1)} custom-call(bf16[128,512]{1,0:T(8,128)(2,1)} %k_ref.1, bf16[128,512]{1,0:T(8,128)(2,1)} %v_ref.1, f32[1,128]{1,0:T(1,128)} %bitcast.49), custom_call_target="tpu_custom_call" | custom-call | tf_op jit(solution)/shard_map/pallas_call | solution.py:63
  1.9 3.0 %collective-permute-start.1 = (bf16[256,512]{1,0:T(8,128)(2,1)}, bf16[256,512]{1,0:T(8,128)(2,1)S(1)}, u32[]{:S(2)}, u32[]{:S(2)}) collective-permute-start(bf16[256,512]{1,0:T(8,128)(2,1)} %shard_map.73), channel_id=1, source_target_pairs={{0,4},{1,5},{4,8},{5,9},{8,12},{9,13},{12,14},{13,15},{14,10},{15,... | collective-permute-start | bytes 786440 | tf_op jit(solution)/shard_map/ppermute | solution.py:177
  4.9 1.2 %fusion.4 = f32[512]{0:T(512)S(1)} fusion(bf16[512,512]{1,0:T(8,128)(2,1)} %param.13), kind=kLoop, calls=%fused_computation.18 | loop fusion | flops 785920 | bytes 526336 | tf_op jit(solution)/shard_map/reduce_sum | solution.py:19
  6.1 1.0 %fusion.83 = (bf16[64,512]{1,0:T(8,128)(2,1)S(1)}, bf16[64,512]{1,0:T(8,128)(2,1)S(1)}, bf16[64,512]{1,0:T(8,128)(2,1)S(1)}, bf16[64,512]{1,0:T(8,128)(2,1)S(1)}) fusion(bf16[256,512]{1,0:T(8,128)(2,1)} %shard_map.73), kind=kLoop, calls=%fused_computation.176 | loop fusion | bytes 524288 | tf_op jit(solution)/shard_map/slice | solution.py:149
  7.8 0.5 %multiply_convert_fusion.17 = (bf16[256,512]{1,0:T(8,128)(2,1)S(1)}, bf16[256,512]{1,0:T(8,128)(2,1)S(1)}) fusion(f32[256,512]{1,0:T(8,128)S(1)} %fusion.81, f32[256,512]{1,0:T(8,128)S(1)} %fusion.82, bf16[512,512]{1,0:T(8,128)(2,1)S(1)} %copy-done.3, bf16[64,512]{1,0:T(8,128)(2,1)S(1)} %get-tuple-element.74, bf16[64,512]{1,0:T(8,128)(2,1)S(1)} %get-tuple-element.75, ...), kind=kOutput, calls=%fused_computation.57 | convolution fusion | flops 136970240 | bytes 2359296 | tf_op jit(solution)/shard_map/dot_general | solution.py:32
  8.3 0.5 %fusion.19 = f32[512,1024]{1,0:T(8,128)S(1)} fusion(bf16[256,512]{1,0:T(8,128)(2,1)S(1)} %get-tuple-element.32, bf16[256,512]{1,0:T(8,128)(2,1)S(1)} %get-tuple-element.31, bf16[64,512]{1,0:T(8,128)(2,1)S(1)} %get-tuple-element.76, bf16[64,512]{1,0:T(8,128)(2,1)S(1)} %get-tuple-element.73, bf16[64,512]{1,0:T(8,128)(2,1)S(1)} %get-tuple-element.72, ...), kind=kOutput, calls=%fused_computation.51 | convolution fusion | flops 270532608 | bytes 2883584 | tf_op jit(solution)/shard_map/dot_general | solution.py:37
  8.8 2.6 %collective-permute-done.1 = bf16[256,512]{1,0:T(8,128)(2,1)S(1)} collective-permute-done((bf16[256,512]{1,0:T(8,128)(2,1)}, bf16[256,512]{1,0:T(8,128)(2,1)S(1)}, u32[]{:S(2)}, u32[]{:S(2)}) %collective-permute-start.1) | collective-permute-done | bytes 262176 | tf_op jit(solution)/shard_map/ppermute | solution.py:177
  11.3 1.8 %collective-permute-start.5 = (bf16[256,512]{1,0:T(8,128)(2,1)S(1)}, bf16[256,512]{1,0:T(8,128)(2,1)S(1)}, u32[]{:S(2)}, u32[]{:S(2)}) collective-permute-start(bf16[256,512]{1,0:T(8,128)(2,1)S(1)} %collective-permute-done.1), channel_id=1, source_target_pairs={{0,4},{1,5},{4,8},{5,9},{8,12},{9,13},{12,14},{13,15},{14,10},{15,... | collective-permute-start | bytes 786440 | tf_op jit(solution)/shard_map/ppermute | solution.py:177
  14.2 0.6 %collective-permute-done.4 = bf16[256,512]{1,0:T(8,128)(2,1)S(1)} collective-permute-done((bf16[256,512]{1,0:T(8,128)(2,1)S(1)}, bf16[256,512]{1,0:T(8,128)(2,1)S(1)}, u32[]{:S(2)}, u32[]{:S(2)}) %collective-permute-start.4) | collective-permute-done | bytes 262176 | tf_op jit(solution)/shard_map/ppermute | solution.py:182
  14.8 0.5 %fusion.89 = f32[512,512]{0,1:T(8,128)S(1)} fusion(bf16[512,512]{1,0:T(8,128)(2,1)S(1)} %get-tuple-element.54, bf16[512,512]{1,0:T(8,128)(2,1)S(1)} %copy-done.1), kind=kOutput, calls=%fused_computation.182 | convolution fusion | flops 268435456 | bytes 2097152 | tf_op jit(solution)/shard_map/dot_general | solution.py:31
  15.3 0.5 %fusion.90 = f32[512,512]{0,1:T(8,128)S(1)} fusion(bf16[512,512]{1,0:T(8,128)(2,1)S(1)} %get-tuple-element.54, bf16[512,512]{1,0:T(8,128)(2,1)S(1)} %copy-done.2), kind=kOutput, calls=%fused_computation.183 | convolution fusion | flops 268435456 | bytes 2097152 | tf_op jit(solution)/shard_map/dot_general | solution.py:30
  15.8 0.8 %multiply_convert_fusion.11 = (bf16[512,512]{0,1:T(8,128)(2,1)S(1)}, bf16[512,512]{0,1:T(8,128)(2,1)S(1)}) fusion(f32[512,512]{0,1:T(8,128)S(1)} %fusion.90, f32[512,512]{0,1:T(8,128)S(1)} %fusion.89, bf16[512,512]{1,0:T(8,128)(2,1)S(1)} %get-tuple-element.53, bf16[512,512]{1,0:T(8,128)(2,1)S(1)} %copy-done.3), kind=kOutput, calls=%fused_computation.48 | convolution fusion | flops 271843328 | bytes 4194304 | tf_op jit(solution)/shard_map/dot_general | solution.py:32
  17.1 3.0 %collective-permute-done.5 = bf16[256,512]{1,0:T(8,128)(2,1)S(1)} collective-permute-done((bf16[256,512]{1,0:T(8,128)(2,1)S(1)}, bf16[256,512]{1,0:T(8,128)(2,1)S(1)}, u32[]{:S(2)}, u32[]{:S(2)}) %collective-permute-start.5) | collective-permute-done | bytes 262176 | tf_op jit(solution)/shard_map/ppermute | solution.py:177
  20.1 1.8 %collective-permute-start.9 = (bf16[256,512]{1,0:T(8,128)(2,1)S(1)}, bf16[256,512]{1,0:T(8,128)(2,1)S(1)}, u32[]{:S(2)}, u32[]{:S(2)}) collective-permute-start(bf16[256,512]{1,0:T(8,128)(2,1)S(1)} %collective-permute-done.5), channel_id=1, source_target_pairs={{0,4},{1,5},{4,8},{5,9},{8,12},{9,13},{12,14},{13,15},{14,10},{15,... | collective-permute-start | bytes 786440 | tf_op jit(solution)/shard_map/ppermute | solution.py:177
  22.5 0.8 %fusion.5 = f32[512,1024]{1,0:T(8,128)S(1)} fusion(bf16[512,512]{1,0:T(8,128)(2,1)S(1)} %get-tuple-element.54, bf16[512,512]{0,1:T(8,128)(2,1)S(1)} %get-tuple-element.28, bf16[512,512]{0,1:T(8,128)(2,1)S(1)} %get-tuple-element.27), kind=kOutput, calls=%fused_computation.19 | convolution fusion | flops 538968064 | bytes 3670016 | tf_op jit(solution)/shard_map/dot_general | solution.py:37
  23.5 0.5 %fusion.91 = f32[512,512]{0,1:T(8,128)S(1)} fusion(bf16[512,512]{1,0:T(8,128)(2,1)S(1)} %get-tuple-element.78, bf16[512,512]{1,0:T(8,128)(2,1)S(1)} %copy-done.1), kind=kOutput, calls=%fused_computation.184 | convolution fusion | flops 268435456 | bytes 2097152 | tf_op jit(solution)/shard_map/dot_general | solution.py:31
  24.0 0.5 %fusion.92 = f32[512,512]{0,1:T(8,128)S(1)} fusion(bf16[512,512]{1,0:T(8,128)(2,1)S(1)} %get-tuple-element.78, bf16[512,512]{1,0:T(8,128)(2,1)S(1)} %copy-done.2), kind=kOutput, calls=%fused_computation.185 | convolution fusion | flops 268435456 | bytes 2097152 | tf_op jit(solution)/shard_map/dot_general | solution.py:30
  24.5 4.3 %collective-permute-done.9 = bf16[256,512]{1,0:T(8,128)(2,1)S(1)} collective-permute-done((bf16[256,512]{1,0:T(8,128)(2,1)S(1)}, bf16[256,512]{1,0:T(8,128)(2,1)S(1)}, u32[]{:S(2)}, u32[]{:S(2)}) %collective-permute-start.9) | collective-permute-done | bytes 262176 | tf_op jit(solution)/shard_map/ppermute | solution.py:177
  28.8 1.9 %collective-permute-start.13 = (bf16[128,512]{1,0:T(8,128)(2,1)S(1)}, bf16[128,512]{1,0:T(8,128)(2,1)S(1)}, u32[]{:S(2)}, u32[]{:S(2)}) collective-permute-start(bf16[128,512]{1,0:T(8,128)(2,1)S(1)} %slice.328), channel_id=1, source_target_pairs={{0,4},{1,5},{4,8},{5,9},{8,12},{9,13},{12,14},{13,15},{14,10},{15,... | collective-permute-start | bytes 393224 | tf_op jit(solution)/shard_map/ppermute | solution.py:172
  30.7 0.8 %multiply_convert_fusion.9 = (bf16[512,512]{0,1:T(8,128)(2,1)S(1)}, bf16[512,512]{0,1:T(8,128)(2,1)S(1)}) fusion(f32[512,512]{0,1:T(8,128)S(1)} %fusion.92, f32[512,512]{0,1:T(8,128)S(1)} %fusion.91, bf16[512,512]{1,0:T(8,128)(2,1)S(1)} %get-tuple-element.77, bf16[512,512]{1,0:T(8,128)(2,1)S(1)} %copy-done.3), kind=kOutput, calls=%fused_computation.44 | convolution fusion | flops 271843328 | bytes 4194304 | tf_op jit(solution)/shard_map/dot_general | solution.py:32
  31.5 0.5 %convolution_add_fusion.1 = f32[512,512]{1,0:T(8,128)S(1)} fusion(f32[512,512]{1,0:T(8,128)S(1)} %convolution_add_fusion.2, bf16[512,512]{1,0:T(8,128)(2,1)S(1)} %get-tuple-element.77, f32[512,512]{0,1:T(8,128)S(1)} %fusion.91, f32[512,512]{0,1:T(8,128)S(1)} %fusion.92), kind=kOutput, calls=%fused_computation.3 | convolution fusion | flops 270270464 | bytes 4718592 | tf_op jit(solution)/shard_map/dot_general | solution.py:38
  32.5 0.5 %collective-permute-start.12 = (bf16[256,512]{1,0:T(8,128)(2,1)S(1)}, bf16[256,512]{1,0:T(8,128)(2,1)S(1)}, u32[]{:S(2)}, u32[]{:S(2)}) collective-permute-start(bf16[256,512]{1,0:T(8,128)(2,1)S(1)} %collective-permute-done.10), channel_id=1, source_target_pairs={{0,1},{1,0},{2,3},{3,2},{4,5},{5,4},{6,7},{7,6},{8,9},{9,8},{10,11... | collective-permute-start | bytes 786440 | tf_op jit(solution)/shard_map/ppermute | solution.py:182
  33.1 0.8 %fusion.9 = f32[512,1024]{1,0:T(8,128)S(1)} fusion(bf16[512,512]{1,0:T(8,128)(2,1)S(1)} %get-tuple-element.78, bf16[512,512]{0,1:T(8,128)(2,1)S(1)} %get-tuple-element.30, bf16[512,512]{0,1:T(8,128)(2,1)S(1)} %get-tuple-element.29), kind=kOutput, calls=%fused_computation.23 | convolution fusion | flops 538968064 | bytes 3670016 | tf_op jit(solution)/shard_map/dot_general | solution.py:37
  34.4 0.5 %fusion.93 = f32[512,512]{0,1:T(8,128)S(1)} fusion(bf16[512,512]{1,0:T(8,128)(2,1)S(1)} %get-tuple-element.38, bf16[512,512]{1,0:T(8,128)(2,1)S(1)} %copy-done.1), kind=kOutput, calls=%fused_computation.186 | convolution fusion | flops 268435456 | bytes 2097152 | tf_op jit(solution)/shard_map/dot_general | solution.py:31
  34.9 0.5 %fusion.94 = f32[512,512]{0,1:T(8,128)S(1)} fusion(bf16[512,512]{1,0:T(8,128)(2,1)S(1)} %get-tuple-element.38, bf16[512,512]{1,0:T(8,128)(2,1)S(1)} %copy-done.2), kind=kOutput, calls=%fused_computation.187 | convolution fusion | flops 268435456 | bytes 2097152 | tf_op jit(solution)/shard_map/dot_general | solution.py:30
  35.4 0.8 %multiply_convert_fusion.7 = (bf16[512,512]{0,1:T(8,128)(2,1)S(1)}, bf16[512,512]{0,1:T(8,128)(2,1)S(1)}) fusion(f32[512,512]{0,1:T(8,128)S(1)} %fusion.94, f32[512,512]{0,1:T(8,128)S(1)} %fusion.93, bf16[512,512]{1,0:T(8,128)(2,1)S(1)} %get-tuple-element.37, bf16[512,512]{1,0:T(8,128)(2,1)S(1)} %copy-done.3), kind=kOutput, calls=%fused_computation.40 | convolution fusion | flops 271843328 | bytes 4194304 | tf_op jit(solution)/shard_map/dot_general | solution.py:32
  36.2 0.8 %add_add_fusion.1 = f32[512,1024]{1,0:T(8,128)S(1)} fusion(f32[512,1024]{1,0:T(8,128)S(1)} %fusion.9, f32[512,1024]{1,0:T(8,128)S(1)} %fusion.19, f32[512,1024]{1,0:T(8,128)S(1)} %fusion.5, bf16[512,512]{1,0:T(8,128)(2,1)S(1)} %get-tuple-element.38, bf16[512,512]{0,1:T(8,128)(2,1)S(1)} %get-tuple-element.26, bf16[512,512]{0,1:T(8,128)(2,1)S(1)} %get-tuple-element.25), kind=kOutput, calls=%fused_computation.1 | convolution fusion | flops 540540928 | bytes 9961472 | tf_op jit(solution)/shard_map/dot_general | solution.py:37
  37.0 0.5 %convolution_add_fusion = f32[512,512]{1,0:T(8,128)S(1)} fusion(f32[512,512]{1,0:T(8,128)S(1)} %convolution_add_fusion.1, bf16[512,512]{1,0:T(8,128)(2,1)S(1)} %get-tuple-element.37, f32[512,512]{0,1:T(8,128)S(1)} %fusion.93, f32[512,512]{0,1:T(8,128)S(1)} %fusion.94), kind=kOutput, calls=%fused_computation.2 | convolution fusion | flops 270270464 | bytes 4718592 | tf_op jit(solution)/shard_map/dot_general | solution.py:38
  40.7 0.5 %add_add_fusion = f32[512,1024]{1,0:T(8,128)S(1)} fusion(f32[512,1024]{1,0:T(8,128)S(1)} %add_add_fusion.1, f32[512,1024]{1,0:T(8,128)S(1)} %fusion.25, bf16[128,512]{1,0:T(8,128)(2,1)S(1)} %get-tuple-element.34, bf16[128,512]{1,0:T(8,128)(2,1)S(1)} %get-tuple-element.33, bf16[64,512]{1,0:T(8,128)(2,1)S(1)} %get-tuple-element.95, ...), kind=kOutput, calls=%fused_computation | convolution fusion | flops 136052736 | bytes 6684672 | tf_op jit(solution)/shard_map/dot_general | solution.py:37
  41.3 0.5 %multiply_reduce_fusion.1 = (f32[512]{0:T(512)S(1)}, f32[512]{0:T(512)S(1)}, f32[512]{0:T(512)S(1)}, f32[512]{0:T(512)S(1)}) fusion(f32[512,1024]{1,0:T(8,128)S(1)} %add_add_fusion, bf16[512,512]{1,0:T(8,128)(2,1)S(1)} %copy-done.1, bf16[512,512]{1,0:T(8,128)(2,1)S(1)} %copy-done.2), kind=kLoop, calls=%fused_computation.33 | loop fusion | flops 3143680 | bytes 3153920 | tf_op jit(solution)/shard_map/reduce_sum | solution.py:20
  41.8 0.5 %multiply_reduce_fusion = (f32[512]{0:T(512)S(1)}, f32[512,512]{1,0:T(8,128)S(1)}) fusion(bf16[64,512]{1,0:T(8,128)(2,1)S(1)} %get-tuple-element.96, bf16[64,512]{1,0:T(8,128)(2,1)S(1)} %get-tuple-element.94, f32[128,512]{1,0:T(8,128)S(1)} %fusion.55, f32[128,512]{1,0:T(8,128)S(1)} %fusion.54, f32[512,512]{1,0:T(8,128)S(1)} %convolution_add_fusion, ...), kind=kOutput, calls=%fused_computation.31 | convolution fusion | flops 69336576 | bytes 4327424 | tf_op jit(solution)/shard_map/dot_general | solution.py:38
  43.1 1.1 %convolution_convert_fusion = bf16[128,512]{1,0:T(8,128)(2,1)} fusion(bf16[512,512]{1,0:T(8,128)(2,1)S(1)} %multiply_convert_fusion, bf16[128,512]{1,0:T(8,128)(2,1)S(1)} %copy-done, bf16[512,512]{1,0:T(8,128)(2,1)S(1)} %get-tuple-element.17, f32[128,512]{1,0:T(8,128)S(1)} %convolution_bitcast_fusion.1), kind=kOutput, calls=%fused_computation.15 | convolution fusion | flops 134676480 | bytes 1572864 | tf_op jit(solution)/shard_map/dot_general | solution.py:46
  (81 shorter events, 8.0 us)
Async XLA Ops:
  0.0 42.9 %copy-start = (bf16[128,512]{1,0:T(8,128)(2,1)S(1)}, bf16[128,512]{1,0:T(8,128)(2,1)}, u32[]{:S(2)}) copy-start(bf16[128,512]{1,0:T(8,128)(2,1)} %param.9) | copy-start | bytes 393220
  0.0 7.2 %copy-start.2 = (bf16[512,512]{1,0:T(8,128)(2,1)S(1)}, bf16[512,512]{1,0:T(8,128)(2,1)}, u32[]{:S(2)}) copy-start(bf16[512,512]{1,0:T(8,128)(2,1)} %param.11) | copy-start | bytes 1572868
  0.0 7.5 %copy-start.1 = (bf16[512,512]{1,0:T(8,128)(2,1)S(1)}, bf16[512,512]{1,0:T(8,128)(2,1)}, u32[]{:S(2)}) copy-start(bf16[512,512]{1,0:T(8,128)(2,1)} %param.12) | copy-start | bytes 1572868
  1.9 9.5 %collective-permute-start.1 = (bf16[256,512]{1,0:T(8,128)(2,1)}, bf16[256,512]{1,0:T(8,128)(2,1)S(1)}, u32[]{:S(2)}, u32[]{:S(2)}) collective-permute-start(bf16[256,512]{1,0:T(8,128)(2,1)} %shard_map.73), channel_id=1, source_target_pairs={{0,4},{1,5},{4,8},{5,9},{8,12},{9,13},{12,14},{13,15},{14,10},{15,... | collective-permute-start | bytes 786440 | tf_op jit(solution)/shard_map/ppermute | solution.py:177
  4.9 8.3 %collective-permute-start.2 = (bf16[256,512]{1,0:T(8,128)(2,1)}, bf16[256,512]{1,0:T(8,128)(2,1)S(1)}, u32[]{:S(2)}, u32[]{:S(2)}) collective-permute-start(bf16[256,512]{1,0:T(8,128)(2,1)} %shard_map.73), channel_id=1, source_target_pairs={{0,2},{1,3},{4,0},{5,1},{8,4},{9,5},{12,8},{13,9},{14,12},{15,13},... | collective-permute-start | bytes 786440 | tf_op jit(solution)/shard_map/ppermute | solution.py:178
  4.9 2.3 %collective-permute-start = (bf16[256,512]{1,0:T(8,128)(2,1)}, bf16[256,512]{1,0:T(8,128)(2,1)S(1)}, u32[]{:S(2)}, u32[]{:S(2)}) collective-permute-start(bf16[256,512]{1,0:T(8,128)(2,1)} %shard_map.73), channel_id=1, source_target_pairs={{0,1},{1,0},{2,3},{3,2},{4,5},{5,4},{6,7},{7,6},{8,9},{9,8},{10,11... | collective-permute-start | bytes 786440 | tf_op jit(solution)/shard_map/ppermute | solution.py:166
  6.1 1.7 %copy-start.3 = (bf16[512,512]{1,0:T(8,128)(2,1)S(1)}, bf16[512,512]{1,0:T(8,128)(2,1)}, u32[]{:S(2)}) copy-start(bf16[512,512]{1,0:T(8,128)(2,1)} %param.13) | copy-start | bytes 1572868
  11.3 2.8 %collective-permute-start.3 = (bf16[256,512]{1,0:T(8,128)(2,1)S(1)}, bf16[256,512]{1,0:T(8,128)(2,1)S(1)}, u32[]{:S(2)}, u32[]{:S(2)}) collective-permute-start(bf16[256,512]{1,0:T(8,128)(2,1)S(1)} %collective-permute-done.1), channel_id=1, source_target_pairs={{0,1},{1,0},{2,3},{3,2},{4,5},{5,4},{6,7},{7,6},{8,9},{9,8},{10,11... | collective-permute-start | bytes 786440 | tf_op jit(solution)/shard_map/ppermute | solution.py:182
  11.3 8.7 %collective-permute-start.5 = (bf16[256,512]{1,0:T(8,128)(2,1)S(1)}, bf16[256,512]{1,0:T(8,128)(2,1)S(1)}, u32[]{:S(2)}, u32[]{:S(2)}) collective-permute-start(bf16[256,512]{1,0:T(8,128)(2,1)S(1)} %collective-permute-done.1), channel_id=1, source_target_pairs={{0,4},{1,5},{4,8},{5,9},{8,12},{9,13},{12,14},{13,15},{14,10},{15,... | collective-permute-start | bytes 786440 | tf_op jit(solution)/shard_map/ppermute | solution.py:177
  13.2 1.6 %collective-permute-start.4 = (bf16[256,512]{1,0:T(8,128)(2,1)S(1)}, bf16[256,512]{1,0:T(8,128)(2,1)S(1)}, u32[]{:S(2)}, u32[]{:S(2)}) collective-permute-start(bf16[256,512]{1,0:T(8,128)(2,1)S(1)} %collective-permute-done.2), channel_id=1, source_target_pairs={{0,1},{1,0},{2,3},{3,2},{4,5},{5,4},{6,7},{7,6},{8,9},{9,8},{10,11... | collective-permute-start | bytes 786440 | tf_op jit(solution)/shard_map/ppermute | solution.py:182
  13.5 8.5 %collective-permute-start.6 = (bf16[256,512]{1,0:T(8,128)(2,1)S(1)}, bf16[256,512]{1,0:T(8,128)(2,1)S(1)}, u32[]{:S(2)}, u32[]{:S(2)}) collective-permute-start(bf16[256,512]{1,0:T(8,128)(2,1)S(1)} %collective-permute-done.2), channel_id=1, source_target_pairs={{0,2},{1,3},{4,0},{5,1},{8,4},{9,5},{12,8},{13,9},{14,12},{15,13},... | collective-permute-start | bytes 786440 | tf_op jit(solution)/shard_map/ppermute | solution.py:178
  20.1 3.2 %collective-permute-start.7 = (bf16[256,512]{1,0:T(8,128)(2,1)S(1)}, bf16[256,512]{1,0:T(8,128)(2,1)S(1)}, u32[]{:S(2)}, u32[]{:S(2)}) collective-permute-start(bf16[256,512]{1,0:T(8,128)(2,1)S(1)} %collective-permute-done.5), channel_id=1, source_target_pairs={{0,1},{1,0},{2,3},{3,2},{4,5},{5,4},{6,7},{7,6},{8,9},{9,8},{10,11... | collective-permute-start | bytes 786440 | tf_op jit(solution)/shard_map/ppermute | solution.py:182
  20.1 8.7 %collective-permute-start.9 = (bf16[256,512]{1,0:T(8,128)(2,1)S(1)}, bf16[256,512]{1,0:T(8,128)(2,1)S(1)}, u32[]{:S(2)}, u32[]{:S(2)}) collective-permute-start(bf16[256,512]{1,0:T(8,128)(2,1)S(1)} %collective-permute-done.5), channel_id=1, source_target_pairs={{0,4},{1,5},{4,8},{5,9},{8,12},{9,13},{12,14},{13,15},{14,10},{15,... | collective-permute-start | bytes 786440 | tf_op jit(solution)/shard_map/ppermute | solution.py:177
  22.0 1.5 %collective-permute-start.8 = (bf16[256,512]{1,0:T(8,128)(2,1)S(1)}, bf16[256,512]{1,0:T(8,128)(2,1)S(1)}, u32[]{:S(2)}, u32[]{:S(2)}) collective-permute-start(bf16[256,512]{1,0:T(8,128)(2,1)S(1)} %collective-permute-done.6), channel_id=1, source_target_pairs={{0,1},{1,0},{2,3},{3,2},{4,5},{5,4},{6,7},{7,6},{8,9},{9,8},{10,11... | collective-permute-start | bytes 786440 | tf_op jit(solution)/shard_map/ppermute | solution.py:182
  22.2 9.7 %collective-permute-start.10 = (bf16[256,512]{1,0:T(8,128)(2,1)S(1)}, bf16[256,512]{1,0:T(8,128)(2,1)S(1)}, u32[]{:S(2)}, u32[]{:S(2)}) collective-permute-start(bf16[256,512]{1,0:T(8,128)(2,1)S(1)} %collective-permute-done.6), channel_id=1, source_target_pairs={{0,2},{1,3},{4,0},{5,1},{8,4},{9,5},{12,8},{13,9},{14,12},{15,13},... | collective-permute-start | bytes 786440 | tf_op jit(solution)/shard_map/ppermute | solution.py:178
  28.8 8.7 %collective-permute-start.13 = (bf16[128,512]{1,0:T(8,128)(2,1)S(1)}, bf16[128,512]{1,0:T(8,128)(2,1)S(1)}, u32[]{:S(2)}, u32[]{:S(2)}) collective-permute-start(bf16[128,512]{1,0:T(8,128)(2,1)S(1)} %slice.328), channel_id=1, source_target_pairs={{0,4},{1,5},{4,8},{5,9},{8,12},{9,13},{12,14},{13,15},{14,10},{15,... | collective-permute-start | bytes 393224 | tf_op jit(solution)/shard_map/ppermute | solution.py:172
  32.0 5.5 %collective-permute-start.14 = (bf16[128,512]{1,0:T(8,128)(2,1)S(1)}, bf16[128,512]{1,0:T(8,128)(2,1)S(1)}, u32[]{:S(2)}, u32[]{:S(2)}) collective-permute-start(bf16[128,512]{1,0:T(8,128)(2,1)S(1)} %slice.329), channel_id=1, source_target_pairs={{0,2},{1,3},{4,0},{5,1},{8,4},{9,5},{12,8},{13,9},{14,12},{15,13},... | collective-permute-start | bytes 393224 | tf_op jit(solution)/shard_map/ppermute | solution.py:173
  32.4 1.6 %collective-permute-start.11 = (bf16[256,512]{1,0:T(8,128)(2,1)S(1)}, bf16[256,512]{1,0:T(8,128)(2,1)S(1)}, u32[]{:S(2)}, u32[]{:S(2)}) collective-permute-start(bf16[256,512]{1,0:T(8,128)(2,1)S(1)} %collective-permute-done.9), channel_id=1, source_target_pairs={{0,1},{1,0},{2,3},{3,2},{4,5},{5,4},{6,7},{7,6},{8,9},{9,8},{10,11... | collective-permute-start | bytes 786440 | tf_op jit(solution)/shard_map/ppermute | solution.py:182
  32.5 1.9 %collective-permute-start.12 = (bf16[256,512]{1,0:T(8,128)(2,1)S(1)}, bf16[256,512]{1,0:T(8,128)(2,1)S(1)}, u32[]{:S(2)}, u32[]{:S(2)}) collective-permute-start(bf16[256,512]{1,0:T(8,128)(2,1)S(1)} %collective-permute-done.10), channel_id=1, source_target_pairs={{0,1},{1,0},{2,3},{3,2},{4,5},{5,4},{6,7},{7,6},{8,9},{9,8},{10,11... | collective-permute-start | bytes 786440 | tf_op jit(solution)/shard_map/ppermute | solution.py:182
  37.5 2.4 %collective-permute-start.15 = (bf16[128,512]{1,0:T(8,128)(2,1)S(1)}, bf16[128,512]{1,0:T(8,128)(2,1)S(1)}, u32[]{:S(2)}, u32[]{:S(2)}) collective-permute-start(bf16[128,512]{1,0:T(8,128)(2,1)S(1)} %collective-permute-done.13), channel_id=1, source_target_pairs={{0,1},{1,0},{2,3},{3,2},{4,5},{5,4},{6,7},{7,6},{8,9},{9,8},{10,11... | collective-permute-start | bytes 393224 | tf_op jit(solution)/shard_map/ppermute | solution.py:182
  37.7 2.2 %collective-permute-start.16 = (bf16[128,512]{1,0:T(8,128)(2,1)S(1)}, bf16[128,512]{1,0:T(8,128)(2,1)S(1)}, u32[]{:S(2)}, u32[]{:S(2)}) collective-permute-start(bf16[128,512]{1,0:T(8,128)(2,1)S(1)} %collective-permute-done.14), channel_id=1, source_target_pairs={{0,1},{1,0},{2,3},{3,2},{4,5},{5,4},{6,7},{7,6},{8,9},{9,8},{10,11... | collective-permute-start | bytes 393224 | tf_op jit(solution)/shard_map/ppermute | solution.py:182

commit v15 on v12

--- a/solution.py
+++ b/solution.py
@@ -41,7 +41,7 @@
 def apply(queries, full_gate, full_up, full_out_w):
     q_gate = jnp.dot(queries, full_gate, preferred_element_type=jnp.float32)
     q_up = jnp.dot(queries, full_up, preferred_element_type=jnp.float32)
-    q_act = (jax.nn.silu(q_gate) * q_up).astype(jnp.bfloat16)
+    q_act = lax.optimization_barrier((jax.nn.silu(q_gate) * q_up).astype(jnp.bfloat16))
     return jnp.dot(q_act, full_out_w, preferred_element_type=jnp.float32).astype(jnp.bfloat16)
 
 

time: 44.3 us -> 44.4 us (level)
  no operation moved by 1% of the time
where the time goes in v15:
time: 44.4 us; the launch traced here: 44.2 us
  matrix products  15.7 us (35%)
  waiting for transfers between devices  12 us (27%)
  starting transfers between devices  11.2 us (25%)
  other arithmetic  4.29 us (10%)
  between operations  0.51 us (1%)
  local copies, waits for them, and re-layouts  0.45 us (1%)
    ppermute x3, waiting for transfers between devices, local_ring(): lax.ppermute(arrived[0], axes, cw_perm)  10.3 us
    ppermute x3, starting transfers between devices, local_ring(): lax.ppermute(arrived[0], axes, cw_perm)  6.73 us
    dot_general x6, matrix products, gradients(): lax.dot_general(keys, both_grads, contract_first, preferred_element_type=...  3.67 us
    dot_general x6, matrix products, gradients(): lax.dot_general(scaled, w_out, contract_last, preferred_element_type=jnp....  3.51 us
    dot_general x6, matrix products, gradients(): lax.dot_general(activation, scaled, contract_first, preferred_element_typ...  2.64 us
    dot_general x6, matrix products, gradients(): gate_pre = jnp.dot(keys, w_gate, preferred_element_type=jnp.float32)  2.31 us
    dot_general x6, matrix products, gradients(): up_pre = jnp.dot(keys, w_up, preferred_element_type=jnp.float32)  2.19 us
    ppermute x1, starting transfers between devices, local_ring(): lax.ppermute(arrived[0][:2 * half], axes, cw_perm)  1.88 us
  transfers between devices with their start and end apart: 17, of which 9 were waited for; matrix products, arithmetic and copies ran while one was open for 32% of the time, Pallas kernels for 0%

profile of v15, /device:TPU:0, one launch (start us, length us, event | category | flops | bytes accessed | tf_op | source)
XLA Modules:
  0.0 44.2 jit_solution(4554982062824956998)
XLA Ops:
  0.0 1.1 %multiply_convert_fusion.25 = bf16[128,512]{1,0:T(8,128)(2,1)S(1)} fusion(bf16[128,512]{1,0:T(8,128)(2,1)} %param.8, f32[128]{0:T(128)} %param.10), kind=kLoop, calls=%fused_computation.82 | loop fusion | flops 196608 | bytes 262656 | tf_op jit(solution)/shard_map/convert_element_type | solution.py:137
  1.1 0.9 %pad_maximum_fusion = bf16[2,2,64,512]{3,2,1,0:T(8,128)(2,1)S(1)} fusion(bf16[2,1,64,512]{3,2,1,0:T(8,128)(2,1)S(1)} %bitcast.54, bf16[2,1,64,512]{3,2,1,0:T(8,128)(2,1)} %bitcast.55), kind=kLoop, calls=%fused_computation.61 | loop fusion | flops 131072 | bytes 524288 | tf_op jit(solution)/shard_map/stack | solution.py:139
  2.0 3.1 %collective-permute-start.1 = (bf16[256,512]{1,0:T(8,128)(2,1)S(1)}, bf16[256,512]{1,0:T(8,128)(2,1)S(1)}, u32[]{:S(2)}, u32[]{:S(2)}) collective-permute-start(bf16[256,512]{1,0:T(8,128)(2,1)S(1)} %bitcast.50), channel_id=1, source_target_pairs={{0,4},{1,5},{4,8},{5,9},{8,12},{9,13},{12,14},{13,15},{14,10},{15,... | collective-permute-start | bytes 786440 | tf_op jit(solution)/shard_map/ppermute | solution.py:153
  5.1 1.2 %fusion.4 = f32[512]{0:T(512)S(1)} fusion(bf16[512,512]{1,0:T(8,128)(2,1)} %param.13), kind=kLoop, calls=%fused_computation.18 | loop fusion | flops 785920 | bytes 526336 | tf_op jit(solution)/shard_map/reduce_sum | solution.py:18
  7.4 0.5 %multiply_convert_fusion.17 = (bf16[256,512]{1,0:T(8,128)(2,1)S(1)}, bf16[256,512]{1,0:T(8,128)(2,1)S(1)}) fusion(f32[256,512]{1,0:T(8,128)S(1)} %fusion.74, f32[256,512]{1,0:T(8,128)S(1)} %fusion.75, bf16[512,512]{1,0:T(8,128)(2,1)S(1)} %copy-done.3, bf16[64,512]{1,0:T(8,128)(2,1)S(1)} %get-tuple-element.74, bf16[64,512]{1,0:T(8,128)(2,1)S(1)} %get-tuple-element.75, ...), kind=kOutput, calls=%fused_computation.57 | convolution fusion | flops 136970240 | bytes 2359296 | tf_op jit(solution)/shard_map/dot_general | solution.py:31
  8.3 3.0 %collective-permute-done.1 = bf16[256,512]{1,0:T(8,128)(2,1)S(1)} collective-permute-done((bf16[256,512]{1,0:T(8,128)(2,1)S(1)}, bf16[256,512]{1,0:T(8,128)(2,1)S(1)}, u32[]{:S(2)}, u32[]{:S(2)}) %collective-permute-start.1) | collective-permute-done | bytes 262176 | tf_op jit(solution)/shard_map/ppermute | solution.py:153
  11.3 1.8 %collective-permute-start.5 = (bf16[256,512]{1,0:T(8,128)(2,1)S(1)}, bf16[256,512]{1,0:T(8,128)(2,1)S(1)}, u32[]{:S(2)}, u32[]{:S(2)}) collective-permute-start(bf16[256,512]{1,0:T(8,128)(2,1)S(1)} %collective-permute-done.1), channel_id=1, source_target_pairs={{0,4},{1,5},{4,8},{5,9},{8,12},{9,13},{12,14},{13,15},{14,10},{15,... | collective-permute-start | bytes 786440 | tf_op jit(solution)/shard_map/ppermute | solution.py:153
  14.2 0.6 %collective-permute-done.4 = bf16[256,512]{1,0:T(8,128)(2,1)S(1)} collective-permute-done((bf16[256,512]{1,0:T(8,128)(2,1)S(1)}, bf16[256,512]{1,0:T(8,128)(2,1)S(1)}, u32[]{:S(2)}, u32[]{:S(2)}) %collective-permute-start.4) | collective-permute-done | bytes 262176 | tf_op jit(solution)/shard_map/ppermute | solution.py:158
  14.8 0.5 %fusion.82 = f32[512,512]{0,1:T(8,128)S(1)} fusion(bf16[512,512]{1,0:T(8,128)(2,1)S(1)} %get-tuple-element.54, bf16[512,512]{1,0:T(8,128)(2,1)S(1)} %copy-done.1), kind=kOutput, calls=%fused_computation.177 | convolution fusion | flops 268435456 | bytes 2097152 | tf_op jit(solution)/shard_map/dot_general | solution.py:30
  15.3 0.5 %fusion.83 = f32[512,512]{0,1:T(8,128)S(1)} fusion(bf16[512,512]{1,0:T(8,128)(2,1)S(1)} %get-tuple-element.54, bf16[512,512]{1,0:T(8,128)(2,1)S(1)} %copy-done.2), kind=kOutput, calls=%fused_computation.178 | convolution fusion | flops 268435456 | bytes 2097152 | tf_op jit(solution)/shard_map/dot_general | solution.py:29
  15.8 0.8 %multiply_convert_fusion.11 = (bf16[512,512]{0,1:T(8,128)(2,1)S(1)}, bf16[512,512]{0,1:T(8,128)(2,1)S(1)}) fusion(f32[512,512]{0,1:T(8,128)S(1)} %fusion.83, f32[512,512]{0,1:T(8,128)S(1)} %fusion.82, bf16[512,512]{1,0:T(8,128)(2,1)S(1)} %get-tuple-element.53, bf16[512,512]{1,0:T(8,128)(2,1)S(1)} %copy-done.3), kind=kOutput, calls=%fused_computation.48 | convolution fusion | flops 271843328 | bytes 4194304 | tf_op jit(solution)/shard_map/dot_general | solution.py:31
  16.6 0.5 %convolution_add_fusion.2 = f32[512,512]{1,0:T(8,128)S(1)} fusion(f32[512,512]{1,0:T(8,128)S(1)} %fusion.24, bf16[512,512]{1,0:T(8,128)(2,1)S(1)} %get-tuple-element.53, f32[512,512]{0,1:T(8,128)S(1)} %fusion.82, f32[512,512]{0,1:T(8,128)S(1)} %fusion.83), kind=kOutput, calls=%fused_computation.4 | convolution fusion | flops 270270464 | bytes 4718592 | tf_op jit(solution)/shard_map/dot_general | solution.py:37
  17.1 3.0 %collective-permute-done.5 = bf16[256,512]{1,0:T(8,128)(2,1)S(1)} collective-permute-done((bf16[256,512]{1,0:T(8,128)(2,1)S(1)}, bf16[256,512]{1,0:T(8,128)(2,1)S(1)}, u32[]{:S(2)}, u32[]{:S(2)}) %collective-permute-start.5) | collective-permute-done | bytes 262176 | tf_op jit(solution)/shard_map/ppermute | solution.py:153
  20.1 1.8 %collective-permute-start.9 = (bf16[256,512]{1,0:T(8,128)(2,1)S(1)}, bf16[256,512]{1,0:T(8,128)(2,1)S(1)}, u32[]{:S(2)}, u32[]{:S(2)}) collective-permute-start(bf16[256,512]{1,0:T(8,128)(2,1)S(1)} %collective-permute-done.5), channel_id=1, source_target_pairs={{0,4},{1,5},{4,8},{5,9},{8,12},{9,13},{12,14},{13,15},{14,10},{15,... | collective-permute-start | bytes 786440 | tf_op jit(solution)/shard_map/ppermute | solution.py:153
  22.5 0.8 %fusion.5 = f32[512,1024]{1,0:T(8,128)S(1)} fusion(bf16[512,512]{1,0:T(8,128)(2,1)S(1)} %get-tuple-element.54, bf16[512,512]{0,1:T(8,128)(2,1)S(1)} %get-tuple-element.28, bf16[512,512]{0,1:T(8,128)(2,1)S(1)} %get-tuple-element.27), kind=kOutput, calls=%fused_computation.19 | convolution fusion | flops 538968064 | bytes 3670016 | tf_op jit(solution)/shard_map/dot_general | solution.py:36
  23.5 0.5 %fusion.84 = f32[512,512]{0,1:T(8,128)S(1)} fusion(bf16[512,512]{1,0:T(8,128)(2,1)S(1)} %get-tuple-element.78, bf16[512,512]{1,0:T(8,128)(2,1)S(1)} %copy-done.1), kind=kOutput, calls=%fused_computation.179 | convolution fusion | flops 268435456 | bytes 2097152 | tf_op jit(solution)/shard_map/dot_general | solution.py:30
  24.0 0.5 %fusion.85 = f32[512,512]{0,1:T(8,128)S(1)} fusion(bf16[512,512]{1,0:T(8,128)(2,1)S(1)} %get-tuple-element.78, bf16[512,512]{1,0:T(8,128)(2,1)S(1)} %copy-done.2), kind=kOutput, calls=%fused_computation.180 | convolution fusion | flops 268435456 | bytes 2097152 | tf_op jit(solution)/shard_map/dot_general | solution.py:29
  24.5 4.3 %collective-permute-done.9 = bf16[256,512]{1,0:T(8,128)(2,1)S(1)} collective-permute-done((bf16[256,512]{1,0:T(8,128)(2,1)S(1)}, bf16[256,512]{1,0:T(8,128)(2,1)S(1)}, u32[]{:S(2)}, u32[]{:S(2)}) %collective-permute-start.9) | collective-permute-done | bytes 262176 | tf_op jit(solution)/shard_map/ppermute | solution.py:153
  28.8 1.9 %collective-permute-start.13 = (bf16[128,512]{1,0:T(8,128)(2,1)S(1)}, bf16[128,512]{1,0:T(8,128)(2,1)S(1)}, u32[]{:S(2)}, u32[]{:S(2)}) collective-permute-start(bf16[128,512]{1,0:T(8,128)(2,1)S(1)} %slice.328), channel_id=1, source_target_pairs={{0,4},{1,5},{4,8},{5,9},{8,12},{9,13},{12,14},{13,15},{14,10},{15,... | collective-permute-start | bytes 393224 | tf_op jit(solution)/shard_map/ppermute | solution.py:148
  30.7 0.8 %multiply_convert_fusion.9 = (bf16[512,512]{0,1:T(8,128)(2,1)S(1)}, bf16[512,512]{0,1:T(8,128)(2,1)S(1)}) fusion(f32[512,512]{0,1:T(8,128)S(1)} %fusion.85, f32[512,512]{0,1:T(8,128)S(1)} %fusion.84, bf16[512,512]{1,0:T(8,128)(2,1)S(1)} %get-tuple-element.77, bf16[512,512]{1,0:T(8,128)(2,1)S(1)} %copy-done.3), kind=kOutput, calls=%fused_computation.44 | convolution fusion | flops 271843328 | bytes 4194304 | tf_op jit(solution)/shard_map/dot_general | solution.py:31
  31.5 0.5 %convolution_add_fusion.1 = f32[512,512]{1,0:T(8,128)S(1)} fusion(f32[512,512]{1,0:T(8,128)S(1)} %convolution_add_fusion.2, bf16[512,512]{1,0:T(8,128)(2,1)S(1)} %get-tuple-element.77, f32[512,512]{0,1:T(8,128)S(1)} %fusion.84, f32[512,512]{0,1:T(8,128)S(1)} %fusion.85), kind=kOutput, calls=%fused_computation.3 | convolution fusion | flops 270270464 | bytes 4718592 | tf_op jit(solution)/shard_map/dot_general | solution.py:37
  32.5 0.5 %collective-permute-start.12 = (bf16[256,512]{1,0:T(8,128)(2,1)S(1)}, bf16[256,512]{1,0:T(8,128)(2,1)S(1)}, u32[]{:S(2)}, u32[]{:S(2)}) collective-permute-start(bf16[256,512]{1,0:T(8,128)(2,1)S(1)} %collective-permute-done.10), channel_id=1, source_target_pairs={{0,1},{1,0},{2,3},{3,2},{4,5},{5,4},{6,7},{7,6},{8,9},{9,8},{10,11... | collective-permute-start | bytes 786440 | tf_op jit(solution)/shard_map/ppermute | solution.py:158
  33.0 0.8 %fusion.9 = f32[512,1024]{1,0:T(8,128)S(1)} fusion(bf16[512,512]{1,0:T(8,128)(2,1)S(1)} %get-tuple-element.78, bf16[512,512]{0,1:T(8,128)(2,1)S(1)} %get-tuple-element.30, bf16[512,512]{0,1:T(8,128)(2,1)S(1)} %get-tuple-element.29), kind=kOutput, calls=%fused_computation.23 | convolution fusion | flops 538968064 | bytes 3670016 | tf_op jit(solution)/shard_map/dot_general | solution.py:36
  34.4 0.5 %fusion.86 = f32[512,512]{0,1:T(8,128)S(1)} fusion(bf16[512,512]{1,0:T(8,128)(2,1)S(1)} %get-tuple-element.38, bf16[512,512]{1,0:T(8,128)(2,1)S(1)} %copy-done.1), kind=kOutput, calls=%fused_computation.181 | convolution fusion | flops 268435456 | bytes 2097152 | tf_op jit(solution)/shard_map/dot_general | solution.py:30
  34.9 0.5 %fusion.87 = f32[512,512]{0,1:T(8,128)S(1)} fusion(bf16[512,512]{1,0:T(8,128)(2,1)S(1)} %get-tuple-element.38, bf16[512,512]{1,0:T(8,128)(2,1)S(1)} %copy-done.2), kind=kOutput, calls=%fused_computation.182 | convolution fusion | flops 268435456 | bytes 2097152 | tf_op jit(solution)/shard_map/dot_general | solution.py:29
  35.4 0.8 %multiply_convert_fusion.7 = (bf16[512,512]{0,1:T(8,128)(2,1)S(1)}, bf16[512,512]{0,1:T(8,128)(2,1)S(1)}) fusion(f32[512,512]{0,1:T(8,128)S(1)} %fusion.87, f32[512,512]{0,1:T(8,128)S(1)} %fusion.86, bf16[512,512]{1,0:T(8,128)(2,1)S(1)} %get-tuple-element.37, bf16[512,512]{1,0:T(8,128)(2,1)S(1)} %copy-done.3), kind=kOutput, calls=%fused_computation.40 | convolution fusion | flops 271843328 | bytes 4194304 | tf_op jit(solution)/shard_map/dot_general | solution.py:31
  36.2 0.8 %add_add_fusion.1 = f32[512,1024]{1,0:T(8,128)S(1)} fusion(f32[512,1024]{1,0:T(8,128)S(1)} %fusion.9, f32[512,1024]{1,0:T(8,128)S(1)} %fusion.19, f32[512,1024]{1,0:T(8,128)S(1)} %fusion.5, bf16[512,512]{1,0:T(8,128)(2,1)S(1)} %get-tuple-element.38, bf16[512,512]{0,1:T(8,128)(2,1)S(1)} %get-tuple-element.26, bf16[512,512]{0,1:T(8,128)(2,1)S(1)} %get-tuple-element.25), kind=kOutput, calls=%fused_computation.1 | convolution fusion | flops 540540928 | bytes 9961472 | tf_op jit(solution)/shard_map/dot_general | solution.py:36
  37.0 0.5 %convolution_add_fusion = f32[512,512]{1,0:T(8,128)S(1)} fusion(f32[512,512]{1,0:T(8,128)S(1)} %convolution_add_fusion.1, bf16[512,512]{1,0:T(8,128)(2,1)S(1)} %get-tuple-element.37, f32[512,512]{0,1:T(8,128)S(1)} %fusion.86, f32[512,512]{0,1:T(8,128)S(1)} %fusion.87), kind=kOutput, calls=%fused_computation.2 | convolution fusion | flops 270270464 | bytes 4718592 | tf_op jit(solution)/shard_map/dot_general | solution.py:37
  40.7 0.5 %add_add_fusion = f32[512,1024]{1,0:T(8,128)S(1)} fusion(f32[512,1024]{1,0:T(8,128)S(1)} %add_add_fusion.1, f32[512,1024]{1,0:T(8,128)S(1)} %fusion.25, bf16[128,512]{1,0:T(8,128)(2,1)S(1)} %get-tuple-element.34, bf16[128,512]{1,0:T(8,128)(2,1)S(1)} %get-tuple-element.33, bf16[64,512]{1,0:T(8,128)(2,1)S(1)} %get-tuple-element.95, ...), kind=kOutput, calls=%fused_computation | convolution fusion | flops 136052736 | bytes 6684672 | tf_op jit(solution)/shard_map/dot_general | solution.py:36
  41.2 0.5 %multiply_reduce_fusion.1 = (f32[512]{0:T(512)S(1)}, f32[512]{0:T(512)S(1)}, f32[512]{0:T(512)S(1)}, f32[512]{0:T(512)S(1)}) fusion(f32[512,1024]{1,0:T(8,128)S(1)} %add_add_fusion, bf16[512,512]{1,0:T(8,128)(2,1)S(1)} %copy-done.1, bf16[512,512]{1,0:T(8,128)(2,1)S(1)} %copy-done.2), kind=kLoop, calls=%fused_computation.33 | loop fusion | flops 3143680 | bytes 3153920 | tf_op jit(solution)/shard_map/reduce_sum | solution.py:19
  41.7 0.5 %multiply_reduce_fusion = (f32[512]{0:T(512)S(1)}, f32[512,512]{1,0:T(8,128)S(1)}) fusion(bf16[64,512]{1,0:T(8,128)(2,1)S(1)} %get-tuple-element.96, bf16[64,512]{1,0:T(8,128)(2,1)S(1)} %get-tuple-element.94, f32[128,512]{1,0:T(8,128)S(1)} %fusion.49, f32[128,512]{1,0:T(8,128)S(1)} %fusion.48, f32[512,512]{1,0:T(8,128)S(1)} %convolution_add_fusion, ...), kind=kOutput, calls=%fused_computation.31 | convolution fusion | flops 69336576 | bytes 4327424 | tf_op jit(solution)/shard_map/dot_general | solution.py:37
  43.3 0.9 %convolution_convert_fusion = bf16[128,512]{1,0:T(8,128)(2,1)} fusion(bf16[128,512]{1,0:T(8,128)(2,1)S(1)} %fusion.1, bf16[512,512]{1,0:T(8,128)(2,1)S(1)} %multiply_convert_fusion), kind=kOutput, calls=%fused_computation.15 | convolution fusion | flops 67174400 | bytes 786432 | tf_op jit(solution)/shard_map/dot_general | solution.py:45
  (83 shorter events, 8.5 us)
Async XLA Ops:
  0.0 42.8 %copy-start = (bf16[128,512]{1,0:T(8,128)(2,1)S(1)}, bf16[128,512]{1,0:T(8,128)(2,1)}, u32[]{:S(2)}) copy-start(bf16[128,512]{1,0:T(8,128)(2,1)} %param.9) | copy-start | bytes 393220
  0.0 6.7 %copy-start.2 = (bf16[512,512]{1,0:T(8,128)(2,1)S(1)}, bf16[512,512]{1,0:T(8,128)(2,1)}, u32[]{:S(2)}) copy-start(bf16[512,512]{1,0:T(8,128)(2,1)} %param.11) | copy-start | bytes 1572868
  0.0 7.0 %copy-start.1 = (bf16[512,512]{1,0:T(8,128)(2,1)S(1)}, bf16[512,512]{1,0:T(8,128)(2,1)}, u32[]{:S(2)}) copy-start(bf16[512,512]{1,0:T(8,128)(2,1)} %param.12) | copy-start | bytes 1572868
  2.0 9.3 %collective-permute-start.1 = (bf16[256,512]{1,0:T(8,128)(2,1)S(1)}, bf16[256,512]{1,0:T(8,128)(2,1)S(1)}, u32[]{:S(2)}, u32[]{:S(2)}) collective-permute-start(bf16[256,512]{1,0:T(8,128)(2,1)S(1)} %bitcast.50), channel_id=1, source_target_pairs={{0,4},{1,5},{4,8},{5,9},{8,12},{9,13},{12,14},{13,15},{14,10},{15,... | collective-permute-start | bytes 786440 | tf_op jit(solution)/shard_map/ppermute | solution.py:153
  5.1 8.1 %collective-permute-start.2 = (bf16[256,512]{1,0:T(8,128)(2,1)S(1)}, bf16[256,512]{1,0:T(8,128)(2,1)S(1)}, u32[]{:S(2)}, u32[]{:S(2)}) collective-permute-start(bf16[256,512]{1,0:T(8,128)(2,1)S(1)} %bitcast.51), channel_id=1, source_target_pairs={{0,2},{1,3},{4,0},{5,1},{8,4},{9,5},{12,8},{13,9},{14,12},{15,13},... | collective-permute-start | bytes 786440 | tf_op jit(solution)/shard_map/ppermute | solution.py:154
  5.1 1.5 %collective-permute-start = (bf16[256,512]{1,0:T(8,128)(2,1)S(1)}, bf16[256,512]{1,0:T(8,128)(2,1)S(1)}, u32[]{:S(2)}, u32[]{:S(2)}) collective-permute-start(bf16[256,512]{1,0:T(8,128)(2,1)S(1)} %bitcast.52), channel_id=1, source_target_pairs={{0,1},{1,0},{2,3},{3,2},{4,5},{5,4},{6,7},{7,6},{8,9},{9,8},{10,11... | collective-permute-start | bytes 786440 | tf_op jit(solution)/shard_map/ppermute | solution.py:142
  6.3 1.0 %copy-start.3 = (bf16[512,512]{1,0:T(8,128)(2,1)S(1)}, bf16[512,512]{1,0:T(8,128)(2,1)}, u32[]{:S(2)}) copy-start(bf16[512,512]{1,0:T(8,128)(2,1)} %param.13) | copy-start | bytes 1572868
  11.3 2.8 %collective-permute-start.3 = (bf16[256,512]{1,0:T(8,128)(2,1)S(1)}, bf16[256,512]{1,0:T(8,128)(2,1)S(1)}, u32[]{:S(2)}, u32[]{:S(2)}) collective-permute-start(bf16[256,512]{1,0:T(8,128)(2,1)S(1)} %collective-permute-done.1), channel_id=1, source_target_pairs={{0,1},{1,0},{2,3},{3,2},{4,5},{5,4},{6,7},{7,6},{8,9},{9,8},{10,11... | collective-permute-start | bytes 786440 | tf_op jit(solution)/shard_map/ppermute | solution.py:158
  11.3 8.7 %collective-permute-start.5 = (bf16[256,512]{1,0:T(8,128)(2,1)S(1)}, bf16[256,512]{1,0:T(8,128)(2,1)S(1)}, u32[]{:S(2)}, u32[]{:S(2)}) collective-permute-start(bf16[256,512]{1,0:T(8,128)(2,1)S(1)} %collective-permute-done.1), channel_id=1, source_target_pairs={{0,4},{1,5},{4,8},{5,9},{8,12},{9,13},{12,14},{13,15},{14,10},{15,... | collective-permute-start | bytes 786440 | tf_op jit(solution)/shard_map/ppermute | solution.py:153
  13.2 1.6 %collective-permute-start.4 = (bf16[256,512]{1,0:T(8,128)(2,1)S(1)}, bf16[256,512]{1,0:T(8,128)(2,1)S(1)}, u32[]{:S(2)}, u32[]{:S(2)}) collective-permute-start(bf16[256,512]{1,0:T(8,128)(2,1)S(1)} %collective-permute-done.2), channel_id=1, source_target_pairs={{0,1},{1,0},{2,3},{3,2},{4,5},{5,4},{6,7},{7,6},{8,9},{9,8},{10,11... | collective-permute-start | bytes 786440 | tf_op jit(solution)/shard_map/ppermute | solution.py:158
  13.5 8.5 %collective-permute-start.6 = (bf16[256,512]{1,0:T(8,128)(2,1)S(1)}, bf16[256,512]{1,0:T(8,128)(2,1)S(1)}, u32[]{:S(2)}, u32[]{:S(2)}) collective-permute-start(bf16[256,512]{1,0:T(8,128)(2,1)S(1)} %collective-permute-done.2), channel_id=1, source_target_pairs={{0,2},{1,3},{4,0},{5,1},{8,4},{9,5},{12,8},{13,9},{14,12},{15,13},... | collective-permute-start | bytes 786440 | tf_op jit(solution)/shard_map/ppermute | solution.py:154
  20.1 3.2 %collective-permute-start.7 = (bf16[256,512]{1,0:T(8,128)(2,1)S(1)}, bf16[256,512]{1,0:T(8,128)(2,1)S(1)}, u32[]{:S(2)}, u32[]{:S(2)}) collective-permute-start(bf16[256,512]{1,0:T(8,128)(2,1)S(1)} %collective-permute-done.5), channel_id=1, source_target_pairs={{0,1},{1,0},{2,3},{3,2},{4,5},{5,4},{6,7},{7,6},{8,9},{9,8},{10,11... | collective-permute-start | bytes 786440 | tf_op jit(solution)/shard_map/ppermute | solution.py:158
  20.1 8.7 %collective-permute-start.9 = (bf16[256,512]{1,0:T(8,128)(2,1)S(1)}, bf16[256,512]{1,0:T(8,128)(2,1)S(1)}, u32[]{:S(2)}, u32[]{:S(2)}) collective-permute-start(bf16[256,512]{1,0:T(8,128)(2,1)S(1)} %collective-permute-done.5), channel_id=1, source_target_pairs={{0,4},{1,5},{4,8},{5,9},{8,12},{9,13},{12,14},{13,15},{14,10},{15,... | collective-permute-start | bytes 786440 | tf_op jit(solution)/shard_map/ppermute | solution.py:153
  22.0 1.5 %collective-permute-start.8 = (bf16[256,512]{1,0:T(8,128)(2,1)S(1)}, bf16[256,512]{1,0:T(8,128)(2,1)S(1)}, u32[]{:S(2)}, u32[]{:S(2)}) collective-permute-start(bf16[256,512]{1,0:T(8,128)(2,1)S(1)} %collective-permute-done.6), channel_id=1, source_target_pairs={{0,1},{1,0},{2,3},{3,2},{4,5},{5,4},{6,7},{7,6},{8,9},{9,8},{10,11... | collective-permute-start | bytes 786440 | tf_op jit(solution)/shard_map/ppermute | solution.py:158
  22.2 9.7 %collective-permute-start.10 = (bf16[256,512]{1,0:T(8,128)(2,1)S(1)}, bf16[256,512]{1,0:T(8,128)(2,1)S(1)}, u32[]{:S(2)}, u32[]{:S(2)}) collective-permute-start(bf16[256,512]{1,0:T(8,128)(2,1)S(1)} %collective-permute-done.6), channel_id=1, source_target_pairs={{0,2},{1,3},{4,0},{5,1},{8,4},{9,5},{12,8},{13,9},{14,12},{15,13},... | collective-permute-start | bytes 786440 | tf_op jit(solution)/shard_map/ppermute | solution.py:154
  28.8 8.7 %collective-permute-start.13 = (bf16[128,512]{1,0:T(8,128)(2,1)S(1)}, bf16[128,512]{1,0:T(8,128)(2,1)S(1)}, u32[]{:S(2)}, u32[]{:S(2)}) collective-permute-start(bf16[128,512]{1,0:T(8,128)(2,1)S(1)} %slice.328), channel_id=1, source_target_pairs={{0,4},{1,5},{4,8},{5,9},{8,12},{9,13},{12,14},{13,15},{14,10},{15,... | collective-permute-start | bytes 393224 | tf_op jit(solution)/shard_map/ppermute | solution.py:148
  32.0 5.5 %collective-permute-start.14 = (bf16[128,512]{1,0:T(8,128)(2,1)S(1)}, bf16[128,512]{1,0:T(8,128)(2,1)S(1)}, u32[]{:S(2)}, u32[]{:S(2)}) collective-permute-start(bf16[128,512]{1,0:T(8,128)(2,1)S(1)} %slice.329), channel_id=1, source_target_pairs={{0,2},{1,3},{4,0},{5,1},{8,4},{9,5},{12,8},{13,9},{14,12},{15,13},... | collective-permute-start | bytes 393224 | tf_op jit(solution)/shard_map/ppermute | solution.py:149
  32.4 1.6 %collective-permute-start.11 = (bf16[256,512]{1,0:T(8,128)(2,1)S(1)}, bf16[256,512]{1,0:T(8,128)(2,1)S(1)}, u32[]{:S(2)}, u32[]{:S(2)}) collective-permute-start(bf16[256,512]{1,0:T(8,128)(2,1)S(1)} %collective-permute-done.9), channel_id=1, source_target_pairs={{0,1},{1,0},{2,3},{3,2},{4,5},{5,4},{6,7},{7,6},{8,9},{9,8},{10,11... | collective-permute-start | bytes 786440 | tf_op jit(solution)/shard_map/ppermute | solution.py:158
  32.5 1.9 %collective-permute-start.12 = (bf16[256,512]{1,0:T(8,128)(2,1)S(1)}, bf16[256,512]{1,0:T(8,128)(2,1)S(1)}, u32[]{:S(2)}, u32[]{:S(2)}) collective-permute-start(bf16[256,512]{1,0:T(8,128)(2,1)S(1)} %collective-permute-done.10), channel_id=1, source_target_pairs={{0,1},{1,0},{2,3},{3,2},{4,5},{5,4},{6,7},{7,6},{8,9},{9,8},{10,11... | collective-permute-start | bytes 786440 | tf_op jit(solution)/shard_map/ppermute | solution.py:158
  37.5 2.3 %collective-permute-start.15 = (bf16[128,512]{1,0:T(8,128)(2,1)S(1)}, bf16[128,512]{1,0:T(8,128)(2,1)S(1)}, u32[]{:S(2)}, u32[]{:S(2)}) collective-permute-start(bf16[128,512]{1,0:T(8,128)(2,1)S(1)} %collective-permute-done.13), channel_id=1, source_target_pairs={{0,1},{1,0},{2,3},{3,2},{4,5},{5,4},{6,7},{7,6},{8,9},{9,8},{10,11... | collective-permute-start | bytes 393224 | tf_op jit(solution)/shard_map/ppermute | solution.py:158
  37.7 2.2 %collective-permute-start.16 = (bf16[128,512]{1,0:T(8,128)(2,1)S(1)}, bf16[128,512]{1,0:T(8,128)(2,1)S(1)}, u32[]{:S(2)}, u32[]{:S(2)}) collective-permute-start(bf16[128,512]{1,0:T(8,128)(2,1)S(1)} %collective-permute-done.14), channel_id=1, source_target_pairs={{0,1},{1,0},{2,3},{3,2},{4,5},{5,4},{6,7},{7,6},{8,9},{9,8},{10,11... | collective-permute-start | bytes 393224 | tf_op jit(solution)/shard_map/ppermute | solution.py:158

commit v16 on v12

--- a/solution.py
+++ b/solution.py
@@ -129,8 +129,14 @@
                 scaled_parts.append(ch[(2 * j + 1) * half:(2 * j + 2) * half])
         return jnp.concatenate(keys_parts, axis=0), jnp.concatenate(scaled_parts, axis=0)
 
-    def local_ring(keys, values, queries, learn_rate, w_gate, w_up, w_out):
-        hidden = w_gate.shape[1]
+    def local_ring(keys, values, queries, learn_rate, w_gate_all, w_up_all, w_out_all):
+        hidden = w_gate_all.shape[1]
+        part = hidden // 2
+        core = lax.axis_index("outer")
+        w_gate = lax.dynamic_slice_in_dim(w_gate_all, core * part, part, axis=1)
+        w_up = lax.dynamic_slice_in_dim(w_up_all, core * part, part, axis=1)
+        w_out = lax.dynamic_slice_in_dim(w_out_all, core * part, part, axis=0)
+        q_sib = lax.ppermute(queries, axes, swap)
         rows = keys.shape[0]
         halves = 2 if rows % 16 == 0 else 1
         half = rows // halves
@@ -162,11 +168,30 @@
             else:
                 total = add_grads(total, *split(arrived + from_sib, half), w_gate, w_up, w_out)
         full_in, full_out = total
-        new_gate = renorm(w_gate, full_in[:, :hidden])
-        new_up = renorm(w_up, full_in[:, hidden:])
+        up_gate = w_gate.astype(jnp.float32) + full_in[:, :part]
+        up_up = w_up.astype(jnp.float32) + full_in[:, part:]
+        sums = jnp.stack([jnp.sum(up_gate * up_gate, axis=1), jnp.sum(up_up * up_up, axis=1)])
+        sums = sums + lax.ppermute(sums, axes, swap)
+
+        def scale(weight_all, update, row_sums):
+            old = weight_all.astype(jnp.float32)
+            factor = jnp.sqrt(jnp.mean(old * old, axis=1, keepdims=True) + epsilon) / jnp.sqrt(
+                row_sums[:, None] / hidden + epsilon
+            )
+            return (update * factor).astype(jnp.bfloat16)
+
+        new_gate = scale(w_gate_all, up_gate, sums[0])
+        new_up = scale(w_up_all, up_up, sums[1])
         new_out = renorm(w_out, full_out)
         new_gate, new_up, new_out = lax.optimization_barrier((new_gate, new_up, new_out))
-        return apply(queries, new_gate, new_up, new_out)
+        rows = queries.shape[0]
+        both_queries = jnp.concatenate([queries, q_sib], axis=0)
+        q_gate = jnp.dot(both_queries, new_gate, preferred_element_type=jnp.float32)
+        q_up = jnp.dot(both_queries, new_up, preferred_element_type=jnp.float32)
+        q_act = (jax.nn.silu(q_gate) * q_up).astype(jnp.bfloat16)
+        partial = jnp.dot(q_act, new_out, preferred_element_type=jnp.float32)
+        from_sib = lax.ppermute(partial[rows:], axes, swap)
+        return (partial[:rows] + from_sib).astype(jnp.bfloat16)
 
     return local_ring
 
@@ -189,7 +214,7 @@
         gathered_bytes = 2 * per_part * keys.shape[1] * keys.dtype.itemsize
         if gathered_bytes > GATHER_LIMIT_BYTES:
             body = local_scatter
-        elif local_ring is not None:
+        elif local_ring is not None and w_gate.shape[1] % 256 == 0:
             body = local_ring
         else:
             body = local_gather

time: 44.3 us -> 44.4 us (level)
  waiting for transfers between devices: 12 us -> 17.1 us
  matrix products: 15.6 us -> 10.8 us
  other arithmetic: 4.29 us -> 2.84 us
  local copies, waits for them, and re-layouts: 0.45 us -> 1.25 us
    ppermute x0 -> x3, waiting for transfers between devices: none -> 1.98 us  [the longest x1 1.36 us: local_ring(): from_sib = lax.ppermute(partial[rows:], axes, swap)]
    ppermute x3, waiting for transfers between devices: 10.3 us -> 12.2 us  [local_ring(): lax.ppermute(arrived[0], axes, cw_perm)]
    dot_general x6, matrix products: 3.51 us -> 2.08 us  [gradients(): lax.dot_general(scaled, w_out, contract_last, preferred_element_type=jnp....]
    dot_general x6, matrix products: 3.67 us -> 2.45 us  [gradients(): lax.dot_general(keys, both_grads, contract_first, preferred_element_type=...]
    reduce_sum x1, other arithmetic: 1.22 us -> 0.13 us  [renorm(): jnp.mean(old * old, axis=1, keepdims=True) + epsilon]
    another operation x1, other arithmetic: 0.94 us -> 0.03 us  [local_ring(): jnp.stack([keys.reshape(halves, half, width), scaled.reshape(halves, half...]
    convert_element_type x0 -> x2, other arithmetic: none -> 0.9 us  [the longest x1 0.69 us: local_ring(): return (partial[:rows] + from_sib).astype(jnp.bfloat16)]
    dot_general x6, matrix products: 2.64 us -> 1.86 us  [gradients(): lax.dot_general(activation, scaled, contract_first, preferred_element_typ...]
  transfers between devices with their start and end apart: 17 -> 20, of which waited for: 9 -> 10; matrix products, arithmetic and copies ran while one was open for 32% -> 22% of each run, Pallas kernels for 0% -> 0%
where the time goes in v16:
time: 44.4 us; the launch traced here: 44.2 us
  waiting for transfers between devices  17.1 us (39%)
  starting transfers between devices  11.6 us (26%)
  matrix products  10.8 us (24%)
  other arithmetic  2.84 us (6%)
  local copies, waits for them, and re-layouts  1.25 us (3%)
  between operations  0.63 us (1%)
    ppermute x3, waiting for transfers between devices, local_ring(): lax.ppermute(arrived[0], axes, cw_perm)  12.2 us
    ppermute x3, starting transfers between devices, local_ring(): lax.ppermute(arrived[0], axes, cw_perm)  6.35 us
    dot_general x6, matrix products, gradients(): lax.dot_general(keys, both_grads, contract_first, preferred_element_type=...  2.45 us
    ppermute x8, waiting for transfers between devices, local_ring(): from_sib = [lax.ppermute(chunk, axes, swap) for chunk in arrived]  2.18 us
    dot_general x6, matrix products, gradients(): lax.dot_general(scaled, w_out, contract_last, preferred_element_type=jnp....  2.08 us
    ppermute x1, starting transfers between devices, local_ring(): lax.ppermute(arrived[0][:2 * half], axes, cw_perm)  1.88 us
    dot_general x6, matrix products, gradients(): lax.dot_general(activation, scaled, contract_first, preferred_element_typ...  1.86 us
    dot_general x6, matrix products, gradients(): gate_pre = jnp.dot(keys, w_gate, preferred_element_type=jnp.float32)  1.77 us
  transfers between devices with their start and end apart: 20, of which 10 were waited for; matrix products, arithmetic and copies ran while one was open for 22% of the time, Pallas kernels for 0%

profile of v16, /device:TPU:0, one launch (start us, length us, event | category | flops | bytes accessed | tf_op | source)
XLA Modules:
  0.0 44.2 jit_solution(5622480758464749086)
XLA Ops:
  0.0 1.0 %multiply_convert_fusion.19 = bf16[128,512]{1,0:T(8,128)(2,1)S(1)} fusion(bf16[128,512]{1,0:T(8,128)(2,1)} %param.8, f32[128]{0:T(128)} %param.10), kind=kLoop, calls=%fused_computation.59 | loop fusion | flops 196608 | bytes 262656 | tf_op jit(solution)/shard_map/convert_element_type | solution.py:143
  1.1 0.5 %collective-permute-start.1 = (bf16[256,512]{1,0:T(8,128)(2,1)S(1)}, bf16[256,512]{1,0:T(8,128)(2,1)S(1)}, u32[]{:S(2)}, u32[]{:S(2)}) collective-permute-start(bf16[256,512]{1,0:T(8,128)(2,1)S(1)} %bitcast.27), channel_id=1, source_target_pairs={{0,1},{1,0},{2,3},{3,2},{4,5},{5,4},{6,7},{7,6},{8,9},{9,8},{10,11... | collective-permute-start | bytes 786440 | tf_op jit(solution)/shard_map/ppermute | solution.py:148
  1.6 2.6 %collective-permute-start.2 = (bf16[256,512]{1,0:T(8,128)(2,1)S(1)}, bf16[256,512]{1,0:T(8,128)(2,1)S(1)}, u32[]{:S(2)}, u32[]{:S(2)}) collective-permute-start(bf16[256,512]{1,0:T(8,128)(2,1)S(1)} %bitcast.28), channel_id=1, source_target_pairs={{0,4},{1,5},{4,8},{5,9},{8,12},{9,13},{12,14},{13,15},{14,10},{15,... | collective-permute-start | bytes 786440 | tf_op jit(solution)/shard_map/ppermute | solution.py:159
  4.7 0.8 %copy-done.2 = bf16[512,512]{1,0:T(8,128)(2,1)S(1)} copy-done((bf16[512,512]{1,0:T(8,128)(2,1)S(1)}, bf16[512,512]{1,0:T(8,128)(2,1)}, u32[]{:S(2)}) %copy-start.2) | copy-done | bytes 524312
  7.1 4.0 %collective-permute-done.2 = bf16[256,512]{1,0:T(8,128)(2,1)S(1)} collective-permute-done((bf16[256,512]{1,0:T(8,128)(2,1)S(1)}, bf16[256,512]{1,0:T(8,128)(2,1)S(1)}, u32[]{:S(2)}, u32[]{:S(2)}) %collective-permute-start.2) | collective-permute-done | bytes 262176 | tf_op jit(solution)/shard_map/ppermute | solution.py:159
  11.1 1.8 %collective-permute-start.6 = (bf16[256,512]{1,0:T(8,128)(2,1)S(1)}, bf16[256,512]{1,0:T(8,128)(2,1)S(1)}, u32[]{:S(2)}, u32[]{:S(2)}) collective-permute-start(bf16[256,512]{1,0:T(8,128)(2,1)S(1)} %collective-permute-done.2), channel_id=1, source_target_pairs={{0,4},{1,5},{4,8},{5,9},{8,12},{9,13},{12,14},{13,15},{14,10},{15,... | collective-permute-start | bytes 786440 | tf_op jit(solution)/shard_map/ppermute | solution.py:159
  13.8 0.8 %collective-permute-done.5 = bf16[256,512]{1,0:T(8,128)(2,1)S(1)} collective-permute-done((bf16[256,512]{1,0:T(8,128)(2,1)S(1)}, bf16[256,512]{1,0:T(8,128)(2,1)S(1)}, u32[]{:S(2)}, u32[]{:S(2)}) %collective-permute-start.5) | collective-permute-done | bytes 262176 | tf_op jit(solution)/shard_map/ppermute | solution.py:164
  14.9 0.3 fusion.51
  15.6 4.2 %collective-permute-done.6 = bf16[256,512]{1,0:T(8,128)(2,1)S(1)} collective-permute-done((bf16[256,512]{1,0:T(8,128)(2,1)S(1)}, bf16[256,512]{1,0:T(8,128)(2,1)S(1)}, u32[]{:S(2)}, u32[]{:S(2)}) %collective-permute-start.6) | collective-permute-done | bytes 262176 | tf_op jit(solution)/shard_map/ppermute | solution.py:159
  19.9 1.9 %collective-permute-start.10 = (bf16[256,512]{1,0:T(8,128)(2,1)S(1)}, bf16[256,512]{1,0:T(8,128)(2,1)S(1)}, u32[]{:S(2)}, u32[]{:S(2)}) collective-permute-start(bf16[256,512]{1,0:T(8,128)(2,1)S(1)} %collective-permute-done.6), channel_id=1, source_target_pairs={{0,4},{1,5},{4,8},{5,9},{8,12},{9,13},{12,14},{13,15},{14,10},{15,... | collective-permute-start | bytes 786440 | tf_op jit(solution)/shard_map/ppermute | solution.py:159
  21.8 0.5 %multiply_convert_fusion.11 = (bf16[512,256]{0,1:T(8,128)(2,1)S(1)}, bf16[512,256]{0,1:T(8,128)(2,1)S(1)}) fusion(f32[512,256]{0,1:T(8,128)S(1)} %fusion.72, f32[512,256]{0,1:T(8,128)S(1)} %fusion.51, bf16[512,512]{1,0:T(8,128)(2,1)S(1)} %get-tuple-element.67, bf16[512,512]{1,0:T(8,128)(2,1)S(1)} %copy-done.2, s32[]{:T(128)S(6)} %select_n.2), kind=kOutput, calls=%fused_computation.41 | convolution fusion | flops 135921664 | bytes 2359300 | tf_op jit(solution)/shard_map/dot_general | solution.py:31
  22.7 0.5 %convolution_add_fusion.2 = f32[512,512]{1,0:T(8,128)S(1)} fusion(f32[512,512]{1,0:T(8,128)S(1)} %fusion.14, bf16[512,512]{1,0:T(8,128)(2,1)S(1)} %get-tuple-element.68, bf16[512,256]{0,1:T(8,128)(2,1)S(1)} %get-tuple-element.28, bf16[512,256]{0,1:T(8,128)(2,1)S(1)} %get-tuple-element.27), kind=kOutput, calls=%fused_computation.2 | convolution fusion | flops 269746176 | bytes 3145728 | tf_op jit(solution)/shard_map/dot_general | solution.py:36
  23.3 0.6 %collective-permute-done.9 = bf16[256,512]{1,0:T(8,128)(2,1)S(1)} collective-permute-done((bf16[256,512]{1,0:T(8,128)(2,1)S(1)}, bf16[256,512]{1,0:T(8,128)(2,1)S(1)}, u32[]{:S(2)}, u32[]{:S(2)}) %collective-permute-start.9) | collective-permute-done | bytes 262176 | tf_op jit(solution)/shard_map/ppermute | solution.py:164
  23.9 0.3 fusion.70
  24.2 0.3 fusion.49
  24.6 4.0 %collective-permute-done.10 = bf16[256,512]{1,0:T(8,128)(2,1)S(1)} collective-permute-done((bf16[256,512]{1,0:T(8,128)(2,1)S(1)}, bf16[256,512]{1,0:T(8,128)(2,1)S(1)}, u32[]{:S(2)}, u32[]{:S(2)}) %collective-permute-start.10) | collective-permute-done | bytes 262176 | tf_op jit(solution)/shard_map/ppermute | solution.py:159
  28.6 1.9 %collective-permute-start.14 = (bf16[128,512]{1,0:T(8,128)(2,1)S(1)}, bf16[128,512]{1,0:T(8,128)(2,1)S(1)}, u32[]{:S(2)}, u32[]{:S(2)}) collective-permute-start(bf16[128,512]{1,0:T(8,128)(2,1)S(1)} %slice.344), channel_id=1, source_target_pairs={{0,4},{1,5},{4,8},{5,9},{8,12},{9,13},{12,14},{13,15},{14,10},{15,... | collective-permute-start | bytes 393224 | tf_op jit(solution)/shard_map/ppermute | solution.py:154
  30.8 0.5 %multiply_convert_fusion.9 = (bf16[512,256]{0,1:T(8,128)(2,1)S(1)}, bf16[512,256]{0,1:T(8,128)(2,1)S(1)}) fusion(f32[512,256]{0,1:T(8,128)S(1)} %fusion.70, f32[512,256]{0,1:T(8,128)S(1)} %fusion.49, bf16[512,512]{1,0:T(8,128)(2,1)S(1)} %get-tuple-element.51, bf16[512,512]{1,0:T(8,128)(2,1)S(1)} %copy-done.2, s32[]{:T(128)S(6)} %select_n.2), kind=kOutput, calls=%fused_computation.37 | convolution fusion | flops 135921664 | bytes 2359300 | tf_op jit(solution)/shard_map/dot_general | solution.py:31
  31.7 0.5 %collective-permute-start.13 = (bf16[256,512]{1,0:T(8,128)(2,1)S(1)}, bf16[256,512]{1,0:T(8,128)(2,1)S(1)}, u32[]{:S(2)}, u32[]{:S(2)}) collective-permute-start(bf16[256,512]{1,0:T(8,128)(2,1)S(1)} %collective-permute-done.11), channel_id=1, source_target_pairs={{0,1},{1,0},{2,3},{3,2},{4,5},{5,4},{6,7},{7,6},{8,9},{9,8},{10,11... | collective-permute-start | bytes 786440 | tf_op jit(solution)/shard_map/ppermute | solution.py:164
  32.2 0.5 %convolution_add_fusion.1 = f32[512,512]{1,0:T(8,128)S(1)} fusion(f32[512,512]{1,0:T(8,128)S(1)} %convolution_add_fusion.2, bf16[512,512]{1,0:T(8,128)(2,1)S(1)} %get-tuple-element.52, bf16[512,256]{0,1:T(8,128)(2,1)S(1)} %get-tuple-element.26, bf16[512,256]{0,1:T(8,128)(2,1)S(1)} %get-tuple-element.25), kind=kOutput, calls=%fused_computation.1 | convolution fusion | flops 269746176 | bytes 3145728 | tf_op jit(solution)/shard_map/dot_general | solution.py:36
  32.7 0.5 %collective-permute-done.12 = bf16[256,512]{1,0:T(8,128)(2,1)S(1)} collective-permute-done((bf16[256,512]{1,0:T(8,128)(2,1)S(1)}, bf16[256,512]{1,0:T(8,128)(2,1)S(1)}, u32[]{:S(2)}, u32[]{:S(2)}) %collective-permute-start.12) | collective-permute-done | bytes 262176 | tf_op jit(solution)/shard_map/ppermute | solution.py:164
  33.6 0.4 fusion.68
  34.0 0.3 fusion.47
  34.3 0.5 %multiply_convert_fusion.7 = (bf16[512,256]{0,1:T(8,128)(2,1)S(1)}, bf16[512,256]{0,1:T(8,128)(2,1)S(1)}) fusion(f32[512,256]{0,1:T(8,128)S(1)} %fusion.68, f32[512,256]{0,1:T(8,128)S(1)} %fusion.47, bf16[512,512]{1,0:T(8,128)(2,1)S(1)} %get-tuple-element.35, bf16[512,512]{1,0:T(8,128)(2,1)S(1)} %copy-done.2, s32[]{:T(128)S(6)} %select_n.2), kind=kOutput, calls=%fused_computation.33 | convolution fusion | flops 135921664 | bytes 2359300 | tf_op jit(solution)/shard_map/dot_general | solution.py:31
  35.1 0.5 %convolution_add_fusion = f32[512,512]{1,0:T(8,128)S(1)} fusion(f32[512,512]{1,0:T(8,128)S(1)} %convolution_add_fusion.1, bf16[512,512]{1,0:T(8,128)(2,1)S(1)} %get-tuple-element.36, bf16[512,256]{0,1:T(8,128)(2,1)S(1)} %get-tuple-element.24, bf16[512,256]{0,1:T(8,128)(2,1)S(1)} %get-tuple-element.23), kind=kOutput, calls=%fused_computation | convolution fusion | flops 269746176 | bytes 3145728 | tf_op jit(solution)/shard_map/dot_general | solution.py:36
  35.6 0.7 %collective-permute-done.15 = bf16[128,512]{1,0:T(8,128)(2,1)S(1)} collective-permute-done((bf16[128,512]{1,0:T(8,128)(2,1)S(1)}, bf16[128,512]{1,0:T(8,128)(2,1)S(1)}, u32[]{:S(2)}, u32[]{:S(2)}) %collective-permute-start.15) | collective-permute-done | bytes 131104 | tf_op jit(solution)/shard_map/ppermute | solution.py:155
  36.4 0.6 %collective-permute-start.16 = (bf16[128,512]{1,0:T(8,128)(2,1)S(1)}, bf16[128,512]{1,0:T(8,128)(2,1)S(1)}, u32[]{:S(2)}, u32[]{:S(2)}) collective-permute-start(bf16[128,512]{1,0:T(8,128)(2,1)S(1)} %collective-permute-done.14), channel_id=1, source_target_pairs={{0,1},{1,0},{2,3},{3,2},{4,5},{5,4},{6,7},{7,6},{8,9},{9,8},{10,11... | collective-permute-start | bytes 393224 | tf_op jit(solution)/shard_map/ppermute | solution.py:164
  39.6 0.4 multiply_reduce_fusion.2
  40.1 0.6 %collective-permute-done.18 = f32[2,512]{1,0:T(2,128)S(1)} collective-permute-done((f32[2,512]{1,0:T(2,128)S(1)}, f32[2,512]{1,0:T(2,128)S(1)}, u32[]{:S(2)}, u32[]{:S(2)}) %collective-permute-start.18) | collective-permute-done | bytes 4128 | tf_op jit(solution)/shard_map/ppermute | solution.py:174
  41.3 0.6 %fusion.20 = f32[256,512]{1,0:T(8,128)S(1)} fusion(bf16[256,512]{1,0:T(8,128)(2,1)S(1)} %multiply_convert_fusion, f32[256,256]{0,1:T(8,128)S(1)} %fusion.132, bf16[256,512]{1,0:T(8,128)(2,1)S(1)} %constant_dynamic-update-slice_fusion, bf16[512,256]{1,0:T(8,128)(2,1)S(1)} %get-tuple-element.17), kind=kOutput, calls=%fused_computation.61 | convolution fusion | flops 134610944 | bytes 1572864 | tf_op jit(solution)/shard_map/dot_general | solution.py:192
  42.2 1.4 %collective-permute-done.19 = f32[128,512]{1,0:T(8,128)S(1)} collective-permute-done((f32[128,512]{1,0:T(8,128)S(1)}, f32[128,512]{1,0:T(8,128)S(1)}, u32[]{:S(2)}, u32[]{:S(2)}) %collective-permute-start.19) | collective-permute-done | bytes 262176 | tf_op jit(solution)/shard_map/ppermute | solution.py:193
  43.5 0.7 %fusion.13 = bf16[128,512]{1,0:T(8,128)(2,1)} fusion(f32[128,512]{1,0:T(8,128)S(1)} %collective-permute-done.19, f32[256,512]{1,0:T(8,128)S(1)} %fusion.20), kind=kLoop, calls=%fused_computation.45 | loop fusion | flops 131072 | bytes 655360 | tf_op jit(solution)/shard_map/convert_element_type | solution.py:194
  (99 shorter events, 9.0 us)
Async XLA Ops:
  0.0 1.0 %copy-start.4 = (bf16[128,512]{1,0:T(8,128)(2,1)S(1)}, bf16[128,512]{1,0:T(8,128)(2,1)}, u32[]{:S(2)}) copy-start(bf16[128,512]{1,0:T(8,128)(2,1)} %param.7) | copy-start | bytes 393220
  1.0 3.2 %copy-start.3 = (bf16[128,512]{1,0:T(8,128)(2,1)S(1)}, bf16[128,512]{1,0:T(8,128)(2,1)}, u32[]{:S(2)}) copy-start(bf16[128,512]{1,0:T(8,128)(2,1)} %param.9) | copy-start | bytes 393220
  1.1 3.4 %copy-start = (bf16[512,512]{1,0:T(8,128)(2,1)S(1)}, bf16[512,512]{1,0:T(8,128)(2,1)}, u32[]{:S(2)}) copy-start(bf16[512,512]{1,0:T(8,128)(2,1)} %param.12) | copy-start | bytes 1572868
  1.1 4.7 %collective-permute-start.1 = (bf16[256,512]{1,0:T(8,128)(2,1)S(1)}, bf16[256,512]{1,0:T(8,128)(2,1)S(1)}, u32[]{:S(2)}, u32[]{:S(2)}) collective-permute-start(bf16[256,512]{1,0:T(8,128)(2,1)S(1)} %bitcast.27), channel_id=1, source_target_pairs={{0,1},{1,0},{2,3},{3,2},{4,5},{5,4},{6,7},{7,6},{8,9},{9,8},{10,11... | collective-permute-start | bytes 786440 | tf_op jit(solution)/shard_map/ppermute | solution.py:148
  1.6 9.5 %collective-permute-start.2 = (bf16[256,512]{1,0:T(8,128)(2,1)S(1)}, bf16[256,512]{1,0:T(8,128)(2,1)S(1)}, u32[]{:S(2)}, u32[]{:S(2)}) collective-permute-start(bf16[256,512]{1,0:T(8,128)(2,1)S(1)} %bitcast.28), channel_id=1, source_target_pairs={{0,4},{1,5},{4,8},{5,9},{8,12},{9,13},{12,14},{13,15},{14,10},{15,... | collective-permute-start | bytes 786440 | tf_op jit(solution)/shard_map/ppermute | solution.py:159
  4.3 8.7 %collective-permute-start.3 = (bf16[256,512]{1,0:T(8,128)(2,1)S(1)}, bf16[256,512]{1,0:T(8,128)(2,1)S(1)}, u32[]{:S(2)}, u32[]{:S(2)}) collective-permute-start(bf16[256,512]{1,0:T(8,128)(2,1)S(1)} %bitcast.29), channel_id=1, source_target_pairs={{0,2},{1,3},{4,0},{5,1},{8,4},{9,5},{12,8},{13,9},{14,12},{15,13},... | collective-permute-start | bytes 786440 | tf_op jit(solution)/shard_map/ppermute | solution.py:160
  4.3 1.6 %collective-permute-start = (bf16[128,512]{1,0:T(8,128)(2,1)S(1)}, bf16[128,512]{1,0:T(8,128)(2,1)S(1)}, u32[]{:S(2)}, u32[]{:S(2)}) collective-permute-start(bf16[128,512]{1,0:T(8,128)(2,1)S(1)} %copy-done.3), channel_id=1, source_target_pairs={{0,1},{1,0},{2,3},{3,2},{4,5},{5,4},{6,7},{7,6},{8,9},{9,8},{10,11... | collective-permute-start | bytes 393224 | tf_op jit(solution)/shard_map/ppermute | solution.py:139
  4.4 1.0 %copy-start.2 = (bf16[512,512]{1,0:T(8,128)(2,1)S(1)}, bf16[512,512]{1,0:T(8,128)(2,1)}, u32[]{:S(2)}) copy-start(bf16[512,512]{1,0:T(8,128)(2,1)} %param.13) | copy-start | bytes 1572868
  4.5 1.2 %copy-start.1 = (bf16[512,512]{1,0:T(8,128)(2,1)S(1)}, bf16[512,512]{1,0:T(8,128)(2,1)}, u32[]{:S(2)}) copy-start(bf16[512,512]{1,0:T(8,128)(2,1)} %param.11) | copy-start | bytes 1572868
  11.1 2.6 %collective-permute-start.4 = (bf16[256,512]{1,0:T(8,128)(2,1)S(1)}, bf16[256,512]{1,0:T(8,128)(2,1)S(1)}, u32[]{:S(2)}, u32[]{:S(2)}) collective-permute-start(bf16[256,512]{1,0:T(8,128)(2,1)S(1)} %collective-permute-done.2), channel_id=1, source_target_pairs={{0,1},{1,0},{2,3},{3,2},{4,5},{5,4},{6,7},{7,6},{8,9},{9,8},{10,11... | collective-permute-start | bytes 786440 | tf_op jit(solution)/shard_map/ppermute | solution.py:164
  11.1 8.7 %collective-permute-start.6 = (bf16[256,512]{1,0:T(8,128)(2,1)S(1)}, bf16[256,512]{1,0:T(8,128)(2,1)S(1)}, u32[]{:S(2)}, u32[]{:S(2)}) collective-permute-start(bf16[256,512]{1,0:T(8,128)(2,1)S(1)} %collective-permute-done.2), channel_id=1, source_target_pairs={{0,4},{1,5},{4,8},{5,9},{8,12},{9,13},{12,14},{13,15},{14,10},{15,... | collective-permute-start | bytes 786440 | tf_op jit(solution)/shard_map/ppermute | solution.py:159
  12.9 1.6 %collective-permute-start.5 = (bf16[256,512]{1,0:T(8,128)(2,1)S(1)}, bf16[256,512]{1,0:T(8,128)(2,1)S(1)}, u32[]{:S(2)}, u32[]{:S(2)}) collective-permute-start(bf16[256,512]{1,0:T(8,128)(2,1)S(1)} %collective-permute-done.3), channel_id=1, source_target_pairs={{0,1},{1,0},{2,3},{3,2},{4,5},{5,4},{6,7},{7,6},{8,9},{9,8},{10,11... | collective-permute-start | bytes 786440 | tf_op jit(solution)/shard_map/ppermute | solution.py:164
  13.2 9.0 %collective-permute-start.7 = (bf16[256,512]{1,0:T(8,128)(2,1)S(1)}, bf16[256,512]{1,0:T(8,128)(2,1)S(1)}, u32[]{:S(2)}, u32[]{:S(2)}) collective-permute-start(bf16[256,512]{1,0:T(8,128)(2,1)S(1)} %collective-permute-done.3), channel_id=1, source_target_pairs={{0,2},{1,3},{4,0},{5,1},{8,4},{9,5},{12,8},{13,9},{14,12},{15,13},... | collective-permute-start | bytes 786440 | tf_op jit(solution)/shard_map/ppermute | solution.py:160
  19.8 3.4 %collective-permute-start.8 = (bf16[256,512]{1,0:T(8,128)(2,1)S(1)}, bf16[256,512]{1,0:T(8,128)(2,1)S(1)}, u32[]{:S(2)}, u32[]{:S(2)}) collective-permute-start(bf16[256,512]{1,0:T(8,128)(2,1)S(1)} %collective-permute-done.6), channel_id=1, source_target_pairs={{0,1},{1,0},{2,3},{3,2},{4,5},{5,4},{6,7},{7,6},{8,9},{9,8},{10,11... | collective-permute-start | bytes 786440 | tf_op jit(solution)/shard_map/ppermute | solution.py:164
  19.9 8.7 %collective-permute-start.10 = (bf16[256,512]{1,0:T(8,128)(2,1)S(1)}, bf16[256,512]{1,0:T(8,128)(2,1)S(1)}, u32[]{:S(2)}, u32[]{:S(2)}) collective-permute-start(bf16[256,512]{1,0:T(8,128)(2,1)S(1)} %collective-permute-done.6), channel_id=1, source_target_pairs={{0,4},{1,5},{4,8},{5,9},{8,12},{9,13},{12,14},{13,15},{14,10},{15,... | collective-permute-start | bytes 786440 | tf_op jit(solution)/shard_map/ppermute | solution.py:159
  22.3 1.6 %collective-permute-start.9 = (bf16[256,512]{1,0:T(8,128)(2,1)S(1)}, bf16[256,512]{1,0:T(8,128)(2,1)S(1)}, u32[]{:S(2)}, u32[]{:S(2)}) collective-permute-start(bf16[256,512]{1,0:T(8,128)(2,1)S(1)} %collective-permute-done.7), channel_id=1, source_target_pairs={{0,1},{1,0},{2,3},{3,2},{4,5},{5,4},{6,7},{7,6},{8,9},{9,8},{10,11... | collective-permute-start | bytes 786440 | tf_op jit(solution)/shard_map/ppermute | solution.py:164
  22.5 8.8 %collective-permute-start.11 = (bf16[256,512]{1,0:T(8,128)(2,1)S(1)}, bf16[256,512]{1,0:T(8,128)(2,1)S(1)}, u32[]{:S(2)}, u32[]{:S(2)}) collective-permute-start(bf16[256,512]{1,0:T(8,128)(2,1)S(1)} %collective-permute-done.7), channel_id=1, source_target_pairs={{0,2},{1,3},{4,0},{5,1},{8,4},{9,5},{12,8},{13,9},{14,12},{15,13},... | collective-permute-start | bytes 786440 | tf_op jit(solution)/shard_map/ppermute | solution.py:160
  28.6 7.0 %collective-permute-start.14 = (bf16[128,512]{1,0:T(8,128)(2,1)S(1)}, bf16[128,512]{1,0:T(8,128)(2,1)S(1)}, u32[]{:S(2)}, u32[]{:S(2)}) collective-permute-start(bf16[128,512]{1,0:T(8,128)(2,1)S(1)} %slice.344), channel_id=1, source_target_pairs={{0,4},{1,5},{4,8},{5,9},{8,12},{9,13},{12,14},{13,15},{14,10},{15,... | collective-permute-start | bytes 393224 | tf_op jit(solution)/shard_map/ppermute | solution.py:154
  31.3 5.0 %collective-permute-start.15 = (bf16[128,512]{1,0:T(8,128)(2,1)S(1)}, bf16[128,512]{1,0:T(8,128)(2,1)S(1)}, u32[]{:S(2)}, u32[]{:S(2)}) collective-permute-start(bf16[128,512]{1,0:T(8,128)(2,1)S(1)} %slice.345), channel_id=1, source_target_pairs={{0,2},{1,3},{4,0},{5,1},{8,4},{9,5},{12,8},{13,9},{14,12},{15,13},... | collective-permute-start | bytes 393224 | tf_op jit(solution)/shard_map/ppermute | solution.py:155
  31.6 1.6 %collective-permute-start.12 = (bf16[256,512]{1,0:T(8,128)(2,1)S(1)}, bf16[256,512]{1,0:T(8,128)(2,1)S(1)}, u32[]{:S(2)}, u32[]{:S(2)}) collective-permute-start(bf16[256,512]{1,0:T(8,128)(2,1)S(1)} %collective-permute-done.10), channel_id=1, source_target_pairs={{0,1},{1,0},{2,3},{3,2},{4,5},{5,4},{6,7},{7,6},{8,9},{9,8},{10,11... | collective-permute-start | bytes 786440 | tf_op jit(solution)/shard_map/ppermute | solution.py:164
  31.7 1.9 %collective-permute-start.13 = (bf16[256,512]{1,0:T(8,128)(2,1)S(1)}, bf16[256,512]{1,0:T(8,128)(2,1)S(1)}, u32[]{:S(2)}, u32[]{:S(2)}) collective-permute-start(bf16[256,512]{1,0:T(8,128)(2,1)S(1)} %collective-permute-done.11), channel_id=1, source_target_pairs={{0,1},{1,0},{2,3},{3,2},{4,5},{5,4},{6,7},{7,6},{8,9},{9,8},{10,11... | collective-permute-start | bytes 786440 | tf_op jit(solution)/shard_map/ppermute | solution.py:164
  36.4 1.9 %collective-permute-start.17 = (bf16[128,512]{1,0:T(8,128)(2,1)S(1)}, bf16[128,512]{1,0:T(8,128)(2,1)S(1)}, u32[]{:S(2)}, u32[]{:S(2)}) collective-permute-start(bf16[128,512]{1,0:T(8,128)(2,1)S(1)} %collective-permute-done.15), channel_id=1, source_target_pairs={{0,1},{1,0},{2,3},{3,2},{4,5},{5,4},{6,7},{7,6},{8,9},{9,8},{10,11... | collective-permute-start | bytes 393224 | tf_op jit(solution)/shard_map/ppermute | solution.py:164
  36.4 1.9 %collective-permute-start.16 = (bf16[128,512]{1,0:T(8,128)(2,1)S(1)}, bf16[128,512]{1,0:T(8,128)(2,1)S(1)}, u32[]{:S(2)}, u32[]{:S(2)}) collective-permute-start(bf16[128,512]{1,0:T(8,128)(2,1)S(1)} %collective-permute-done.14), channel_id=1, source_target_pairs={{0,1},{1,0},{2,3},{3,2},{4,5},{5,4},{6,7},{7,6},{8,9},{9,8},{10,11... | collective-permute-start | bytes 393224 | tf_op jit(solution)/shard_map/ppermute | solution.py:164
  39.5 1.2 %collective-permute-start.18 = (f32[2,512]{1,0:T(2,128)S(1)}, f32[2,512]{1,0:T(2,128)S(1)}, u32[]{:S(2)}, u32[]{:S(2)}) collective-permute-start(f32[2,512]{1,0:T(2,128)S(1)} %pad_maximum_fusion.21), channel_id=1, source_target_pairs={{0,1},{1,0},{2,3},{3,2},{4,5},{5,4},{6,7},{7,6},{8,9},{9,8},{10,11... | collective-permute-start | bytes 12296 | tf_op jit(solution)/shard_map/ppermute | solution.py:174
  41.9 1.6 %collective-permute-start.19 = (f32[128,512]{1,0:T(8,128)S(1)}, f32[128,512]{1,0:T(8,128)S(1)}, u32[]{:S(2)}, u32[]{:S(2)}) collective-permute-start(f32[128,512]{1,0:T(8,128)S(1)} %slice.355), channel_id=1, source_target_pairs={{0,1},{1,0},{2,3},{3,2},{4,5},{5,4},{6,7},{7,6},{8,9},{9,8},{10,11... | collective-permute-start | bytes 786440 | tf_op jit(solution)/shard_map/ppermute | solution.py:193

commit v17 on v16

--- a/solution.py
+++ b/solution.py
@@ -185,13 +185,16 @@
         new_out = renorm(w_out, full_out)
         new_gate, new_up, new_out = lax.optimization_barrier((new_gate, new_up, new_out))
         rows = queries.shape[0]
+        sib_out = lax.ppermute(new_out, axes, swap)
         both_queries = jnp.concatenate([queries, q_sib], axis=0)
         q_gate = jnp.dot(both_queries, new_gate, preferred_element_type=jnp.float32)
         q_up = jnp.dot(both_queries, new_up, preferred_element_type=jnp.float32)
         q_act = (jax.nn.silu(q_gate) * q_up).astype(jnp.bfloat16)
-        partial = jnp.dot(q_act, new_out, preferred_element_type=jnp.float32)
-        from_sib = lax.ppermute(partial[rows:], axes, swap)
-        return (partial[:rows] + from_sib).astype(jnp.bfloat16)
+        sib_act = lax.ppermute(q_act[rows:], axes, swap)
+        result = jnp.dot(q_act[:rows], new_out, preferred_element_type=jnp.float32) + jnp.dot(
+            sib_act, sib_out, preferred_element_type=jnp.float32
+        )
+        return result.astype(jnp.bfloat16)
 
     return local_ring
 

time: 44.4 us -> 44.2 us (level)
  waiting for transfers between devices: 17.1 us -> 16.4 us
  matrix products: 10.8 us -> 11.5 us
  other arithmetic: 2.84 us -> 2.15 us
  starting transfers between devices: 11.6 us -> 12.1 us
    dot_general x1 -> x3, matrix products: 0.61 us -> 1.35 us  [the longest x1 0.87 us: local_ring(): jnp.dot(sib_act, sib_out, preferred_element_type=jnp.float32)]
    convert_element_type x1 -> x0, other arithmetic: 0.69 us -> none  [local_ring(): return (partial[:rows] + from_sib).astype(jnp.bfloat16)]
    ppermute x1 -> x2, waiting for transfers between devices: 1.36 us -> 0.71 us  [the longest x1 0.71 us: local_ring(): sib_act = lax.ppermute(q_act[rows:], axes, swap)]
  transfers between devices with their start and end apart: 20 -> 21, of which waited for: 10 -> 10; matrix products, arithmetic and copies ran while one was open for 22% -> 24% of each run, Pallas kernels for 0% -> 0%
where the time goes in v17:
time: 44.2 us; the launch traced here: 44 us
  waiting for transfers between devices  16.4 us (37%)
  starting transfers between devices  12.1 us (27%)
  matrix products  11.5 us (26%)
  other arithmetic  2.15 us (5%)
  local copies, waits for them, and re-layouts  1.23 us (3%)
  between operations  0.65 us (1%)
    ppermute x3, waiting for transfers between devices, local_ring(): lax.ppermute(arrived[0], axes, cw_perm)  12.2 us
    ppermute x3, starting transfers between devices, local_ring(): lax.ppermute(arrived[0], axes, cw_perm)  6.35 us
    dot_general x6, matrix products, gradients(): lax.dot_general(keys, both_grads, contract_first, preferred_element_type=...  2.45 us
    ppermute x8, waiting for transfers between devices, local_ring(): from_sib = [lax.ppermute(chunk, axes, swap) for chunk in arrived]  2.18 us
    dot_general x6, matrix products, gradients(): lax.dot_general(scaled, w_out, contract_last, preferred_element_type=jnp....  2.08 us
    ppermute x1, starting transfers between devices, local_ring(): lax.ppermute(arrived[0][:2 * half], axes, cw_perm)  1.88 us
    dot_general x6, matrix products, gradients(): lax.dot_general(activation, scaled, contract_first, preferred_element_typ...  1.86 us
    dot_general x6, matrix products, gradients(): gate_pre = jnp.dot(keys, w_gate, preferred_element_type=jnp.float32)  1.77 us
  transfers between devices with their start and end apart: 21, of which 10 were waited for; matrix products, arithmetic and copies ran while one was open for 24% of the time, Pallas kernels for 0%

profile of v17, /device:TPU:0, one launch (start us, length us, event | category | flops | bytes accessed | tf_op | source)
XLA Modules:
  0.0 44.0 jit_solution(5982113923063395815)
XLA Ops:
  0.0 1.0 %multiply_convert_fusion.19 = bf16[128,512]{1,0:T(8,128)(2,1)S(1)} fusion(bf16[128,512]{1,0:T(8,128)(2,1)} %param.8, f32[128]{0:T(128)} %param.10), kind=kLoop, calls=%fused_computation.59 | loop fusion | flops 196608 | bytes 262656 | tf_op jit(solution)/shard_map/convert_element_type | solution.py:143
  1.1 0.5 %collective-permute-start.1 = (bf16[256,512]{1,0:T(8,128)(2,1)S(1)}, bf16[256,512]{1,0:T(8,128)(2,1)S(1)}, u32[]{:S(2)}, u32[]{:S(2)}) collective-permute-start(bf16[256,512]{1,0:T(8,128)(2,1)S(1)} %bitcast.29), channel_id=1, source_target_pairs={{0,1},{1,0},{2,3},{3,2},{4,5},{5,4},{6,7},{7,6},{8,9},{9,8},{10,11... | collective-permute-start | bytes 786440 | tf_op jit(solution)/shard_map/ppermute | solution.py:148
  1.6 2.6 %collective-permute-start.2 = (bf16[256,512]{1,0:T(8,128)(2,1)S(1)}, bf16[256,512]{1,0:T(8,128)(2,1)S(1)}, u32[]{:S(2)}, u32[]{:S(2)}) collective-permute-start(bf16[256,512]{1,0:T(8,128)(2,1)S(1)} %bitcast.30), channel_id=1, source_target_pairs={{0,4},{1,5},{4,8},{5,9},{8,12},{9,13},{12,14},{13,15},{14,10},{15,... | collective-permute-start | bytes 786440 | tf_op jit(solution)/shard_map/ppermute | solution.py:159
  4.7 0.8 %copy-done.2 = bf16[512,512]{1,0:T(8,128)(2,1)S(1)} copy-done((bf16[512,512]{1,0:T(8,128)(2,1)S(1)}, bf16[512,512]{1,0:T(8,128)(2,1)}, u32[]{:S(2)}) %copy-start.2) | copy-done | bytes 524312
  7.1 4.0 %collective-permute-done.2 = bf16[256,512]{1,0:T(8,128)(2,1)S(1)} collective-permute-done((bf16[256,512]{1,0:T(8,128)(2,1)S(1)}, bf16[256,512]{1,0:T(8,128)(2,1)S(1)}, u32[]{:S(2)}, u32[]{:S(2)}) %collective-permute-start.2) | collective-permute-done | bytes 262176 | tf_op jit(solution)/shard_map/ppermute | solution.py:159
  11.1 1.8 %collective-permute-start.6 = (bf16[256,512]{1,0:T(8,128)(2,1)S(1)}, bf16[256,512]{1,0:T(8,128)(2,1)S(1)}, u32[]{:S(2)}, u32[]{:S(2)}) collective-permute-start(bf16[256,512]{1,0:T(8,128)(2,1)S(1)} %collective-permute-done.2), channel_id=1, source_target_pairs={{0,4},{1,5},{4,8},{5,9},{8,12},{9,13},{12,14},{13,15},{14,10},{15,... | collective-permute-start | bytes 786440 | tf_op jit(solution)/shard_map/ppermute | solution.py:159
  13.8 0.8 %collective-permute-done.5 = bf16[256,512]{1,0:T(8,128)(2,1)S(1)} collective-permute-done((bf16[256,512]{1,0:T(8,128)(2,1)S(1)}, bf16[256,512]{1,0:T(8,128)(2,1)S(1)}, u32[]{:S(2)}, u32[]{:S(2)}) %collective-permute-start.5) | collective-permute-done | bytes 262176 | tf_op jit(solution)/shard_map/ppermute | solution.py:164
  14.9 0.3 fusion.51
  15.6 4.2 %collective-permute-done.6 = bf16[256,512]{1,0:T(8,128)(2,1)S(1)} collective-permute-done((bf16[256,512]{1,0:T(8,128)(2,1)S(1)}, bf16[256,512]{1,0:T(8,128)(2,1)S(1)}, u32[]{:S(2)}, u32[]{:S(2)}) %collective-permute-start.6) | collective-permute-done | bytes 262176 | tf_op jit(solution)/shard_map/ppermute | solution.py:159
  19.9 1.9 %collective-permute-start.10 = (bf16[256,512]{1,0:T(8,128)(2,1)S(1)}, bf16[256,512]{1,0:T(8,128)(2,1)S(1)}, u32[]{:S(2)}, u32[]{:S(2)}) collective-permute-start(bf16[256,512]{1,0:T(8,128)(2,1)S(1)} %collective-permute-done.6), channel_id=1, source_target_pairs={{0,4},{1,5},{4,8},{5,9},{8,12},{9,13},{12,14},{13,15},{14,10},{15,... | collective-permute-start | bytes 786440 | tf_op jit(solution)/shard_map/ppermute | solution.py:159
  21.8 0.5 %multiply_convert_fusion.11 = (bf16[512,256]{0,1:T(8,128)(2,1)S(1)}, bf16[512,256]{0,1:T(8,128)(2,1)S(1)}) fusion(f32[512,256]{0,1:T(8,128)S(1)} %fusion.72, f32[512,256]{0,1:T(8,128)S(1)} %fusion.51, bf16[512,512]{1,0:T(8,128)(2,1)S(1)} %get-tuple-element.67, bf16[512,512]{1,0:T(8,128)(2,1)S(1)} %copy-done.2, s32[]{:T(128)S(6)} %select_n.2), kind=kOutput, calls=%fused_computation.43 | convolution fusion | flops 135921664 | bytes 2359300 | tf_op jit(solution)/shard_map/dot_general | solution.py:31
  22.7 0.5 %convolution_add_fusion.2 = f32[512,512]{1,0:T(8,128)S(1)} fusion(f32[512,512]{1,0:T(8,128)S(1)} %fusion.14, bf16[512,512]{1,0:T(8,128)(2,1)S(1)} %get-tuple-element.68, bf16[512,256]{0,1:T(8,128)(2,1)S(1)} %get-tuple-element.28, bf16[512,256]{0,1:T(8,128)(2,1)S(1)} %get-tuple-element.27), kind=kOutput, calls=%fused_computation.2 | convolution fusion | flops 269746176 | bytes 3145728 | tf_op jit(solution)/shard_map/dot_general | solution.py:36
  23.3 0.6 %collective-permute-done.9 = bf16[256,512]{1,0:T(8,128)(2,1)S(1)} collective-permute-done((bf16[256,512]{1,0:T(8,128)(2,1)S(1)}, bf16[256,512]{1,0:T(8,128)(2,1)S(1)}, u32[]{:S(2)}, u32[]{:S(2)}) %collective-permute-start.9) | collective-permute-done | bytes 262176 | tf_op jit(solution)/shard_map/ppermute | solution.py:164
  23.9 0.3 fusion.70
  24.2 0.3 fusion.49
  24.6 4.0 %collective-permute-done.10 = bf16[256,512]{1,0:T(8,128)(2,1)S(1)} collective-permute-done((bf16[256,512]{1,0:T(8,128)(2,1)S(1)}, bf16[256,512]{1,0:T(8,128)(2,1)S(1)}, u32[]{:S(2)}, u32[]{:S(2)}) %collective-permute-start.10) | collective-permute-done | bytes 262176 | tf_op jit(solution)/shard_map/ppermute | solution.py:159
  28.6 1.9 %collective-permute-start.14 = (bf16[128,512]{1,0:T(8,128)(2,1)S(1)}, bf16[128,512]{1,0:T(8,128)(2,1)S(1)}, u32[]{:S(2)}, u32[]{:S(2)}) collective-permute-start(bf16[128,512]{1,0:T(8,128)(2,1)S(1)} %slice.344), channel_id=1, source_target_pairs={{0,4},{1,5},{4,8},{5,9},{8,12},{9,13},{12,14},{13,15},{14,10},{15,... | collective-permute-start | bytes 393224 | tf_op jit(solution)/shard_map/ppermute | solution.py:154
  30.8 0.5 %multiply_convert_fusion.9 = (bf16[512,256]{0,1:T(8,128)(2,1)S(1)}, bf16[512,256]{0,1:T(8,128)(2,1)S(1)}) fusion(f32[512,256]{0,1:T(8,128)S(1)} %fusion.70, f32[512,256]{0,1:T(8,128)S(1)} %fusion.49, bf16[512,512]{1,0:T(8,128)(2,1)S(1)} %get-tuple-element.51, bf16[512,512]{1,0:T(8,128)(2,1)S(1)} %copy-done.2, s32[]{:T(128)S(6)} %select_n.2), kind=kOutput, calls=%fused_computation.39 | convolution fusion | flops 135921664 | bytes 2359300 | tf_op jit(solution)/shard_map/dot_general | solution.py:31
  31.7 0.5 %collective-permute-start.13 = (bf16[256,512]{1,0:T(8,128)(2,1)S(1)}, bf16[256,512]{1,0:T(8,128)(2,1)S(1)}, u32[]{:S(2)}, u32[]{:S(2)}) collective-permute-start(bf16[256,512]{1,0:T(8,128)(2,1)S(1)} %collective-permute-done.11), channel_id=1, source_target_pairs={{0,1},{1,0},{2,3},{3,2},{4,5},{5,4},{6,7},{7,6},{8,9},{9,8},{10,11... | collective-permute-start | bytes 786440 | tf_op jit(solution)/shard_map/ppermute | solution.py:164
  32.2 0.5 %convolution_add_fusion.1 = f32[512,512]{1,0:T(8,128)S(1)} fusion(f32[512,512]{1,0:T(8,128)S(1)} %convolution_add_fusion.2, bf16[512,512]{1,0:T(8,128)(2,1)S(1)} %get-tuple-element.52, bf16[512,256]{0,1:T(8,128)(2,1)S(1)} %get-tuple-element.26, bf16[512,256]{0,1:T(8,128)(2,1)S(1)} %get-tuple-element.25), kind=kOutput, calls=%fused_computation.1 | convolution fusion | flops 269746176 | bytes 3145728 | tf_op jit(solution)/shard_map/dot_general | solution.py:36
  32.7 0.5 %collective-permute-done.12 = bf16[256,512]{1,0:T(8,128)(2,1)S(1)} collective-permute-done((bf16[256,512]{1,0:T(8,128)(2,1)S(1)}, bf16[256,512]{1,0:T(8,128)(2,1)S(1)}, u32[]{:S(2)}, u32[]{:S(2)}) %collective-permute-start.12) | collective-permute-done | bytes 262176 | tf_op jit(solution)/shard_map/ppermute | solution.py:164
  33.6 0.4 fusion.68
  34.0 0.3 fusion.47
  34.3 0.5 %multiply_convert_fusion.7 = (bf16[512,256]{0,1:T(8,128)(2,1)S(1)}, bf16[512,256]{0,1:T(8,128)(2,1)S(1)}) fusion(f32[512,256]{0,1:T(8,128)S(1)} %fusion.68, f32[512,256]{0,1:T(8,128)S(1)} %fusion.47, bf16[512,512]{1,0:T(8,128)(2,1)S(1)} %get-tuple-element.35, bf16[512,512]{1,0:T(8,128)(2,1)S(1)} %copy-done.2, s32[]{:T(128)S(6)} %select_n.2), kind=kOutput, calls=%fused_computation.35 | convolution fusion | flops 135921664 | bytes 2359300 | tf_op jit(solution)/shard_map/dot_general | solution.py:31
  35.1 0.5 %convolution_add_fusion = f32[512,512]{1,0:T(8,128)S(1)} fusion(f32[512,512]{1,0:T(8,128)S(1)} %convolution_add_fusion.1, bf16[512,512]{1,0:T(8,128)(2,1)S(1)} %get-tuple-element.36, bf16[512,256]{0,1:T(8,128)(2,1)S(1)} %get-tuple-element.24, bf16[512,256]{0,1:T(8,128)(2,1)S(1)} %get-tuple-element.23), kind=kOutput, calls=%fused_computation | convolution fusion | flops 269746176 | bytes 3145728 | tf_op jit(solution)/shard_map/dot_general | solution.py:36
  35.6 0.7 %collective-permute-done.15 = bf16[128,512]{1,0:T(8,128)(2,1)S(1)} collective-permute-done((bf16[128,512]{1,0:T(8,128)(2,1)S(1)}, bf16[128,512]{1,0:T(8,128)(2,1)S(1)}, u32[]{:S(2)}, u32[]{:S(2)}) %collective-permute-start.15) | collective-permute-done | bytes 131104 | tf_op jit(solution)/shard_map/ppermute | solution.py:155
  36.4 0.6 %collective-permute-start.16 = (bf16[128,512]{1,0:T(8,128)(2,1)S(1)}, bf16[128,512]{1,0:T(8,128)(2,1)S(1)}, u32[]{:S(2)}, u32[]{:S(2)}) collective-permute-start(bf16[128,512]{1,0:T(8,128)(2,1)S(1)} %collective-permute-done.14), channel_id=1, source_target_pairs={{0,1},{1,0},{2,3},{3,2},{4,5},{5,4},{6,7},{7,6},{8,9},{9,8},{10,11... | collective-permute-start | bytes 393224 | tf_op jit(solution)/shard_map/ppermute | solution.py:164
  39.6 0.4 multiply_reduce_fusion.2
  40.1 0.6 %collective-permute-done.18 = f32[2,512]{1,0:T(2,128)S(1)} collective-permute-done((f32[2,512]{1,0:T(2,128)S(1)}, f32[2,512]{1,0:T(2,128)S(1)}, u32[]{:S(2)}, u32[]{:S(2)}) %collective-permute-start.18) | collective-permute-done | bytes 4128 | tf_op jit(solution)/shard_map/ppermute | solution.py:174
  41.8 0.4 collective-permute-start.19
  42.4 0.7 %collective-permute-done.19 = bf16[128,256]{0,1:T(8,128)(2,1)S(1)} collective-permute-done((bf16[128,256]{0,1:T(8,128)(2,1)S(1)}, bf16[128,256]{0,1:T(8,128)(2,1)S(1)}, u32[]{:S(2)}, u32[]{:S(2)}) %collective-permute-start.19) | collective-permute-done | bytes 65568 | tf_op jit(solution)/shard_map/ppermute | solution.py:193
  43.2 0.9 %fusion = bf16[128,512]{1,0:T(8,128)(2,1)} fusion(f32[128,512]{1,0:T(8,128)S(1)} %fusion.39, bf16[128,256]{0,1:T(8,128)(2,1)S(1)} %collective-permute-done.19, bf16[256,512]{1,0:T(8,128)(2,1)S(1)} %collective-permute-done.20), kind=kOutput, calls=%fused_computation.7 | convolution fusion | flops 33685504 | bytes 720896 | tf_op jit(solution)/shard_map/dot_general | solution.py:194
  (102 shorter events, 9.5 us)
Async XLA Ops:
  0.0 1.0 %copy-start.4 = (bf16[128,512]{1,0:T(8,128)(2,1)S(1)}, bf16[128,512]{1,0:T(8,128)(2,1)}, u32[]{:S(2)}) copy-start(bf16[128,512]{1,0:T(8,128)(2,1)} %param.7) | copy-start | bytes 393220
  1.0 3.2 %copy-start.3 = (bf16[128,512]{1,0:T(8,128)(2,1)S(1)}, bf16[128,512]{1,0:T(8,128)(2,1)}, u32[]{:S(2)}) copy-start(bf16[128,512]{1,0:T(8,128)(2,1)} %param.9) | copy-start | bytes 393220
  1.1 3.4 %copy-start = (bf16[512,512]{1,0:T(8,128)(2,1)S(1)}, bf16[512,512]{1,0:T(8,128)(2,1)}, u32[]{:S(2)}) copy-start(bf16[512,512]{1,0:T(8,128)(2,1)} %param.12) | copy-start | bytes 1572868
  1.1 4.7 %collective-permute-start.1 = (bf16[256,512]{1,0:T(8,128)(2,1)S(1)}, bf16[256,512]{1,0:T(8,128)(2,1)S(1)}, u32[]{:S(2)}, u32[]{:S(2)}) collective-permute-start(bf16[256,512]{1,0:T(8,128)(2,1)S(1)} %bitcast.29), channel_id=1, source_target_pairs={{0,1},{1,0},{2,3},{3,2},{4,5},{5,4},{6,7},{7,6},{8,9},{9,8},{10,11... | collective-permute-start | bytes 786440 | tf_op jit(solution)/shard_map/ppermute | solution.py:148
  1.6 9.5 %collective-permute-start.2 = (bf16[256,512]{1,0:T(8,128)(2,1)S(1)}, bf16[256,512]{1,0:T(8,128)(2,1)S(1)}, u32[]{:S(2)}, u32[]{:S(2)}) collective-permute-start(bf16[256,512]{1,0:T(8,128)(2,1)S(1)} %bitcast.30), channel_id=1, source_target_pairs={{0,4},{1,5},{4,8},{5,9},{8,12},{9,13},{12,14},{13,15},{14,10},{15,... | collective-permute-start | bytes 786440 | tf_op jit(solution)/shard_map/ppermute | solution.py:159
  4.3 8.7 %collective-permute-start.3 = (bf16[256,512]{1,0:T(8,128)(2,1)S(1)}, bf16[256,512]{1,0:T(8,128)(2,1)S(1)}, u32[]{:S(2)}, u32[]{:S(2)}) collective-permute-start(bf16[256,512]{1,0:T(8,128)(2,1)S(1)} %bitcast.31), channel_id=1, source_target_pairs={{0,2},{1,3},{4,0},{5,1},{8,4},{9,5},{12,8},{13,9},{14,12},{15,13},... | collective-permute-start | bytes 786440 | tf_op jit(solution)/shard_map/ppermute | solution.py:160
  4.3 1.6 %collective-permute-start = (bf16[128,512]{1,0:T(8,128)(2,1)S(1)}, bf16[128,512]{1,0:T(8,128)(2,1)S(1)}, u32[]{:S(2)}, u32[]{:S(2)}) collective-permute-start(bf16[128,512]{1,0:T(8,128)(2,1)S(1)} %copy-done.3), channel_id=1, source_target_pairs={{0,1},{1,0},{2,3},{3,2},{4,5},{5,4},{6,7},{7,6},{8,9},{9,8},{10,11... | collective-permute-start | bytes 393224 | tf_op jit(solution)/shard_map/ppermute | solution.py:139
  4.4 1.0 %copy-start.2 = (bf16[512,512]{1,0:T(8,128)(2,1)S(1)}, bf16[512,512]{1,0:T(8,128)(2,1)}, u32[]{:S(2)}) copy-start(bf16[512,512]{1,0:T(8,128)(2,1)} %param.13) | copy-start | bytes 1572868
  4.5 1.2 %copy-start.1 = (bf16[512,512]{1,0:T(8,128)(2,1)S(1)}, bf16[512,512]{1,0:T(8,128)(2,1)}, u32[]{:S(2)}) copy-start(bf16[512,512]{1,0:T(8,128)(2,1)} %param.11) | copy-start | bytes 1572868
  11.1 2.6 %collective-permute-start.4 = (bf16[256,512]{1,0:T(8,128)(2,1)S(1)}, bf16[256,512]{1,0:T(8,128)(2,1)S(1)}, u32[]{:S(2)}, u32[]{:S(2)}) collective-permute-start(bf16[256,512]{1,0:T(8,128)(2,1)S(1)} %collective-permute-done.2), channel_id=1, source_target_pairs={{0,1},{1,0},{2,3},{3,2},{4,5},{5,4},{6,7},{7,6},{8,9},{9,8},{10,11... | collective-permute-start | bytes 786440 | tf_op jit(solution)/shard_map/ppermute | solution.py:164
  11.1 8.7 %collective-permute-start.6 = (bf16[256,512]{1,0:T(8,128)(2,1)S(1)}, bf16[256,512]{1,0:T(8,128)(2,1)S(1)}, u32[]{:S(2)}, u32[]{:S(2)}) collective-permute-start(bf16[256,512]{1,0:T(8,128)(2,1)S(1)} %collective-permute-done.2), channel_id=1, source_target_pairs={{0,4},{1,5},{4,8},{5,9},{8,12},{9,13},{12,14},{13,15},{14,10},{15,... | collective-permute-start | bytes 786440 | tf_op jit(solution)/shard_map/ppermute | solution.py:159
  12.9 1.6 %collective-permute-start.5 = (bf16[256,512]{1,0:T(8,128)(2,1)S(1)}, bf16[256,512]{1,0:T(8,128)(2,1)S(1)}, u32[]{:S(2)}, u32[]{:S(2)}) collective-permute-start(bf16[256,512]{1,0:T(8,128)(2,1)S(1)} %collective-permute-done.3), channel_id=1, source_target_pairs={{0,1},{1,0},{2,3},{3,2},{4,5},{5,4},{6,7},{7,6},{8,9},{9,8},{10,11... | collective-permute-start | bytes 786440 | tf_op jit(solution)/shard_map/ppermute | solution.py:164
  13.2 9.0 %collective-permute-start.7 = (bf16[256,512]{1,0:T(8,128)(2,1)S(1)}, bf16[256,512]{1,0:T(8,128)(2,1)S(1)}, u32[]{:S(2)}, u32[]{:S(2)}) collective-permute-start(bf16[256,512]{1,0:T(8,128)(2,1)S(1)} %collective-permute-done.3), channel_id=1, source_target_pairs={{0,2},{1,3},{4,0},{5,1},{8,4},{9,5},{12,8},{13,9},{14,12},{15,13},... | collective-permute-start | bytes 786440 | tf_op jit(solution)/shard_map/ppermute | solution.py:160
  19.8 3.4 %collective-permute-start.8 = (bf16[256,512]{1,0:T(8,128)(2,1)S(1)}, bf16[256,512]{1,0:T(8,128)(2,1)S(1)}, u32[]{:S(2)}, u32[]{:S(2)}) collective-permute-start(bf16[256,512]{1,0:T(8,128)(2,1)S(1)} %collective-permute-done.6), channel_id=1, source_target_pairs={{0,1},{1,0},{2,3},{3,2},{4,5},{5,4},{6,7},{7,6},{8,9},{9,8},{10,11... | collective-permute-start | bytes 786440 | tf_op jit(solution)/shard_map/ppermute | solution.py:164
  19.9 8.7 %collective-permute-start.10 = (bf16[256,512]{1,0:T(8,128)(2,1)S(1)}, bf16[256,512]{1,0:T(8,128)(2,1)S(1)}, u32[]{:S(2)}, u32[]{:S(2)}) collective-permute-start(bf16[256,512]{1,0:T(8,128)(2,1)S(1)} %collective-permute-done.6), channel_id=1, source_target_pairs={{0,4},{1,5},{4,8},{5,9},{8,12},{9,13},{12,14},{13,15},{14,10},{15,... | collective-permute-start | bytes 786440 | tf_op jit(solution)/shard_map/ppermute | solution.py:159
  22.3 1.6 %collective-permute-start.9 = (bf16[256,512]{1,0:T(8,128)(2,1)S(1)}, bf16[256,512]{1,0:T(8,128)(2,1)S(1)}, u32[]{:S(2)}, u32[]{:S(2)}) collective-permute-start(bf16[256,512]{1,0:T(8,128)(2,1)S(1)} %collective-permute-done.7), channel_id=1, source_target_pairs={{0,1},{1,0},{2,3},{3,2},{4,5},{5,4},{6,7},{7,6},{8,9},{9,8},{10,11... | collective-permute-start | bytes 786440 | tf_op jit(solution)/shard_map/ppermute | solution.py:164
  22.5 8.8 %collective-permute-start.11 = (bf16[256,512]{1,0:T(8,128)(2,1)S(1)}, bf16[256,512]{1,0:T(8,128)(2,1)S(1)}, u32[]{:S(2)}, u32[]{:S(2)}) collective-permute-start(bf16[256,512]{1,0:T(8,128)(2,1)S(1)} %collective-permute-done.7), channel_id=1, source_target_pairs={{0,2},{1,3},{4,0},{5,1},{8,4},{9,5},{12,8},{13,9},{14,12},{15,13},... | collective-permute-start | bytes 786440 | tf_op jit(solution)/shard_map/ppermute | solution.py:160
  28.6 7.0 %collective-permute-start.14 = (bf16[128,512]{1,0:T(8,128)(2,1)S(1)}, bf16[128,512]{1,0:T(8,128)(2,1)S(1)}, u32[]{:S(2)}, u32[]{:S(2)}) collective-permute-start(bf16[128,512]{1,0:T(8,128)(2,1)S(1)} %slice.344), channel_id=1, source_target_pairs={{0,4},{1,5},{4,8},{5,9},{8,12},{9,13},{12,14},{13,15},{14,10},{15,... | collective-permute-start | bytes 393224 | tf_op jit(solution)/shard_map/ppermute | solution.py:154
  31.3 5.0 %collective-permute-start.15 = (bf16[128,512]{1,0:T(8,128)(2,1)S(1)}, bf16[128,512]{1,0:T(8,128)(2,1)S(1)}, u32[]{:S(2)}, u32[]{:S(2)}) collective-permute-start(bf16[128,512]{1,0:T(8,128)(2,1)S(1)} %slice.345), channel_id=1, source_target_pairs={{0,2},{1,3},{4,0},{5,1},{8,4},{9,5},{12,8},{13,9},{14,12},{15,13},... | collective-permute-start | bytes 393224 | tf_op jit(solution)/shard_map/ppermute | solution.py:155
  31.6 1.6 %collective-permute-start.12 = (bf16[256,512]{1,0:T(8,128)(2,1)S(1)}, bf16[256,512]{1,0:T(8,128)(2,1)S(1)}, u32[]{:S(2)}, u32[]{:S(2)}) collective-permute-start(bf16[256,512]{1,0:T(8,128)(2,1)S(1)} %collective-permute-done.10), channel_id=1, source_target_pairs={{0,1},{1,0},{2,3},{3,2},{4,5},{5,4},{6,7},{7,6},{8,9},{9,8},{10,11... | collective-permute-start | bytes 786440 | tf_op jit(solution)/shard_map/ppermute | solution.py:164
  31.7 1.9 %collective-permute-start.13 = (bf16[256,512]{1,0:T(8,128)(2,1)S(1)}, bf16[256,512]{1,0:T(8,128)(2,1)S(1)}, u32[]{:S(2)}, u32[]{:S(2)}) collective-permute-start(bf16[256,512]{1,0:T(8,128)(2,1)S(1)} %collective-permute-done.11), channel_id=1, source_target_pairs={{0,1},{1,0},{2,3},{3,2},{4,5},{5,4},{6,7},{7,6},{8,9},{9,8},{10,11... | collective-permute-start | bytes 786440 | tf_op jit(solution)/shard_map/ppermute | solution.py:164
  36.4 1.9 %collective-permute-start.17 = (bf16[128,512]{1,0:T(8,128)(2,1)S(1)}, bf16[128,512]{1,0:T(8,128)(2,1)S(1)}, u32[]{:S(2)}, u32[]{:S(2)}) collective-permute-start(bf16[128,512]{1,0:T(8,128)(2,1)S(1)} %collective-permute-done.15), channel_id=1, source_target_pairs={{0,1},{1,0},{2,3},{3,2},{4,5},{5,4},{6,7},{7,6},{8,9},{9,8},{10,11... | collective-permute-start | bytes 393224 | tf_op jit(solution)/shard_map/ppermute | solution.py:164
  36.4 1.9 %collective-permute-start.16 = (bf16[128,512]{1,0:T(8,128)(2,1)S(1)}, bf16[128,512]{1,0:T(8,128)(2,1)S(1)}, u32[]{:S(2)}, u32[]{:S(2)}) collective-permute-start(bf16[128,512]{1,0:T(8,128)(2,1)S(1)} %collective-permute-done.14), channel_id=1, source_target_pairs={{0,1},{1,0},{2,3},{3,2},{4,5},{5,4},{6,7},{7,6},{8,9},{9,8},{10,11... | collective-permute-start | bytes 393224 | tf_op jit(solution)/shard_map/ppermute | solution.py:164
  39.5 1.2 %collective-permute-start.18 = (f32[2,512]{1,0:T(2,128)S(1)}, f32[2,512]{1,0:T(2,128)S(1)}, u32[]{:S(2)}, u32[]{:S(2)}) collective-permute-start(f32[2,512]{1,0:T(2,128)S(1)} %pad_maximum_fusion.21), channel_id=1, source_target_pairs={{0,1},{1,0},{2,3},{3,2},{4,5},{5,4},{6,7},{7,6},{8,9},{9,8},{10,11... | collective-permute-start | bytes 12296 | tf_op jit(solution)/shard_map/ppermute | solution.py:174
  41.0 2.1 %collective-permute-start.20 = (bf16[256,512]{1,0:T(8,128)(2,1)S(1)}, bf16[256,512]{1,0:T(8,128)(2,1)S(1)}, u32[]{:S(2)}, u32[]{:S(2)}) collective-permute-start(bf16[256,512]{1,0:T(8,128)(2,1)S(1)} %multiply_convert_fusion), channel_id=1, source_target_pairs={{0,1},{1,0},{2,3},{3,2},{4,5},{5,4},{6,7},{7,6},{8,9},{9,8},{10,11... | collective-permute-start | bytes 786440 | tf_op jit(solution)/shard_map/ppermute | solution.py:188
  41.8 1.3 %collective-permute-start.19 = (bf16[128,256]{0,1:T(8,128)(2,1)S(1)}, bf16[128,256]{0,1:T(8,128)(2,1)S(1)}, u32[]{:S(2)}, u32[]{:S(2)}) collective-permute-start(bf16[128,256]{0,1:T(8,128)(2,1)S(1)} %slice.355), channel_id=1, source_target_pairs={{0,1},{1,0},{2,3},{3,2},{4,5},{5,4},{6,7},{7,6},{8,9},{9,8},{10,11... | collective-permute-start | bytes 196616 | tf_op jit(solution)/shard_map/ppermute | solution.py:193

commit v18 on v12

--- a/solution.py
+++ b/solution.py
@@ -26,8 +26,10 @@
 
 
 def gradients(keys, scaled, w_gate, w_up, w_out):
-    gate_pre = jnp.dot(keys, w_gate, preferred_element_type=jnp.float32)
-    up_pre = jnp.dot(keys, w_up, preferred_element_type=jnp.float32)
+    hidden = w_gate.shape[1]
+    both_pre = jnp.dot(keys, jnp.concatenate([w_gate, w_up], axis=1), preferred_element_type=jnp.float32)
+    gate_pre = both_pre[:, :hidden]
+    up_pre = both_pre[:, hidden:]
     back_grad = lax.dot_general(scaled, w_out, contract_last, preferred_element_type=jnp.float32)
     activation = (jax.nn.silu(gate_pre) * up_pre).astype(jnp.bfloat16)
     d_gate = (back_grad * up_pre * silu_grad(gate_pre)).astype(jnp.bfloat16)

time: 44.3 us -> 45.8 us (1.034)
  local copies, waits for them, and re-layouts: 0.45 us -> 2.56 us
  matrix products: 15.6 us -> 14.4 us
  waiting for transfers between devices: 12 us -> 12.9 us
    unnamed x29 -> x30, local copies, waits for them, and re-layouts: 0.32 us -> 2.36 us
    dot_general x12 -> x6, matrix products: 4.51 us -> 3.32 us  [gradients(): jnp.dot(keys, jnp.concatenate([w_gate, w_up], axis=1), preferred_element_...]
    ppermute x3, waiting for transfers between devices: 0.08 us -> 1.08 us  [local_ring(): lax.ppermute(arrived[1], axes, ccw_perm)]
  transfers between devices with their start and end apart: 17 -> 17, of which waited for: 9 -> 9; matrix products, arithmetic and copies ran while one was open for 32% -> 31% of each run, Pallas kernels for 0% -> 0%
where the time goes in v18:
time: 45.8 us; the launch traced here: 45.5 us
  matrix products  14.4 us (31%)
  waiting for transfers between devices  12.9 us (28%)
  starting transfers between devices  10.9 us (24%)
  other arithmetic  4.23 us (9%)
  local copies, waits for them, and re-layouts  2.56 us (6%)
  between operations  0.48 us (1%)
    ppermute x3, waiting for transfers between devices, local_ring(): lax.ppermute(arrived[0], axes, cw_perm)  10.5 us
    ppermute x3, starting transfers between devices, local_ring(): lax.ppermute(arrived[0], axes, cw_perm)  6.73 us
    dot_general x6, matrix products, gradients(): lax.dot_general(keys, both_grads, contract_first, preferred_element_type=...  3.66 us
    dot_general x6, matrix products, gradients(): lax.dot_general(scaled, w_out, contract_last, preferred_element_type=jnp....  3.54 us
    dot_general x6, matrix products, gradients(): jnp.dot(keys, jnp.concatenate([w_gate, w_up], axis=1), preferred_element_...  3.32 us
    dot_general x6, matrix products, gradients(): lax.dot_general(activation, scaled, contract_first, preferred_element_typ...  2.62 us
    unnamed x30, local copies, waits for them, and re-layouts  2.36 us
    ppermute x1, starting transfers between devices, local_ring(): lax.ppermute(arrived[0][:2 * half], axes, cw_perm)  1.88 us
  transfers between devices with their start and end apart: 17, of which 9 were waited for; matrix products, arithmetic and copies ran while one was open for 31% of the time, Pallas kernels for 0%

profile of v18, /device:TPU:0, one launch (start us, length us, event | category | flops | bytes accessed | tf_op | source)
XLA Modules:
  0.0 45.5 jit_solution(9753629729825900541)
XLA Ops:
  0.0 1.1 %multiply_convert_fusion.25 = bf16[128,512]{1,0:T(8,128)(2,1)S(1)} fusion(bf16[128,512]{1,0:T(8,128)(2,1)} %param.8, f32[128]{0:T(128)} %param.10), kind=kLoop, calls=%fused_computation.87 | loop fusion | flops 196608 | bytes 262656 | tf_op jit(solution)/shard_map/convert_element_type | solution.py:139
  1.1 0.9 %pad_maximum_fusion = bf16[2,2,64,512]{3,2,1,0:T(8,128)(2,1)S(1)} fusion(bf16[2,1,64,512]{3,2,1,0:T(8,128)(2,1)S(1)} %bitcast.46, bf16[2,1,64,512]{3,2,1,0:T(8,128)(2,1)} %bitcast.47), kind=kLoop, calls=%fused_computation.61 | loop fusion | flops 131072 | bytes 524288 | tf_op jit(solution)/shard_map/stack | solution.py:141
  2.0 3.1 %collective-permute-start.1 = (bf16[256,512]{1,0:T(8,128)(2,1)S(1)}, bf16[256,512]{1,0:T(8,128)(2,1)S(1)}, u32[]{:S(2)}, u32[]{:S(2)}) collective-permute-start(bf16[256,512]{1,0:T(8,128)(2,1)S(1)} %bitcast.42), channel_id=1, source_target_pairs={{0,4},{1,5},{4,8},{5,9},{8,12},{9,13},{12,14},{13,15},{14,10},{15,... | collective-permute-start | bytes 786440 | tf_op jit(solution)/shard_map/ppermute | solution.py:155
  5.1 1.2 %fusion.4 = f32[512]{0:T(512)S(1)} fusion(bf16[512,512]{1,0:T(8,128)(2,1)} %param.13), kind=kLoop, calls=%fused_computation.18 | loop fusion | flops 785920 | bytes 526336 | tf_op jit(solution)/shard_map/reduce_sum | solution.py:18
  6.4 1.1 %constant_dynamic-update-slice_fusion.1 = bf16[512,1024]{1,0:T(8,128)(2,1)S(1)} fusion(bf16[512,512]{1,0:T(8,128)(2,1)} %param.11), kind=kLoop, calls=%fused_computation.96 | loop fusion | bytes 1048576
  8.5 0.5 %multiply_convert_fusion.17 = (bf16[256,512]{1,0:T(8,128)(2,1)S(1)}, bf16[256,512]{1,0:T(8,128)(2,1)S(1)}) fusion(f32[256,1024]{1,0:T(8,128)S(1)} %fusion.54, bf16[512,512]{1,0:T(8,128)(2,1)S(1)} %copy-done.3, bf16[64,512]{1,0:T(8,128)(2,1)S(1)} %get-tuple-element.74, bf16[64,512]{1,0:T(8,128)(2,1)S(1)} %get-tuple-element.75, ...), kind=kOutput, calls=%fused_computation.57 | convolution fusion | flops 136970240 | bytes 2359296 | tf_op jit(solution)/shard_map/dot_general | solution.py:33
  9.0 2.3 %collective-permute-done.1 = bf16[256,512]{1,0:T(8,128)(2,1)S(1)} collective-permute-done((bf16[256,512]{1,0:T(8,128)(2,1)S(1)}, bf16[256,512]{1,0:T(8,128)(2,1)S(1)}, u32[]{:S(2)}, u32[]{:S(2)}) %collective-permute-start.1) | collective-permute-done | bytes 262176 | tf_op jit(solution)/shard_map/ppermute | solution.py:155
  11.3 1.8 %collective-permute-start.5 = (bf16[256,512]{1,0:T(8,128)(2,1)S(1)}, bf16[256,512]{1,0:T(8,128)(2,1)S(1)}, u32[]{:S(2)}, u32[]{:S(2)}) collective-permute-start(bf16[256,512]{1,0:T(8,128)(2,1)S(1)} %collective-permute-done.1), channel_id=1, source_target_pairs={{0,4},{1,5},{4,8},{5,9},{8,12},{9,13},{12,14},{13,15},{14,10},{15,... | collective-permute-start | bytes 786440 | tf_op jit(solution)/shard_map/ppermute | solution.py:155
  13.1 0.5 fusion.19
  14.6 0.8 %collective-permute-done.4 = bf16[256,512]{1,0:T(8,128)(2,1)S(1)} collective-permute-done((bf16[256,512]{1,0:T(8,128)(2,1)S(1)}, bf16[256,512]{1,0:T(8,128)(2,1)S(1)}, u32[]{:S(2)}, u32[]{:S(2)}) %collective-permute-start.4) | collective-permute-done | bytes 262176 | tf_op jit(solution)/shard_map/ppermute | solution.py:160
  15.4 0.8 %fusion.85 = f32[512,1024]{0,1:T(8,128)S(1)} fusion(bf16[512,512]{1,0:T(8,128)(2,1)S(1)} %get-tuple-element.54, bf16[512,1024]{1,0:T(8,128)(2,1)S(1)} %constant_dynamic-update-slice_fusion), kind=kOutput, calls=%fused_computation.182 | convolution fusion | flops 536870912 | bytes 3670016 | tf_op jit(solution)/shard_map/dot_general | solution.py:30
  16.1 0.8 %multiply_convert_fusion.11 = (bf16[512,512]{0,1:T(8,128)(2,1)S(1)}, bf16[512,512]{0,1:T(8,128)(2,1)S(1)}) fusion(f32[512,1024]{0,1:T(8,128)S(1)} %fusion.85, bf16[512,512]{1,0:T(8,128)(2,1)S(1)} %get-tuple-element.53, bf16[512,512]{1,0:T(8,128)(2,1)S(1)} %copy-done.3), kind=kOutput, calls=%fused_computation.48 | convolution fusion | flops 271843328 | bytes 4194304 | tf_op jit(solution)/shard_map/dot_general | solution.py:33
  16.9 3.1 %collective-permute-done.5 = bf16[256,512]{1,0:T(8,128)(2,1)S(1)} collective-permute-done((bf16[256,512]{1,0:T(8,128)(2,1)S(1)}, bf16[256,512]{1,0:T(8,128)(2,1)S(1)}, u32[]{:S(2)}, u32[]{:S(2)}) %collective-permute-start.5) | collective-permute-done | bytes 262176 | tf_op jit(solution)/shard_map/ppermute | solution.py:155
  20.0 1.8 %collective-permute-start.9 = (bf16[256,512]{1,0:T(8,128)(2,1)S(1)}, bf16[256,512]{1,0:T(8,128)(2,1)S(1)}, u32[]{:S(2)}, u32[]{:S(2)}) collective-permute-start(bf16[256,512]{1,0:T(8,128)(2,1)S(1)} %collective-permute-done.5), channel_id=1, source_target_pairs={{0,4},{1,5},{4,8},{5,9},{8,12},{9,13},{12,14},{13,15},{14,10},{15,... | collective-permute-start | bytes 786440 | tf_op jit(solution)/shard_map/ppermute | solution.py:155
  22.9 0.8 %fusion.5 = f32[512,1024]{1,0:T(8,128)S(1)} fusion(bf16[512,512]{1,0:T(8,128)(2,1)S(1)} %get-tuple-element.54, bf16[512,512]{0,1:T(8,128)(2,1)S(1)} %get-tuple-element.26, bf16[512,512]{0,1:T(8,128)(2,1)S(1)} %get-tuple-element.25), kind=kOutput, calls=%fused_computation.19 | convolution fusion | flops 538968064 | bytes 3670016 | tf_op jit(solution)/shard_map/dot_general | solution.py:38
  23.7 5.1 %collective-permute-done.9 = bf16[256,512]{1,0:T(8,128)(2,1)S(1)} collective-permute-done((bf16[256,512]{1,0:T(8,128)(2,1)S(1)}, bf16[256,512]{1,0:T(8,128)(2,1)S(1)}, u32[]{:S(2)}, u32[]{:S(2)}) %collective-permute-start.9) | collective-permute-done | bytes 262176 | tf_op jit(solution)/shard_map/ppermute | solution.py:155
  28.8 1.9 %collective-permute-start.13 = (bf16[128,512]{1,0:T(8,128)(2,1)S(1)}, bf16[128,512]{1,0:T(8,128)(2,1)S(1)}, u32[]{:S(2)}, u32[]{:S(2)}) collective-permute-start(bf16[128,512]{1,0:T(8,128)(2,1)S(1)} %slice.384), channel_id=1, source_target_pairs={{0,4},{1,5},{4,8},{5,9},{8,12},{9,13},{12,14},{13,15},{14,10},{15,... | collective-permute-start | bytes 393224 | tf_op jit(solution)/shard_map/ppermute | solution.py:150
  30.6 0.6 %collective-permute-done.10 = bf16[256,512]{1,0:T(8,128)(2,1)S(1)} collective-permute-done((bf16[256,512]{1,0:T(8,128)(2,1)S(1)}, bf16[256,512]{1,0:T(8,128)(2,1)S(1)}, u32[]{:S(2)}, u32[]{:S(2)}) %collective-permute-start.10) | collective-permute-done | bytes 262176 | tf_op jit(solution)/shard_map/ppermute | solution.py:156
  31.3 0.5 %collective-permute-start.14 = (bf16[128,512]{1,0:T(8,128)(2,1)S(1)}, bf16[128,512]{1,0:T(8,128)(2,1)S(1)}, u32[]{:S(2)}, u32[]{:S(2)}) collective-permute-start(bf16[128,512]{1,0:T(8,128)(2,1)S(1)} %slice.385), channel_id=1, source_target_pairs={{0,2},{1,3},{4,0},{5,1},{8,4},{9,5},{12,8},{13,9},{14,12},{15,13},... | collective-permute-start | bytes 393224 | tf_op jit(solution)/shard_map/ppermute | solution.py:151
  31.9 0.8 %fusion.86 = f32[512,1024]{0,1:T(8,128)S(1)} fusion(bf16[512,512]{1,0:T(8,128)(2,1)S(1)} %get-tuple-element.78, bf16[512,1024]{1,0:T(8,128)(2,1)S(1)} %constant_dynamic-update-slice_fusion), kind=kOutput, calls=%fused_computation.183 | convolution fusion | flops 536870912 | bytes 3670016 | tf_op jit(solution)/shard_map/dot_general | solution.py:30
  32.6 0.8 %multiply_convert_fusion.9 = (bf16[512,512]{0,1:T(8,128)(2,1)S(1)}, bf16[512,512]{0,1:T(8,128)(2,1)S(1)}) fusion(f32[512,1024]{0,1:T(8,128)S(1)} %fusion.86, bf16[512,512]{1,0:T(8,128)(2,1)S(1)} %get-tuple-element.77, bf16[512,512]{1,0:T(8,128)(2,1)S(1)} %copy-done.3), kind=kOutput, calls=%fused_computation.44 | convolution fusion | flops 271843328 | bytes 4194304 | tf_op jit(solution)/shard_map/dot_general | solution.py:33
  33.4 0.5 %convolution_add_fusion.1 = f32[512,512]{1,0:T(8,128)S(1)} fusion(f32[512,512]{1,0:T(8,128)S(1)} %convolution_add_fusion.2, bf16[512,512]{1,0:T(8,128)(2,1)S(1)} %get-tuple-element.77, f32[512,1024]{0,1:T(8,128)S(1)} %fusion.86), kind=kOutput, calls=%fused_computation.3 | convolution fusion | flops 270270464 | bytes 4718592 | tf_op jit(solution)/shard_map/dot_general | solution.py:39
  34.0 0.5 %collective-permute-start.12 = (bf16[256,512]{1,0:T(8,128)(2,1)S(1)}, bf16[256,512]{1,0:T(8,128)(2,1)S(1)}, u32[]{:S(2)}, u32[]{:S(2)}) collective-permute-start(bf16[256,512]{1,0:T(8,128)(2,1)S(1)} %collective-permute-done.10), channel_id=1, source_target_pairs={{0,1},{1,0},{2,3},{3,2},{4,5},{5,4},{6,7},{7,6},{8,9},{9,8},{10,11... | collective-permute-start | bytes 786440 | tf_op jit(solution)/shard_map/ppermute | solution.py:160
  34.6 0.8 %fusion.9 = f32[512,1024]{1,0:T(8,128)S(1)} fusion(bf16[512,512]{1,0:T(8,128)(2,1)S(1)} %get-tuple-element.78, bf16[512,512]{0,1:T(8,128)(2,1)S(1)} %get-tuple-element.28, bf16[512,512]{0,1:T(8,128)(2,1)S(1)} %get-tuple-element.27), kind=kOutput, calls=%fused_computation.23 | convolution fusion | flops 538968064 | bytes 3670016 | tf_op jit(solution)/shard_map/dot_general | solution.py:38
  35.9 0.8 %fusion.87 = f32[512,1024]{0,1:T(8,128)S(1)} fusion(bf16[512,512]{1,0:T(8,128)(2,1)S(1)} %get-tuple-element.38, bf16[512,1024]{1,0:T(8,128)(2,1)S(1)} %constant_dynamic-update-slice_fusion), kind=kOutput, calls=%fused_computation.184 | convolution fusion | flops 536870912 | bytes 3670016 | tf_op jit(solution)/shard_map/dot_general | solution.py:30
  36.7 0.8 %multiply_convert_fusion.7 = (bf16[512,512]{0,1:T(8,128)(2,1)S(1)}, bf16[512,512]{0,1:T(8,128)(2,1)S(1)}) fusion(f32[512,1024]{0,1:T(8,128)S(1)} %fusion.87, bf16[512,512]{1,0:T(8,128)(2,1)S(1)} %get-tuple-element.37, bf16[512,512]{1,0:T(8,128)(2,1)S(1)} %copy-done.3), kind=kOutput, calls=%fused_computation.40 | convolution fusion | flops 271843328 | bytes 4194304 | tf_op jit(solution)/shard_map/dot_general | solution.py:33
  37.5 0.8 %add_add_fusion.1 = f32[512,1024]{1,0:T(8,128)S(1)} fusion(f32[512,1024]{1,0:T(8,128)S(1)} %fusion.9, f32[512,1024]{1,0:T(8,128)S(1)} %fusion.19, f32[512,1024]{1,0:T(8,128)S(1)} %fusion.5, bf16[512,512]{1,0:T(8,128)(2,1)S(1)} %get-tuple-element.38, bf16[512,512]{0,1:T(8,128)(2,1)S(1)} %get-tuple-element.24, bf16[512,512]{0,1:T(8,128)(2,1)S(1)} %get-tuple-element.23), kind=kOutput, calls=%fused_computation.1 | convolution fusion | flops 540540928 | bytes 9961472 | tf_op jit(solution)/shard_map/dot_general | solution.py:38
  38.3 0.5 %convolution_add_fusion = f32[512,512]{1,0:T(8,128)S(1)} fusion(f32[512,512]{1,0:T(8,128)S(1)} %convolution_add_fusion.1, bf16[512,512]{1,0:T(8,128)(2,1)S(1)} %get-tuple-element.37, f32[512,1024]{0,1:T(8,128)S(1)} %fusion.87), kind=kOutput, calls=%fused_computation.2 | convolution fusion | flops 270270464 | bytes 4718592 | tf_op jit(solution)/shard_map/dot_general | solution.py:39
  42.0 0.6 %copy-done.1 = bf16[512,512]{1,0:T(8,128)(2,1)S(1)} copy-done((bf16[512,512]{1,0:T(8,128)(2,1)S(1)}, bf16[512,512]{1,0:T(8,128)(2,1)}, u32[]{:S(2)}) %copy-start.1) | copy-done | bytes 524312
  42.6 0.5 %multiply_reduce_fusion.1 = (f32[512]{0:T(512)S(1)}, f32[512]{0:T(512)S(1)}, f32[512]{0:T(512)S(1)}, f32[512]{0:T(512)S(1)}) fusion(f32[512,1024]{1,0:T(8,128)S(1)} %add_add_fusion, bf16[512,512]{1,0:T(8,128)(2,1)S(1)} %copy-done.2, bf16[512,512]{1,0:T(8,128)(2,1)S(1)} %copy-done.1), kind=kLoop, calls=%fused_computation.33 | loop fusion | flops 3143680 | bytes 3153920 | tf_op jit(solution)/shard_map/reduce_sum | solution.py:19
  43.1 0.5 %multiply_reduce_fusion = (f32[512]{0:T(512)S(1)}, f32[512,512]{1,0:T(8,128)S(1)}) fusion(bf16[64,512]{1,0:T(8,128)(2,1)S(1)} %get-tuple-element.96, bf16[64,512]{1,0:T(8,128)(2,1)S(1)} %get-tuple-element.94, f32[128,1024]{1,0:T(8,128)S(1)} %fusion.49, f32[512,512]{1,0:T(8,128)S(1)} %convolution_add_fusion, f32[512,512]{1,0:T(8,128)S(1)} %fusion.42, ...), kind=kOutput, calls=%fused_computation.31 | convolution fusion | flops 69336576 | bytes 4327424 | tf_op jit(solution)/shard_map/dot_general | solution.py:39
  44.4 1.1 %convolution_convert_fusion = bf16[128,512]{1,0:T(8,128)(2,1)} fusion(bf16[512,512]{1,0:T(8,128)(2,1)S(1)} %multiply_convert_fusion, bf16[128,512]{1,0:T(8,128)(2,1)S(1)} %copy-done, bf16[512,512]{1,0:T(8,128)(2,1)S(1)} %get-tuple-element.17, f32[128,512]{1,0:T(8,128)S(1)} %convolution_bitcast_fusion.1), kind=kOutput, calls=%fused_computation.15 | convolution fusion | flops 134676480 | bytes 1572864 | tf_op jit(solution)/shard_map/dot_general | solution.py:47
  (78 shorter events, 7.7 us)
Async XLA Ops:
  0.0 44.2 %copy-start = (bf16[128,512]{1,0:T(8,128)(2,1)S(1)}, bf16[128,512]{1,0:T(8,128)(2,1)}, u32[]{:S(2)}) copy-start(bf16[128,512]{1,0:T(8,128)(2,1)} %param.9) | copy-start | bytes 393220
  0.0 7.5 %copy-start.2 = (bf16[512,512]{1,0:T(8,128)(2,1)S(1)}, bf16[512,512]{1,0:T(8,128)(2,1)}, u32[]{:S(2)}) copy-start(bf16[512,512]{1,0:T(8,128)(2,1)} %param.12) | copy-start | bytes 1572868
  2.0 9.3 %collective-permute-start.1 = (bf16[256,512]{1,0:T(8,128)(2,1)S(1)}, bf16[256,512]{1,0:T(8,128)(2,1)S(1)}, u32[]{:S(2)}, u32[]{:S(2)}) collective-permute-start(bf16[256,512]{1,0:T(8,128)(2,1)S(1)} %bitcast.42), channel_id=1, source_target_pairs={{0,4},{1,5},{4,8},{5,9},{8,12},{9,13},{12,14},{13,15},{14,10},{15,... | collective-permute-start | bytes 786440 | tf_op jit(solution)/shard_map/ppermute | solution.py:155
  5.1 2.5 %collective-permute-start = (bf16[256,512]{1,0:T(8,128)(2,1)S(1)}, bf16[256,512]{1,0:T(8,128)(2,1)S(1)}, u32[]{:S(2)}, u32[]{:S(2)}) collective-permute-start(bf16[256,512]{1,0:T(8,128)(2,1)S(1)} %bitcast.43), channel_id=1, source_target_pairs={{0,1},{1,0},{2,3},{3,2},{4,5},{5,4},{6,7},{7,6},{8,9},{9,8},{10,11... | collective-permute-start | bytes 786440 | tf_op jit(solution)/shard_map/ppermute | solution.py:144
  5.1 8.7 %collective-permute-start.2 = (bf16[256,512]{1,0:T(8,128)(2,1)S(1)}, bf16[256,512]{1,0:T(8,128)(2,1)S(1)}, u32[]{:S(2)}, u32[]{:S(2)}) collective-permute-start(bf16[256,512]{1,0:T(8,128)(2,1)S(1)} %bitcast.44), channel_id=1, source_target_pairs={{0,2},{1,3},{4,0},{5,1},{8,4},{9,5},{12,8},{13,9},{14,12},{15,13},... | collective-permute-start | bytes 786440 | tf_op jit(solution)/shard_map/ppermute | solution.py:156
  7.5 1.0 %copy-start.3 = (bf16[512,512]{1,0:T(8,128)(2,1)S(1)}, bf16[512,512]{1,0:T(8,128)(2,1)}, u32[]{:S(2)}) copy-start(bf16[512,512]{1,0:T(8,128)(2,1)} %param.13) | copy-start | bytes 1572868
  11.3 3.2 %collective-permute-start.3 = (bf16[256,512]{1,0:T(8,128)(2,1)S(1)}, bf16[256,512]{1,0:T(8,128)(2,1)S(1)}, u32[]{:S(2)}, u32[]{:S(2)}) collective-permute-start(bf16[256,512]{1,0:T(8,128)(2,1)S(1)} %collective-permute-done.1), channel_id=1, source_target_pairs={{0,1},{1,0},{2,3},{3,2},{4,5},{5,4},{6,7},{7,6},{8,9},{9,8},{10,11... | collective-permute-start | bytes 786440 | tf_op jit(solution)/shard_map/ppermute | solution.py:160
  11.3 8.7 %collective-permute-start.5 = (bf16[256,512]{1,0:T(8,128)(2,1)S(1)}, bf16[256,512]{1,0:T(8,128)(2,1)S(1)}, u32[]{:S(2)}, u32[]{:S(2)}) collective-permute-start(bf16[256,512]{1,0:T(8,128)(2,1)S(1)} %collective-permute-done.1), channel_id=1, source_target_pairs={{0,4},{1,5},{4,8},{5,9},{8,12},{9,13},{12,14},{13,15},{14,10},{15,... | collective-permute-start | bytes 786440 | tf_op jit(solution)/shard_map/ppermute | solution.py:155
  13.8 1.5 %collective-permute-start.4 = (bf16[256,512]{1,0:T(8,128)(2,1)S(1)}, bf16[256,512]{1,0:T(8,128)(2,1)S(1)}, u32[]{:S(2)}, u32[]{:S(2)}) collective-permute-start(bf16[256,512]{1,0:T(8,128)(2,1)S(1)} %collective-permute-done.2), channel_id=1, source_target_pairs={{0,1},{1,0},{2,3},{3,2},{4,5},{5,4},{6,7},{7,6},{8,9},{9,8},{10,11... | collective-permute-start | bytes 786440 | tf_op jit(solution)/shard_map/ppermute | solution.py:160
  13.9 8.6 %collective-permute-start.6 = (bf16[256,512]{1,0:T(8,128)(2,1)S(1)}, bf16[256,512]{1,0:T(8,128)(2,1)S(1)}, u32[]{:S(2)}, u32[]{:S(2)}) collective-permute-start(bf16[256,512]{1,0:T(8,128)(2,1)S(1)} %collective-permute-done.2), channel_id=1, source_target_pairs={{0,2},{1,3},{4,0},{5,1},{8,4},{9,5},{12,8},{13,9},{14,12},{15,13},... | collective-permute-start | bytes 786440 | tf_op jit(solution)/shard_map/ppermute | solution.py:156
  20.0 11.8 %collective-permute-start.7 = (bf16[256,512]{1,0:T(8,128)(2,1)S(1)}, bf16[256,512]{1,0:T(8,128)(2,1)S(1)}, u32[]{:S(2)}, u32[]{:S(2)}) collective-permute-start(bf16[256,512]{1,0:T(8,128)(2,1)S(1)} %collective-permute-done.5), channel_id=1, source_target_pairs={{0,1},{1,0},{2,3},{3,2},{4,5},{5,4},{6,7},{7,6},{8,9},{9,8},{10,11... | collective-permute-start | bytes 786440 | tf_op jit(solution)/shard_map/ppermute | solution.py:160
  20.0 8.7 %collective-permute-start.9 = (bf16[256,512]{1,0:T(8,128)(2,1)S(1)}, bf16[256,512]{1,0:T(8,128)(2,1)S(1)}, u32[]{:S(2)}, u32[]{:S(2)}) collective-permute-start(bf16[256,512]{1,0:T(8,128)(2,1)S(1)} %collective-permute-done.5), channel_id=1, source_target_pairs={{0,4},{1,5},{4,8},{5,9},{8,12},{9,13},{12,14},{13,15},{14,10},{15,... | collective-permute-start | bytes 786440 | tf_op jit(solution)/shard_map/ppermute | solution.py:155
  22.5 9.3 %collective-permute-start.8 = (bf16[256,512]{1,0:T(8,128)(2,1)S(1)}, bf16[256,512]{1,0:T(8,128)(2,1)S(1)}, u32[]{:S(2)}, u32[]{:S(2)}) collective-permute-start(bf16[256,512]{1,0:T(8,128)(2,1)S(1)} %collective-permute-done.6), channel_id=1, source_target_pairs={{0,1},{1,0},{2,3},{3,2},{4,5},{5,4},{6,7},{7,6},{8,9},{9,8},{10,11... | collective-permute-start | bytes 786440 | tf_op jit(solution)/shard_map/ppermute | solution.py:160
  22.6 8.7 %collective-permute-start.10 = (bf16[256,512]{1,0:T(8,128)(2,1)S(1)}, bf16[256,512]{1,0:T(8,128)(2,1)S(1)}, u32[]{:S(2)}, u32[]{:S(2)}) collective-permute-start(bf16[256,512]{1,0:T(8,128)(2,1)S(1)} %collective-permute-done.6), channel_id=1, source_target_pairs={{0,2},{1,3},{4,0},{5,1},{8,4},{9,5},{12,8},{13,9},{14,12},{15,13},... | collective-permute-start | bytes 786440 | tf_op jit(solution)/shard_map/ppermute | solution.py:156
  28.8 10.0 %collective-permute-start.13 = (bf16[128,512]{1,0:T(8,128)(2,1)S(1)}, bf16[128,512]{1,0:T(8,128)(2,1)S(1)}, u32[]{:S(2)}, u32[]{:S(2)}) collective-permute-start(bf16[128,512]{1,0:T(8,128)(2,1)S(1)} %slice.384), channel_id=1, source_target_pairs={{0,4},{1,5},{4,8},{5,9},{8,12},{9,13},{12,14},{13,15},{14,10},{15,... | collective-permute-start | bytes 393224 | tf_op jit(solution)/shard_map/ppermute | solution.py:150
  31.3 7.5 %collective-permute-start.14 = (bf16[128,512]{1,0:T(8,128)(2,1)S(1)}, bf16[128,512]{1,0:T(8,128)(2,1)S(1)}, u32[]{:S(2)}, u32[]{:S(2)}) collective-permute-start(bf16[128,512]{1,0:T(8,128)(2,1)S(1)} %slice.385), channel_id=1, source_target_pairs={{0,2},{1,3},{4,0},{5,1},{8,4},{9,5},{12,8},{13,9},{14,12},{15,13},... | collective-permute-start | bytes 393224 | tf_op jit(solution)/shard_map/ppermute | solution.py:151
  33.9 1.6 %collective-permute-start.11 = (bf16[256,512]{1,0:T(8,128)(2,1)S(1)}, bf16[256,512]{1,0:T(8,128)(2,1)S(1)}, u32[]{:S(2)}, u32[]{:S(2)}) collective-permute-start(bf16[256,512]{1,0:T(8,128)(2,1)S(1)} %collective-permute-done.9), channel_id=1, source_target_pairs={{0,1},{1,0},{2,3},{3,2},{4,5},{5,4},{6,7},{7,6},{8,9},{9,8},{10,11... | collective-permute-start | bytes 786440 | tf_op jit(solution)/shard_map/ppermute | solution.py:160
  34.0 1.9 %collective-permute-start.12 = (bf16[256,512]{1,0:T(8,128)(2,1)S(1)}, bf16[256,512]{1,0:T(8,128)(2,1)S(1)}, u32[]{:S(2)}, u32[]{:S(2)}) collective-permute-start(bf16[256,512]{1,0:T(8,128)(2,1)S(1)} %collective-permute-done.10), channel_id=1, source_target_pairs={{0,1},{1,0},{2,3},{3,2},{4,5},{5,4},{6,7},{7,6},{8,9},{9,8},{10,11... | collective-permute-start | bytes 786440 | tf_op jit(solution)/shard_map/ppermute | solution.py:160
  38.8 2.0 %collective-permute-start.15 = (bf16[128,512]{1,0:T(8,128)(2,1)S(1)}, bf16[128,512]{1,0:T(8,128)(2,1)S(1)}, u32[]{:S(2)}, u32[]{:S(2)}) collective-permute-start(bf16[128,512]{1,0:T(8,128)(2,1)S(1)} %collective-permute-done.13), channel_id=1, source_target_pairs={{0,1},{1,0},{2,3},{3,2},{4,5},{5,4},{6,7},{7,6},{8,9},{9,8},{10,11... | collective-permute-start | bytes 393224 | tf_op jit(solution)/shard_map/ppermute | solution.py:160
  39.0 1.9 %collective-permute-start.16 = (bf16[128,512]{1,0:T(8,128)(2,1)S(1)}, bf16[128,512]{1,0:T(8,128)(2,1)S(1)}, u32[]{:S(2)}, u32[]{:S(2)}) collective-permute-start(bf16[128,512]{1,0:T(8,128)(2,1)S(1)} %collective-permute-done.14), channel_id=1, source_target_pairs={{0,1},{1,0},{2,3},{3,2},{4,5},{5,4},{6,7},{7,6},{8,9},{9,8},{10,11... | collective-permute-start | bytes 393224 | tf_op jit(solution)/shard_map/ppermute | solution.py:160
  41.5 1.0 %copy-start.1 = (bf16[512,512]{1,0:T(8,128)(2,1)S(1)}, bf16[512,512]{1,0:T(8,128)(2,1)}, u32[]{:S(2)}) copy-start(bf16[512,512]{1,0:T(8,128)(2,1)} %param.11) | copy-start | bytes 1572868

commit v19 on v12

--- a/solution.py
+++ b/solution.py
@@ -156,7 +156,7 @@
             if step == steps:
                 total, arrived = lax.optimization_barrier((total, arrived))
             from_sib = [lax.ppermute(chunk, axes, swap) for chunk in arrived]
-            if step == steps:
+            if step >= steps - 1:
                 total = add_grads(total, *split(arrived, half), w_gate, w_up, w_out)
                 total = add_grads(total, *split(from_sib, half), w_gate, w_up, w_out)
             else:

time: 44.3 us -> 47.4 us (1.070)
  waiting for transfers between devices: 12 us -> 14.1 us
  matrix products: 15.6 us -> 16.6 us
    ppermute x3, waiting for transfers between devices: 0.08 us -> 1.49 us  [local_ring(): lax.ppermute(arrived[1], axes, ccw_perm)]
    ppermute x3, waiting for transfers between devices: 10.3 us -> 10.7 us  [local_ring(): lax.ppermute(arrived[0], axes, cw_perm)]
    dot_general x6 -> x7, matrix products: 2.64 us -> 2.96 us  [gradients(): lax.dot_general(activation, scaled, contract_first, preferred_element_typ...]
    dot_general x6 -> x7, matrix products: 3.67 us -> 3.98 us  [gradients(): lax.dot_general(keys, both_grads, contract_first, preferred_element_type=...]
    dot_general x6 -> x7, matrix products: 3.51 us -> 3.64 us  [gradients(): lax.dot_general(scaled, w_out, contract_last, preferred_element_type=jnp....]
    dot_general x6 -> x7, matrix products: 2.19 us -> 2.3 us  [gradients(): up_pre = jnp.dot(keys, w_up, preferred_element_type=jnp.float32)]
    dot_general x6 -> x7, matrix products: 2.31 us -> 2.42 us  [gradients(): gate_pre = jnp.dot(keys, w_gate, preferred_element_type=jnp.float32)]
  transfers between devices with their start and end apart: 17 -> 17, of which waited for: 9 -> 9; matrix products, arithmetic and copies ran while one was open for 32% -> 30% of each run, Pallas kernels for 0% -> 0%
where the time goes in v19:
time: 47.4 us; the launch traced here: 47.1 us
  matrix products  16.6 us (35%)
  waiting for transfers between devices  14.1 us (30%)
  starting transfers between devices  11.3 us (24%)
  other arithmetic  4.29 us (9%)
  between operations  0.51 us (1%)
    ppermute x3, waiting for transfers between devices, local_ring(): lax.ppermute(arrived[0], axes, cw_perm)  10.7 us
    ppermute x3, starting transfers between devices, local_ring(): lax.ppermute(arrived[0], axes, cw_perm)  6.73 us
    dot_general x7, matrix products, gradients(): lax.dot_general(keys, both_grads, contract_first, preferred_element_type=...  3.98 us
    dot_general x7, matrix products, gradients(): lax.dot_general(scaled, w_out, contract_last, preferred_element_type=jnp....  3.64 us
    dot_general x7, matrix products, gradients(): lax.dot_general(activation, scaled, contract_first, preferred_element_typ...  2.96 us
    dot_general x7, matrix products, gradients(): gate_pre = jnp.dot(keys, w_gate, preferred_element_type=jnp.float32)  2.42 us
    dot_general x7, matrix products, gradients(): up_pre = jnp.dot(keys, w_up, preferred_element_type=jnp.float32)  2.3 us
    ppermute x8, starting transfers between devices, local_ring(): from_sib = [lax.ppermute(chunk, axes, swap) for chunk in arrived]  1.79 us
  transfers between devices with their start and end apart: 17, of which 9 were waited for; matrix products, arithmetic and copies ran while one was open for 30% of the time, Pallas kernels for 0%

profile of v19, /device:TPU:0, one launch (start us, length us, event | category | flops | bytes accessed | tf_op | source)
XLA Modules:
  0.0 47.1 jit_solution(11397388047802684203)
XLA Ops:
  0.0 1.1 %multiply_convert_fusion.29 = bf16[128,512]{1,0:T(8,128)(2,1)S(1)} fusion(bf16[128,512]{1,0:T(8,128)(2,1)} %param.8, f32[128]{0:T(128)} %param.10), kind=kLoop, calls=%fused_computation.102 | loop fusion | flops 196608 | bytes 262656 | tf_op jit(solution)/shard_map/convert_element_type | solution.py:137
  1.1 0.9 %pad_maximum_fusion = bf16[2,2,64,512]{3,2,1,0:T(8,128)(2,1)S(1)} fusion(bf16[2,1,64,512]{3,2,1,0:T(8,128)(2,1)S(1)} %bitcast.53, bf16[2,1,64,512]{3,2,1,0:T(8,128)(2,1)} %bitcast.54), kind=kLoop, calls=%fused_computation.72 | loop fusion | flops 131072 | bytes 524288 | tf_op jit(solution)/shard_map/stack | solution.py:139
  2.0 3.1 %collective-permute-start.1 = (bf16[256,512]{1,0:T(8,128)(2,1)S(1)}, bf16[256,512]{1,0:T(8,128)(2,1)S(1)}, u32[]{:S(2)}, u32[]{:S(2)}) collective-permute-start(bf16[256,512]{1,0:T(8,128)(2,1)S(1)} %bitcast.49), channel_id=1, source_target_pairs={{0,4},{1,5},{4,8},{5,9},{8,12},{9,13},{12,14},{13,15},{14,10},{15,... | collective-permute-start | bytes 786440 | tf_op jit(solution)/shard_map/ppermute | solution.py:153
  5.1 1.2 %fusion.5 = f32[512]{0:T(512)S(1)} fusion(bf16[512,512]{1,0:T(8,128)(2,1)} %param.13), kind=kLoop, calls=%fused_computation.19 | loop fusion | flops 785920 | bytes 526336 | tf_op jit(solution)/shard_map/reduce_sum | solution.py:18
  7.4 0.5 multiply_convert_fusion.19
  8.3 3.0 %collective-permute-done.1 = bf16[256,512]{1,0:T(8,128)(2,1)S(1)} collective-permute-done((bf16[256,512]{1,0:T(8,128)(2,1)S(1)}, bf16[256,512]{1,0:T(8,128)(2,1)S(1)}, u32[]{:S(2)}, u32[]{:S(2)}) %collective-permute-start.1) | collective-permute-done | bytes 262176 | tf_op jit(solution)/shard_map/ppermute | solution.py:153
  11.3 1.8 %collective-permute-start.5 = (bf16[256,512]{1,0:T(8,128)(2,1)S(1)}, bf16[256,512]{1,0:T(8,128)(2,1)S(1)}, u32[]{:S(2)}, u32[]{:S(2)}) collective-permute-start(bf16[256,512]{1,0:T(8,128)(2,1)S(1)} %collective-permute-done.1), channel_id=1, source_target_pairs={{0,4},{1,5},{4,8},{5,9},{8,12},{9,13},{12,14},{13,15},{14,10},{15,... | collective-permute-start | bytes 786440 | tf_op jit(solution)/shard_map/ppermute | solution.py:153
  14.2 0.6 %collective-permute-done.4 = bf16[256,512]{1,0:T(8,128)(2,1)S(1)} collective-permute-done((bf16[256,512]{1,0:T(8,128)(2,1)S(1)}, bf16[256,512]{1,0:T(8,128)(2,1)S(1)}, u32[]{:S(2)}, u32[]{:S(2)}) %collective-permute-start.4) | collective-permute-done | bytes 262176 | tf_op jit(solution)/shard_map/ppermute | solution.py:158
  14.8 0.5 %fusion.113 = f32[512,512]{0,1:T(8,128)S(1)} fusion(bf16[512,512]{1,0:T(8,128)(2,1)S(1)} %get-tuple-element.48, bf16[512,512]{1,0:T(8,128)(2,1)S(1)} %copy-done.1), kind=kOutput, calls=%fused_computation.199 | convolution fusion | flops 268435456 | bytes 2097152 | tf_op jit(solution)/shard_map/dot_general | solution.py:30
  15.3 0.5 %fusion.114 = f32[512,512]{0,1:T(8,128)S(1)} fusion(bf16[512,512]{1,0:T(8,128)(2,1)S(1)} %get-tuple-element.48, bf16[512,512]{1,0:T(8,128)(2,1)S(1)} %copy-done.2), kind=kOutput, calls=%fused_computation.200 | convolution fusion | flops 268435456 | bytes 2097152 | tf_op jit(solution)/shard_map/dot_general | solution.py:29
  15.8 0.8 %multiply_convert_fusion.8 = (bf16[512,512]{0,1:T(8,128)(2,1)S(1)}, bf16[512,512]{0,1:T(8,128)(2,1)S(1)}) fusion(f32[512,512]{0,1:T(8,128)S(1)} %fusion.114, f32[512,512]{0,1:T(8,128)S(1)} %fusion.113, bf16[512,512]{1,0:T(8,128)(2,1)S(1)} %get-tuple-element.47, bf16[512,512]{1,0:T(8,128)(2,1)S(1)} %copy-done.3), kind=kOutput, calls=%fused_computation.41 | convolution fusion | flops 271843328 | bytes 4194304 | tf_op jit(solution)/shard_map/dot_general | solution.py:31
  16.6 0.5 convolution_add_fusion.1
  17.1 3.0 %collective-permute-done.5 = bf16[256,512]{1,0:T(8,128)(2,1)S(1)} collective-permute-done((bf16[256,512]{1,0:T(8,128)(2,1)S(1)}, bf16[256,512]{1,0:T(8,128)(2,1)S(1)}, u32[]{:S(2)}, u32[]{:S(2)}) %collective-permute-start.5) | collective-permute-done | bytes 262176 | tf_op jit(solution)/shard_map/ppermute | solution.py:153
  20.1 1.8 %collective-permute-start.9 = (bf16[256,512]{1,0:T(8,128)(2,1)S(1)}, bf16[256,512]{1,0:T(8,128)(2,1)S(1)}, u32[]{:S(2)}, u32[]{:S(2)}) collective-permute-start(bf16[256,512]{1,0:T(8,128)(2,1)S(1)} %collective-permute-done.5), channel_id=1, source_target_pairs={{0,4},{1,5},{4,8},{5,9},{8,12},{9,13},{12,14},{13,15},{14,10},{15,... | collective-permute-start | bytes 786440 | tf_op jit(solution)/shard_map/ppermute | solution.py:153
  22.5 0.8 %fusion.6 = f32[512,1024]{1,0:T(8,128)S(1)} fusion(bf16[512,512]{1,0:T(8,128)(2,1)S(1)} %get-tuple-element.48, bf16[512,512]{0,1:T(8,128)(2,1)S(1)} %get-tuple-element.26, bf16[512,512]{0,1:T(8,128)(2,1)S(1)} %get-tuple-element.25), kind=kOutput, calls=%fused_computation.20 | convolution fusion | flops 538968064 | bytes 3670016 | tf_op jit(solution)/shard_map/dot_general | solution.py:36
  23.5 0.5 %fusion.115 = f32[512,512]{0,1:T(8,128)S(1)} fusion(bf16[512,512]{1,0:T(8,128)(2,1)S(1)} %get-tuple-element.72, bf16[512,512]{1,0:T(8,128)(2,1)S(1)} %copy-done.1), kind=kOutput, calls=%fused_computation.201 | convolution fusion | flops 268435456 | bytes 2097152 | tf_op jit(solution)/shard_map/dot_general | solution.py:30
  24.0 4.7 %collective-permute-done.9 = bf16[256,512]{1,0:T(8,128)(2,1)S(1)} collective-permute-done((bf16[256,512]{1,0:T(8,128)(2,1)S(1)}, bf16[256,512]{1,0:T(8,128)(2,1)S(1)}, u32[]{:S(2)}, u32[]{:S(2)}) %collective-permute-start.9) | collective-permute-done | bytes 262176 | tf_op jit(solution)/shard_map/ppermute | solution.py:153
  28.8 0.5 %fusion.116 = f32[512,512]{0,1:T(8,128)S(1)} fusion(bf16[512,512]{1,0:T(8,128)(2,1)S(1)} %get-tuple-element.72, bf16[512,512]{1,0:T(8,128)(2,1)S(1)} %copy-done.2), kind=kOutput, calls=%fused_computation.202 | convolution fusion | flops 268435456 | bytes 2097152 | tf_op jit(solution)/shard_map/dot_general | solution.py:29
  29.3 1.4 %collective-permute-done.10 = bf16[256,512]{1,0:T(8,128)(2,1)S(1)} collective-permute-done((bf16[256,512]{1,0:T(8,128)(2,1)S(1)}, bf16[256,512]{1,0:T(8,128)(2,1)S(1)}, u32[]{:S(2)}, u32[]{:S(2)}) %collective-permute-start.10) | collective-permute-done | bytes 262176 | tf_op jit(solution)/shard_map/ppermute | solution.py:154
  31.3 1.6 %collective-permute-start.13 = (bf16[128,512]{1,0:T(8,128)(2,1)S(1)}, bf16[128,512]{1,0:T(8,128)(2,1)S(1)}, u32[]{:S(2)}, u32[]{:S(2)}) collective-permute-start(bf16[128,512]{1,0:T(8,128)(2,1)S(1)} %slice.328), channel_id=1, source_target_pairs={{0,4},{1,5},{4,8},{5,9},{8,12},{9,13},{12,14},{13,15},{14,10},{15,... | collective-permute-start | bytes 393224 | tf_op jit(solution)/shard_map/ppermute | solution.py:148
  33.0 0.7 %collective-permute-start.14 = (bf16[128,512]{1,0:T(8,128)(2,1)S(1)}, bf16[128,512]{1,0:T(8,128)(2,1)S(1)}, u32[]{:S(2)}, u32[]{:S(2)}) collective-permute-start(bf16[128,512]{1,0:T(8,128)(2,1)S(1)} %slice.329), channel_id=1, source_target_pairs={{0,2},{1,3},{4,0},{5,1},{8,4},{9,5},{12,8},{13,9},{14,12},{15,13},... | collective-permute-start | bytes 393224 | tf_op jit(solution)/shard_map/ppermute | solution.py:149
  33.7 0.8 %multiply_convert_fusion.6 = (bf16[512,512]{0,1:T(8,128)(2,1)S(1)}, bf16[512,512]{0,1:T(8,128)(2,1)S(1)}) fusion(f32[512,512]{0,1:T(8,128)S(1)} %fusion.116, f32[512,512]{0,1:T(8,128)S(1)} %fusion.115, bf16[512,512]{1,0:T(8,128)(2,1)S(1)} %get-tuple-element.71, bf16[512,512]{1,0:T(8,128)(2,1)S(1)} %copy-done.3), kind=kOutput, calls=%fused_computation.37 | convolution fusion | flops 271843328 | bytes 4194304 | tf_op jit(solution)/shard_map/dot_general | solution.py:31
  34.8 0.5 %fusion = f32[512,512]{1,0:T(8,128)S(1)} fusion(f32[512,512]{1,0:T(8,128)S(1)} %fusion.31, f32[512,512]{1,0:T(8,128)S(1)} %convolution_add_fusion.1, bf16[512,512]{1,0:T(8,128)(2,1)S(1)} %get-tuple-element.71, f32[512,512]{0,1:T(8,128)S(1)} %fusion.115, f32[512,512]{0,1:T(8,128)S(1)} %fusion.116), kind=kOutput, calls=%fused_computation.3 | convolution fusion | flops 270532608 | bytes 5767168 | tf_op jit(solution)/shard_map/dot_general | solution.py:37
  35.3 0.8 %fusion.10 = f32[512,1024]{1,0:T(8,128)S(1)} fusion(bf16[512,512]{1,0:T(8,128)(2,1)S(1)} %get-tuple-element.72, bf16[512,512]{0,1:T(8,128)(2,1)S(1)} %get-tuple-element.28, bf16[512,512]{0,1:T(8,128)(2,1)S(1)} %get-tuple-element.27), kind=kOutput, calls=%fused_computation.24 | convolution fusion | flops 538968064 | bytes 3670016 | tf_op jit(solution)/shard_map/dot_general | solution.py:36
  36.2 0.5 multiply_convert_fusion.17
  36.7 0.6 %collective-permute-start.12 = (bf16[256,512]{1,0:T(8,128)(2,1)S(1)}, bf16[256,512]{1,0:T(8,128)(2,1)S(1)}, u32[]{:S(2)}, u32[]{:S(2)}) collective-permute-start(bf16[256,512]{1,0:T(8,128)(2,1)S(1)} %collective-permute-done.10), channel_id=1, source_target_pairs={{0,1},{1,0},{2,3},{3,2},{4,5},{5,4},{6,7},{7,6},{8,9},{9,8},{10,11... | collective-permute-start | bytes 786440 | tf_op jit(solution)/shard_map/ppermute | solution.py:158
  37.7 0.7 %collective-permute-done.12 = bf16[256,512]{1,0:T(8,128)(2,1)S(1)} collective-permute-done((bf16[256,512]{1,0:T(8,128)(2,1)S(1)}, bf16[256,512]{1,0:T(8,128)(2,1)S(1)}, u32[]{:S(2)}, u32[]{:S(2)}) %collective-permute-start.12) | collective-permute-done | bytes 262176 | tf_op jit(solution)/shard_map/ppermute | solution.py:158
  39.5 0.6 %add_add_fusion.1 = f32[512,1024]{1,0:T(8,128)S(1)} fusion(f32[512,1024]{1,0:T(8,128)S(1)} %fusion.20, f32[512,1024]{1,0:T(8,128)S(1)} %fusion.10, f32[512,1024]{1,0:T(8,128)S(1)} %fusion.16, f32[512,1024]{1,0:T(8,128)S(1)} %fusion.6, bf16[256,512]{1,0:T(8,128)(2,1)S(1)} %get-tuple-element.30, bf16[256,512]{1,0:T(8,128)(2,1)S(1)} %get-tuple-element.29, ...), kind=kOutput, calls=%fused_computation.1 | convolution fusion | flops 272629760 | bytes 11272192 | tf_op jit(solution)/shard_map/dot_general | solution.py:36
  43.7 0.5 %add_add_fusion = f32[512,1024]{1,0:T(8,128)S(1)} fusion(f32[512,1024]{1,0:T(8,128)S(1)} %add_add_fusion.1, f32[512,1024]{1,0:T(8,128)S(1)} %fusion.32, bf16[128,512]{1,0:T(8,128)(2,1)S(1)} %get-tuple-element.36, bf16[128,512]{1,0:T(8,128)(2,1)S(1)} %get-tuple-element.35, bf16[64,512]{1,0:T(8,128)(2,1)S(1)} %get-tuple-element.97, ...), kind=kOutput, calls=%fused_computation | convolution fusion | flops 136052736 | bytes 6684672 | tf_op jit(solution)/shard_map/dot_general | solution.py:36
  44.2 0.5 %multiply_reduce_fusion.1 = (f32[512]{0:T(512)S(1)}, f32[512]{0:T(512)S(1)}, f32[512]{0:T(512)S(1)}, f32[512]{0:T(512)S(1)}) fusion(f32[512,1024]{1,0:T(8,128)S(1)} %add_add_fusion, bf16[512,512]{1,0:T(8,128)(2,1)S(1)} %copy-done.1, bf16[512,512]{1,0:T(8,128)(2,1)S(1)} %copy-done.2), kind=kLoop, calls=%fused_computation.31 | loop fusion | flops 3143680 | bytes 3153920 | tf_op jit(solution)/shard_map/reduce_sum | solution.py:19
  44.8 0.5 %multiply_reduce_fusion = (f32[512]{0:T(512)S(1)}, f32[512,512]{1,0:T(8,128)S(1)}) fusion(bf16[64,512]{1,0:T(8,128)(2,1)S(1)} %get-tuple-element.98, bf16[64,512]{1,0:T(8,128)(2,1)S(1)} %get-tuple-element.96, f32[128,512]{1,0:T(8,128)S(1)} %fusion.65, f32[128,512]{1,0:T(8,128)S(1)} %fusion.64, f32[512,512]{1,0:T(8,128)S(1)} %convolution_add_fusion.2, ...), kind=kOutput, calls=%fused_computation.29 | convolution fusion | flops 69336576 | bytes 4327424 | tf_op jit(solution)/shard_map/dot_general | solution.py:37
  46.1 1.1 %convolution_convert_fusion = bf16[128,512]{1,0:T(8,128)(2,1)} fusion(bf16[512,512]{1,0:T(8,128)(2,1)S(1)} %multiply_convert_fusion, bf16[128,512]{1,0:T(8,128)(2,1)S(1)} %copy-done, bf16[512,512]{1,0:T(8,128)(2,1)S(1)} %get-tuple-element.17, f32[128,512]{1,0:T(8,128)S(1)} %convolution_bitcast_fusion.1), kind=kOutput, calls=%fused_computation.16 | convolution fusion | flops 134676480 | bytes 1572864 | tf_op jit(solution)/shard_map/dot_general | solution.py:45
  (83 shorter events, 10.2 us)
Async XLA Ops:
  0.0 45.8 %copy-start = (bf16[128,512]{1,0:T(8,128)(2,1)S(1)}, bf16[128,512]{1,0:T(8,128)(2,1)}, u32[]{:S(2)}) copy-start(bf16[128,512]{1,0:T(8,128)(2,1)} %param.9) | copy-start | bytes 393220
  0.0 6.7 %copy-start.2 = (bf16[512,512]{1,0:T(8,128)(2,1)S(1)}, bf16[512,512]{1,0:T(8,128)(2,1)}, u32[]{:S(2)}) copy-start(bf16[512,512]{1,0:T(8,128)(2,1)} %param.11) | copy-start | bytes 1572868
  0.0 7.0 %copy-start.1 = (bf16[512,512]{1,0:T(8,128)(2,1)S(1)}, bf16[512,512]{1,0:T(8,128)(2,1)}, u32[]{:S(2)}) copy-start(bf16[512,512]{1,0:T(8,128)(2,1)} %param.12) | copy-start | bytes 1572868
  2.0 9.3 %collective-permute-start.1 = (bf16[256,512]{1,0:T(8,128)(2,1)S(1)}, bf16[256,512]{1,0:T(8,128)(2,1)S(1)}, u32[]{:S(2)}, u32[]{:S(2)}) collective-permute-start(bf16[256,512]{1,0:T(8,128)(2,1)S(1)} %bitcast.49), channel_id=1, source_target_pairs={{0,4},{1,5},{4,8},{5,9},{8,12},{9,13},{12,14},{13,15},{14,10},{15,... | collective-permute-start | bytes 786440 | tf_op jit(solution)/shard_map/ppermute | solution.py:153
  5.1 8.1 %collective-permute-start.2 = (bf16[256,512]{1,0:T(8,128)(2,1)S(1)}, bf16[256,512]{1,0:T(8,128)(2,1)S(1)}, u32[]{:S(2)}, u32[]{:S(2)}) collective-permute-start(bf16[256,512]{1,0:T(8,128)(2,1)S(1)} %bitcast.50), channel_id=1, source_target_pairs={{0,2},{1,3},{4,0},{5,1},{8,4},{9,5},{12,8},{13,9},{14,12},{15,13},... | collective-permute-start | bytes 786440 | tf_op jit(solution)/shard_map/ppermute | solution.py:154
  5.1 1.5 %collective-permute-start = (bf16[256,512]{1,0:T(8,128)(2,1)S(1)}, bf16[256,512]{1,0:T(8,128)(2,1)S(1)}, u32[]{:S(2)}, u32[]{:S(2)}) collective-permute-start(bf16[256,512]{1,0:T(8,128)(2,1)S(1)} %bitcast.51), channel_id=1, source_target_pairs={{0,1},{1,0},{2,3},{3,2},{4,5},{5,4},{6,7},{7,6},{8,9},{9,8},{10,11... | collective-permute-start | bytes 786440 | tf_op jit(solution)/shard_map/ppermute | solution.py:142
  6.3 1.0 %copy-start.3 = (bf16[512,512]{1,0:T(8,128)(2,1)S(1)}, bf16[512,512]{1,0:T(8,128)(2,1)}, u32[]{:S(2)}) copy-start(bf16[512,512]{1,0:T(8,128)(2,1)} %param.13) | copy-start | bytes 1572868
  11.3 2.8 %collective-permute-start.3 = (bf16[256,512]{1,0:T(8,128)(2,1)S(1)}, bf16[256,512]{1,0:T(8,128)(2,1)S(1)}, u32[]{:S(2)}, u32[]{:S(2)}) collective-permute-start(bf16[256,512]{1,0:T(8,128)(2,1)S(1)} %collective-permute-done.1), channel_id=1, source_target_pairs={{0,1},{1,0},{2,3},{3,2},{4,5},{5,4},{6,7},{7,6},{8,9},{9,8},{10,11... | collective-permute-start | bytes 786440 | tf_op jit(solution)/shard_map/ppermute | solution.py:158
  11.3 8.7 %collective-permute-start.5 = (bf16[256,512]{1,0:T(8,128)(2,1)S(1)}, bf16[256,512]{1,0:T(8,128)(2,1)S(1)}, u32[]{:S(2)}, u32[]{:S(2)}) collective-permute-start(bf16[256,512]{1,0:T(8,128)(2,1)S(1)} %collective-permute-done.1), channel_id=1, source_target_pairs={{0,4},{1,5},{4,8},{5,9},{8,12},{9,13},{12,14},{13,15},{14,10},{15,... | collective-permute-start | bytes 786440 | tf_op jit(solution)/shard_map/ppermute | solution.py:153
  13.2 1.6 %collective-permute-start.4 = (bf16[256,512]{1,0:T(8,128)(2,1)S(1)}, bf16[256,512]{1,0:T(8,128)(2,1)S(1)}, u32[]{:S(2)}, u32[]{:S(2)}) collective-permute-start(bf16[256,512]{1,0:T(8,128)(2,1)S(1)} %collective-permute-done.2), channel_id=1, source_target_pairs={{0,1},{1,0},{2,3},{3,2},{4,5},{5,4},{6,7},{7,6},{8,9},{9,8},{10,11... | collective-permute-start | bytes 786440 | tf_op jit(solution)/shard_map/ppermute | solution.py:158
  13.5 8.5 %collective-permute-start.6 = (bf16[256,512]{1,0:T(8,128)(2,1)S(1)}, bf16[256,512]{1,0:T(8,128)(2,1)S(1)}, u32[]{:S(2)}, u32[]{:S(2)}) collective-permute-start(bf16[256,512]{1,0:T(8,128)(2,1)S(1)} %collective-permute-done.2), channel_id=1, source_target_pairs={{0,2},{1,3},{4,0},{5,1},{8,4},{9,5},{12,8},{13,9},{14,12},{15,13},... | collective-permute-start | bytes 786440 | tf_op jit(solution)/shard_map/ppermute | solution.py:154
  20.1 3.2 %collective-permute-start.7 = (bf16[256,512]{1,0:T(8,128)(2,1)S(1)}, bf16[256,512]{1,0:T(8,128)(2,1)S(1)}, u32[]{:S(2)}, u32[]{:S(2)}) collective-permute-start(bf16[256,512]{1,0:T(8,128)(2,1)S(1)} %collective-permute-done.5), channel_id=1, source_target_pairs={{0,1},{1,0},{2,3},{3,2},{4,5},{5,4},{6,7},{7,6},{8,9},{9,8},{10,11... | collective-permute-start | bytes 786440 | tf_op jit(solution)/shard_map/ppermute | solution.py:158
  20.1 8.7 %collective-permute-start.9 = (bf16[256,512]{1,0:T(8,128)(2,1)S(1)}, bf16[256,512]{1,0:T(8,128)(2,1)S(1)}, u32[]{:S(2)}, u32[]{:S(2)}) collective-permute-start(bf16[256,512]{1,0:T(8,128)(2,1)S(1)} %collective-permute-done.5), channel_id=1, source_target_pairs={{0,4},{1,5},{4,8},{5,9},{8,12},{9,13},{12,14},{13,15},{14,10},{15,... | collective-permute-start | bytes 786440 | tf_op jit(solution)/shard_map/ppermute | solution.py:153
  22.0 1.5 %collective-permute-start.8 = (bf16[256,512]{1,0:T(8,128)(2,1)S(1)}, bf16[256,512]{1,0:T(8,128)(2,1)S(1)}, u32[]{:S(2)}, u32[]{:S(2)}) collective-permute-start(bf16[256,512]{1,0:T(8,128)(2,1)S(1)} %collective-permute-done.6), channel_id=1, source_target_pairs={{0,1},{1,0},{2,3},{3,2},{4,5},{5,4},{6,7},{7,6},{8,9},{9,8},{10,11... | collective-permute-start | bytes 786440 | tf_op jit(solution)/shard_map/ppermute | solution.py:158
  22.2 8.5 %collective-permute-start.10 = (bf16[256,512]{1,0:T(8,128)(2,1)S(1)}, bf16[256,512]{1,0:T(8,128)(2,1)S(1)}, u32[]{:S(2)}, u32[]{:S(2)}) collective-permute-start(bf16[256,512]{1,0:T(8,128)(2,1)S(1)} %collective-permute-done.6), channel_id=1, source_target_pairs={{0,2},{1,3},{4,0},{5,1},{8,4},{9,5},{12,8},{13,9},{14,12},{15,13},... | collective-permute-start | bytes 786440 | tf_op jit(solution)/shard_map/ppermute | solution.py:154
  31.3 9.1 %collective-permute-start.13 = (bf16[128,512]{1,0:T(8,128)(2,1)S(1)}, bf16[128,512]{1,0:T(8,128)(2,1)S(1)}, u32[]{:S(2)}, u32[]{:S(2)}) collective-permute-start(bf16[128,512]{1,0:T(8,128)(2,1)S(1)} %slice.328), channel_id=1, source_target_pairs={{0,4},{1,5},{4,8},{5,9},{8,12},{9,13},{12,14},{13,15},{14,10},{15,... | collective-permute-start | bytes 393224 | tf_op jit(solution)/shard_map/ppermute | solution.py:148
  33.0 7.5 %collective-permute-start.14 = (bf16[128,512]{1,0:T(8,128)(2,1)S(1)}, bf16[128,512]{1,0:T(8,128)(2,1)S(1)}, u32[]{:S(2)}, u32[]{:S(2)}) collective-permute-start(bf16[128,512]{1,0:T(8,128)(2,1)S(1)} %slice.329), channel_id=1, source_target_pairs={{0,2},{1,3},{4,0},{5,1},{8,4},{9,5},{12,8},{13,9},{14,12},{15,13},... | collective-permute-start | bytes 393224 | tf_op jit(solution)/shard_map/ppermute | solution.py:149
  36.1 1.6 %collective-permute-start.11 = (bf16[256,512]{1,0:T(8,128)(2,1)S(1)}, bf16[256,512]{1,0:T(8,128)(2,1)S(1)}, u32[]{:S(2)}, u32[]{:S(2)}) collective-permute-start(bf16[256,512]{1,0:T(8,128)(2,1)S(1)} %collective-permute-done.9), channel_id=1, source_target_pairs={{0,1},{1,0},{2,3},{3,2},{4,5},{5,4},{6,7},{7,6},{8,9},{9,8},{10,11... | collective-permute-start | bytes 786440 | tf_op jit(solution)/shard_map/ppermute | solution.py:158
  36.7 1.7 %collective-permute-start.12 = (bf16[256,512]{1,0:T(8,128)(2,1)S(1)}, bf16[256,512]{1,0:T(8,128)(2,1)S(1)}, u32[]{:S(2)}, u32[]{:S(2)}) collective-permute-start(bf16[256,512]{1,0:T(8,128)(2,1)S(1)} %collective-permute-done.10), channel_id=1, source_target_pairs={{0,1},{1,0},{2,3},{3,2},{4,5},{5,4},{6,7},{7,6},{8,9},{9,8},{10,11... | collective-permute-start | bytes 786440 | tf_op jit(solution)/shard_map/ppermute | solution.py:158
  40.5 2.3 %collective-permute-start.15 = (bf16[128,512]{1,0:T(8,128)(2,1)S(1)}, bf16[128,512]{1,0:T(8,128)(2,1)S(1)}, u32[]{:S(2)}, u32[]{:S(2)}) collective-permute-start(bf16[128,512]{1,0:T(8,128)(2,1)S(1)} %collective-permute-done.13), channel_id=1, source_target_pairs={{0,1},{1,0},{2,3},{3,2},{4,5},{5,4},{6,7},{7,6},{8,9},{9,8},{10,11... | collective-permute-start | bytes 393224 | tf_op jit(solution)/shard_map/ppermute | solution.py:158
  40.9 1.9 %collective-permute-start.16 = (bf16[128,512]{1,0:T(8,128)(2,1)S(1)}, bf16[128,512]{1,0:T(8,128)(2,1)S(1)}, u32[]{:S(2)}, u32[]{:S(2)}) collective-permute-start(bf16[128,512]{1,0:T(8,128)(2,1)S(1)} %collective-permute-done.14), channel_id=1, source_target_pairs={{0,1},{1,0},{2,3},{3,2},{4,5},{5,4},{6,7},{7,6},{8,9},{9,8},{10,11... | collective-permute-start | bytes 393224 | tf_op jit(solution)/shard_map/ppermute | solution.py:158

commit v20 on v12

--- a/solution.py
+++ b/solution.py
@@ -142,6 +142,7 @@
         sib = lax.ppermute(own, axes, swap)
         total = add_grads(None, *split([own, sib], half), w_gate, w_up, w_out)
         arrived = [own, own]
+        pending = None
         for step in range(1, steps + 1):
             last = step == steps and chips % 2 == 0
             if last and halves == 2:
@@ -153,14 +154,18 @@
                 sent = [lax.ppermute(arrived[0], axes, cw_perm),
                         lax.ppermute(arrived[1], axes, ccw_perm)]
             arrived = sent
-            if step == steps:
-                total, arrived = lax.optimization_barrier((total, arrived))
+            if step == steps and pending is not None:
+                pending, arrived = lax.optimization_barrier((pending, arrived))
             from_sib = [lax.ppermute(chunk, axes, swap) for chunk in arrived]
             if step == steps:
                 total = add_grads(total, *split(arrived, half), w_gate, w_up, w_out)
                 total = add_grads(total, *split(from_sib, half), w_gate, w_up, w_out)
+            elif step == steps - 1:
+                pending = gradients(*split(arrived + from_sib, half), w_gate, w_up, w_out)
             else:
                 total = add_grads(total, *split(arrived + from_sib, half), w_gate, w_up, w_out)
+        if pending is not None:
+            total = (total[0] + pending[0], total[1] + pending[1])
         full_in, full_out = total
         new_gate = renorm(w_gate, full_in[:, :hidden])
         new_up = renorm(w_up, full_in[:, hidden:])

time: 44.3 us -> 45.4 us (1.025)
  waiting for transfers between devices: 12 us -> 13 us
    ppermute x8, waiting for transfers between devices: 1.42 us -> 1.96 us  [local_ring(): from_sib = [lax.ppermute(chunk, axes, swap) for chunk in arrived]]
  transfers between devices with their start and end apart: 17 -> 17, of which waited for: 9 -> 8; matrix products, arithmetic and copies ran while one was open for 32% -> 29% of each run, Pallas kernels for 0% -> 0%
where the time goes in v20:
time: 45.4 us; the launch traced here: 45.1 us
  matrix products  15.6 us (34%)
  waiting for transfers between devices  13 us (29%)
  starting transfers between devices  11.3 us (25%)
  other arithmetic  4.21 us (9%)
  between operations  0.51 us (1%)
  local copies, waits for them, and re-layouts  0.46 us (1%)
    ppermute x3, waiting for transfers between devices, local_ring(): lax.ppermute(arrived[0], axes, cw_perm)  10.7 us
    ppermute x3, starting transfers between devices, local_ring(): lax.ppermute(arrived[0], axes, cw_perm)  6.73 us
    dot_general x6, matrix products, gradients(): lax.dot_general(keys, both_grads, contract_first, preferred_element_type=...  3.84 us
    dot_general x6, matrix products, gradients(): lax.dot_general(scaled, w_out, contract_last, preferred_element_type=jnp....  3.43 us
    dot_general x6, matrix products, gradients(): lax.dot_general(activation, scaled, contract_first, preferred_element_typ...  2.58 us
    dot_general x6, matrix products, gradients(): gate_pre = jnp.dot(keys, w_gate, preferred_element_type=jnp.float32)  2.31 us
    dot_general x6, matrix products, gradients(): up_pre = jnp.dot(keys, w_up, preferred_element_type=jnp.float32)  2.19 us
    ppermute x8, waiting for transfers between devices, local_ring(): from_sib = [lax.ppermute(chunk, axes, swap) for chunk in arrived]  1.96 us
  transfers between devices with their start and end apart: 17, of which 8 were waited for; matrix products, arithmetic and copies ran while one was open for 29% of the time, Pallas kernels for 0%

profile of v20, /device:TPU:0, one launch (start us, length us, event | category | flops | bytes accessed | tf_op | source)
XLA Modules:
  0.0 45.1 jit_solution(6434752498497887253)
XLA Ops:
  0.0 1.1 %multiply_convert_fusion.25 = bf16[128,512]{1,0:T(8,128)(2,1)S(1)} fusion(bf16[128,512]{1,0:T(8,128)(2,1)} %param.8, f32[128]{0:T(128)} %param.10), kind=kLoop, calls=%fused_computation.89 | loop fusion | flops 196608 | bytes 262656 | tf_op jit(solution)/shard_map/convert_element_type | solution.py:137
  1.1 0.9 %pad_maximum_fusion = bf16[2,2,64,512]{3,2,1,0:T(8,128)(2,1)S(1)} fusion(bf16[2,1,64,512]{3,2,1,0:T(8,128)(2,1)S(1)} %bitcast.55, bf16[2,1,64,512]{3,2,1,0:T(8,128)(2,1)} %bitcast.56), kind=kLoop, calls=%fused_computation.63 | loop fusion | flops 131072 | bytes 524288 | tf_op jit(solution)/shard_map/stack | solution.py:139
  2.0 3.1 %collective-permute-start.1 = (bf16[256,512]{1,0:T(8,128)(2,1)S(1)}, bf16[256,512]{1,0:T(8,128)(2,1)S(1)}, u32[]{:S(2)}, u32[]{:S(2)}) collective-permute-start(bf16[256,512]{1,0:T(8,128)(2,1)S(1)} %bitcast.51), channel_id=1, source_target_pairs={{0,4},{1,5},{4,8},{5,9},{8,12},{9,13},{12,14},{13,15},{14,10},{15,... | collective-permute-start | bytes 786440 | tf_op jit(solution)/shard_map/ppermute | solution.py:154
  5.1 1.2 %fusion.7 = f32[512]{0:T(512)S(1)} fusion(bf16[512,512]{1,0:T(8,128)(2,1)} %param.13), kind=kLoop, calls=%fused_computation.19 | loop fusion | flops 785920 | bytes 526336 | tf_op jit(solution)/shard_map/reduce_sum | solution.py:18
  7.8 0.5 %fusion.23 = f32[512,1024]{1,0:T(8,128)S(1)} fusion(bf16[256,512]{1,0:T(8,128)(2,1)S(1)} %get-tuple-element.32, bf16[256,512]{1,0:T(8,128)(2,1)S(1)} %get-tuple-element.31, bf16[64,512]{1,0:T(8,128)(2,1)S(1)} %get-tuple-element.76, bf16[64,512]{1,0:T(8,128)(2,1)S(1)} %get-tuple-element.73, bf16[64,512]{1,0:T(8,128)(2,1)S(1)} %get-tuple-element.72, ...), kind=kOutput, calls=%fused_computation.53 | convolution fusion | flops 270532608 | bytes 2883584 | tf_op jit(solution)/shard_map/dot_general | solution.py:36
  8.3 3.0 %collective-permute-done.1 = bf16[256,512]{1,0:T(8,128)(2,1)S(1)} collective-permute-done((bf16[256,512]{1,0:T(8,128)(2,1)S(1)}, bf16[256,512]{1,0:T(8,128)(2,1)S(1)}, u32[]{:S(2)}, u32[]{:S(2)}) %collective-permute-start.1) | collective-permute-done | bytes 262176 | tf_op jit(solution)/shard_map/ppermute | solution.py:154
  11.3 1.8 %collective-permute-start.5 = (bf16[256,512]{1,0:T(8,128)(2,1)S(1)}, bf16[256,512]{1,0:T(8,128)(2,1)S(1)}, u32[]{:S(2)}, u32[]{:S(2)}) collective-permute-start(bf16[256,512]{1,0:T(8,128)(2,1)S(1)} %collective-permute-done.1), channel_id=1, source_target_pairs={{0,4},{1,5},{4,8},{5,9},{8,12},{9,13},{12,14},{13,15},{14,10},{15,... | collective-permute-start | bytes 786440 | tf_op jit(solution)/shard_map/ppermute | solution.py:154
  14.2 0.6 %collective-permute-done.4 = bf16[256,512]{1,0:T(8,128)(2,1)S(1)} collective-permute-done((bf16[256,512]{1,0:T(8,128)(2,1)S(1)}, bf16[256,512]{1,0:T(8,128)(2,1)S(1)}, u32[]{:S(2)}, u32[]{:S(2)}) %collective-permute-start.4) | collective-permute-done | bytes 262176 | tf_op jit(solution)/shard_map/ppermute | solution.py:159
  14.8 0.5 %fusion.90 = f32[512,512]{0,1:T(8,128)S(1)} fusion(bf16[512,512]{1,0:T(8,128)(2,1)S(1)} %get-tuple-element.54, bf16[512,512]{1,0:T(8,128)(2,1)S(1)} %copy-done.1), kind=kOutput, calls=%fused_computation.185 | convolution fusion | flops 268435456 | bytes 2097152 | tf_op jit(solution)/shard_map/dot_general | solution.py:30
  15.3 0.5 %fusion.91 = f32[512,512]{0,1:T(8,128)S(1)} fusion(bf16[512,512]{1,0:T(8,128)(2,1)S(1)} %get-tuple-element.54, bf16[512,512]{1,0:T(8,128)(2,1)S(1)} %copy-done.2), kind=kOutput, calls=%fused_computation.186 | convolution fusion | flops 268435456 | bytes 2097152 | tf_op jit(solution)/shard_map/dot_general | solution.py:29
  15.8 0.8 %multiply_convert_fusion.11 = (bf16[512,512]{0,1:T(8,128)(2,1)S(1)}, bf16[512,512]{0,1:T(8,128)(2,1)S(1)}) fusion(f32[512,512]{0,1:T(8,128)S(1)} %fusion.91, f32[512,512]{0,1:T(8,128)S(1)} %fusion.90, bf16[512,512]{1,0:T(8,128)(2,1)S(1)} %get-tuple-element.53, bf16[512,512]{1,0:T(8,128)(2,1)S(1)} %copy-done.3), kind=kOutput, calls=%fused_computation.49 | convolution fusion | flops 271843328 | bytes 4194304 | tf_op jit(solution)/shard_map/dot_general | solution.py:31
  16.6 0.5 %convolution_add_fusion.2 = f32[512,512]{1,0:T(8,128)S(1)} fusion(f32[512,512]{1,0:T(8,128)S(1)} %fusion.28, bf16[512,512]{1,0:T(8,128)(2,1)S(1)} %get-tuple-element.53, f32[512,512]{0,1:T(8,128)S(1)} %fusion.90, f32[512,512]{0,1:T(8,128)S(1)} %fusion.91), kind=kOutput, calls=%fused_computation.4 | convolution fusion | flops 270270464 | bytes 4718592 | tf_op jit(solution)/shard_map/dot_general | solution.py:37
  17.0 3.0 %collective-permute-done.5 = bf16[256,512]{1,0:T(8,128)(2,1)S(1)} collective-permute-done((bf16[256,512]{1,0:T(8,128)(2,1)S(1)}, bf16[256,512]{1,0:T(8,128)(2,1)S(1)}, u32[]{:S(2)}, u32[]{:S(2)}) %collective-permute-start.5) | collective-permute-done | bytes 262176 | tf_op jit(solution)/shard_map/ppermute | solution.py:154
  20.1 1.8 %collective-permute-start.9 = (bf16[256,512]{1,0:T(8,128)(2,1)S(1)}, bf16[256,512]{1,0:T(8,128)(2,1)S(1)}, u32[]{:S(2)}, u32[]{:S(2)}) collective-permute-start(bf16[256,512]{1,0:T(8,128)(2,1)S(1)} %collective-permute-done.5), channel_id=1, source_target_pairs={{0,4},{1,5},{4,8},{5,9},{8,12},{9,13},{12,14},{13,15},{14,10},{15,... | collective-permute-start | bytes 786440 | tf_op jit(solution)/shard_map/ppermute | solution.py:154
  22.6 0.8 %fusion.8 = f32[512,1024]{1,0:T(8,128)S(1)} fusion(bf16[512,512]{1,0:T(8,128)(2,1)S(1)} %get-tuple-element.54, bf16[512,512]{0,1:T(8,128)(2,1)S(1)} %get-tuple-element.28, bf16[512,512]{0,1:T(8,128)(2,1)S(1)} %get-tuple-element.27), kind=kOutput, calls=%fused_computation.20 | convolution fusion | flops 538968064 | bytes 3670016 | tf_op jit(solution)/shard_map/dot_general | solution.py:36
  23.4 4.6 %collective-permute-done.9 = bf16[256,512]{1,0:T(8,128)(2,1)S(1)} collective-permute-done((bf16[256,512]{1,0:T(8,128)(2,1)S(1)}, bf16[256,512]{1,0:T(8,128)(2,1)S(1)}, u32[]{:S(2)}, u32[]{:S(2)}) %collective-permute-start.9) | collective-permute-done | bytes 262176 | tf_op jit(solution)/shard_map/ppermute | solution.py:154
  28.0 1.9 %collective-permute-start.13 = (bf16[128,512]{1,0:T(8,128)(2,1)S(1)}, bf16[128,512]{1,0:T(8,128)(2,1)S(1)}, u32[]{:S(2)}, u32[]{:S(2)}) collective-permute-start(bf16[128,512]{1,0:T(8,128)(2,1)S(1)} %slice.328), channel_id=1, source_target_pairs={{0,4},{1,5},{4,8},{5,9},{8,12},{9,13},{12,14},{13,15},{14,10},{15,... | collective-permute-start | bytes 393224 | tf_op jit(solution)/shard_map/ppermute | solution.py:149
  30.0 0.5 %fusion.92 = f32[512,512]{0,1:T(8,128)S(1)} fusion(bf16[512,512]{1,0:T(8,128)(2,1)S(1)} %get-tuple-element.38, bf16[512,512]{1,0:T(8,128)(2,1)S(1)} %copy-done.1), kind=kOutput, calls=%fused_computation.187 | convolution fusion | flops 268435456 | bytes 2097152 | tf_op jit(solution)/shard_map/dot_general | solution.py:30
  30.5 0.5 %fusion.93 = f32[512,512]{0,1:T(8,128)S(1)} fusion(bf16[512,512]{1,0:T(8,128)(2,1)S(1)} %get-tuple-element.38, bf16[512,512]{1,0:T(8,128)(2,1)S(1)} %copy-done.2), kind=kOutput, calls=%fused_computation.188 | convolution fusion | flops 268435456 | bytes 2097152 | tf_op jit(solution)/shard_map/dot_general | solution.py:29
  31.4 0.8 %multiply_convert_fusion.9 = (bf16[512,512]{0,1:T(8,128)(2,1)S(1)}, bf16[512,512]{0,1:T(8,128)(2,1)S(1)}) fusion(f32[512,512]{0,1:T(8,128)S(1)} %fusion.93, f32[512,512]{0,1:T(8,128)S(1)} %fusion.92, bf16[512,512]{1,0:T(8,128)(2,1)S(1)} %get-tuple-element.37, bf16[512,512]{1,0:T(8,128)(2,1)S(1)} %copy-done.3), kind=kOutput, calls=%fused_computation.45 | convolution fusion | flops 271843328 | bytes 4194304 | tf_op jit(solution)/shard_map/dot_general | solution.py:31
  32.3 0.5 %collective-permute-start.12 = (bf16[256,512]{1,0:T(8,128)(2,1)S(1)}, bf16[256,512]{1,0:T(8,128)(2,1)S(1)}, u32[]{:S(2)}, u32[]{:S(2)}) collective-permute-start(bf16[256,512]{1,0:T(8,128)(2,1)S(1)} %collective-permute-done.10), channel_id=1, source_target_pairs={{0,1},{1,0},{2,3},{3,2},{4,5},{5,4},{6,7},{7,6},{8,9},{9,8},{10,11... | collective-permute-start | bytes 786440 | tf_op jit(solution)/shard_map/ppermute | solution.py:159
  32.8 1.0 %collective-permute-done.11 = bf16[256,512]{1,0:T(8,128)(2,1)S(1)} collective-permute-done((bf16[256,512]{1,0:T(8,128)(2,1)S(1)}, bf16[256,512]{1,0:T(8,128)(2,1)S(1)}, u32[]{:S(2)}, u32[]{:S(2)}) %collective-permute-start.11) | collective-permute-done | bytes 262176 | tf_op jit(solution)/shard_map/ppermute | solution.py:159
  34.2 0.5 %fusion.94 = f32[512,512]{0,1:T(8,128)S(1)} fusion(bf16[512,512]{1,0:T(8,128)(2,1)S(1)} %get-tuple-element.78, bf16[512,512]{1,0:T(8,128)(2,1)S(1)} %copy-done.1), kind=kOutput, calls=%fused_computation.189 | convolution fusion | flops 268435456 | bytes 2097152 | tf_op jit(solution)/shard_map/dot_general | solution.py:30
  34.7 0.5 %fusion.95 = f32[512,512]{0,1:T(8,128)S(1)} fusion(bf16[512,512]{1,0:T(8,128)(2,1)S(1)} %get-tuple-element.78, bf16[512,512]{1,0:T(8,128)(2,1)S(1)} %copy-done.2), kind=kOutput, calls=%fused_computation.190 | convolution fusion | flops 268435456 | bytes 2097152 | tf_op jit(solution)/shard_map/dot_general | solution.py:29
  35.2 0.5 %fusion.22 = f32[512,512]{1,0:T(8,128)S(1)} fusion(bf16[512,512]{1,0:T(8,128)(2,1)S(1)} %get-tuple-element.77, f32[512,512]{0,1:T(8,128)S(1)} %fusion.94, f32[512,512]{0,1:T(8,128)S(1)} %fusion.95), kind=kOutput, calls=%fused_computation.52 | convolution fusion | flops 270008320 | bytes 3670016 | tf_op jit(solution)/shard_map/dot_general | solution.py:37
  35.7 0.8 %multiply_convert_fusion.7 = (bf16[512,512]{0,1:T(8,128)(2,1)S(1)}, bf16[512,512]{0,1:T(8,128)(2,1)S(1)}) fusion(f32[512,512]{0,1:T(8,128)S(1)} %fusion.95, f32[512,512]{0,1:T(8,128)S(1)} %fusion.94, bf16[512,512]{1,0:T(8,128)(2,1)S(1)} %get-tuple-element.77, bf16[512,512]{1,0:T(8,128)(2,1)S(1)} %copy-done.3), kind=kOutput, calls=%fused_computation.41 | convolution fusion | flops 271843328 | bytes 4194304 | tf_op jit(solution)/shard_map/dot_general | solution.py:31
  36.5 0.8 %fusion.15 = f32[512,1024]{1,0:T(8,128)S(1)} fusion(bf16[512,512]{1,0:T(8,128)(2,1)S(1)} %get-tuple-element.78, bf16[512,512]{0,1:T(8,128)(2,1)S(1)} %get-tuple-element.30, bf16[512,512]{0,1:T(8,128)(2,1)S(1)} %get-tuple-element.29), kind=kOutput, calls=%fused_computation.27 | convolution fusion | flops 538968064 | bytes 3670016 | tf_op jit(solution)/shard_map/dot_general | solution.py:36
  39.1 0.5 %fusion = f32[512,512]{1,0:T(8,128)S(1)} fusion(f32[512,512]{1,0:T(8,128)S(1)} %fusion.47, f32[512,512]{1,0:T(8,128)S(1)} %convolution_add_fusion.2, bf16[512,512]{1,0:T(8,128)(2,1)S(1)} %get-tuple-element.37, f32[512,512]{0,1:T(8,128)S(1)} %fusion.92, f32[512,512]{0,1:T(8,128)S(1)} %fusion.93), kind=kOutput, calls=%fused_computation.3 | convolution fusion | flops 270532608 | bytes 5767168 | tf_op jit(solution)/shard_map/dot_general | solution.py:37
  41.4 1.0 %add_add_fusion = f32[512,1024]{1,0:T(8,128)S(1)} fusion(f32[512,1024]{1,0:T(8,128)S(1)} %fusion.15, f32[512,1024]{1,0:T(8,128)S(1)} %fusion.33, f32[512,1024]{1,0:T(8,128)S(1)} %fusion.29, f32[512,1024]{1,0:T(8,128)S(1)} %fusion.23, f32[512,1024]{1,0:T(8,128)S(1)} %fusion.8, bf16[512,512]{1,0:T(8,128)(2,1)S(1)} %get-tuple-element.38, ...), kind=kOutput, calls=%fused_computation | convolution fusion | flops 541589504 | bytes 14155776 | tf_op jit(solution)/shard_map/dot_general | solution.py:36
  42.3 0.5 %multiply_reduce_fusion.1 = (f32[512]{0:T(512)S(1)}, f32[512]{0:T(512)S(1)}, f32[512]{0:T(512)S(1)}, f32[512]{0:T(512)S(1)}) fusion(f32[512,1024]{1,0:T(8,128)S(1)} %add_add_fusion, bf16[512,512]{1,0:T(8,128)(2,1)S(1)} %copy-done.1, bf16[512,512]{1,0:T(8,128)(2,1)S(1)} %copy-done.2), kind=kLoop, calls=%fused_computation.36 | loop fusion | flops 3143680 | bytes 3153920 | tf_op jit(solution)/shard_map/reduce_sum | solution.py:19
  42.8 0.5 %multiply_reduce_fusion = (f32[512]{0:T(512)S(1)}, f32[512,512]{1,0:T(8,128)S(1)}) fusion(f32[512,512]{1,0:T(8,128)S(1)} %fusion.22, f32[512,512]{1,0:T(8,128)S(1)} %fusion, bf16[64,512]{1,0:T(8,128)(2,1)S(1)} %get-tuple-element.100, bf16[64,512]{1,0:T(8,128)(2,1)S(1)} %get-tuple-element.98, f32[128,512]{1,0:T(8,128)S(1)} %fusion.56, ...), kind=kOutput, calls=%fused_computation.32 | convolution fusion | flops 69336576 | bytes 4327424 | tf_op jit(solution)/shard_map/dot_general | solution.py:37
  44.1 1.1 %convolution_convert_fusion = bf16[128,512]{1,0:T(8,128)(2,1)} fusion(bf16[512,512]{1,0:T(8,128)(2,1)S(1)} %multiply_convert_fusion, bf16[128,512]{1,0:T(8,128)(2,1)S(1)} %copy-done, bf16[512,512]{1,0:T(8,128)(2,1)S(1)} %get-tuple-element.17, f32[128,512]{1,0:T(8,128)S(1)} %convolution_bitcast_fusion.1), kind=kOutput, calls=%fused_computation.16 | convolution fusion | flops 134676480 | bytes 1572864 | tf_op jit(solution)/shard_map/dot_general | solution.py:45
  (82 shorter events, 8.4 us)
Async XLA Ops:
  0.0 43.8 %copy-start = (bf16[128,512]{1,0:T(8,128)(2,1)S(1)}, bf16[128,512]{1,0:T(8,128)(2,1)}, u32[]{:S(2)}) copy-start(bf16[128,512]{1,0:T(8,128)(2,1)} %param.9) | copy-start | bytes 393220
  0.0 6.7 %copy-start.2 = (bf16[512,512]{1,0:T(8,128)(2,1)S(1)}, bf16[512,512]{1,0:T(8,128)(2,1)}, u32[]{:S(2)}) copy-start(bf16[512,512]{1,0:T(8,128)(2,1)} %param.11) | copy-start | bytes 1572868
  0.0 7.0 %copy-start.1 = (bf16[512,512]{1,0:T(8,128)(2,1)S(1)}, bf16[512,512]{1,0:T(8,128)(2,1)}, u32[]{:S(2)}) copy-start(bf16[512,512]{1,0:T(8,128)(2,1)} %param.12) | copy-start | bytes 1572868
  2.0 9.3 %collective-permute-start.1 = (bf16[256,512]{1,0:T(8,128)(2,1)S(1)}, bf16[256,512]{1,0:T(8,128)(2,1)S(1)}, u32[]{:S(2)}, u32[]{:S(2)}) collective-permute-start(bf16[256,512]{1,0:T(8,128)(2,1)S(1)} %bitcast.51), channel_id=1, source_target_pairs={{0,4},{1,5},{4,8},{5,9},{8,12},{9,13},{12,14},{13,15},{14,10},{15,... | collective-permute-start | bytes 786440 | tf_op jit(solution)/shard_map/ppermute | solution.py:154
  5.1 8.1 %collective-permute-start.2 = (bf16[256,512]{1,0:T(8,128)(2,1)S(1)}, bf16[256,512]{1,0:T(8,128)(2,1)S(1)}, u32[]{:S(2)}, u32[]{:S(2)}) collective-permute-start(bf16[256,512]{1,0:T(8,128)(2,1)S(1)} %bitcast.52), channel_id=1, source_target_pairs={{0,2},{1,3},{4,0},{5,1},{8,4},{9,5},{12,8},{13,9},{14,12},{15,13},... | collective-permute-start | bytes 786440 | tf_op jit(solution)/shard_map/ppermute | solution.py:155
  5.1 1.5 %collective-permute-start = (bf16[256,512]{1,0:T(8,128)(2,1)S(1)}, bf16[256,512]{1,0:T(8,128)(2,1)S(1)}, u32[]{:S(2)}, u32[]{:S(2)}) collective-permute-start(bf16[256,512]{1,0:T(8,128)(2,1)S(1)} %bitcast.53), channel_id=1, source_target_pairs={{0,1},{1,0},{2,3},{3,2},{4,5},{5,4},{6,7},{7,6},{8,9},{9,8},{10,11... | collective-permute-start | bytes 786440 | tf_op jit(solution)/shard_map/ppermute | solution.py:142
  6.3 1.0 %copy-start.3 = (bf16[512,512]{1,0:T(8,128)(2,1)S(1)}, bf16[512,512]{1,0:T(8,128)(2,1)}, u32[]{:S(2)}) copy-start(bf16[512,512]{1,0:T(8,128)(2,1)} %param.13) | copy-start | bytes 1572868
  11.3 2.8 %collective-permute-start.3 = (bf16[256,512]{1,0:T(8,128)(2,1)S(1)}, bf16[256,512]{1,0:T(8,128)(2,1)S(1)}, u32[]{:S(2)}, u32[]{:S(2)}) collective-permute-start(bf16[256,512]{1,0:T(8,128)(2,1)S(1)} %collective-permute-done.1), channel_id=1, source_target_pairs={{0,1},{1,0},{2,3},{3,2},{4,5},{5,4},{6,7},{7,6},{8,9},{9,8},{10,11... | collective-permute-start | bytes 786440 | tf_op jit(solution)/shard_map/ppermute | solution.py:159
  11.3 8.7 %collective-permute-start.5 = (bf16[256,512]{1,0:T(8,128)(2,1)S(1)}, bf16[256,512]{1,0:T(8,128)(2,1)S(1)}, u32[]{:S(2)}, u32[]{:S(2)}) collective-permute-start(bf16[256,512]{1,0:T(8,128)(2,1)S(1)} %collective-permute-done.1), channel_id=1, source_target_pairs={{0,4},{1,5},{4,8},{5,9},{8,12},{9,13},{12,14},{13,15},{14,10},{15,... | collective-permute-start | bytes 786440 | tf_op jit(solution)/shard_map/ppermute | solution.py:154
  13.2 1.6 %collective-permute-start.4 = (bf16[256,512]{1,0:T(8,128)(2,1)S(1)}, bf16[256,512]{1,0:T(8,128)(2,1)S(1)}, u32[]{:S(2)}, u32[]{:S(2)}) collective-permute-start(bf16[256,512]{1,0:T(8,128)(2,1)S(1)} %collective-permute-done.2), channel_id=1, source_target_pairs={{0,1},{1,0},{2,3},{3,2},{4,5},{5,4},{6,7},{7,6},{8,9},{9,8},{10,11... | collective-permute-start | bytes 786440 | tf_op jit(solution)/shard_map/ppermute | solution.py:159
  13.5 8.5 %collective-permute-start.6 = (bf16[256,512]{1,0:T(8,128)(2,1)S(1)}, bf16[256,512]{1,0:T(8,128)(2,1)S(1)}, u32[]{:S(2)}, u32[]{:S(2)}) collective-permute-start(bf16[256,512]{1,0:T(8,128)(2,1)S(1)} %collective-permute-done.2), channel_id=1, source_target_pairs={{0,2},{1,3},{4,0},{5,1},{8,4},{9,5},{12,8},{13,9},{14,12},{15,13},... | collective-permute-start | bytes 786440 | tf_op jit(solution)/shard_map/ppermute | solution.py:155
  20.1 7.9 %collective-permute-start.9 = (bf16[256,512]{1,0:T(8,128)(2,1)S(1)}, bf16[256,512]{1,0:T(8,128)(2,1)S(1)}, u32[]{:S(2)}, u32[]{:S(2)}) collective-permute-start(bf16[256,512]{1,0:T(8,128)(2,1)S(1)} %collective-permute-done.5), channel_id=1, source_target_pairs={{0,4},{1,5},{4,8},{5,9},{8,12},{9,13},{12,14},{13,15},{14,10},{15,... | collective-permute-start | bytes 786440 | tf_op jit(solution)/shard_map/ppermute | solution.py:154
  21.9 8.0 %collective-permute-start.7 = (bf16[256,512]{1,0:T(8,128)(2,1)S(1)}, bf16[256,512]{1,0:T(8,128)(2,1)S(1)}, u32[]{:S(2)}, u32[]{:S(2)}) collective-permute-start(bf16[256,512]{1,0:T(8,128)(2,1)S(1)} %collective-permute-done.5), channel_id=1, source_target_pairs={{0,1},{1,0},{2,3},{3,2},{4,5},{5,4},{6,7},{7,6},{8,9},{9,8},{10,11... | collective-permute-start | bytes 786440 | tf_op jit(solution)/shard_map/ppermute | solution.py:159
  22.0 9.0 %collective-permute-start.10 = (bf16[256,512]{1,0:T(8,128)(2,1)S(1)}, bf16[256,512]{1,0:T(8,128)(2,1)S(1)}, u32[]{:S(2)}, u32[]{:S(2)}) collective-permute-start(bf16[256,512]{1,0:T(8,128)(2,1)S(1)} %collective-permute-done.6), channel_id=1, source_target_pairs={{0,2},{1,3},{4,0},{5,1},{8,4},{9,5},{12,8},{13,9},{14,12},{15,13},... | collective-permute-start | bytes 786440 | tf_op jit(solution)/shard_map/ppermute | solution.py:155
  22.3 7.7 %collective-permute-start.8 = (bf16[256,512]{1,0:T(8,128)(2,1)S(1)}, bf16[256,512]{1,0:T(8,128)(2,1)S(1)}, u32[]{:S(2)}, u32[]{:S(2)}) collective-permute-start(bf16[256,512]{1,0:T(8,128)(2,1)S(1)} %collective-permute-done.6), channel_id=1, source_target_pairs={{0,1},{1,0},{2,3},{3,2},{4,5},{5,4},{6,7},{7,6},{8,9},{9,8},{10,11... | collective-permute-start | bytes 786440 | tf_op jit(solution)/shard_map/ppermute | solution.py:159
  28.0 9.2 %collective-permute-start.13 = (bf16[128,512]{1,0:T(8,128)(2,1)S(1)}, bf16[128,512]{1,0:T(8,128)(2,1)S(1)}, u32[]{:S(2)}, u32[]{:S(2)}) collective-permute-start(bf16[128,512]{1,0:T(8,128)(2,1)S(1)} %slice.328), channel_id=1, source_target_pairs={{0,4},{1,5},{4,8},{5,9},{8,12},{9,13},{12,14},{13,15},{14,10},{15,... | collective-permute-start | bytes 393224 | tf_op jit(solution)/shard_map/ppermute | solution.py:149
  31.0 6.3 %collective-permute-start.14 = (bf16[128,512]{1,0:T(8,128)(2,1)S(1)}, bf16[128,512]{1,0:T(8,128)(2,1)S(1)}, u32[]{:S(2)}, u32[]{:S(2)}) collective-permute-start(bf16[128,512]{1,0:T(8,128)(2,1)S(1)} %slice.329), channel_id=1, source_target_pairs={{0,2},{1,3},{4,0},{5,1},{8,4},{9,5},{12,8},{13,9},{14,12},{15,13},... | collective-permute-start | bytes 393224 | tf_op jit(solution)/shard_map/ppermute | solution.py:150
  32.2 1.6 %collective-permute-start.11 = (bf16[256,512]{1,0:T(8,128)(2,1)S(1)}, bf16[256,512]{1,0:T(8,128)(2,1)S(1)}, u32[]{:S(2)}, u32[]{:S(2)}) collective-permute-start(bf16[256,512]{1,0:T(8,128)(2,1)S(1)} %collective-permute-done.9), channel_id=1, source_target_pairs={{0,1},{1,0},{2,3},{3,2},{4,5},{5,4},{6,7},{7,6},{8,9},{9,8},{10,11... | collective-permute-start | bytes 786440 | tf_op jit(solution)/shard_map/ppermute | solution.py:159
  32.3 1.9 %collective-permute-start.12 = (bf16[256,512]{1,0:T(8,128)(2,1)S(1)}, bf16[256,512]{1,0:T(8,128)(2,1)S(1)}, u32[]{:S(2)}, u32[]{:S(2)}) collective-permute-start(bf16[256,512]{1,0:T(8,128)(2,1)S(1)} %collective-permute-done.10), channel_id=1, source_target_pairs={{0,1},{1,0},{2,3},{3,2},{4,5},{5,4},{6,7},{7,6},{8,9},{9,8},{10,11... | collective-permute-start | bytes 786440 | tf_op jit(solution)/shard_map/ppermute | solution.py:159
  37.2 2.8 %collective-permute-start.15 = (bf16[128,512]{1,0:T(8,128)(2,1)S(1)}, bf16[128,512]{1,0:T(8,128)(2,1)S(1)}, u32[]{:S(2)}, u32[]{:S(2)}) collective-permute-start(bf16[128,512]{1,0:T(8,128)(2,1)S(1)} %collective-permute-done.13), channel_id=1, source_target_pairs={{0,1},{1,0},{2,3},{3,2},{4,5},{5,4},{6,7},{7,6},{8,9},{9,8},{10,11... | collective-permute-start | bytes 393224 | tf_op jit(solution)/shard_map/ppermute | solution.py:159
  37.5 2.6 %collective-permute-start.16 = (bf16[128,512]{1,0:T(8,128)(2,1)S(1)}, bf16[128,512]{1,0:T(8,128)(2,1)S(1)}, u32[]{:S(2)}, u32[]{:S(2)}) collective-permute-start(bf16[128,512]{1,0:T(8,128)(2,1)S(1)} %collective-permute-done.14), channel_id=1, source_target_pairs={{0,1},{1,0},{2,3},{3,2},{4,5},{5,4},{6,7},{7,6},{8,9},{9,8},{10,11... | collective-permute-start | bytes 393224 | tf_op jit(solution)/shard_map/ppermute | solution.py:159

commit v21 on v12

--- a/solution.py
+++ b/solution.py
@@ -98,7 +98,8 @@
         return None
     first = sorted((p[2], s) for s, p in enumerate(places) if p[0] == columns[0])
     second = sorted((p[2], s) for s, p in enumerate(places) if p[0] == columns[1])
-    return [s for _, s in first] + [s for _, s in reversed(second)]
+    order = [s for _, s in first] + [s for _, s in reversed(second)]
+    return order[:1] + order[:0:-1]
 
 
 def add_grads(total, keys_part, scaled_part, w_gate, w_up, w_out):

time: 44.3 us -> 44.4 us (level)
    ppermute x3, starting transfers between devices: 0.42 us -> 0.89 us  [local_ring(): lax.ppermute(arrived[1], axes, ccw_perm)]
where the time goes in v21:
time: 44.4 us; the launch traced here: 44.2 us
  matrix products  15.6 us (35%)
  waiting for transfers between devices  12.1 us (27%)
  starting transfers between devices  11.2 us (25%)
  other arithmetic  4.29 us (10%)
  between operations  0.5 us (1%)
  local copies, waits for them, and re-layouts  0.45 us (1%)
    ppermute x3, waiting for transfers between devices, local_ring(): lax.ppermute(arrived[0], axes, cw_perm)  10.6 us
    ppermute x3, starting transfers between devices, local_ring(): lax.ppermute(arrived[0], axes, cw_perm)  6.3 us
    dot_general x6, matrix products, gradients(): lax.dot_general(keys, both_grads, contract_first, preferred_element_type=...  3.67 us
    dot_general x6, matrix products, gradients(): lax.dot_general(scaled, w_out, contract_last, preferred_element_type=jnp....  3.51 us
    dot_general x6, matrix products, gradients(): lax.dot_general(activation, scaled, contract_first, preferred_element_typ...  2.64 us
    dot_general x6, matrix products, gradients(): gate_pre = jnp.dot(keys, w_gate, preferred_element_type=jnp.float32)  2.31 us
    dot_general x6, matrix products, gradients(): up_pre = jnp.dot(keys, w_up, preferred_element_type=jnp.float32)  2.19 us
    ppermute x8, starting transfers between devices, local_ring(): from_sib = [lax.ppermute(chunk, axes, swap) for chunk in arrived]  1.73 us
  transfers between devices with their start and end apart: 17, of which 9 were waited for; matrix products, arithmetic and copies ran while one was open for 32% of the time, Pallas kernels for 0%

profile of v21, /device:TPU:0, one launch (start us, length us, event | category | flops | bytes accessed | tf_op | source)
XLA Modules:
  0.0 44.2 jit_solution(34237583105107861)
XLA Ops:
  0.0 1.1 %multiply_convert_fusion.25 = bf16[128,512]{1,0:T(8,128)(2,1)S(1)} fusion(bf16[128,512]{1,0:T(8,128)(2,1)} %param.8, f32[128]{0:T(128)} %param.10), kind=kLoop, calls=%fused_computation.87 | loop fusion | flops 196608 | bytes 262656 | tf_op jit(solution)/shard_map/convert_element_type | solution.py:138
  1.1 0.9 %pad_maximum_fusion = bf16[2,2,64,512]{3,2,1,0:T(8,128)(2,1)S(1)} fusion(bf16[2,1,64,512]{3,2,1,0:T(8,128)(2,1)S(1)} %bitcast.55, bf16[2,1,64,512]{3,2,1,0:T(8,128)(2,1)} %bitcast.56), kind=kLoop, calls=%fused_computation.61 | loop fusion | flops 131072 | bytes 524288 | tf_op jit(solution)/shard_map/stack | solution.py:140
  2.0 3.0 %collective-permute-start.1 = (bf16[256,512]{1,0:T(8,128)(2,1)S(1)}, bf16[256,512]{1,0:T(8,128)(2,1)S(1)}, u32[]{:S(2)}, u32[]{:S(2)}) collective-permute-start(bf16[256,512]{1,0:T(8,128)(2,1)S(1)} %bitcast.51), channel_id=1, source_target_pairs={{0,2},{1,3},{2,6},{3,7},{6,10},{7,11},{10,14},{11,15},{14,12},{15,... | collective-permute-start | bytes 786440 | tf_op jit(solution)/shard_map/ppermute | solution.py:154
  5.2 1.2 %fusion.4 = f32[512]{0:T(512)S(1)} fusion(bf16[512,512]{1,0:T(8,128)(2,1)} %param.13), kind=kLoop, calls=%fused_computation.18 | loop fusion | flops 785920 | bytes 526336 | tf_op jit(solution)/shard_map/reduce_sum | solution.py:18
  7.4 0.5 %multiply_convert_fusion.17 = (bf16[256,512]{1,0:T(8,128)(2,1)S(1)}, bf16[256,512]{1,0:T(8,128)(2,1)S(1)}) fusion(f32[256,512]{1,0:T(8,128)S(1)} %fusion.81, f32[256,512]{1,0:T(8,128)S(1)} %fusion.82, bf16[512,512]{1,0:T(8,128)(2,1)S(1)} %copy-done.3, bf16[64,512]{1,0:T(8,128)(2,1)S(1)} %get-tuple-element.74, bf16[64,512]{1,0:T(8,128)(2,1)S(1)} %get-tuple-element.75, ...), kind=kOutput, calls=%fused_computation.57 | convolution fusion | flops 136970240 | bytes 2359296 | tf_op jit(solution)/shard_map/dot_general | solution.py:31
  8.4 3.0 %collective-permute-done.1 = bf16[256,512]{1,0:T(8,128)(2,1)S(1)} collective-permute-done((bf16[256,512]{1,0:T(8,128)(2,1)S(1)}, bf16[256,512]{1,0:T(8,128)(2,1)S(1)}, u32[]{:S(2)}, u32[]{:S(2)}) %collective-permute-start.1) | collective-permute-done | bytes 262176 | tf_op jit(solution)/shard_map/ppermute | solution.py:154
  11.4 1.7 %collective-permute-start.5 = (bf16[256,512]{1,0:T(8,128)(2,1)S(1)}, bf16[256,512]{1,0:T(8,128)(2,1)S(1)}, u32[]{:S(2)}, u32[]{:S(2)}) collective-permute-start(bf16[256,512]{1,0:T(8,128)(2,1)S(1)} %collective-permute-done.1), channel_id=1, source_target_pairs={{0,2},{1,3},{2,6},{3,7},{6,10},{7,11},{10,14},{11,15},{14,12},{15,... | collective-permute-start | bytes 786440 | tf_op jit(solution)/shard_map/ppermute | solution.py:154
  14.2 0.5 %collective-permute-done.4 = bf16[256,512]{1,0:T(8,128)(2,1)S(1)} collective-permute-done((bf16[256,512]{1,0:T(8,128)(2,1)S(1)}, bf16[256,512]{1,0:T(8,128)(2,1)S(1)}, u32[]{:S(2)}, u32[]{:S(2)}) %collective-permute-start.4) | collective-permute-done | bytes 262176 | tf_op jit(solution)/shard_map/ppermute | solution.py:159
  14.7 0.5 %fusion.89 = f32[512,512]{0,1:T(8,128)S(1)} fusion(bf16[512,512]{1,0:T(8,128)(2,1)S(1)} %get-tuple-element.54, bf16[512,512]{1,0:T(8,128)(2,1)S(1)} %copy-done.1), kind=kOutput, calls=%fused_computation.184 | convolution fusion | flops 268435456 | bytes 2097152 | tf_op jit(solution)/shard_map/dot_general | solution.py:30
  15.2 0.5 %fusion.90 = f32[512,512]{0,1:T(8,128)S(1)} fusion(bf16[512,512]{1,0:T(8,128)(2,1)S(1)} %get-tuple-element.54, bf16[512,512]{1,0:T(8,128)(2,1)S(1)} %copy-done.2), kind=kOutput, calls=%fused_computation.185 | convolution fusion | flops 268435456 | bytes 2097152 | tf_op jit(solution)/shard_map/dot_general | solution.py:29
  15.7 0.8 %multiply_convert_fusion.11 = (bf16[512,512]{0,1:T(8,128)(2,1)S(1)}, bf16[512,512]{0,1:T(8,128)(2,1)S(1)}) fusion(f32[512,512]{0,1:T(8,128)S(1)} %fusion.90, f32[512,512]{0,1:T(8,128)S(1)} %fusion.89, bf16[512,512]{1,0:T(8,128)(2,1)S(1)} %get-tuple-element.53, bf16[512,512]{1,0:T(8,128)(2,1)S(1)} %copy-done.3), kind=kOutput, calls=%fused_computation.48 | convolution fusion | flops 271843328 | bytes 4194304 | tf_op jit(solution)/shard_map/dot_general | solution.py:31
  16.5 0.5 %convolution_add_fusion.2 = f32[512,512]{1,0:T(8,128)S(1)} fusion(f32[512,512]{1,0:T(8,128)S(1)} %fusion.24, bf16[512,512]{1,0:T(8,128)(2,1)S(1)} %get-tuple-element.53, f32[512,512]{0,1:T(8,128)S(1)} %fusion.89, f32[512,512]{0,1:T(8,128)S(1)} %fusion.90), kind=kOutput, calls=%fused_computation.4 | convolution fusion | flops 270270464 | bytes 4718592 | tf_op jit(solution)/shard_map/dot_general | solution.py:37
  17.0 3.1 %collective-permute-done.5 = bf16[256,512]{1,0:T(8,128)(2,1)S(1)} collective-permute-done((bf16[256,512]{1,0:T(8,128)(2,1)S(1)}, bf16[256,512]{1,0:T(8,128)(2,1)S(1)}, u32[]{:S(2)}, u32[]{:S(2)}) %collective-permute-start.5) | collective-permute-done | bytes 262176 | tf_op jit(solution)/shard_map/ppermute | solution.py:154
  20.1 1.7 %collective-permute-start.9 = (bf16[256,512]{1,0:T(8,128)(2,1)S(1)}, bf16[256,512]{1,0:T(8,128)(2,1)S(1)}, u32[]{:S(2)}, u32[]{:S(2)}) collective-permute-start(bf16[256,512]{1,0:T(8,128)(2,1)S(1)} %collective-permute-done.5), channel_id=1, source_target_pairs={{0,2},{1,3},{2,6},{3,7},{6,10},{7,11},{10,14},{11,15},{14,12},{15,... | collective-permute-start | bytes 786440 | tf_op jit(solution)/shard_map/ppermute | solution.py:154
  22.5 0.8 %fusion.5 = f32[512,1024]{1,0:T(8,128)S(1)} fusion(bf16[512,512]{1,0:T(8,128)(2,1)S(1)} %get-tuple-element.54, bf16[512,512]{0,1:T(8,128)(2,1)S(1)} %get-tuple-element.28, bf16[512,512]{0,1:T(8,128)(2,1)S(1)} %get-tuple-element.27), kind=kOutput, calls=%fused_computation.19 | convolution fusion | flops 538968064 | bytes 3670016 | tf_op jit(solution)/shard_map/dot_general | solution.py:36
  23.5 0.5 %fusion.91 = f32[512,512]{0,1:T(8,128)S(1)} fusion(bf16[512,512]{1,0:T(8,128)(2,1)S(1)} %get-tuple-element.78, bf16[512,512]{1,0:T(8,128)(2,1)S(1)} %copy-done.1), kind=kOutput, calls=%fused_computation.186 | convolution fusion | flops 268435456 | bytes 2097152 | tf_op jit(solution)/shard_map/dot_general | solution.py:30
  24.0 0.5 %fusion.92 = f32[512,512]{0,1:T(8,128)S(1)} fusion(bf16[512,512]{1,0:T(8,128)(2,1)S(1)} %get-tuple-element.78, bf16[512,512]{1,0:T(8,128)(2,1)S(1)} %copy-done.2), kind=kOutput, calls=%fused_computation.187 | convolution fusion | flops 268435456 | bytes 2097152 | tf_op jit(solution)/shard_map/dot_general | solution.py:29
  24.4 4.4 %collective-permute-done.9 = bf16[256,512]{1,0:T(8,128)(2,1)S(1)} collective-permute-done((bf16[256,512]{1,0:T(8,128)(2,1)S(1)}, bf16[256,512]{1,0:T(8,128)(2,1)S(1)}, u32[]{:S(2)}, u32[]{:S(2)}) %collective-permute-start.9) | collective-permute-done | bytes 262176 | tf_op jit(solution)/shard_map/ppermute | solution.py:154
  28.9 1.7 %collective-permute-start.13 = (bf16[128,512]{1,0:T(8,128)(2,1)S(1)}, bf16[128,512]{1,0:T(8,128)(2,1)S(1)}, u32[]{:S(2)}, u32[]{:S(2)}) collective-permute-start(bf16[128,512]{1,0:T(8,128)(2,1)S(1)} %slice.328), channel_id=1, source_target_pairs={{0,2},{1,3},{2,6},{3,7},{6,10},{7,11},{10,14},{11,15},{14,12},{15,... | collective-permute-start | bytes 393224 | tf_op jit(solution)/shard_map/ppermute | solution.py:149
  30.6 0.8 %multiply_convert_fusion.9 = (bf16[512,512]{0,1:T(8,128)(2,1)S(1)}, bf16[512,512]{0,1:T(8,128)(2,1)S(1)}) fusion(f32[512,512]{0,1:T(8,128)S(1)} %fusion.92, f32[512,512]{0,1:T(8,128)S(1)} %fusion.91, bf16[512,512]{1,0:T(8,128)(2,1)S(1)} %get-tuple-element.77, bf16[512,512]{1,0:T(8,128)(2,1)S(1)} %copy-done.3), kind=kOutput, calls=%fused_computation.44 | convolution fusion | flops 271843328 | bytes 4194304 | tf_op jit(solution)/shard_map/dot_general | solution.py:31
  31.4 0.5 %convolution_add_fusion.1 = f32[512,512]{1,0:T(8,128)S(1)} fusion(f32[512,512]{1,0:T(8,128)S(1)} %convolution_add_fusion.2, bf16[512,512]{1,0:T(8,128)(2,1)S(1)} %get-tuple-element.77, f32[512,512]{0,1:T(8,128)S(1)} %fusion.91, f32[512,512]{0,1:T(8,128)S(1)} %fusion.92), kind=kOutput, calls=%fused_computation.3 | convolution fusion | flops 270270464 | bytes 4718592 | tf_op jit(solution)/shard_map/dot_general | solution.py:37
  31.9 0.6 %collective-permute-start.14 = (bf16[128,512]{1,0:T(8,128)(2,1)S(1)}, bf16[128,512]{1,0:T(8,128)(2,1)S(1)}, u32[]{:S(2)}, u32[]{:S(2)}) collective-permute-start(bf16[128,512]{1,0:T(8,128)(2,1)S(1)} %slice.329), channel_id=1, source_target_pairs={{0,4},{1,5},{2,0},{3,1},{6,2},{7,3},{10,6},{11,7},{14,10},{15,11},... | collective-permute-start | bytes 393224 | tf_op jit(solution)/shard_map/ppermute | solution.py:150
  32.6 0.5 %collective-permute-start.12 = (bf16[256,512]{1,0:T(8,128)(2,1)S(1)}, bf16[256,512]{1,0:T(8,128)(2,1)S(1)}, u32[]{:S(2)}, u32[]{:S(2)}) collective-permute-start(bf16[256,512]{1,0:T(8,128)(2,1)S(1)} %collective-permute-done.10), channel_id=1, source_target_pairs={{0,1},{1,0},{2,3},{3,2},{4,5},{5,4},{6,7},{7,6},{8,9},{9,8},{10,11... | collective-permute-start | bytes 786440 | tf_op jit(solution)/shard_map/ppermute | solution.py:159
  33.1 0.8 %fusion.9 = f32[512,1024]{1,0:T(8,128)S(1)} fusion(bf16[512,512]{1,0:T(8,128)(2,1)S(1)} %get-tuple-element.78, bf16[512,512]{0,1:T(8,128)(2,1)S(1)} %get-tuple-element.30, bf16[512,512]{0,1:T(8,128)(2,1)S(1)} %get-tuple-element.29), kind=kOutput, calls=%fused_computation.23 | convolution fusion | flops 538968064 | bytes 3670016 | tf_op jit(solution)/shard_map/dot_general | solution.py:36
  34.5 0.5 %fusion.93 = f32[512,512]{0,1:T(8,128)S(1)} fusion(bf16[512,512]{1,0:T(8,128)(2,1)S(1)} %get-tuple-element.38, bf16[512,512]{1,0:T(8,128)(2,1)S(1)} %copy-done.1), kind=kOutput, calls=%fused_computation.188 | convolution fusion | flops 268435456 | bytes 2097152 | tf_op jit(solution)/shard_map/dot_general | solution.py:30
  35.0 0.5 %fusion.94 = f32[512,512]{0,1:T(8,128)S(1)} fusion(bf16[512,512]{1,0:T(8,128)(2,1)S(1)} %get-tuple-element.38, bf16[512,512]{1,0:T(8,128)(2,1)S(1)} %copy-done.2), kind=kOutput, calls=%fused_computation.189 | convolution fusion | flops 268435456 | bytes 2097152 | tf_op jit(solution)/shard_map/dot_general | solution.py:29
  35.5 0.8 %multiply_convert_fusion.7 = (bf16[512,512]{0,1:T(8,128)(2,1)S(1)}, bf16[512,512]{0,1:T(8,128)(2,1)S(1)}) fusion(f32[512,512]{0,1:T(8,128)S(1)} %fusion.94, f32[512,512]{0,1:T(8,128)S(1)} %fusion.93, bf16[512,512]{1,0:T(8,128)(2,1)S(1)} %get-tuple-element.37, bf16[512,512]{1,0:T(8,128)(2,1)S(1)} %copy-done.3), kind=kOutput, calls=%fused_computation.40 | convolution fusion | flops 271843328 | bytes 4194304 | tf_op jit(solution)/shard_map/dot_general | solution.py:31
  36.3 0.8 %add_add_fusion.1 = f32[512,1024]{1,0:T(8,128)S(1)} fusion(f32[512,1024]{1,0:T(8,128)S(1)} %fusion.9, f32[512,1024]{1,0:T(8,128)S(1)} %fusion.19, f32[512,1024]{1,0:T(8,128)S(1)} %fusion.5, bf16[512,512]{1,0:T(8,128)(2,1)S(1)} %get-tuple-element.38, bf16[512,512]{0,1:T(8,128)(2,1)S(1)} %get-tuple-element.26, bf16[512,512]{0,1:T(8,128)(2,1)S(1)} %get-tuple-element.25), kind=kOutput, calls=%fused_computation.1 | convolution fusion | flops 540540928 | bytes 9961472 | tf_op jit(solution)/shard_map/dot_general | solution.py:36
  37.1 0.5 %convolution_add_fusion = f32[512,512]{1,0:T(8,128)S(1)} fusion(f32[512,512]{1,0:T(8,128)S(1)} %convolution_add_fusion.1, bf16[512,512]{1,0:T(8,128)(2,1)S(1)} %get-tuple-element.37, f32[512,512]{0,1:T(8,128)S(1)} %fusion.93, f32[512,512]{0,1:T(8,128)S(1)} %fusion.94), kind=kOutput, calls=%fused_computation.2 | convolution fusion | flops 270270464 | bytes 4718592 | tf_op jit(solution)/shard_map/dot_general | solution.py:37
  41.2 0.5 %multiply_reduce_fusion.1 = (f32[512]{0:T(512)S(1)}, f32[512]{0:T(512)S(1)}, f32[512]{0:T(512)S(1)}, f32[512]{0:T(512)S(1)}) fusion(f32[512,1024]{1,0:T(8,128)S(1)} %add_add_fusion, bf16[512,512]{1,0:T(8,128)(2,1)S(1)} %copy-done.1, bf16[512,512]{1,0:T(8,128)(2,1)S(1)} %copy-done.2), kind=kLoop, calls=%fused_computation.33 | loop fusion | flops 3143680 | bytes 3153920 | tf_op jit(solution)/shard_map/reduce_sum | solution.py:19
  41.8 0.5 %multiply_reduce_fusion = (f32[512]{0:T(512)S(1)}, f32[512,512]{1,0:T(8,128)S(1)}) fusion(bf16[64,512]{1,0:T(8,128)(2,1)S(1)} %get-tuple-element.96, bf16[64,512]{1,0:T(8,128)(2,1)S(1)} %get-tuple-element.94, f32[128,512]{1,0:T(8,128)S(1)} %fusion.55, f32[128,512]{1,0:T(8,128)S(1)} %fusion.54, f32[512,512]{1,0:T(8,128)S(1)} %convolution_add_fusion, ...), kind=kOutput, calls=%fused_computation.31 | convolution fusion | flops 69336576 | bytes 4327424 | tf_op jit(solution)/shard_map/dot_general | solution.py:37
  43.1 1.1 %convolution_convert_fusion = bf16[128,512]{1,0:T(8,128)(2,1)} fusion(bf16[512,512]{1,0:T(8,128)(2,1)S(1)} %multiply_convert_fusion, bf16[128,512]{1,0:T(8,128)(2,1)S(1)} %copy-done, bf16[512,512]{1,0:T(8,128)(2,1)S(1)} %get-tuple-element.17, f32[128,512]{1,0:T(8,128)S(1)} %convolution_bitcast_fusion.1), kind=kOutput, calls=%fused_computation.15 | convolution fusion | flops 134676480 | bytes 1572864 | tf_op jit(solution)/shard_map/dot_general | solution.py:45
  (82 shorter events, 8.6 us)
Async XLA Ops:
  0.0 42.9 %copy-start = (bf16[128,512]{1,0:T(8,128)(2,1)S(1)}, bf16[128,512]{1,0:T(8,128)(2,1)}, u32[]{:S(2)}) copy-start(bf16[128,512]{1,0:T(8,128)(2,1)} %param.9) | copy-start | bytes 393220
  0.0 6.7 %copy-start.2 = (bf16[512,512]{1,0:T(8,128)(2,1)S(1)}, bf16[512,512]{1,0:T(8,128)(2,1)}, u32[]{:S(2)}) copy-start(bf16[512,512]{1,0:T(8,128)(2,1)} %param.11) | copy-start | bytes 1572868
  0.0 7.0 %copy-start.1 = (bf16[512,512]{1,0:T(8,128)(2,1)S(1)}, bf16[512,512]{1,0:T(8,128)(2,1)}, u32[]{:S(2)}) copy-start(bf16[512,512]{1,0:T(8,128)(2,1)} %param.12) | copy-start | bytes 1572868
  2.0 9.4 %collective-permute-start.1 = (bf16[256,512]{1,0:T(8,128)(2,1)S(1)}, bf16[256,512]{1,0:T(8,128)(2,1)S(1)}, u32[]{:S(2)}, u32[]{:S(2)}) collective-permute-start(bf16[256,512]{1,0:T(8,128)(2,1)S(1)} %bitcast.51), channel_id=1, source_target_pairs={{0,2},{1,3},{2,6},{3,7},{6,10},{7,11},{10,14},{11,15},{14,12},{15,... | collective-permute-start | bytes 786440 | tf_op jit(solution)/shard_map/ppermute | solution.py:154
  5.0 8.1 %collective-permute-start.2 = (bf16[256,512]{1,0:T(8,128)(2,1)S(1)}, bf16[256,512]{1,0:T(8,128)(2,1)S(1)}, u32[]{:S(2)}, u32[]{:S(2)}) collective-permute-start(bf16[256,512]{1,0:T(8,128)(2,1)S(1)} %bitcast.52), channel_id=1, source_target_pairs={{0,4},{1,5},{2,0},{3,1},{6,2},{7,3},{10,6},{11,7},{14,10},{15,11},... | collective-permute-start | bytes 786440 | tf_op jit(solution)/shard_map/ppermute | solution.py:155
  5.2 1.5 %collective-permute-start = (bf16[256,512]{1,0:T(8,128)(2,1)S(1)}, bf16[256,512]{1,0:T(8,128)(2,1)S(1)}, u32[]{:S(2)}, u32[]{:S(2)}) collective-permute-start(bf16[256,512]{1,0:T(8,128)(2,1)S(1)} %bitcast.53), channel_id=1, source_target_pairs={{0,1},{1,0},{2,3},{3,2},{4,5},{5,4},{6,7},{7,6},{8,9},{9,8},{10,11... | collective-permute-start | bytes 786440 | tf_op jit(solution)/shard_map/ppermute | solution.py:143
  6.4 1.0 %copy-start.3 = (bf16[512,512]{1,0:T(8,128)(2,1)S(1)}, bf16[512,512]{1,0:T(8,128)(2,1)}, u32[]{:S(2)}) copy-start(bf16[512,512]{1,0:T(8,128)(2,1)} %param.13) | copy-start | bytes 1572868
  11.4 2.8 %collective-permute-start.3 = (bf16[256,512]{1,0:T(8,128)(2,1)S(1)}, bf16[256,512]{1,0:T(8,128)(2,1)S(1)}, u32[]{:S(2)}, u32[]{:S(2)}) collective-permute-start(bf16[256,512]{1,0:T(8,128)(2,1)S(1)} %collective-permute-done.1), channel_id=1, source_target_pairs={{0,1},{1,0},{2,3},{3,2},{4,5},{5,4},{6,7},{7,6},{8,9},{9,8},{10,11... | collective-permute-start | bytes 786440 | tf_op jit(solution)/shard_map/ppermute | solution.py:159
  11.4 8.7 %collective-permute-start.5 = (bf16[256,512]{1,0:T(8,128)(2,1)S(1)}, bf16[256,512]{1,0:T(8,128)(2,1)S(1)}, u32[]{:S(2)}, u32[]{:S(2)}) collective-permute-start(bf16[256,512]{1,0:T(8,128)(2,1)S(1)} %collective-permute-done.1), channel_id=1, source_target_pairs={{0,2},{1,3},{2,6},{3,7},{6,10},{7,11},{10,14},{11,15},{14,12},{15,... | collective-permute-start | bytes 786440 | tf_op jit(solution)/shard_map/ppermute | solution.py:154
  13.1 1.6 %collective-permute-start.4 = (bf16[256,512]{1,0:T(8,128)(2,1)S(1)}, bf16[256,512]{1,0:T(8,128)(2,1)S(1)}, u32[]{:S(2)}, u32[]{:S(2)}) collective-permute-start(bf16[256,512]{1,0:T(8,128)(2,1)S(1)} %collective-permute-done.2), channel_id=1, source_target_pairs={{0,1},{1,0},{2,3},{3,2},{4,5},{5,4},{6,7},{7,6},{8,9},{9,8},{10,11... | collective-permute-start | bytes 786440 | tf_op jit(solution)/shard_map/ppermute | solution.py:159
  13.4 8.5 %collective-permute-start.6 = (bf16[256,512]{1,0:T(8,128)(2,1)S(1)}, bf16[256,512]{1,0:T(8,128)(2,1)S(1)}, u32[]{:S(2)}, u32[]{:S(2)}) collective-permute-start(bf16[256,512]{1,0:T(8,128)(2,1)S(1)} %collective-permute-done.2), channel_id=1, source_target_pairs={{0,4},{1,5},{2,0},{3,1},{6,2},{7,3},{10,6},{11,7},{14,10},{15,11},... | collective-permute-start | bytes 786440 | tf_op jit(solution)/shard_map/ppermute | solution.py:155
  20.1 3.2 %collective-permute-start.7 = (bf16[256,512]{1,0:T(8,128)(2,1)S(1)}, bf16[256,512]{1,0:T(8,128)(2,1)S(1)}, u32[]{:S(2)}, u32[]{:S(2)}) collective-permute-start(bf16[256,512]{1,0:T(8,128)(2,1)S(1)} %collective-permute-done.5), channel_id=1, source_target_pairs={{0,1},{1,0},{2,3},{3,2},{4,5},{5,4},{6,7},{7,6},{8,9},{9,8},{10,11... | collective-permute-start | bytes 786440 | tf_op jit(solution)/shard_map/ppermute | solution.py:159
  20.1 8.7 %collective-permute-start.9 = (bf16[256,512]{1,0:T(8,128)(2,1)S(1)}, bf16[256,512]{1,0:T(8,128)(2,1)S(1)}, u32[]{:S(2)}, u32[]{:S(2)}) collective-permute-start(bf16[256,512]{1,0:T(8,128)(2,1)S(1)} %collective-permute-done.5), channel_id=1, source_target_pairs={{0,2},{1,3},{2,6},{3,7},{6,10},{7,11},{10,14},{11,15},{14,12},{15,... | collective-permute-start | bytes 786440 | tf_op jit(solution)/shard_map/ppermute | solution.py:154
  21.9 1.5 %collective-permute-start.8 = (bf16[256,512]{1,0:T(8,128)(2,1)S(1)}, bf16[256,512]{1,0:T(8,128)(2,1)S(1)}, u32[]{:S(2)}, u32[]{:S(2)}) collective-permute-start(bf16[256,512]{1,0:T(8,128)(2,1)S(1)} %collective-permute-done.6), channel_id=1, source_target_pairs={{0,1},{1,0},{2,3},{3,2},{4,5},{5,4},{6,7},{7,6},{8,9},{9,8},{10,11... | collective-permute-start | bytes 786440 | tf_op jit(solution)/shard_map/ppermute | solution.py:159
  22.1 9.7 %collective-permute-start.10 = (bf16[256,512]{1,0:T(8,128)(2,1)S(1)}, bf16[256,512]{1,0:T(8,128)(2,1)S(1)}, u32[]{:S(2)}, u32[]{:S(2)}) collective-permute-start(bf16[256,512]{1,0:T(8,128)(2,1)S(1)} %collective-permute-done.6), channel_id=1, source_target_pairs={{0,4},{1,5},{2,0},{3,1},{6,2},{7,3},{10,6},{11,7},{14,10},{15,11},... | collective-permute-start | bytes 786440 | tf_op jit(solution)/shard_map/ppermute | solution.py:155
  28.9 8.7 %collective-permute-start.13 = (bf16[128,512]{1,0:T(8,128)(2,1)S(1)}, bf16[128,512]{1,0:T(8,128)(2,1)S(1)}, u32[]{:S(2)}, u32[]{:S(2)}) collective-permute-start(bf16[128,512]{1,0:T(8,128)(2,1)S(1)} %slice.328), channel_id=1, source_target_pairs={{0,2},{1,3},{2,6},{3,7},{6,10},{7,11},{10,14},{11,15},{14,12},{15,... | collective-permute-start | bytes 393224 | tf_op jit(solution)/shard_map/ppermute | solution.py:149
  31.9 5.7 %collective-permute-start.14 = (bf16[128,512]{1,0:T(8,128)(2,1)S(1)}, bf16[128,512]{1,0:T(8,128)(2,1)S(1)}, u32[]{:S(2)}, u32[]{:S(2)}) collective-permute-start(bf16[128,512]{1,0:T(8,128)(2,1)S(1)} %slice.329), channel_id=1, source_target_pairs={{0,4},{1,5},{2,0},{3,1},{6,2},{7,3},{10,6},{11,7},{14,10},{15,11},... | collective-permute-start | bytes 393224 | tf_op jit(solution)/shard_map/ppermute | solution.py:150
  32.5 1.6 %collective-permute-start.11 = (bf16[256,512]{1,0:T(8,128)(2,1)S(1)}, bf16[256,512]{1,0:T(8,128)(2,1)S(1)}, u32[]{:S(2)}, u32[]{:S(2)}) collective-permute-start(bf16[256,512]{1,0:T(8,128)(2,1)S(1)} %collective-permute-done.9), channel_id=1, source_target_pairs={{0,1},{1,0},{2,3},{3,2},{4,5},{5,4},{6,7},{7,6},{8,9},{9,8},{10,11... | collective-permute-start | bytes 786440 | tf_op jit(solution)/shard_map/ppermute | solution.py:159
  32.6 1.9 %collective-permute-start.12 = (bf16[256,512]{1,0:T(8,128)(2,1)S(1)}, bf16[256,512]{1,0:T(8,128)(2,1)S(1)}, u32[]{:S(2)}, u32[]{:S(2)}) collective-permute-start(bf16[256,512]{1,0:T(8,128)(2,1)S(1)} %collective-permute-done.10), channel_id=1, source_target_pairs={{0,1},{1,0},{2,3},{3,2},{4,5},{5,4},{6,7},{7,6},{8,9},{9,8},{10,11... | collective-permute-start | bytes 786440 | tf_op jit(solution)/shard_map/ppermute | solution.py:159
  37.6 2.3 %collective-permute-start.15 = (bf16[128,512]{1,0:T(8,128)(2,1)S(1)}, bf16[128,512]{1,0:T(8,128)(2,1)S(1)}, u32[]{:S(2)}, u32[]{:S(2)}) collective-permute-start(bf16[128,512]{1,0:T(8,128)(2,1)S(1)} %collective-permute-done.13), channel_id=1, source_target_pairs={{0,1},{1,0},{2,3},{3,2},{4,5},{5,4},{6,7},{7,6},{8,9},{9,8},{10,11... | collective-permute-start | bytes 393224 | tf_op jit(solution)/shard_map/ppermute | solution.py:159
  37.8 2.2 %collective-permute-start.16 = (bf16[128,512]{1,0:T(8,128)(2,1)S(1)}, bf16[128,512]{1,0:T(8,128)(2,1)S(1)}, u32[]{:S(2)}, u32[]{:S(2)}) collective-permute-start(bf16[128,512]{1,0:T(8,128)(2,1)S(1)} %collective-permute-done.14), channel_id=1, source_target_pairs={{0,1},{1,0},{2,3},{3,2},{4,5},{5,4},{6,7},{7,6},{8,9},{9,8},{10,11... | collective-permute-start | bytes 393224 | tf_op jit(solution)/shard_map/ppermute | solution.py:159
